TPU v7x, 32 devices: a whole 2x2x4 slice. The times are simulated.
32 devices in a mesh: dp: 8 (over y, x, core), tensor: 4 (over z).
Axes of the slice: x: 2, y: 2, z: 4, core: 2. Of those that a mesh axis runs over, the one named last changes fastest.
Arguments:
- inputs: bfloat16 [4096, 2048], P('dp'), may hold values from -6 to 6
- active: int32 [4096], P('dp'), may hold values from 0 to 1, as said below
- block_table: int32 [16], replicated, may hold values from 0 to 15, as said below
- gain_one: bfloat16 [2048], replicated, may hold values from 0.099609375 to 1.8984375
- w_query: bfloat16 [2048, 2048], P(None, 'tensor'), may hold values from -0.125 to 0.125
- w_key: bfloat16 [2048, 1024], P(None, 'tensor'), may hold values from -0.125 to 0.125
- w_value: bfloat16 [2048, 1024], P(None, 'tensor'), may hold values from -0.125 to 0.125
- w_out: bfloat16 [2048, 2048], P('tensor'), may hold values from -4 to 4
- gain_two: bfloat16 [2048], replicated, may hold values from 0.099609375 to 1.8984375
- w_gate: bfloat16 [2048, 5632], P(None, 'tensor'), may hold values from -0.125 to 0.125
- w_up: bfloat16 [2048, 5632], P(None, 'tensor'), may hold values from -0.125 to 0.125
- w_down: bfloat16 [5632, 2048], P('tensor'), may hold values from -0.078125 to 0.078125
- cotangent: bfloat16 [4096, 2048], P('dp'), may hold values from -6 to 6
Outputs:
- output: bfloat16 [4096, 2048], P('dp')
- grad_input: float32 [4096, 2048], P('dp')
- grad_gain_one: float32 [2048], replicated
- grad_w_query: float32 [2048, 2048], P(None, 'tensor')
- grad_w_key: float32 [2048, 1024], P(None, 'tensor')
- grad_w_value: float32 [2048, 1024], P(None, 'tensor')
- grad_w_out: float32 [2048, 2048], P('tensor')
- grad_gain_two: float32 [2048], replicated
- grad_w_gate: float32 [2048, 5632], P(None, 'tensor')
- grad_w_up: float32 [2048, 5632], P(None, 'tensor')
- grad_w_down: float32 [5632, 2048], P('tensor')
Inputs may be any that keep to these rules, and one draw needn't show every extreme that they name: `active`: 0 or 1 for every token; the share of 1s differs from one causal block to another. `block_table`: each causal block appears once; entries 2i and 2i+1 sum to 15.
All inputs are finite; a program needn't handle non-finite values.
Results may differ from a plain program's by a relative error of at most 0.014.
Values may be sent and summed in bfloat16 or wider, within the bound.
No kernel may reach another device: no remote copies, remote signals or barrier semaphores. Data moves between devices by JAX's collectives and lax.ppermute only.
A program may use at most 256 MiB of HBM per device.

v0:
```python
import jax
import jax.numpy as jnp
from jax import lax
from jax.sharding import PartitionSpec as P


HEAD_DIM = 128


EPS = 1e-05
MASKED_SCORE = -1e30


def rms_norm(values, scales):
    return values * lax.rsqrt(jnp.mean(values * values, axis=-1, keepdims=True) + EPS) * scales


def rotate(values, cos_table, sin_table):
    middle = values.shape[-1] // 2
    leading = values[..., :middle]
    trailing = values[..., middle:]
    return jnp.concatenate(
        [leading * cos_table - trailing * sin_table, trailing * cos_table + leading * sin_table],
        axis=-1,
    )


def angles_of(positions, head_size):
    frequency = 10000.0 ** (-jnp.arange(0, head_size, 2, dtype=jnp.float32) / head_size)
    angles = positions.astype(jnp.float32)[:, None] * frequency[None, :]
    return (jnp.cos(angles)[:, None, :], jnp.sin(angles)[:, None, :])


def swiglu(gate_value, up_value):
    return jax.nn.silu(gate_value) * up_value


def left_trans(left, right):
    return lax.dot_general(
        left, right, (((0,), (0,)), ((), ())), preferred_element_type=jnp.float32
    )


def right_trans(left, right):
    return lax.dot_general(
        left, right, (((1,), (1,)), ((), ())), preferred_element_type=jnp.float32
    )


def partner_perm(axis_size, mask):
    return [(index, index ^ mask) for index in range(axis_size)]


def permute_sum(parts, dims, axis):
    size = lax.axis_size(axis)
    steps = size.bit_length() - 1
    assert 1 << steps == size
    me = lax.axis_index(axis)
    pieces = list(parts)
    for step in range(steps):
        bit = (me >> step) & 1
        keep, send = [], []
        for piece, dim in zip(pieces, dims):
            half = piece.shape[dim] // 2
            keep.append(lax.dynamic_slice_in_dim(piece, bit * half, half, axis=dim))
            send.append(
                lax.dynamic_slice_in_dim(piece, (1 - bit) * half, half, axis=dim).astype(jnp.bfloat16)
            )
        got = lax.ppermute(send, axis, partner_perm(size, 1 << step))
        pieces = [mine + theirs.astype(jnp.float32) for mine, theirs in zip(keep, got)]
    pieces = [piece.astype(jnp.bfloat16) for piece in pieces]
    for step in reversed(range(steps)):
        first = ((me >> step) & 1) == 0
        got = lax.ppermute(pieces, axis, partner_perm(size, 1 << step))
        pieces = [
            jnp.concatenate(
                [jnp.where(first, mine, theirs), jnp.where(first, theirs, mine)], axis=dim
            )
            for mine, theirs, dim in zip(pieces, got, dims)
        ]
    return [piece.astype(jnp.float32) for piece in pieces]


def permute_allsum(value, axis):
    size = lax.axis_size(axis)
    steps = size.bit_length() - 1
    for step in range(steps):
        value = value + lax.ppermute(value, axis, partner_perm(size, 1 << step))
    return value


def on_device(
    inputs,
    active,
    block_table,
    gain_one,
    w_query,
    w_key,
    w_value,
    w_out,
    gain_two,
    w_gate,
    w_up,
    w_down,
    cotangent,
):
    row_count = inputs.shape[0]
    local_heads = w_query.shape[1] // HEAD_DIM
    local_groups = w_key.shape[1] // HEAD_DIM
    group_size = local_heads // local_groups
    half_rows = row_count // 2
    length = row_count * lax.axis_size("dp")
    score_scale = HEAD_DIM ** (-0.5)
    key_pos = (
        block_table[:, None] * half_rows + jnp.arange(half_rows, dtype=jnp.int32)[None, :]
    ).reshape(length)
    row_start = lax.axis_index("dp") * row_count
    query_pos = lax.dynamic_slice_in_dim(key_pos, row_start, row_count)
    slot_ids = jnp.arange(length, dtype=jnp.int32)
    own_ids = row_start + jnp.arange(row_count, dtype=jnp.int32)
    cos_table, sin_table = angles_of(query_pos, HEAD_DIM)
    keep_rows = active.astype(jnp.float32)[:, None]
    source = inputs.astype(jnp.float32)
    normed_full, norm_one_back = jax.vjp(rms_norm, source, gain_one.astype(jnp.float32))
    normed = normed_full.astype(jnp.bfloat16)
    query_raw = jnp.dot(normed, w_query, preferred_element_type=jnp.float32).reshape(
        row_count, local_heads, HEAD_DIM
    )
    key_raw = jnp.dot(normed, w_key, preferred_element_type=jnp.float32).reshape(
        row_count, local_groups, HEAD_DIM
    )
    value_low = jnp.dot(normed, w_value, preferred_element_type=jnp.float32).astype(jnp.bfloat16)
    query_low = (
        rotate(query_raw, cos_table, sin_table)
        .reshape(row_count, local_heads * HEAD_DIM)
        .astype(jnp.bfloat16)
    )
    key_low = (
        rotate(key_raw, cos_table, sin_table)
        .reshape(row_count, local_groups * HEAD_DIM)
        .astype(jnp.bfloat16)
    )
    alive_low = active.astype(jnp.bfloat16)

    def allowed_of(alive_all):
        return (key_pos[None, :] <= query_pos[:, None]) & (
            (alive_all[None, :] > 0) | (slot_ids[None, :] == own_ids[:, None])
        )

    def head_scores(head_index, keys_all, allowed):
        query_part = query_low[:, head_index * HEAD_DIM : (head_index + 1) * HEAD_DIM]
        group_index = head_index // group_size
        key_part = keys_all[:, group_index * HEAD_DIM : (group_index + 1) * HEAD_DIM]
        raw_scores = right_trans(query_part, key_part) * score_scale
        return jnp.where(allowed, raw_scores, MASKED_SCORE)

    kv_width = local_groups * HEAD_DIM
    all_kv = lax.all_gather(
        jnp.concatenate([key_low, value_low], axis=1), "dp", axis=0, tiled=True
    )
    all_keys = all_kv[:, :kv_width]
    all_values = all_kv[:, kv_width:]
    all_alive = lax.all_gather(alive_low, "dp", axis=0, tiled=True)
    allowed_fwd = allowed_of(all_alive)
    mixed_parts = []
    lse_parts = []
    for head_index in range(local_heads):
        masked = head_scores(head_index, all_keys, allowed_fwd)
        row_max = jnp.max(masked, axis=1, keepdims=True)
        shifted = jnp.exp(masked - row_max)
        row_total = jnp.sum(shifted, axis=1, keepdims=True)
        probs_low = (shifted / row_total).astype(jnp.bfloat16)
        lse_parts.append(row_max + jnp.log(row_total))
        group_index = head_index // group_size
        value_part = all_values[:, group_index * HEAD_DIM : (group_index + 1) * HEAD_DIM]
        mixed_parts.append(jnp.dot(probs_low, value_part, preferred_element_type=jnp.float32))
    attended = jnp.concatenate(mixed_parts, axis=1).astype(jnp.bfloat16)
    (branch,) = permute_sum(
        [jnp.dot(attended, w_out, preferred_element_type=jnp.float32)], [0], "tensor"
    )
    middle = source + keep_rows * branch
    normed_two_full, norm_two_back = jax.vjp(rms_norm, middle, gain_two.astype(jnp.float32))
    normed_two = normed_two_full.astype(jnp.bfloat16)
    gate_value = jnp.dot(normed_two, w_gate, preferred_element_type=jnp.float32)
    up_value = jnp.dot(normed_two, w_up, preferred_element_type=jnp.float32)
    hidden_full, swiglu_back = jax.vjp(swiglu, gate_value, up_value)
    hidden = hidden_full.astype(jnp.bfloat16)
    down_part = jnp.dot(hidden, w_down, preferred_element_type=jnp.float32)
    grad_out = cotangent.astype(jnp.float32)

    def dp_sum(grads):
        return [lax.psum(grad.astype(jnp.bfloat16), "dp").astype(jnp.float32) for grad in grads]

    d_down = (keep_rows * grad_out).astype(jnp.bfloat16)
    grad_w_down = left_trans(hidden, d_down)
    d_hidden = right_trans(d_down, w_down)
    d_gate_full, d_up_full = swiglu_back(d_hidden)
    d_gate = d_gate_full.astype(jnp.bfloat16)
    d_up = d_up_full.astype(jnp.bfloat16)
    grad_w_gate = left_trans(normed_two, d_gate)
    grad_w_up = left_trans(normed_two, d_up)
    d_normed_two_part = right_trans(d_gate, w_gate) + right_trans(d_up, w_up)
    grad_w_gate, grad_w_up, grad_w_down, d_normed_two_part = lax.optimization_barrier(
        (grad_w_gate, grad_w_up, grad_w_down, d_normed_two_part)
    )
    grad_w_gate, grad_w_up, grad_w_down = dp_sum([grad_w_gate, grad_w_up, grad_w_down])
    (d_normed_two,) = permute_sum([d_normed_two_part], [0], "tensor")
    down_part, d_normed_two = lax.optimization_barrier((down_part, d_normed_two))
    (down_sum,) = permute_sum([down_part], [0], "tensor")
    d_middle_norm, grad_gain_two = norm_two_back(d_normed_two)
    grad_middle = grad_out + d_middle_norm
    d_branch = (keep_rows * grad_middle).astype(jnp.bfloat16)
    grad_w_out = left_trans(attended, d_branch)
    grad_w_gate, grad_w_up, grad_w_down, grad_w_out = lax.optimization_barrier(
        (grad_w_gate, grad_w_up, grad_w_down, grad_w_out)
    )
    d_attended = right_trans(d_branch, w_out).astype(jnp.bfloat16)
    back_keys, back_values = all_keys, all_values
    allowed_back = allowed_fwd
    d_query_parts = []
    d_key_parts = [jnp.zeros((length, HEAD_DIM), jnp.float32) for _ in range(local_groups)]
    d_value_parts = [jnp.zeros((length, HEAD_DIM), jnp.float32) for _ in range(local_groups)]
    for head_index in range(local_heads):
        group_index = head_index // group_size
        masked = head_scores(head_index, back_keys, allowed_back)
        probs = jnp.where(allowed_back, jnp.exp(masked - lse_parts[head_index]), 0.0)
        probs_low = probs.astype(jnp.bfloat16)
        d_out_part = d_attended[:, head_index * HEAD_DIM : (head_index + 1) * HEAD_DIM]
        key_part = back_keys[:, group_index * HEAD_DIM : (group_index + 1) * HEAD_DIM]
        value_part = back_values[:, group_index * HEAD_DIM : (group_index + 1) * HEAD_DIM]
        query_part = query_low[:, head_index * HEAD_DIM : (head_index + 1) * HEAD_DIM]
        d_probs = right_trans(d_out_part, value_part)
        row_delta = jnp.sum(probs * d_probs, axis=1, keepdims=True)
        d_scores = (probs * (d_probs - row_delta)).astype(jnp.bfloat16)
        d_query_parts.append(
            jnp.dot(d_scores, key_part, preferred_element_type=jnp.float32) * score_scale
        )
        d_key_parts[group_index] = (
            d_key_parts[group_index] + left_trans(d_scores, query_part) * score_scale
        )
        d_value_parts[group_index] = d_value_parts[group_index] + left_trans(probs_low, d_out_part)
    d_key_all = jnp.concatenate(d_key_parts, axis=1)
    d_value_all = jnp.concatenate(d_value_parts, axis=1)
    d_kv_cat = jnp.concatenate([d_key_all, d_value_all], axis=1).astype(jnp.bfloat16)
    d_kv_own = lax.psum_scatter(
        d_kv_cat,
        "dp",
        scatter_dimension=0,
        tiled=True,
    ).astype(jnp.float32)
    d_kv_own, grad_w_out = lax.optimization_barrier((d_kv_own, grad_w_out))
    (grad_w_out,) = dp_sum([grad_w_out])
    d_key_own = d_kv_own[:, :kv_width]
    d_value_own = d_kv_own[:, kv_width:]
    d_queries = jnp.concatenate(d_query_parts, axis=1).reshape(row_count, local_heads, HEAD_DIM)
    d_query_low = (
        rotate(d_queries, cos_table, -sin_table)
        .reshape(row_count, local_heads * HEAD_DIM)
        .astype(jnp.bfloat16)
    )
    d_key_low = (
        rotate(d_key_own.reshape(row_count, local_groups, HEAD_DIM), cos_table, -sin_table)
        .reshape(row_count, local_groups * HEAD_DIM)
        .astype(jnp.bfloat16)
    )
    d_value_low = d_value_own.astype(jnp.bfloat16)
    grad_w_query = left_trans(normed, d_query_low)
    grad_w_key = left_trans(normed, d_key_low)
    grad_w_value = left_trans(normed, d_value_low)
    d_normed_part = (
        right_trans(d_query_low, w_query)
        + right_trans(d_key_low, w_key)
        + right_trans(d_value_low, w_value)
    )
    down_sum, d_normed_part = lax.optimization_barrier((down_sum, d_normed_part))
    output = (middle + keep_rows * down_sum).astype(jnp.bfloat16)
    (d_normed,) = permute_sum([d_normed_part], [0], "tensor")
    d_source_norm, grad_gain_one = norm_one_back(d_normed)
    grad_input = grad_middle + d_source_norm
    grad_gain_one = permute_allsum(grad_gain_one, "dp")
    grad_gain_two = permute_allsum(grad_gain_two, "dp")
    grad_w_query, grad_w_key, grad_w_value = dp_sum([grad_w_query, grad_w_key, grad_w_value])
    return (
        output,
        grad_input,
        grad_gain_one,
        grad_w_query,
        grad_w_key,
        grad_w_value,
        grad_w_out,
        grad_gain_two,
        grad_w_gate,
        grad_w_up,
        grad_w_down,
    )


def solution(mesh):
    placed = (
        P("dp", None),
        P("dp"),
        P(),
        P(),
        P(None, "tensor"),
        P(None, "tensor"),
        P(None, "tensor"),
        P("tensor", None),
        P(),
        P(None, "tensor"),
        P(None, "tensor"),
        P("tensor", None),
        P("dp", None),
    )
    return jax.shard_map(
        on_device,
        mesh=mesh,
        in_specs=placed,
        out_specs=(
            P("dp", None),
            P("dp", None),
            P(),
            P(None, "tensor"),
            P(None, "tensor"),
            P(None, "tensor"),
            P("tensor", None),
            P(),
            P(None, "tensor"),
            P(None, "tensor"),
            P("tensor", None),
        ),
        check_vma=False,
    )
```

profile of v0, /device:TPU:0, one launch (start us, length us, event | category | flops | bytes accessed | tf_op | source)
XLA Modules:
  0.0 795.5 jit_solution(4594292434458131571)
XLA Ops:
  11.1 3.6 fusion.92
  19.1 10.6 %all-gather = bf16[8,1,512]{2,1,0:T(2,128)(2,1)S(1)} all-gather(bf16[1,1,512]{2,1,0:T(2,128)(2,1)S(1)} %reshape.231), channel_id=1, replica_groups=mesh['dp'=8,'tensor'=4] {'dp'}, dimensions={0}, use_global_device_ids=true | all-gather | bytes 9216 | tf_op jit(solution)/shard_map/all_gather | solution.py:163
  29.8 3.7 fusion.94
  33.8 25.4 %all-gather.3.cloned.1.call-done = bf16[4096,512]{0,1:T(8,128)(2,1)} async-done(((bf16[512,512]{0,1:T(8,128)(2,1)}), bf16[4096,512]{0,1:T(8,128)(2,1)}) %all-gather.3.cloned.1.call-update) | async-done | bytes 4194320 | tf_op jit(solution)/shard_map/all_gather | solution.py:158
  59.2 4.7 fusion.105
  65.2 5.5 fusion.104
  72.0 5.9 fusion.103
  79.3 7.7 fusion.102
  87.0 4.6 fusion.5
  91.6 3.2 fusion.37
  94.8 3.3 fusion.36
  107.4 23.9 %collective-permute-done = bf16[256,2048]{1,0:T(8,128)(2,1)} collective-permute-done((bf16[256,2048]{1,0:T(8,128)(2,1)S(1)}, bf16[256,2048]{1,0:T(8,128)(2,1)}, u32[]{:S(2)}, u32[]{:S(2)}) %collective-permute-start) | collective-permute-done | bytes 1048608 | tf_op jit(solution)/shard_map/ppermute | solution.py:69
  137.4 23.0 %collective-permute-done.1 = bf16[128,2048]{1,0:T(8,128)(2,1)S(1)} collective-permute-done((bf16[128,2048]{1,0:T(8,128)(2,1)S(1)}, bf16[128,2048]{1,0:T(8,128)(2,1)S(1)}, u32[]{:S(2)}, u32[]{:S(2)}) %collective-permute-start.1) | collective-permute-done | bytes 524320 | tf_op jit(solution)/shard_map/ppermute | solution.py:69
  161.8 25.0 %collective-permute-done.2 = bf16[128,2048]{1,0:T(8,128)(2,1)S(1)} collective-permute-done((bf16[128,2048]{1,0:T(8,128)(2,1)S(1)}, bf16[128,2048]{1,0:T(8,128)(2,1)S(1)}, u32[]{:S(2)}, u32[]{:S(2)}) %collective-permute-start.2) | collective-permute-done | bytes 524320 | tf_op jit(solution)/shard_map/ppermute | solution.py:74
  187.9 6.8 fusion.40
  194.7 16.7 %collective-permute-done.3 = bf16[256,2048]{1,0:T(8,128)(2,1)} collective-permute-done((bf16[256,2048]{1,0:T(8,128)(2,1)S(1)}, bf16[256,2048]{1,0:T(8,128)(2,1)}, u32[]{:S(2)}, u32[]{:S(2)}) %collective-permute-start.3) | collective-permute-done | bytes 1048608 | tf_op jit(solution)/shard_map/ppermute | solution.py:74
  215.6 3.4 fusion.106
  219.1 4.6 multiply_convert_fusion.6
  223.7 3.4 fusion.110
  227.1 5.5 fusion.108
  232.6 5.3 fusion.109
  237.9 5.0 convolution_add_fusion.4
  242.9 5.2 fusion.38
  250.2 22.4 %collective-permute-done.4 = bf16[256,2048]{1,0:T(8,128)(2,1)S(1)} collective-permute-done((bf16[256,2048]{1,0:T(8,128)(2,1)S(1)}, bf16[256,2048]{1,0:T(8,128)(2,1)S(1)}, u32[]{:S(2)}, u32[]{:S(2)}) %collective-permute-start.4) | collective-permute-done | bytes 1048608 | tf_op jit(solution)/shard_map/ppermute | solution.py:69
  274.5 3.5 collective-permute-start.5
  278.0 21.9 %collective-permute-done.5 = bf16[128,2048]{1,0:T(8,128)(2,1)S(1)} collective-permute-done((bf16[128,2048]{1,0:T(8,128)(2,1)S(1)}, bf16[128,2048]{1,0:T(8,128)(2,1)S(1)}, u32[]{:S(2)}, u32[]{:S(2)}) %collective-permute-start.5) | collective-permute-done | bytes 524320 | tf_op jit(solution)/shard_map/ppermute | solution.py:69
  300.2 25.4 %collective-permute-done.6 = bf16[128,2048]{1,0:T(8,128)(2,1)S(1)} collective-permute-done((bf16[128,2048]{1,0:T(8,128)(2,1)S(1)}, bf16[128,2048]{1,0:T(8,128)(2,1)S(1)}, u32[]{:S(2)}, u32[]{:S(2)}) %collective-permute-start.6) | collective-permute-done | bytes 524320 | tf_op jit(solution)/shard_map/ppermute | solution.py:74
  328.8 6.3 fusion.107
  335.0 16.9 %collective-permute-done.7 = bf16[256,2048]{1,0:T(8,128)(2,1)} collective-permute-done((bf16[256,2048]{1,0:T(8,128)(2,1)}, bf16[256,2048]{1,0:T(8,128)(2,1)}, u32[]{:S(2)}, u32[]{:S(2)}) %collective-permute-start.7) | collective-permute-done | bytes 1048608 | tf_op jit(solution)/shard_map/ppermute | solution.py:74
  355.7 3.0 multiply_reduce_fusion.4
  358.7 3.4 convert_add_fusion.1
  366.2 4.6 fusion.42
  370.7 5.5 fusion.44
  376.3 5.0 fusion.54
  381.4 22.0 %multiply_reduce_fusion.2 = (f32[512]{0:T(512)S(1)}, f32[512]{0:T(512)S(1)}, f32[512]{0:T(512)S(1)}, f32[512]{0:T(512)}, f32[512,4096]{1,0:T(8,128)}) fusion(f32[512,4096]{1,0:T(8,128)S(1)} %bitcast.50, f32[512]{0:T(512)S(1)} %copy-done.78, s32[512]{0:T(512)S(1)} %copy-done.75, pred[4096]{0:T(1024)(128)(4,1)S(1)} %bitcast.94, s32[512]{0:T(512)S(1)} %copy-done.72, ...), kind=kOutput, calls=%fused_computation.7 | convolution fusion | flops 578811904 | bytes 68329472 | tf_op jit(solution)/shard_map/dot_general | solution.py:45
  403.4 18.7 %multiply_convert_fusion.2 = (bf16[512,4096]{1,0:T(8,128)(2,1)}, bf16[512,4096]{1,0:T(8,128)(2,1)}, bf16[512,4096]{1,0:T(8,128)(2,1)}) fusion(f32[512,4096]{1,0:T(8,128)} %get-tuple-element.101, f32[512]{0:T(512)S(1)} %get-tuple-element.43, f32[512,4096]{1,0:T(8,128)S(1)} %bitcast.50, f32[512]{0:T(512)S(1)} %copy-done.78, s32[512]{0:T(512)S(1)} %copy-done.75, ...), kind=kLoop, calls=%fused_computation.6 | loop fusion | flops 39845888 | bytes 62951424 | tf_op jit(solution)/shard_map/convert_element_type | solution.py:234
  422.1 3.3 fusion.77
  430.5 9.3 %multiply_convert_fusion = bf16[512,4096]{1,0:T(8,128)(2,1)} fusion(f32[512,4096]{1,0:T(8,128)} %fusion.42, f32[512]{0:T(512)S(1)} %copy-done.90, f32[512,4096]{1,0:T(8,128)S(1)} %bitcast.58, f32[512]{0:T(512)S(1)} %copy-done.87, s32[512]{0:T(512)S(1)} %copy-done.76, pred[4096]{0:T(1024)(128)(4,1)S(1)} %bitcast.96, s32[512]{0:T(512)S(1)} %copy-done.73, ...), kind=kLoop, calls=%fused_computation | loop fusion | flops 18874368 | bytes 21000192 | tf_op jit(solution)/shard_map/convert_element_type | solution.py:234
  439.8 3.2 fusion.13
  443.0 4.9 fusion.24
  448.0 3.6 fusion.21
  451.6 3.7 fusion.10
  455.3 3.9 fusion.11
  464.9 3.2 convolution_multiply_fusion
  468.1 19.7 %collective-permute-done.9 = bf16[128,2048]{1,0:T(8,128)(2,1)S(1)} collective-permute-done((bf16[128,2048]{1,0:T(8,128)(2,1)S(1)}, bf16[128,2048]{1,0:T(8,128)(2,1)S(1)}, u32[]{:S(2)}, u32[]{:S(2)}) %collective-permute-start.9) | collective-permute-done | bytes 524320 | tf_op jit(solution)/shard_map/ppermute | solution.py:69
  491.2 22.1 %collective-permute-done.10 = bf16[128,2048]{1,0:T(8,128)(2,1)S(1)} collective-permute-done((bf16[128,2048]{1,0:T(8,128)(2,1)S(1)}, bf16[128,2048]{1,0:T(8,128)(2,1)S(1)}, u32[]{:S(2)}, u32[]{:S(2)}) %collective-permute-start.10) | collective-permute-done | bytes 524320 | tf_op jit(solution)/shard_map/ppermute | solution.py:74
  516.0 2.7 fusion.81
  518.7 18.6 %collective-permute-done.11 = bf16[256,2048]{1,0:T(8,128)(2,1)S(1)} collective-permute-done((bf16[256,2048]{1,0:T(8,128)(2,1)S(1)}, bf16[256,2048]{1,0:T(8,128)(2,1)S(1)}, u32[]{:S(2)}, u32[]{:S(2)}) %collective-permute-start.11) | collective-permute-done | bytes 1048608 | tf_op jit(solution)/shard_map/ppermute | solution.py:74
  537.6 2.6 maximum_convert_fusion.1
  540.2 9.3 %all-reduce.7.cloned.1.call-done = (bf16[2048,1408]{1,0:T(8,128)(2,1)}, bf16[2048,1408]{1,0:T(8,128)(2,1)}, bf16[1408,2048]{1,0:T(8,128)(2,1)}) async-done(((bf16[2048,1408]{1,0:T(8,128)(2,1)}, bf16[2048,1408]{1,0:T(8,128)(2,1)}, bf16[1408,2048]{1,0:T(8,128)(2,1)}), (bf16[2048,1408]{1,0:T(8,128)(2,1)}, bf16[2048,1408]{1,0:T(8,128)(2,1)}, bf16[1408,2048]{1,0:T(8,128)(2,1)})) %all-reduce.7.cloned.1.call-update) | async-done | bytes 17301520 | tf_op jit(solution)/shard_map/psum | solution.py:192
  549.6 8.9 %convert_element_type.274 = f32[2048,1408]{1,0:T(8,128)} convert(bf16[2048,1408]{1,0:T(8,128)(2,1)} %get-tuple-element.51) | non-fusion elementwise | flops 2883584 | bytes 17301504 | tf_op jit(solution)/shard_map/convert_element_type | solution.py:192
  558.5 5.9 convert_element_type.276
  564.4 6.0 convert_element_type.278
  570.4 33.7 %reduce-scatter.2.cloned.1.call-done = bf16[512,512]{0,1:T(8,128)(2,1)} async-done(((bf16[4096,512]{0,1:T(8,128)(2,1)}), bf16[512,512]{0,1:T(8,128)(2,1)}) %reduce-scatter.2.cloned.1.call-update) | async-done | bytes 524304 | tf_op jit(solution)/shard_map/reduce_scatter | solution.py:245
  611.3 23.3 %collective-permute-done.12 = bf16[256,2048]{1,0:T(8,128)(2,1)S(1)} collective-permute-done((bf16[256,2048]{1,0:T(8,128)(2,1)S(1)}, bf16[256,2048]{1,0:T(8,128)(2,1)S(1)}, u32[]{:S(2)}, u32[]{:S(2)}) %collective-permute-start.12) | collective-permute-done | bytes 1048608 | tf_op jit(solution)/shard_map/ppermute | solution.py:69
  637.4 2.8 convolution_convert_fusion
  642.2 17.6 %collective-permute-done.13 = bf16[128,2048]{1,0:T(8,128)(2,1)S(1)} collective-permute-done((bf16[128,2048]{1,0:T(8,128)(2,1)S(1)}, bf16[128,2048]{1,0:T(8,128)(2,1)S(1)}, u32[]{:S(2)}, u32[]{:S(2)}) %collective-permute-start.13) | collective-permute-done | bytes 524320 | tf_op jit(solution)/shard_map/ppermute | solution.py:69
  662.0 23.0 %collective-permute-done.14 = bf16[128,2048]{1,0:T(8,128)(2,1)S(1)} collective-permute-done((bf16[128,2048]{1,0:T(8,128)(2,1)S(1)}, bf16[128,2048]{1,0:T(8,128)(2,1)S(1)}, u32[]{:S(2)}, u32[]{:S(2)}) %collective-permute-start.14) | collective-permute-done | bytes 524320 | tf_op jit(solution)/shard_map/ppermute | solution.py:74
  688.0 2.5 collective-permute-done.20
  691.9 16.8 %collective-permute-done.15 = bf16[256,2048]{1,0:T(8,128)(2,1)S(1)} collective-permute-done((bf16[256,2048]{1,0:T(8,128)(2,1)S(1)}, bf16[256,2048]{1,0:T(8,128)(2,1)S(1)}, u32[]{:S(2)}, u32[]{:S(2)}) %collective-permute-start.15) | collective-permute-done | bytes 1048608 | tf_op jit(solution)/shard_map/ppermute | solution.py:74
  711.4 55.4 %all-reduce.5.cloned.1.call-done = (bf16[2048,512]{1,0:T(8,128)(2,1)}, bf16[2048,256]{1,0:T(8,128)(2,1)}, bf16[2048,256]{1,0:T(8,128)(2,1)}, bf16[512,2048]{1,0:T(8,128)(2,1)}) async-done(((bf16[2048,512]{1,0:T(8,128)(2,1)}, bf16[2048,256]{1,0:T(8,128)(2,1)}, bf16[2048,256]{1,0:T(8,128)(2,1)}, bf16[512,2048]{1,0:T(8,128)(2,1)}), (bf16[2048,512]{1,0:T(8,128)(2,1)}, bf16[2048,256]{1,0:T(8,128)(2,1)}, ...) | async-done | bytes 6291472 | tf_op jit(solution)/shard_map/psum | solution.py:192
  766.8 4.3 convert_element_type.288
  771.2 2.7 convert_element_type.294
  781.8 6.3 fusion.17
  (356 shorter events, 96.0 us)
Async XLA Ops:
  7.2 95.2 %copy-start = (bf16[512,2048]{1,0:T(8,128)(2,1)S(1)}, bf16[512,2048]{1,0:T(8,128)(2,1)}, u32[]{:S(2)}) copy-start(bf16[512,2048]{1,0:T(8,128)(2,1)} %param.20) | copy-start | bytes 6291460
  7.2 52.0 %all-gather.3.cloned.1.call-start = ((), (), s32[]{:S(2)}) async-start(), calls=%async_computation.1 | async-start | bytes 4718592 | tf_op jit(solution)/shard_map/all_gather | solution.py:158
  8.2 71.1 %copy-start.65 = (s32[2,2,8,128]{3,1,2,0:T(2,128)}, s32[2,2,8,128]{3,1,2,0:T(2,128)S(1)}, u32[]{:S(2)}) copy-start(s32[2,2,8,128]{3,1,2,0:T(2,128)S(1)} %copy.24) | copy-start | bytes 49156
  10.4 19.4 %copy-start.84 = (f32[512]{0:T(512)}, f32[512]{0:T(512)S(1)}, u32[]{:S(2)}) copy-start(f32[512]{0:T(512)S(1)} %fusion.84) | copy-start | bytes 6148
  11.1 18.7 %copy-start.67 = (f32[2048]{0:T(1024)}, f32[2048]{0:T(1024)S(1)}, u32[]{:S(2)}) copy-start(f32[2048]{0:T(1024)S(1)} %convert_element_type.226) | copy-start | bytes 24580
  15.7 63.5 %copy-start.71 = (s32[512]{0:T(512)}, s32[512]{0:T(512)S(1)}, u32[]{:S(2)}) copy-start(s32[512]{0:T(512)S(1)} %get-tuple-element.55) | copy-start | bytes 6148
  16.9 16.6 %copy-start.42 = (f32[512,64]{0,1:T(8,128)}, f32[512,64]{0,1:T(8,128)S(1)}, u32[]{:S(2)}) copy-start(f32[512,64]{0,1:T(8,128)S(1)} %get-tuple-element.90) | copy-start | bytes 393220
  19.0 530.6 %all-reduce.7.cloned.1.call-start = ((), (), s32[]{:S(2)}) async-start(), calls=%async_computation.4 | async-start | bytes 34603008 | tf_op jit(solution)/shard_map/psum | solution.py:192
  29.7 49.5 %copy-start.69 = (pred[1,4,8,128]{3,1,2,0:T(4,128)(4,1)}, pred[1,4,8,128]{3,1,2,0:T(4,128)(4,1)S(1)}, u32[]{:S(2)}) copy-start(pred[1,4,8,128]{3,1,2,0:T(4,128)(4,1)S(1)} %copy.25) | copy-start | bytes 12292
  29.8 49.5 %copy-start.74 = (s32[512]{0:T(512)}, s32[512]{0:T(512)S(1)}, u32[]{:S(2)}) copy-start(s32[512]{0:T(512)S(1)} %iota_add_fusion) | copy-start | bytes 6148
  33.8 45.5 %copy-start.45 = (bf16[512,4,128]{0,2,1:T(8,128)(2,1)}, bf16[512,4,128]{0,2,1:T(8,128)(2,1)S(1)}, u32[]{:S(2)}) copy-start(bf16[512,4,128]{0,2,1:T(8,128)(2,1)S(1)} %pad_maximum_fusion.7) | copy-start | bytes 1572868
  63.9 27.7 %copy-start.8 = (f32[512,4096]{1,0:T(8,128)}, f32[512,4096]{1,0:T(8,128)S(1)}, u32[]{:S(2)}) copy-start(f32[512,4096]{1,0:T(8,128)S(1)} %get-tuple-element.100) | copy-start | bytes 25165828
  70.7 24.1 %copy-start.7 = (f32[512,4096]{1,0:T(8,128)}, f32[512,4096]{1,0:T(8,128)S(1)}, u32[]{:S(2)}) copy-start(f32[512,4096]{1,0:T(8,128)S(1)} %get-tuple-element.98) | copy-start | bytes 25165828
  77.9 20.2 %copy-start.9 = (f32[512,4096]{1,0:T(8,128)}, f32[512,4096]{1,0:T(8,128)S(1)}, u32[]{:S(2)}) copy-start(f32[512,4096]{1,0:T(8,128)S(1)} %get-tuple-element.96) | copy-start | bytes 25165828
  105.9 25.5 %collective-permute-start = (bf16[256,2048]{1,0:T(8,128)(2,1)S(1)}, bf16[256,2048]{1,0:T(8,128)(2,1)}, u32[]{:S(2)}, u32[]{:S(2)}) collective-permute-start(bf16[256,2048]{1,0:T(8,128)(2,1)S(1)} %dynamic-slice_convert_fusion.3), channel_id=1, source_target_pairs={{0,1},{1,0},{2,3},{3,2},{4,5},{5,4},{6,7},{7,6},{8,9},{9,8},{10,11... | collective-permute-start | bytes 3145736 | tf_op jit(solution)/shard_map/ppermute | solution.py:69
  134.9 53.0 %copy-start.91 = (bf16[2048]{0:T(1024)(128)(2,1)S(1)}, bf16[2048]{0:T(1024)(128)(2,1)}, u32[]{:S(2)}) copy-start(bf16[2048]{0:T(1024)(128)(2,1)} %param.21) | copy-start | bytes 12292
  134.9 25.4 %collective-permute-start.1 = (bf16[128,2048]{1,0:T(8,128)(2,1)S(1)}, bf16[128,2048]{1,0:T(8,128)(2,1)S(1)}, u32[]{:S(2)}, u32[]{:S(2)}) collective-permute-start(bf16[128,2048]{1,0:T(8,128)(2,1)S(1)} %dynamic-slice_convert_fusion.7), channel_id=1, source_target_pairs={{0,2},{1,3},{2,0},{3,1},{4,6},{5,7},{6,4},{7,5},{8,10},{9,11},{10,... | collective-permute-start | bytes 1572872 | tf_op jit(solution)/shard_map/ppermute | solution.py:69
  161.7 25.1 %collective-permute-start.2 = (bf16[128,2048]{1,0:T(8,128)(2,1)S(1)}, bf16[128,2048]{1,0:T(8,128)(2,1)S(1)}, u32[]{:S(2)}, u32[]{:S(2)}) collective-permute-start(bf16[128,2048]{1,0:T(8,128)(2,1)S(1)} %add_convert_fusion.4), channel_id=1, source_target_pairs={{0,2},{1,3},{2,0},{3,1},{4,6},{5,7},{6,4},{7,5},{8,10},{9,11},{10,... | collective-permute-start | bytes 1572872 | tf_op jit(solution)/shard_map/ppermute | solution.py:74
  187.9 23.6 %collective-permute-start.3 = (bf16[256,2048]{1,0:T(8,128)(2,1)S(1)}, bf16[256,2048]{1,0:T(8,128)(2,1)}, u32[]{:S(2)}, u32[]{:S(2)}) collective-permute-start(bf16[256,2048]{1,0:T(8,128)(2,1)S(1)} %pad_maximum_fusion.2), channel_id=1, source_target_pairs={{0,1},{1,0},{2,3},{3,2},{4,5},{5,4},{6,7},{7,6},{8,9},{9,8},{10,11... | collective-permute-start | bytes 3145736 | tf_op jit(solution)/shard_map/ppermute | solution.py:74
  187.9 23.6 %copy-start.35 = (bf16[128,2048]{1,0:T(8,128)(2,1)S(1)}, bf16[128,2048]{1,0:T(8,128)(2,1)}, u32[]{:S(2)}) copy-start(bf16[128,2048]{1,0:T(8,128)(2,1)} %copy-done.34) | copy-start | bytes 1572868
  187.9 23.6 %copy-start.37 = (bf16[128,2048]{1,0:T(8,128)(2,1)S(1)}, bf16[128,2048]{1,0:T(8,128)(2,1)}, u32[]{:S(2)}) copy-start(bf16[128,2048]{1,0:T(8,128)(2,1)} %copy-done.36) | copy-start | bytes 1572868
  194.7 18.6 %copy-start.3 = (bf16[512,2048]{1,0:T(8,128)(2,1)S(1)}, bf16[512,2048]{1,0:T(8,128)(2,1)}, u32[]{:S(2)}) copy-start(bf16[512,2048]{1,0:T(8,128)(2,1)} %param.13) | copy-start | bytes 6291460
  213.3 145.4 %copy-start.10 = (bf16[256,2048]{1,0:T(8,128)(2,1)}, bf16[256,2048]{1,0:T(8,128)(2,1)S(1)}, u32[]{:S(2)}) copy-start(bf16[256,2048]{1,0:T(8,128)(2,1)S(1)} %get-tuple-element.67) | copy-start | bytes 3145732
  223.7 19.2 %copy-start.94 = (bf16[512,1408]{1,0:T(8,128)(2,1)}, bf16[512,1408]{1,0:T(8,128)(2,1)S(1)}, u32[]{:S(2)}) copy-start(bf16[512,1408]{1,0:T(8,128)(2,1)S(1)} %get-tuple-element.58) | copy-start | bytes 4325380
  249.8 22.7 %collective-permute-start.4 = (bf16[256,2048]{1,0:T(8,128)(2,1)S(1)}, bf16[256,2048]{1,0:T(8,128)(2,1)S(1)}, u32[]{:S(2)}, u32[]{:S(2)}) collective-permute-start(bf16[256,2048]{1,0:T(8,128)(2,1)S(1)} %dynamic-slice_convert_fusion.2), channel_id=1, source_target_pairs={{0,1},{1,0},{2,3},{3,2},{4,5},{5,4},{6,7},{7,6},{8,9},{9,8},{10,11... | collective-permute-start | bytes 3145736 | tf_op jit(solution)/shard_map/ppermute | solution.py:69
  274.5 25.4 %collective-permute-start.5 = (bf16[128,2048]{1,0:T(8,128)(2,1)S(1)}, bf16[128,2048]{1,0:T(8,128)(2,1)S(1)}, u32[]{:S(2)}, u32[]{:S(2)}) collective-permute-start(bf16[128,2048]{1,0:T(8,128)(2,1)S(1)} %dynamic-slice_convert_fusion.6), channel_id=1, source_target_pairs={{0,2},{1,3},{2,0},{3,1},{4,6},{5,7},{6,4},{7,5},{8,10},{9,11},{10,... | collective-permute-start | bytes 1572872 | tf_op jit(solution)/shard_map/ppermute | solution.py:69
  300.1 25.4 %collective-permute-start.6 = (bf16[128,2048]{1,0:T(8,128)(2,1)S(1)}, bf16[128,2048]{1,0:T(8,128)(2,1)S(1)}, u32[]{:S(2)}, u32[]{:S(2)}) collective-permute-start(bf16[128,2048]{1,0:T(8,128)(2,1)S(1)} %add_convert_fusion.3), channel_id=1, source_target_pairs={{0,2},{1,3},{2,0},{3,1},{4,6},{5,7},{6,4},{7,5},{8,10},{9,11},{10,... | collective-permute-start | bytes 1572872 | tf_op jit(solution)/shard_map/ppermute | solution.py:74
  327.5 24.5 %collective-permute-start.7 = (bf16[256,2048]{1,0:T(8,128)(2,1)}, bf16[256,2048]{1,0:T(8,128)(2,1)}, u32[]{:S(2)}, u32[]{:S(2)}) collective-permute-start(bf16[256,2048]{1,0:T(8,128)(2,1)} %pad_maximum_fusion.3), channel_id=1, source_target_pairs={{0,1},{1,0},{2,3},{3,2},{4,5},{5,4},{6,7},{7,6},{8,9},{9,8},{10,11... | collective-permute-start | bytes 3145736 | tf_op jit(solution)/shard_map/ppermute | solution.py:74
  328.7 275.4 %reduce-scatter.2.cloned.1.call-start = ((), (), s32[]{:S(2)}) async-start(), calls=%async_computation.2 | async-start | bytes 4718592 | tf_op jit(solution)/shard_map/reduce_scatter | solution.py:245
  328.7 23.2 %copy-start.31 = (bf16[128,2048]{1,0:T(8,128)(2,1)S(1)}, bf16[128,2048]{1,0:T(8,128)(2,1)}, u32[]{:S(2)}) copy-start(bf16[128,2048]{1,0:T(8,128)(2,1)} %copy-done.30) | copy-start | bytes 1572868
  328.8 23.2 %copy-start.33 = (bf16[128,2048]{1,0:T(8,128)(2,1)S(1)}, bf16[128,2048]{1,0:T(8,128)(2,1)}, u32[]{:S(2)}) copy-start(bf16[128,2048]{1,0:T(8,128)(2,1)} %copy-done.32) | copy-start | bytes 1572868
  335.0 28.4 %copy-start.44 = (f32[512,2048]{1,0:T(8,128)}, f32[512,2048]{1,0:T(8,128)S(1)}, u32[]{:S(2)}) copy-start(f32[512,2048]{1,0:T(8,128)S(1)} %fusion.107) | copy-start | bytes 12582916
  364.7 96.9 %collective-permute-start.8 = (bf16[256,2048]{1,0:T(8,128)(2,1)}, bf16[256,2048]{1,0:T(8,128)(2,1)}, u32[]{:S(2)}, u32[]{:S(2)}) collective-permute-start(bf16[256,2048]{1,0:T(8,128)(2,1)} %dynamic-slice_convert_fusion.1), channel_id=1, source_target_pairs={{0,1},{1,0},{2,3},{3,2},{4,5},{5,4},{6,7},{7,6},{8,9},{9,8},{10,11... | collective-permute-start | bytes 3145736 | tf_op jit(solution)/shard_map/ppermute | solution.py:69
  366.2 15.2 %slice-start.2 = ((s8[8388608]{0:T(1024)(128)(4,1)}), s8[4194304]{0:T(1024)(128)(4,1)S(1)}, s32[]{:S(2)}) async-start(s8[8388608]{0:T(1024)(128)(4,1)} %bitcast.51), calls=%async_computation.7 | async-start | bytes 8388608
  370.7 10.6 %slice-start = ((s8[8388608]{0:T(1024)(128)(4,1)}), s8[4194304]{0:T(1024)(128)(4,1)S(1)}, s32[]{:S(2)}) async-start(s8[8388608]{0:T(1024)(128)(4,1)} %bitcast.49), calls=%async_computation.5 | async-start | bytes 8388608
  370.7 10.6 %slice-start.3 = ((s8[8388608]{0:T(1024)(128)(4,1)}), s8[4194304]{0:T(1024)(128)(4,1)S(1)}, s32[]{:S(2)}) async-start(s8[8388608]{0:T(1024)(128)(4,1)} %bitcast.51), calls=%async_computation.8 | async-start | bytes 8388608
  403.4 18.7 %copy-start.46 = (bf16[512,4,128]{0,2,1:T(8,128)(2,1)S(1)}, bf16[512,4,128]{0,2,1:T(8,128)(2,1)}, u32[]{:S(2)}) copy-start(bf16[512,4,128]{0,2,1:T(8,128)(2,1)} %copy-done.45) | copy-start | bytes 1572868
  461.5 305.3 %all-reduce.5.cloned.1.call-start = ((), (), s32[]{:S(2)}) async-start(), calls=%async_computation.3 | async-start | bytes 12582912 | tf_op jit(solution)/shard_map/psum | solution.py:192
  464.0 24.0 %copy-start.40 = (bf16[4096,512]{0,1:T(8,128)(2,1)S(1)}, bf16[4096,512]{0,1:T(8,128)(2,1)}, u32[]{:S(2)}) copy-start(bf16[4096,512]{0,1:T(8,128)(2,1)} %all-gather.3.cloned.1.call-done) | copy-start | bytes 12582916
  464.1 24.0 %copy-start.22 = (bf16[512,4096]{1,0:T(8,128)(2,1)S(1)}, bf16[512,4096]{1,0:T(8,128)(2,1)}, u32[]{:S(2)}) copy-start(bf16[512,4096]{1,0:T(8,128)(2,1)} %get-tuple-element.87) | copy-start | bytes 12582916
  464.1 23.7 %collective-permute-start.9 = (bf16[128,2048]{1,0:T(8,128)(2,1)S(1)}, bf16[128,2048]{1,0:T(8,128)(2,1)S(1)}, u32[]{:S(2)}, u32[]{:S(2)}) collective-permute-start(bf16[128,2048]{1,0:T(8,128)(2,1)S(1)} %dynamic-slice_convert_fusion.5), channel_id=1, source_target_pairs={{0,2},{1,3},{2,0},{3,1},{4,6},{5,7},{6,4},{7,5},{8,10},{9,11},{10,... | collective-permute-start | bytes 1572872 | tf_op jit(solution)/shard_map/ppermute | solution.py:69
  468.1 21.5 %copy-start.19 = (bf16[512,4096]{1,0:T(8,128)(2,1)S(1)}, bf16[512,4096]{1,0:T(8,128)(2,1)}, u32[]{:S(2)}) copy-start(bf16[512,4096]{1,0:T(8,128)(2,1)} %get-tuple-element.85) | copy-start | bytes 12582916
  488.0 25.3 %collective-permute-start.10 = (bf16[128,2048]{1,0:T(8,128)(2,1)S(1)}, bf16[128,2048]{1,0:T(8,128)(2,1)S(1)}, u32[]{:S(2)}, u32[]{:S(2)}) collective-permute-start(bf16[128,2048]{1,0:T(8,128)(2,1)S(1)} %add_convert_fusion.2), channel_id=1, source_target_pairs={{0,2},{1,3},{2,0},{3,1},{4,6},{5,7},{6,4},{7,5},{8,10},{9,11},{10,... | collective-permute-start | bytes 1572872 | tf_op jit(solution)/shard_map/ppermute | solution.py:74
  489.6 24.0 %copy-start.20 = (bf16[512,4096]{1,0:T(8,128)(2,1)S(1)}, bf16[512,4096]{1,0:T(8,128)(2,1)}, u32[]{:S(2)}) copy-start(bf16[512,4096]{1,0:T(8,128)(2,1)} %get-tuple-element.86) | copy-start | bytes 12582916
  513.5 23.7 %collective-permute-start.11 = (bf16[256,2048]{1,0:T(8,128)(2,1)S(1)}, bf16[256,2048]{1,0:T(8,128)(2,1)S(1)}, u32[]{:S(2)}, u32[]{:S(2)}) collective-permute-start(bf16[256,2048]{1,0:T(8,128)(2,1)S(1)} %pad_maximum_fusion.4), channel_id=1, source_target_pairs={{0,1},{1,0},{2,3},{3,2},{4,5},{5,4},{6,7},{7,6},{8,9},{9,8},{10,11... | collective-permute-start | bytes 3145736 | tf_op jit(solution)/shard_map/ppermute | solution.py:74
  549.6 14.8 %slice-start.10 = ((s8[5767168]{0:T(1024)(128)(4,1)}), s8[4194304]{0:T(1024)(128)(4,1)S(1)}, s32[]{:S(2)}) async-start(s8[5767168]{0:T(1024)(128)(4,1)} %bitcast.59), calls=%async_computation.15 | async-start | bytes 8388608
  564.4 40.9 %copy-start.55 = (bf16[2048,256]{1,0:T(8,128)(2,1)S(1)}, bf16[2048,256]{1,0:T(8,128)(2,1)}, u32[]{:S(2)}) copy-start(bf16[2048,256]{1,0:T(8,128)(2,1)} %param.19) | copy-start | bytes 3145732
  609.6 27.8 %copy-start.5 = (bf16[512,2048]{1,0:T(8,128)(2,1)S(1)}, bf16[512,2048]{1,0:T(8,128)(2,1)}, u32[]{:S(2)}) copy-start(bf16[512,2048]{1,0:T(8,128)(2,1)} %param.13) | copy-start | bytes 6291460
  609.6 27.8 %copy-start.68 = (f32[2048]{0:T(1024)S(1)}, f32[2048]{0:T(1024)}, u32[]{:S(2)}) copy-start(f32[2048]{0:T(1024)} %copy-done.67) | copy-start | bytes 24580
  609.6 27.8 %copy-start.85 = (f32[512]{0:T(512)S(1)}, f32[512]{0:T(512)}, u32[]{:S(2)}) copy-start(f32[512]{0:T(512)} %copy-done.84) | copy-start | bytes 6148
  609.7 24.8 %collective-permute-start.12 = (bf16[256,2048]{1,0:T(8,128)(2,1)S(1)}, bf16[256,2048]{1,0:T(8,128)(2,1)S(1)}, u32[]{:S(2)}, u32[]{:S(2)}) collective-permute-start(bf16[256,2048]{1,0:T(8,128)(2,1)S(1)} %dynamic-slice_convert_fusion), channel_id=1, source_target_pairs={{0,1},{1,0},{2,3},{3,2},{4,5},{5,4},{6,7},{7,6},{8,9},{9,8},{10,11... | collective-permute-start | bytes 3145736 | tf_op jit(solution)/shard_map/ppermute | solution.py:69
  634.9 24.9 %collective-permute-start.13 = (bf16[128,2048]{1,0:T(8,128)(2,1)S(1)}, bf16[128,2048]{1,0:T(8,128)(2,1)S(1)}, u32[]{:S(2)}, u32[]{:S(2)}) collective-permute-start(bf16[128,2048]{1,0:T(8,128)(2,1)S(1)} %dynamic-slice_convert_fusion.4), channel_id=1, source_target_pairs={{0,2},{1,3},{2,0},{3,1},{4,6},{5,7},{6,4},{7,5},{8,10},{9,11},{10,... | collective-permute-start | bytes 1572872 | tf_op jit(solution)/shard_map/ppermute | solution.py:69
  659.9 25.1 %collective-permute-start.14 = (bf16[128,2048]{1,0:T(8,128)(2,1)S(1)}, bf16[128,2048]{1,0:T(8,128)(2,1)S(1)}, u32[]{:S(2)}, u32[]{:S(2)}) collective-permute-start(bf16[128,2048]{1,0:T(8,128)(2,1)S(1)} %add_convert_fusion.1), channel_id=1, source_target_pairs={{0,2},{1,3},{2,0},{3,1},{4,6},{5,7},{6,4},{7,5},{8,10},{9,11},{10,... | collective-permute-start | bytes 1572872 | tf_op jit(solution)/shard_map/ppermute | solution.py:74
  661.9 23.3 %copy-start.77 = (f32[2048]{0:T(1024)S(1)}, f32[2048]{0:T(1024)}, u32[]{:S(2)}) copy-start(f32[2048]{0:T(1024)} %get-tuple-element.39) | copy-start | bytes 24580
  685.2 23.6 %collective-permute-start.15 = (bf16[256,2048]{1,0:T(8,128)(2,1)S(1)}, bf16[256,2048]{1,0:T(8,128)(2,1)S(1)}, u32[]{:S(2)}, u32[]{:S(2)}) collective-permute-start(bf16[256,2048]{1,0:T(8,128)(2,1)S(1)} %pad_maximum_fusion.6), channel_id=1, source_target_pairs={{0,1},{1,0},{2,3},{3,2},{4,5},{5,4},{6,7},{7,6},{8,9},{9,8},{10,11... | collective-permute-start | bytes 3145736 | tf_op jit(solution)/shard_map/ppermute | solution.py:74
  685.3 1.2 collective-permute-start.19
  686.5 4.0 collective-permute-start.20
  690.5 20.3 %collective-permute-start.21 = (f32[2048]{0:T(1024)S(1)}, f32[2048]{0:T(1024)S(1)}, u32[]{:S(2)}, u32[]{:S(2)}) collective-permute-start(f32[2048]{0:T(1024)S(1)} %add.262), channel_id=1, source_target_pairs={{0,16},{4,20},{8,24},{12,28},{16,0},{20,4},{24,8},{28,12},{1,17},{... | collective-permute-start | bytes 24584 | tf_op jit(solution)/shard_map/ppermute | solution.py:88
  710.7 66.1 %collective-permute-start.16 = (f32[2048]{0:T(1024)S(1)}, f32[2048]{0:T(1024)S(1)}, u32[]{:S(2)}, u32[]{:S(2)}) collective-permute-start(f32[2048]{0:T(1024)S(1)} %get-tuple-element.41), channel_id=1, source_target_pairs={{0,4},{4,0},{8,12},{12,8},{16,20},{20,16},{24,28},{28,24},{1,5},{5... | collective-permute-start | bytes 24584 | tf_op jit(solution)/shard_map/ppermute | solution.py:88
  766.8 15.0 %copy-start.27 = (bf16[256,2048]{1,0:T(8,128)(2,1)S(1)}, bf16[256,2048]{1,0:T(8,128)(2,1)}, u32[]{:S(2)}) copy-start(bf16[256,2048]{1,0:T(8,128)(2,1)} %copy-done.26) | copy-start | bytes 3145732
  771.2 10.6 %copy-start.17 = (f32[512,2048]{1,0:T(8,128)S(1)}, f32[512,2048]{1,0:T(8,128)}, u32[]{:S(2)}) copy-start(f32[512,2048]{1,0:T(8,128)} %copy-done.15) | copy-start | bytes 12582916
  771.2 10.6 %copy-start.24 = (f32[512,2048]{1,0:T(8,128)S(1)}, f32[512,2048]{1,0:T(8,128)}, u32[]{:S(2)}) copy-start(f32[512,2048]{1,0:T(8,128)} %maximum_convert_fusion.1) | copy-start | bytes 12582916
  776.8 3.7 collective-permute-start.17
  780.5 7.6 collective-permute-start.18
  (73 other events, 297.7 us)
Sparse Core Ops, SparseCore 0:
  19.1 40.0 all-gather.2
  328.8 220.6 all-reduce.6
  552.9 51.1 reduce-scatter.1
  662.1 104.6 all-reduce.4
where the time goes:
time: 799 us; the launch traced here: 795 us
  waiting for transfers between devices  446 us (56%)
  matrix products  173 us (22%)
  other arithmetic  115 us (14%)
  starting transfers between devices  19.3 us (2%)
  local copies, waits for them, and re-layouts  16.3 us (2%)
  between operations  15.7 us (2%)
  blocking collectives  10.6 us (1%)
    ppermute x8, waiting for transfers between devices, permute_sum(): got = lax.ppermute(pieces, axis, partner_perm(size, 1 << step))  164 us
    ppermute x8, waiting for transfers between devices, permute_sum(): got = lax.ppermute(send, axis, partner_perm(size, 1 << step))  152 us
    dot_general x15, matrix products, right_trans(): lax.dot_general(left, right, (((1,), (1,)), ((), ())), preferred_element_...  80.6 us
    psum x2, waiting for transfers between devices, dp_sum(): lax.psum(grad.astype(jnp.bfloat16), 'dp').astype(jnp.float32)  64.7 us
    dot_general x15, matrix products, left_trans(): lax.dot_general(left, right, (((0,), (0,)), ((), ())), preferred_element_...  50.7 us
    reduce_scatter x1, waiting for transfers between devices, on_device(): lax.psum_scatter(d_kv_cat, 'dp', scatter_dimension=0, tiled=True)  33.7 us
    convert_element_type x7, other arithmetic, dp_sum(): lax.psum(grad.astype(jnp.bfloat16), 'dp').astype(jnp.float32)  30.8 us
    convert_element_type x2, other arithmetic, on_device(): d_scores = (probs * (d_probs - row_delta)).astype(jnp.bfloat16)  28 us
  transfers between devices with their start and end apart: 26, of which 22 were waited for; matrix products, arithmetic and copies ran while one was open for 23% of the time, Pallas kernels for 0%

commit v1 on v0

--- a/solution.py
+++ b/solution.py
@@ -189,7 +189,7 @@
     grad_out = cotangent.astype(jnp.float32)
 
     def dp_sum(grads):
-        return [lax.psum(grad.astype(jnp.bfloat16), "dp").astype(jnp.float32) for grad in grads]
+        return [lax.psum(grad.astype(jnp.bfloat16), "dp") for grad in grads]
 
     d_down = (keep_rows * grad_out).astype(jnp.bfloat16)
     grad_w_down = left_trans(hidden, d_down)
@@ -203,7 +203,8 @@
     grad_w_gate, grad_w_up, grad_w_down, d_normed_two_part = lax.optimization_barrier(
         (grad_w_gate, grad_w_up, grad_w_down, d_normed_two_part)
     )
-    grad_w_gate, grad_w_up, grad_w_down = dp_sum([grad_w_gate, grad_w_up, grad_w_down])
+    mlp_grads = dp_sum([grad_w_gate, grad_w_up, grad_w_down])
+    grad_w_gate, grad_w_up, grad_w_down = mlp_grads
     (d_normed_two,) = permute_sum([d_normed_two_part], [0], "tensor")
     down_part, d_normed_two = lax.optimization_barrier((down_part, d_normed_two))
     (down_sum,) = permute_sum([down_part], [0], "tensor")
@@ -249,7 +250,6 @@
         tiled=True,
     ).astype(jnp.float32)
     d_kv_own, grad_w_out = lax.optimization_barrier((d_kv_own, grad_w_out))
-    (grad_w_out,) = dp_sum([grad_w_out])
     d_key_own = d_kv_own[:, :kv_width]
     d_value_own = d_kv_own[:, kv_width:]
     d_queries = jnp.concatenate(d_query_parts, axis=1).reshape(row_count, local_heads, HEAD_DIM)
@@ -272,14 +272,31 @@
         + right_trans(d_key_low, w_key)
         + right_trans(d_value_low, w_value)
     )
-    down_sum, d_normed_part = lax.optimization_barrier((down_sum, d_normed_part))
+    (
+        down_sum,
+        d_normed_part,
+        grad_w_out,
+        grad_w_query,
+        grad_w_key,
+        grad_w_value,
+    ) = lax.optimization_barrier(
+        (down_sum, d_normed_part, grad_w_out, grad_w_query, grad_w_key, grad_w_value)
+    )
+    grad_w_out, grad_w_query, grad_w_key, grad_w_value = dp_sum(
+        [grad_w_out, grad_w_query, grad_w_key, grad_w_value]
+    )
+    grad_w_gate, grad_w_up, grad_w_down = [
+        grad.astype(jnp.float32) for grad in (grad_w_gate, grad_w_up, grad_w_down)
+    ]
     output = (middle + keep_rows * down_sum).astype(jnp.bfloat16)
     (d_normed,) = permute_sum([d_normed_part], [0], "tensor")
     d_source_norm, grad_gain_one = norm_one_back(d_normed)
     grad_input = grad_middle + d_source_norm
     grad_gain_one = permute_allsum(grad_gain_one, "dp")
     grad_gain_two = permute_allsum(grad_gain_two, "dp")
-    grad_w_query, grad_w_key, grad_w_value = dp_sum([grad_w_query, grad_w_key, grad_w_value])
+    grad_w_out, grad_w_query, grad_w_key, grad_w_value = [
+        grad.astype(jnp.float32) for grad in (grad_w_out, grad_w_query, grad_w_key, grad_w_value)
+    ]
     return (
         output,
         grad_input,

time: 799 us -> 802 us (level)
    psum x2, waiting for transfers between devices: 64.7 us -> 41.2 us  [dp_sum(): return [lax.psum(grad.astype(jnp.bfloat16), 'dp') for grad in grads]]
    reduce_scatter x1, waiting for transfers between devices: 33.7 us -> 55.1 us  [on_device(): lax.psum_scatter(d_kv_cat, 'dp', scatter_dimension=0, tiled=True)]
  transfers between devices with their start and end apart: 26 -> 26, of which waited for: 22 -> 22; matrix products, arithmetic and copies ran while one was open for 23% -> 22% of each run, Pallas kernels for 0% -> 0%
where the time goes in v1:
time: 802 us; the launch traced here: 799 us
  waiting for transfers between devices  451 us (56%)
  matrix products  174 us (22%)
  other arithmetic  109 us (14%)
  local copies, waits for them, and re-layouts  19.4 us (2%)
  starting transfers between devices  19.1 us (2%)
  between operations  15.7 us (2%)
  blocking collectives  10.6 us (1%)
    ppermute x8, waiting for transfers between devices, permute_sum(): got = lax.ppermute(pieces, axis, partner_perm(size, 1 << step))  167 us
    ppermute x8, waiting for transfers between devices, permute_sum(): got = lax.ppermute(send, axis, partner_perm(size, 1 << step))  157 us
    dot_general x15, matrix products, right_trans(): lax.dot_general(left, right, (((1,), (1,)), ((), ())), preferred_element_...  77.6 us
    reduce_scatter x1, waiting for transfers between devices, on_device(): lax.psum_scatter(d_kv_cat, 'dp', scatter_dimension=0, tiled=True)  55.1 us
    dot_general x15, matrix products, left_trans(): lax.dot_general(left, right, (((0,), (0,)), ((), ())), preferred_element_...  50.5 us
    psum x2, waiting for transfers between devices, dp_sum(): return [lax.psum(grad.astype(jnp.bfloat16), 'dp') for grad in grads]  41.2 us
    convert_element_type x2, other arithmetic, on_device(): d_scores = (probs * (d_probs - row_delta)).astype(jnp.bfloat16)  29.2 us
    convert_element_type x7, other arithmetic, on_device(): grad.astype(jnp.float32)  27 us
  transfers between devices with their start and end apart: 26, of which 22 were waited for; matrix products, arithmetic and copies ran while one was open for 22% of the time, Pallas kernels for 0%

profile of v1, /device:TPU:0, one launch (start us, length us, event | category | flops | bytes accessed | tf_op | source)
XLA Modules:
  0.0 798.9 jit_solution(14617363964868873217)
XLA Ops:
  11.2 2.8 convolution_convert_fusion.1
  19.2 10.6 %all-gather = bf16[8,1,512]{2,1,0:T(2,128)(2,1)S(1)} all-gather(bf16[1,1,512]{2,1,0:T(2,128)(2,1)S(1)} %reshape.231), channel_id=1, replica_groups=mesh['dp'=8,'tensor'=4] {'dp'}, dimensions={0}, use_global_device_ids=true | all-gather | bytes 9216 | tf_op jit(solution)/shard_map/all_gather | solution.py:163
  29.9 3.7 fusion.97
  33.9 25.4 %all-gather.3.cloned.1.call-done = bf16[4096,512]{0,1:T(8,128)(2,1)} async-done(((bf16[512,512]{0,1:T(8,128)(2,1)}), bf16[4096,512]{0,1:T(8,128)(2,1)}) %all-gather.3.cloned.1.call-update) | async-done | bytes 4194320 | tf_op jit(solution)/shard_map/all_gather | solution.py:158
  59.3 4.7 fusion.105
  64.1 3.4 copy-done.10
  69.6 3.5 fusion.106
  74.5 3.9 fusion.107
  79.7 5.5 fusion.108
  86.5 7.1 fusion.34
  104.8 23.9 %collective-permute-done = bf16[256,2048]{1,0:T(8,128)(2,1)} collective-permute-done((bf16[256,2048]{1,0:T(8,128)(2,1)S(1)}, bf16[256,2048]{1,0:T(8,128)(2,1)}, u32[]{:S(2)}, u32[]{:S(2)}) %collective-permute-start) | collective-permute-done | bytes 1048608 | tf_op jit(solution)/shard_map/ppermute | solution.py:69
  132.3 2.5 collective-permute-start.1
  134.8 22.9 %collective-permute-done.1 = bf16[128,2048]{1,0:T(8,128)(2,1)S(1)} collective-permute-done((bf16[128,2048]{1,0:T(8,128)(2,1)S(1)}, bf16[128,2048]{1,0:T(8,128)(2,1)S(1)}, u32[]{:S(2)}, u32[]{:S(2)}) %collective-permute-start.1) | collective-permute-done | bytes 524320 | tf_op jit(solution)/shard_map/ppermute | solution.py:69
  159.1 25.0 %collective-permute-done.2 = bf16[128,2048]{1,0:T(8,128)(2,1)S(1)} collective-permute-done((bf16[128,2048]{1,0:T(8,128)(2,1)S(1)}, bf16[128,2048]{1,0:T(8,128)(2,1)S(1)}, u32[]{:S(2)}, u32[]{:S(2)}) %collective-permute-start.2) | collective-permute-done | bytes 524320 | tf_op jit(solution)/shard_map/ppermute | solution.py:74
  185.2 6.6 fusion.40
  191.9 16.9 %collective-permute-done.3 = bf16[256,2048]{1,0:T(8,128)(2,1)} collective-permute-done((bf16[256,2048]{1,0:T(8,128)(2,1)S(1)}, bf16[256,2048]{1,0:T(8,128)(2,1)}, u32[]{:S(2)}, u32[]{:S(2)}) %collective-permute-start.3) | collective-permute-done | bytes 1048608 | tf_op jit(solution)/shard_map/ppermute | solution.py:74
  212.9 3.4 fusion.109
  216.3 4.6 multiply_convert_fusion.6
  221.0 3.4 fusion.113
  224.4 5.5 fusion.111
  229.9 5.4 fusion.112
  235.3 5.0 convolution_add_fusion.4
  240.3 5.2 fusion.38
  247.6 22.3 %collective-permute-done.4 = bf16[256,2048]{1,0:T(8,128)(2,1)S(1)} collective-permute-done((bf16[256,2048]{1,0:T(8,128)(2,1)S(1)}, bf16[256,2048]{1,0:T(8,128)(2,1)S(1)}, u32[]{:S(2)}, u32[]{:S(2)}) %collective-permute-start.4) | collective-permute-done | bytes 1048608 | tf_op jit(solution)/shard_map/ppermute | solution.py:69
  271.9 3.6 collective-permute-start.5
  275.5 21.9 %collective-permute-done.5 = bf16[128,2048]{1,0:T(8,128)(2,1)S(1)} collective-permute-done((bf16[128,2048]{1,0:T(8,128)(2,1)S(1)}, bf16[128,2048]{1,0:T(8,128)(2,1)S(1)}, u32[]{:S(2)}, u32[]{:S(2)}) %collective-permute-start.5) | collective-permute-done | bytes 524320 | tf_op jit(solution)/shard_map/ppermute | solution.py:69
  297.6 25.4 %collective-permute-done.6 = bf16[128,2048]{1,0:T(8,128)(2,1)S(1)} collective-permute-done((bf16[128,2048]{1,0:T(8,128)(2,1)S(1)}, bf16[128,2048]{1,0:T(8,128)(2,1)S(1)}, u32[]{:S(2)}, u32[]{:S(2)}) %collective-permute-start.6) | collective-permute-done | bytes 524320 | tf_op jit(solution)/shard_map/ppermute | solution.py:74
  326.2 6.3 fusion.110
  332.4 16.9 %collective-permute-done.7 = bf16[256,2048]{1,0:T(8,128)(2,1)} collective-permute-done((bf16[256,2048]{1,0:T(8,128)(2,1)}, bf16[256,2048]{1,0:T(8,128)(2,1)}, u32[]{:S(2)}, u32[]{:S(2)}) %collective-permute-start.7) | collective-permute-done | bytes 1048608 | tf_op jit(solution)/shard_map/ppermute | solution.py:74
  353.1 3.0 multiply_reduce_fusion.4
  356.1 3.4 convert_add_fusion.1
  363.7 4.6 fusion.42
  368.2 5.5 fusion.44
  373.8 5.0 fusion.54
  378.9 22.0 %multiply_reduce_fusion.2 = (f32[512]{0:T(512)S(1)}, f32[512]{0:T(512)S(1)}, f32[512]{0:T(512)S(1)}, f32[512]{0:T(512)}, f32[512,4096]{1,0:T(8,128)}) fusion(f32[512,4096]{1,0:T(8,128)S(1)} %bitcast.52, f32[512]{0:T(512)S(1)} %copy-done.80, s32[512]{0:T(512)S(1)} %copy-done.75, pred[4096]{0:T(1024)(128)(4,1)S(1)} %bitcast.96, s32[512]{0:T(512)S(1)} %copy-done.72, ...), kind=kOutput, calls=%fused_computation.7 | convolution fusion | flops 578811904 | bytes 68329472 | tf_op jit(solution)/shard_map/dot_general | solution.py:45
  400.9 18.7 %multiply_convert_fusion.2 = (bf16[512,4096]{1,0:T(8,128)(2,1)}, bf16[512,4096]{1,0:T(8,128)(2,1)}, bf16[512,4096]{1,0:T(8,128)(2,1)}) fusion(f32[512,4096]{1,0:T(8,128)} %get-tuple-element.109, f32[512]{0:T(512)S(1)} %get-tuple-element.51, f32[512,4096]{1,0:T(8,128)S(1)} %bitcast.52, f32[512]{0:T(512)S(1)} %copy-done.80, s32[512]{0:T(512)S(1)} %copy-done.75, ...), kind=kLoop, calls=%fused_computation.6 | loop fusion | flops 39845888 | bytes 62951424 | tf_op jit(solution)/shard_map/convert_element_type | solution.py:235
  419.7 3.4 fusion.77
  427.3 10.4 %multiply_convert_fusion = bf16[512,4096]{1,0:T(8,128)(2,1)} fusion(f32[512,4096]{1,0:T(8,128)} %fusion.42, f32[512]{0:T(512)S(1)} %copy-done.90, f32[512,4096]{1,0:T(8,128)} %copy-done.10, f32[512]{0:T(512)S(1)} %copy-done.87, s32[512]{0:T(512)S(1)} %copy-done.76, pred[4096]{0:T(1024)(128)(4,1)S(1)} %bitcast.98, s32[512]{0:T(512)S(1)} %copy-done.73, ...), kind=kLoop, calls=%fused_computation | loop fusion | flops 18874368 | bytes 21000192 | tf_op jit(solution)/shard_map/convert_element_type | solution.py:235
  437.8 3.0 fusion.13
  440.9 4.9 fusion.24
  445.8 3.6 fusion.21
  449.5 3.7 fusion.10
  453.2 3.9 fusion.11
  459.5 4.2 convolution_multiply_fusion.2
  470.0 19.8 %collective-permute-done.9 = bf16[128,2048]{1,0:T(8,128)(2,1)S(1)} collective-permute-done((bf16[128,2048]{1,0:T(8,128)(2,1)S(1)}, bf16[128,2048]{1,0:T(8,128)(2,1)S(1)}, u32[]{:S(2)}, u32[]{:S(2)}) %collective-permute-start.9) | collective-permute-done | bytes 524320 | tf_op jit(solution)/shard_map/ppermute | solution.py:69
  491.6 23.5 %collective-permute-done.10 = bf16[128,2048]{1,0:T(8,128)(2,1)S(1)} collective-permute-done((bf16[128,2048]{1,0:T(8,128)(2,1)S(1)}, bf16[128,2048]{1,0:T(8,128)(2,1)S(1)}, u32[]{:S(2)}, u32[]{:S(2)}) %collective-permute-start.10) | collective-permute-done | bytes 524320 | tf_op jit(solution)/shard_map/ppermute | solution.py:74
  515.8 2.8 fusion.92
  518.6 2.7 fusion.82
  521.3 17.8 %collective-permute-done.11 = bf16[256,2048]{1,0:T(8,128)(2,1)S(1)} collective-permute-done((bf16[256,2048]{1,0:T(8,128)(2,1)S(1)}, bf16[256,2048]{1,0:T(8,128)(2,1)S(1)}, u32[]{:S(2)}, u32[]{:S(2)}) %collective-permute-start.11) | collective-permute-done | bytes 1048608 | tf_op jit(solution)/shard_map/ppermute | solution.py:74
  539.7 2.6 maximum_convert_fusion.1
  542.2 4.8 all-reduce.7.cloned.1.call-done
  547.0 55.1 %reduce-scatter.2.cloned.1.call-done = bf16[512,512]{0,1:T(8,128)(2,1)} async-done(((bf16[4096,512]{0,1:T(8,128)(2,1)}), bf16[512,512]{0,1:T(8,128)(2,1)}) %reduce-scatter.2.cloned.1.call-update) | async-done | bytes 524304 | tf_op jit(solution)/shard_map/reduce_scatter | solution.py:246
  605.5 2.8 fusion.80
  616.6 23.3 %collective-permute-done.12 = bf16[256,2048]{1,0:T(8,128)(2,1)S(1)} collective-permute-done((bf16[256,2048]{1,0:T(8,128)(2,1)S(1)}, bf16[256,2048]{1,0:T(8,128)(2,1)S(1)}, u32[]{:S(2)}, u32[]{:S(2)}) %collective-permute-start.12) | collective-permute-done | bytes 1048608 | tf_op jit(solution)/shard_map/ppermute | solution.py:69
  642.7 22.4 %collective-permute-done.13 = bf16[128,2048]{1,0:T(8,128)(2,1)S(1)} collective-permute-done((bf16[128,2048]{1,0:T(8,128)(2,1)S(1)}, bf16[128,2048]{1,0:T(8,128)(2,1)S(1)}, u32[]{:S(2)}, u32[]{:S(2)}) %collective-permute-start.13) | collective-permute-done | bytes 524320 | tf_op jit(solution)/shard_map/ppermute | solution.py:69
  665.4 25.0 %collective-permute-done.14 = bf16[128,2048]{1,0:T(8,128)(2,1)S(1)} collective-permute-done((bf16[128,2048]{1,0:T(8,128)(2,1)S(1)}, bf16[128,2048]{1,0:T(8,128)(2,1)S(1)}, u32[]{:S(2)}, u32[]{:S(2)}) %collective-permute-start.14) | collective-permute-done | bytes 524320 | tf_op jit(solution)/shard_map/ppermute | solution.py:74
  697.3 16.8 %collective-permute-done.15 = bf16[256,2048]{1,0:T(8,128)(2,1)S(1)} collective-permute-done((bf16[256,2048]{1,0:T(8,128)(2,1)S(1)}, bf16[256,2048]{1,0:T(8,128)(2,1)S(1)}, u32[]{:S(2)}, u32[]{:S(2)}) %collective-permute-start.15) | collective-permute-done | bytes 1048608 | tf_op jit(solution)/shard_map/ppermute | solution.py:74
  716.8 5.8 convert_element_type.292
  722.6 5.2 convert_element_type.293
  727.8 6.0 convert_element_type.294
  733.8 36.4 %all-reduce.5.cloned.1.call-done = (bf16[2048,512]{1,0:T(8,128)(2,1)}, bf16[2048,256]{1,0:T(8,128)(2,1)}, bf16[2048,256]{1,0:T(8,128)(2,1)}, bf16[512,2048]{1,0:T(8,128)(2,1)}) async-done(((bf16[2048,512]{1,0:T(8,128)(2,1)}, bf16[2048,256]{1,0:T(8,128)(2,1)}, bf16[2048,256]{1,0:T(8,128)(2,1)}, bf16[512,2048]{1,0:T(8,128)(2,1)}), (bf16[2048,512]{1,0:T(8,128)(2,1)}, bf16[2048,256]{1,0:T(8,128)(2,1)}, ...) | async-done | bytes 6291472 | tf_op jit(solution)/shard_map/psum | solution.py:192
  770.2 4.3 convert_element_type.285
  777.6 2.7 convert_element_type.291
  785.2 6.3 fusion.17
  (361 shorter events, 100.4 us)
Async XLA Ops:
  7.2 92.6 %copy-start = (bf16[512,2048]{1,0:T(8,128)(2,1)S(1)}, bf16[512,2048]{1,0:T(8,128)(2,1)}, u32[]{:S(2)}) copy-start(bf16[512,2048]{1,0:T(8,128)(2,1)} %param.20) | copy-start | bytes 6291460
  7.2 52.1 %all-gather.3.cloned.1.call-start = ((), (), s32[]{:S(2)}) async-start(), calls=%async_computation.1 | async-start | bytes 4718592 | tf_op jit(solution)/shard_map/all_gather | solution.py:158
  10.4 19.5 %copy-start.84 = (f32[512]{0:T(512)}, f32[512]{0:T(512)S(1)}, u32[]{:S(2)}) copy-start(f32[512]{0:T(512)S(1)} %fusion.85) | copy-start | bytes 6148
  11.1 18.8 %copy-start.67 = (f32[2048]{0:T(1024)}, f32[2048]{0:T(1024)S(1)}, u32[]{:S(2)}) copy-start(f32[2048]{0:T(1024)S(1)} %convert_element_type.226) | copy-start | bytes 24580
  11.2 68.5 %copy-start.65 = (s32[2,2,8,128]{3,1,2,0:T(2,128)}, s32[2,2,8,128]{3,1,2,0:T(2,128)S(1)}, u32[]{:S(2)}) copy-start(s32[2,2,8,128]{3,1,2,0:T(2,128)S(1)} %copy.24) | copy-start | bytes 49156
  15.8 63.8 %copy-start.71 = (s32[512]{0:T(512)}, s32[512]{0:T(512)S(1)}, u32[]{:S(2)}) copy-start(s32[512]{0:T(512)S(1)} %get-tuple-element.63) | copy-start | bytes 6148
  17.1 16.6 %copy-start.43 = (f32[512,64]{0,1:T(8,128)}, f32[512,64]{0,1:T(8,128)S(1)}, u32[]{:S(2)}) copy-start(f32[512,64]{0,1:T(8,128)S(1)} %get-tuple-element.98) | copy-start | bytes 393220
  19.1 527.9 %all-reduce.7.cloned.1.call-start = ((), (), s32[]{:S(2)}) async-start(), calls=%async_computation.4 | async-start | bytes 34603008 | tf_op jit(solution)/shard_map/psum | solution.py:192
  29.9 49.8 %copy-start.69 = (pred[1,4,8,128]{3,1,2,0:T(4,128)(4,1)}, pred[1,4,8,128]{3,1,2,0:T(4,128)(4,1)S(1)}, u32[]{:S(2)}) copy-start(pred[1,4,8,128]{3,1,2,0:T(4,128)(4,1)S(1)} %copy.25) | copy-start | bytes 12292
  29.9 49.8 %copy-start.74 = (s32[512]{0:T(512)}, s32[512]{0:T(512)S(1)}, u32[]{:S(2)}) copy-start(s32[512]{0:T(512)S(1)} %iota_add_fusion) | copy-start | bytes 6148
  33.9 45.8 %copy-start.46 = (bf16[512,4,128]{0,2,1:T(8,128)(2,1)}, bf16[512,4,128]{0,2,1:T(8,128)(2,1)S(1)}, u32[]{:S(2)}) copy-start(bf16[512,4,128]{0,2,1:T(8,128)(2,1)S(1)} %pad_maximum_fusion.7) | copy-start | bytes 1572868
  73.2 20.5 %copy-start.7 = (f32[512,4096]{1,0:T(8,128)}, f32[512,4096]{1,0:T(8,128)S(1)}, u32[]{:S(2)}) copy-start(f32[512,4096]{1,0:T(8,128)S(1)} %get-tuple-element.104) | copy-start | bytes 25165828
  78.4 17.2 %copy-start.8 = (f32[512,4096]{1,0:T(8,128)}, f32[512,4096]{1,0:T(8,128)S(1)}, u32[]{:S(2)}) copy-start(f32[512,4096]{1,0:T(8,128)S(1)} %get-tuple-element.106) | copy-start | bytes 25165828
  85.2 12.5 %copy-start.9 = (f32[512,4096]{1,0:T(8,128)}, f32[512,4096]{1,0:T(8,128)S(1)}, u32[]{:S(2)}) copy-start(f32[512,4096]{1,0:T(8,128)S(1)} %get-tuple-element.108) | copy-start | bytes 25165828
  103.2 25.5 %collective-permute-start = (bf16[256,2048]{1,0:T(8,128)(2,1)S(1)}, bf16[256,2048]{1,0:T(8,128)(2,1)}, u32[]{:S(2)}, u32[]{:S(2)}) collective-permute-start(bf16[256,2048]{1,0:T(8,128)(2,1)S(1)} %dynamic-slice_convert_fusion.3), channel_id=1, source_target_pairs={{0,1},{1,0},{2,3},{3,2},{4,5},{5,4},{6,7},{7,6},{8,9},{9,8},{10,11... | collective-permute-start | bytes 3145736 | tf_op jit(solution)/shard_map/ppermute | solution.py:69
  132.2 53.0 %copy-start.91 = (bf16[2048]{0:T(1024)(128)(2,1)S(1)}, bf16[2048]{0:T(1024)(128)(2,1)}, u32[]{:S(2)}) copy-start(bf16[2048]{0:T(1024)(128)(2,1)} %param.21) | copy-start | bytes 12292
  132.3 25.4 %collective-permute-start.1 = (bf16[128,2048]{1,0:T(8,128)(2,1)S(1)}, bf16[128,2048]{1,0:T(8,128)(2,1)S(1)}, u32[]{:S(2)}, u32[]{:S(2)}) collective-permute-start(bf16[128,2048]{1,0:T(8,128)(2,1)S(1)} %dynamic-slice_convert_fusion.7), channel_id=1, source_target_pairs={{0,2},{1,3},{2,0},{3,1},{4,6},{5,7},{6,4},{7,5},{8,10},{9,11},{10,... | collective-permute-start | bytes 1572872 | tf_op jit(solution)/shard_map/ppermute | solution.py:69
  159.0 25.1 %collective-permute-start.2 = (bf16[128,2048]{1,0:T(8,128)(2,1)S(1)}, bf16[128,2048]{1,0:T(8,128)(2,1)S(1)}, u32[]{:S(2)}, u32[]{:S(2)}) collective-permute-start(bf16[128,2048]{1,0:T(8,128)(2,1)S(1)} %add_convert_fusion.4), channel_id=1, source_target_pairs={{0,2},{1,3},{2,0},{3,1},{4,6},{5,7},{6,4},{7,5},{8,10},{9,11},{10,... | collective-permute-start | bytes 1572872 | tf_op jit(solution)/shard_map/ppermute | solution.py:74
  185.2 23.6 %collective-permute-start.3 = (bf16[256,2048]{1,0:T(8,128)(2,1)S(1)}, bf16[256,2048]{1,0:T(8,128)(2,1)}, u32[]{:S(2)}, u32[]{:S(2)}) collective-permute-start(bf16[256,2048]{1,0:T(8,128)(2,1)S(1)} %pad_maximum_fusion.2), channel_id=1, source_target_pairs={{0,1},{1,0},{2,3},{3,2},{4,5},{5,4},{6,7},{7,6},{8,9},{9,8},{10,11... | collective-permute-start | bytes 3145736 | tf_op jit(solution)/shard_map/ppermute | solution.py:74
  185.2 23.5 %copy-start.35 = (bf16[128,2048]{1,0:T(8,128)(2,1)S(1)}, bf16[128,2048]{1,0:T(8,128)(2,1)}, u32[]{:S(2)}) copy-start(bf16[128,2048]{1,0:T(8,128)(2,1)} %copy-done.34) | copy-start | bytes 1572868
  185.2 23.5 %copy-start.37 = (bf16[128,2048]{1,0:T(8,128)(2,1)S(1)}, bf16[128,2048]{1,0:T(8,128)(2,1)}, u32[]{:S(2)}) copy-start(bf16[128,2048]{1,0:T(8,128)(2,1)} %copy-done.36) | copy-start | bytes 1572868
  191.8 18.7 %copy-start.3 = (bf16[512,2048]{1,0:T(8,128)(2,1)S(1)}, bf16[512,2048]{1,0:T(8,128)(2,1)}, u32[]{:S(2)}) copy-start(bf16[512,2048]{1,0:T(8,128)(2,1)} %param.13) | copy-start | bytes 6291460
  210.6 145.6 %copy-start.11 = (bf16[256,2048]{1,0:T(8,128)(2,1)}, bf16[256,2048]{1,0:T(8,128)(2,1)S(1)}, u32[]{:S(2)}) copy-start(bf16[256,2048]{1,0:T(8,128)(2,1)S(1)} %get-tuple-element.75) | copy-start | bytes 3145732
  221.0 19.3 %copy-start.94 = (bf16[512,1408]{1,0:T(8,128)(2,1)}, bf16[512,1408]{1,0:T(8,128)(2,1)S(1)}, u32[]{:S(2)}) copy-start(bf16[512,1408]{1,0:T(8,128)(2,1)S(1)} %get-tuple-element.66) | copy-start | bytes 4325380
  247.2 22.7 %collective-permute-start.4 = (bf16[256,2048]{1,0:T(8,128)(2,1)S(1)}, bf16[256,2048]{1,0:T(8,128)(2,1)S(1)}, u32[]{:S(2)}, u32[]{:S(2)}) collective-permute-start(bf16[256,2048]{1,0:T(8,128)(2,1)S(1)} %dynamic-slice_convert_fusion.2), channel_id=1, source_target_pairs={{0,1},{1,0},{2,3},{3,2},{4,5},{5,4},{6,7},{7,6},{8,9},{9,8},{10,11... | collective-permute-start | bytes 3145736 | tf_op jit(solution)/shard_map/ppermute | solution.py:69
  271.9 25.5 %collective-permute-start.5 = (bf16[128,2048]{1,0:T(8,128)(2,1)S(1)}, bf16[128,2048]{1,0:T(8,128)(2,1)S(1)}, u32[]{:S(2)}, u32[]{:S(2)}) collective-permute-start(bf16[128,2048]{1,0:T(8,128)(2,1)S(1)} %dynamic-slice_convert_fusion.6), channel_id=1, source_target_pairs={{0,2},{1,3},{2,0},{3,1},{4,6},{5,7},{6,4},{7,5},{8,10},{9,11},{10,... | collective-permute-start | bytes 1572872 | tf_op jit(solution)/shard_map/ppermute | solution.py:69
  297.5 25.4 %collective-permute-start.6 = (bf16[128,2048]{1,0:T(8,128)(2,1)S(1)}, bf16[128,2048]{1,0:T(8,128)(2,1)S(1)}, u32[]{:S(2)}, u32[]{:S(2)}) collective-permute-start(bf16[128,2048]{1,0:T(8,128)(2,1)S(1)} %add_convert_fusion.3), channel_id=1, source_target_pairs={{0,2},{1,3},{2,0},{3,1},{4,6},{5,7},{6,4},{7,5},{8,10},{9,11},{10,... | collective-permute-start | bytes 1572872 | tf_op jit(solution)/shard_map/ppermute | solution.py:74
  324.9 24.5 %collective-permute-start.7 = (bf16[256,2048]{1,0:T(8,128)(2,1)}, bf16[256,2048]{1,0:T(8,128)(2,1)}, u32[]{:S(2)}, u32[]{:S(2)}) collective-permute-start(bf16[256,2048]{1,0:T(8,128)(2,1)} %pad_maximum_fusion.3), channel_id=1, source_target_pairs={{0,1},{1,0},{2,3},{3,2},{4,5},{5,4},{6,7},{7,6},{8,9},{9,8},{10,11... | collective-permute-start | bytes 3145736 | tf_op jit(solution)/shard_map/ppermute | solution.py:74
  326.1 276.1 %reduce-scatter.2.cloned.1.call-start = ((), (), s32[]{:S(2)}) async-start(), calls=%async_computation.2 | async-start | bytes 4718592 | tf_op jit(solution)/shard_map/reduce_scatter | solution.py:246
  326.1 23.2 %copy-start.31 = (bf16[128,2048]{1,0:T(8,128)(2,1)S(1)}, bf16[128,2048]{1,0:T(8,128)(2,1)}, u32[]{:S(2)}) copy-start(bf16[128,2048]{1,0:T(8,128)(2,1)} %copy-done.30) | copy-start | bytes 1572868
  326.1 23.2 %copy-start.33 = (bf16[128,2048]{1,0:T(8,128)(2,1)S(1)}, bf16[128,2048]{1,0:T(8,128)(2,1)}, u32[]{:S(2)}) copy-start(bf16[128,2048]{1,0:T(8,128)(2,1)} %copy-done.32) | copy-start | bytes 1572868
  332.4 28.4 %copy-start.45 = (f32[512,2048]{1,0:T(8,128)}, f32[512,2048]{1,0:T(8,128)S(1)}, u32[]{:S(2)}) copy-start(f32[512,2048]{1,0:T(8,128)S(1)} %fusion.110) | copy-start | bytes 12582916
  362.2 101.4 %collective-permute-start.8 = (bf16[256,2048]{1,0:T(8,128)(2,1)}, bf16[256,2048]{1,0:T(8,128)(2,1)}, u32[]{:S(2)}, u32[]{:S(2)}) collective-permute-start(bf16[256,2048]{1,0:T(8,128)(2,1)} %dynamic-slice_convert_fusion.1), channel_id=1, source_target_pairs={{0,1},{1,0},{2,3},{3,2},{4,5},{5,4},{6,7},{7,6},{8,9},{9,8},{10,11... | collective-permute-start | bytes 3145736 | tf_op jit(solution)/shard_map/ppermute | solution.py:69
  363.7 15.2 %slice-start.2 = ((s8[8388608]{0:T(1024)(128)(4,1)}), s8[4194304]{0:T(1024)(128)(4,1)S(1)}, s32[]{:S(2)}) async-start(s8[8388608]{0:T(1024)(128)(4,1)} %bitcast.51), calls=%async_computation.7 | async-start | bytes 8388608
  400.9 18.7 %copy-start.47 = (bf16[512,4,128]{0,2,1:T(8,128)(2,1)S(1)}, bf16[512,4,128]{0,2,1:T(8,128)(2,1)}, u32[]{:S(2)}) copy-start(bf16[512,4,128]{0,2,1:T(8,128)(2,1)} %copy-done.46) | copy-start | bytes 1572868
  425.6 15.3 %slice-start.4 = ((s8[8388608]{0:T(1024)(128)(4,1)}), s8[4194304]{0:T(1024)(128)(4,1)S(1)}, s32[]{:S(2)}) async-start(s8[8388608]{0:T(1024)(128)(4,1)} %bitcast.53), calls=%async_computation.9 | async-start | bytes 8388608
  427.3 13.5 %slice-start.5 = ((s8[8388608]{0:T(1024)(128)(4,1)}), s8[4194304]{0:T(1024)(128)(4,1)S(1)}, s32[]{:S(2)}) async-start(s8[8388608]{0:T(1024)(128)(4,1)} %bitcast.53), calls=%async_computation.10 | async-start | bytes 8388608
  440.9 12.3 %slice-start.6 = ((s8[8388608]{0:T(1024)(128)(4,1)}), s8[4194304]{0:T(1024)(128)(4,1)S(1)}, s32[]{:S(2)}) async-start(s8[8388608]{0:T(1024)(128)(4,1)} %bitcast.55), calls=%async_computation.11 | async-start | bytes 8388608
  459.4 310.8 %all-reduce.5.cloned.1.call-start = ((), (), s32[]{:S(2)}) async-start(), calls=%async_computation.3 | async-start | bytes 12582912 | tf_op jit(solution)/shard_map/psum | solution.py:192
  466.2 23.6 %collective-permute-start.9 = (bf16[128,2048]{1,0:T(8,128)(2,1)S(1)}, bf16[128,2048]{1,0:T(8,128)(2,1)S(1)}, u32[]{:S(2)}, u32[]{:S(2)}) collective-permute-start(bf16[128,2048]{1,0:T(8,128)(2,1)S(1)} %dynamic-slice_convert_fusion.5), channel_id=1, source_target_pairs={{0,2},{1,3},{2,0},{3,1},{4,6},{5,7},{6,4},{7,5},{8,10},{9,11},{10,... | collective-permute-start | bytes 1572872 | tf_op jit(solution)/shard_map/ppermute | solution.py:69
  468.4 21.5 %copy-start.23 = (bf16[512,4096]{1,0:T(8,128)(2,1)S(1)}, bf16[512,4096]{1,0:T(8,128)(2,1)}, u32[]{:S(2)}) copy-start(bf16[512,4096]{1,0:T(8,128)(2,1)} %multiply_convert_fusion) | copy-start | bytes 12582916
  489.9 25.3 %collective-permute-start.10 = (bf16[128,2048]{1,0:T(8,128)(2,1)S(1)}, bf16[128,2048]{1,0:T(8,128)(2,1)S(1)}, u32[]{:S(2)}, u32[]{:S(2)}) collective-permute-start(bf16[128,2048]{1,0:T(8,128)(2,1)S(1)} %add_convert_fusion.2), channel_id=1, source_target_pairs={{0,2},{1,3},{2,0},{3,1},{4,6},{5,7},{6,4},{7,5},{8,10},{9,11},{10,... | collective-permute-start | bytes 1572872 | tf_op jit(solution)/shard_map/ppermute | solution.py:74
  491.5 24.0 %copy-start.44 = (f32[512,64]{0,1:T(8,128)S(1)}, f32[512,64]{0,1:T(8,128)}, u32[]{:S(2)}) copy-start(f32[512,64]{0,1:T(8,128)} %copy-done.43) | copy-start | bytes 393220
  491.5 24.0 %copy-start.52 = (f32[512,64]{0,1:T(8,128)S(1)}, f32[512,64]{0,1:T(8,128)}, u32[]{:S(2)}) copy-start(f32[512,64]{0,1:T(8,128)} %get-tuple-element.96) | copy-start | bytes 393220
  491.5 24.2 %copy-start.5 = (bf16[512,2048]{1,0:T(8,128)(2,1)S(1)}, bf16[512,2048]{1,0:T(8,128)(2,1)}, u32[]{:S(2)}) copy-start(bf16[512,2048]{1,0:T(8,128)(2,1)} %param.13) | copy-start | bytes 6291460
  491.5 24.2 %copy-start.68 = (f32[2048]{0:T(1024)S(1)}, f32[2048]{0:T(1024)}, u32[]{:S(2)}) copy-start(f32[2048]{0:T(1024)} %copy-done.67) | copy-start | bytes 24580
  491.5 24.2 %copy-start.85 = (f32[512]{0:T(512)S(1)}, f32[512]{0:T(512)}, u32[]{:S(2)}) copy-start(f32[512]{0:T(512)} %copy-done.84) | copy-start | bytes 6148
  515.4 23.7 %collective-permute-start.11 = (bf16[256,2048]{1,0:T(8,128)(2,1)S(1)}, bf16[256,2048]{1,0:T(8,128)(2,1)S(1)}, u32[]{:S(2)}, u32[]{:S(2)}) collective-permute-start(bf16[256,2048]{1,0:T(8,128)(2,1)S(1)} %pad_maximum_fusion.4), channel_id=1, source_target_pairs={{0,1},{1,0},{2,3},{3,2},{4,5},{5,4},{6,7},{7,6},{8,9},{9,8},{10,11... | collective-permute-start | bytes 3145736 | tf_op jit(solution)/shard_map/ppermute | solution.py:74
  615.1 24.8 %collective-permute-start.12 = (bf16[256,2048]{1,0:T(8,128)(2,1)S(1)}, bf16[256,2048]{1,0:T(8,128)(2,1)S(1)}, u32[]{:S(2)}, u32[]{:S(2)}) collective-permute-start(bf16[256,2048]{1,0:T(8,128)(2,1)S(1)} %dynamic-slice_convert_fusion), channel_id=1, source_target_pairs={{0,1},{1,0},{2,3},{3,2},{4,5},{5,4},{6,7},{7,6},{8,9},{9,8},{10,11... | collective-permute-start | bytes 3145736 | tf_op jit(solution)/shard_map/ppermute | solution.py:69
  640.3 24.9 %collective-permute-start.13 = (bf16[128,2048]{1,0:T(8,128)(2,1)S(1)}, bf16[128,2048]{1,0:T(8,128)(2,1)S(1)}, u32[]{:S(2)}, u32[]{:S(2)}) collective-permute-start(bf16[128,2048]{1,0:T(8,128)(2,1)S(1)} %dynamic-slice_convert_fusion.4), channel_id=1, source_target_pairs={{0,2},{1,3},{2,0},{3,1},{4,6},{5,7},{6,4},{7,5},{8,10},{9,11},{10,... | collective-permute-start | bytes 1572872 | tf_op jit(solution)/shard_map/ppermute | solution.py:69
  665.3 25.4 %copy-start.77 = (f32[2048]{0:T(1024)S(1)}, f32[2048]{0:T(1024)}, u32[]{:S(2)}) copy-start(f32[2048]{0:T(1024)} %get-tuple-element.47) | copy-start | bytes 24580
  665.3 25.1 %collective-permute-start.14 = (bf16[128,2048]{1,0:T(8,128)(2,1)S(1)}, bf16[128,2048]{1,0:T(8,128)(2,1)S(1)}, u32[]{:S(2)}, u32[]{:S(2)}) collective-permute-start(bf16[128,2048]{1,0:T(8,128)(2,1)S(1)} %add_convert_fusion.1), channel_id=1, source_target_pairs={{0,2},{1,3},{2,0},{3,1},{4,6},{5,7},{6,4},{7,5},{8,10},{9,11},{10,... | collective-permute-start | bytes 1572872 | tf_op jit(solution)/shard_map/ppermute | solution.py:74
  690.5 26.3 %slice-start.12 = ((s8[5767168]{0:T(1024)(128)(4,1)}), s8[4194304]{0:T(1024)(128)(4,1)S(1)}, s32[]{:S(2)}) async-start(s8[5767168]{0:T(1024)(128)(4,1)} %bitcast.61), calls=%async_computation.17 | async-start | bytes 8388608
  690.6 23.6 %collective-permute-start.15 = (bf16[256,2048]{1,0:T(8,128)(2,1)S(1)}, bf16[256,2048]{1,0:T(8,128)(2,1)S(1)}, u32[]{:S(2)}, u32[]{:S(2)}) collective-permute-start(bf16[256,2048]{1,0:T(8,128)(2,1)S(1)} %pad_maximum_fusion.6), channel_id=1, source_target_pairs={{0,1},{1,0},{2,3},{3,2},{4,5},{5,4},{6,7},{7,6},{8,9},{9,8},{10,11... | collective-permute-start | bytes 3145736 | tf_op jit(solution)/shard_map/ppermute | solution.py:74
  690.6 1.2 collective-permute-start.19
  691.9 4.0 collective-permute-start.20
  695.8 21.0 %slice-start.13 = ((s8[5767168]{0:T(1024)(128)(4,1)}), s8[1572864]{0:T(1024)(128)(4,1)S(1)}, s32[]{:S(2)}) async-start(s8[5767168]{0:T(1024)(128)(4,1)} %bitcast.61), calls=%async_computation.18 | async-start | bytes 3145728
  695.8 20.4 %collective-permute-start.21 = (f32[2048]{0:T(1024)S(1)}, f32[2048]{0:T(1024)S(1)}, u32[]{:S(2)}, u32[]{:S(2)}) collective-permute-start(f32[2048]{0:T(1024)S(1)} %add.262), channel_id=1, source_target_pairs={{0,16},{4,20},{8,24},{12,28},{16,0},{20,4},{24,8},{28,12},{1,17},{... | collective-permute-start | bytes 24584 | tf_op jit(solution)/shard_map/ppermute | solution.py:88
  716.1 64.1 %collective-permute-start.16 = (f32[2048]{0:T(1024)S(1)}, f32[2048]{0:T(1024)S(1)}, u32[]{:S(2)}, u32[]{:S(2)}) collective-permute-start(f32[2048]{0:T(1024)S(1)} %get-tuple-element.49), channel_id=1, source_target_pairs={{0,4},{4,0},{8,12},{12,8},{16,20},{20,16},{24,28},{28,24},{1,5},{5... | collective-permute-start | bytes 24584 | tf_op jit(solution)/shard_map/ppermute | solution.py:88
  716.8 11.0 %slice-start.8 = ((s8[5767168]{0:T(1024)(128)(4,1)}), s8[4194304]{0:T(1024)(128)(4,1)S(1)}, s32[]{:S(2)}) async-start(s8[5767168]{0:T(1024)(128)(4,1)} %bitcast.57), calls=%async_computation.13 | async-start | bytes 8388608
  770.2 15.0 %copy-start.28 = (bf16[256,2048]{1,0:T(8,128)(2,1)S(1)}, bf16[256,2048]{1,0:T(8,128)(2,1)}, u32[]{:S(2)}) copy-start(bf16[256,2048]{1,0:T(8,128)(2,1)} %copy-done.27) | copy-start | bytes 3145732
  774.6 10.6 %copy-start.24 = (f32[512,2048]{1,0:T(8,128)S(1)}, f32[512,2048]{1,0:T(8,128)}, u32[]{:S(2)}) copy-start(f32[512,2048]{1,0:T(8,128)} %maximum_convert_fusion.1) | copy-start | bytes 12582916
  780.3 3.7 collective-permute-start.17
  783.9 7.6 collective-permute-start.18
  (75 other events, 327.0 us)
Sparse Core Ops, SparseCore 0:
  19.2 40.0 all-gather.2
  326.2 220.7 all-reduce.6
  551.0 51.1 reduce-scatter.1
  665.5 104.6 all-reduce.4

commit v2 on v1

--- a/solution.py
+++ b/solution.py
@@ -175,9 +175,10 @@
         value_part = all_values[:, group_index * HEAD_DIM : (group_index + 1) * HEAD_DIM]
         mixed_parts.append(jnp.dot(probs_low, value_part, preferred_element_type=jnp.float32))
     attended = jnp.concatenate(mixed_parts, axis=1).astype(jnp.bfloat16)
-    (branch,) = permute_sum(
-        [jnp.dot(attended, w_out, preferred_element_type=jnp.float32)], [0], "tensor"
-    )
+    branch_part = jnp.dot(attended, w_out, preferred_element_type=jnp.float32)
+    branch_top = lax.psum(branch_part[:half_rows].astype(jnp.bfloat16), "tensor")
+    (branch_bottom,) = permute_sum([branch_part[half_rows:]], [0], "tensor")
+    branch = jnp.concatenate([branch_top.astype(jnp.float32), branch_bottom], axis=0)
     middle = source + keep_rows * branch
     normed_two_full, norm_two_back = jax.vjp(rms_norm, middle, gain_two.astype(jnp.float32))
     normed_two = normed_two_full.astype(jnp.bfloat16)

time: 802 us -> 810 us (level)
    psum x0 -> x1, waiting for transfers between devices: none -> 23.1 us  [on_device(): lax.psum(branch_part[:half_rows].astype(jnp.bfloat16), 'tensor')]
    ppermute x8, waiting for transfers between devices: 157 us -> 138 us  [permute_sum(): got = lax.ppermute(send, axis, partner_perm(size, 1 << step))]
    ppermute x8, waiting for transfers between devices: 167 us -> 159 us  [permute_sum(): got = lax.ppermute(pieces, axis, partner_perm(size, 1 << step))]
    unnamed x229 -> x231, local copies, waits for them, and re-layouts: 16 us -> 16.4 us
  transfers between devices with their start and end apart: 26 -> 27, of which waited for: 22 -> 23; matrix products, arithmetic and copies ran while one was open for 22% -> 23% of each run, Pallas kernels for 0% -> 0%
where the time goes in v2:
time: 810 us; the launch traced here: 806 us
  waiting for transfers between devices  445 us (55%)
  matrix products  178 us (22%)
  other arithmetic  116 us (14%)
  local copies, waits for them, and re-layouts  24.4 us (3%)
  starting transfers between devices  17.5 us (2%)
  between operations  15.8 us (2%)
  blocking collectives  10.6 us (1%)
    ppermute x8, waiting for transfers between devices, permute_sum(): got = lax.ppermute(pieces, axis, partner_perm(size, 1 << step))  159 us
    ppermute x8, waiting for transfers between devices, permute_sum(): got = lax.ppermute(send, axis, partner_perm(size, 1 << step))  138 us
    dot_general x15, matrix products, right_trans(): lax.dot_general(left, right, (((1,), (1,)), ((), ())), preferred_element_...  78.8 us
    reduce_scatter x1, waiting for transfers between devices, on_device(): lax.psum_scatter(d_kv_cat, 'dp', scatter_dimension=0, tiled=True)  55 us
    dot_general x15, matrix products, left_trans(): lax.dot_general(left, right, (((0,), (0,)), ((), ())), preferred_element_...  50.7 us
    psum x2, waiting for transfers between devices, dp_sum(): return [lax.psum(grad.astype(jnp.bfloat16), 'dp') for grad in grads]  38.4 us
    convert_element_type x2, other arithmetic, on_device(): d_scores = (probs * (d_probs - row_delta)).astype(jnp.bfloat16)  29.1 us
    convert_element_type x7, other arithmetic, on_device(): grad.astype(jnp.float32)  27 us
  transfers between devices with their start and end apart: 27, of which 23 were waited for; matrix products, arithmetic and copies ran while one was open for 23% of the time, Pallas kernels for 0%

profile of v2, /device:TPU:0, one launch (start us, length us, event | category | flops | bytes accessed | tf_op | source)
XLA Modules:
  0.0 806.2 jit_solution(9838666598106268058)
XLA Ops:
  11.2 2.8 convolution_convert_fusion.1
  19.2 10.6 %all-gather = bf16[8,1,512]{2,1,0:T(2,128)(2,1)S(1)} all-gather(bf16[1,1,512]{2,1,0:T(2,128)(2,1)S(1)} %reshape.231), channel_id=1, replica_groups=mesh['dp'=8,'tensor'=4] {'dp'}, dimensions={0}, use_global_device_ids=true | all-gather | bytes 9216 | tf_op jit(solution)/shard_map/all_gather | solution.py:163
  29.9 3.7 fusion.97
  33.9 25.4 %all-gather.3.cloned.1.call-done = bf16[4096,512]{0,1:T(8,128)(2,1)} async-done(((bf16[512,512]{0,1:T(8,128)(2,1)}), bf16[4096,512]{0,1:T(8,128)(2,1)}) %all-gather.3.cloned.1.call-update) | async-done | bytes 4194320 | tf_op jit(solution)/shard_map/all_gather | solution.py:158
  59.3 4.7 fusion.105
  64.1 3.4 copy-done.10
  69.6 3.5 fusion.106
  74.4 3.7 fusion.107
  79.5 5.5 fusion.108
  86.3 7.1 fusion.34
  106.3 12.7 %collective-permute-done = bf16[128,2048]{1,0:T(8,128)(2,1)} collective-permute-done((bf16[128,2048]{1,0:T(8,128)(2,1)S(1)}, bf16[128,2048]{1,0:T(8,128)(2,1)}, u32[]{:S(2)}, u32[]{:S(2)}) %collective-permute-start) | collective-permute-done | bytes 524320 | tf_op jit(solution)/shard_map/ppermute | solution.py:69
  123.0 11.8 %collective-permute-done.1 = bf16[64,2048]{1,0:T(8,128)(2,1)} collective-permute-done((bf16[64,2048]{1,0:T(8,128)(2,1)S(1)}, bf16[64,2048]{1,0:T(8,128)(2,1)}, u32[]{:S(2)}, u32[]{:S(2)}) %collective-permute-start.1) | collective-permute-done | bytes 262176 | tf_op jit(solution)/shard_map/ppermute | solution.py:69
  135.9 2.7 slice.235
  138.7 19.0 %collective-permute-done.2 = bf16[64,2048]{1,0:T(8,128)(2,1)S(1)} collective-permute-done((bf16[64,2048]{1,0:T(8,128)(2,1)S(1)}, bf16[64,2048]{1,0:T(8,128)(2,1)S(1)}, u32[]{:S(2)}, u32[]{:S(2)}) %collective-permute-start.2) | collective-permute-done | bytes 262176 | tf_op jit(solution)/shard_map/ppermute | solution.py:74
  157.8 8.4 %fusion.40 = f32[512,1408]{1,0:T(8,128)} fusion(bf16[1408,2048]{1,0:T(8,128)(2,1)} %param.24, bf16[512,2048]{1,0:T(8,128)(2,1)} %param.25, f32[512]{0:T(512)S(1)} %get-tuple-element.99), kind=kOutput, calls=%fused_computation.126 | convolution fusion | flops 2955935744 | bytes 10749952 | tf_op jit(solution)/shard_map/dot_general | solution.py:45
  166.2 11.6 %collective-permute-done.3 = bf16[128,2048]{1,0:T(8,128)(2,1)S(1)} collective-permute-done((bf16[128,2048]{1,0:T(8,128)(2,1)S(1)}, bf16[128,2048]{1,0:T(8,128)(2,1)S(1)}, u32[]{:S(2)}, u32[]{:S(2)}) %collective-permute-start.3) | collective-permute-done | bytes 524320 | tf_op jit(solution)/shard_map/ppermute | solution.py:74
  179.0 23.1 %all-reduce.6.cloned.1.call-done = bf16[256,2048]{1,0:T(8,128)(2,1)} async-done(((bf16[256,2048]{1,0:T(8,128)(2,1)}), bf16[256,2048]{1,0:T(8,128)(2,1)}) %all-reduce.6.cloned.1.call-update) | async-done | bytes 1048592 | tf_op jit(solution)/shard_map/psum | solution.py:179
  202.1 3.3 multiply_reduce_fusion.6
  205.5 3.4 multiply_convert_fusion.5
  209.0 5.9 fusion.109
  214.9 4.6 multiply_convert_fusion.6
  219.6 3.4 fusion.113
  223.1 5.3 fusion.111
  228.3 5.8 fusion.112
  234.1 5.0 convolution_add_fusion.4
  239.1 5.1 fusion.38
  244.3 2.7 dynamic-slice_convert_fusion.2
  248.3 24.0 %collective-permute-done.4 = bf16[256,2048]{1,0:T(8,128)(2,1)} collective-permute-done((bf16[256,2048]{1,0:T(8,128)(2,1)}, bf16[256,2048]{1,0:T(8,128)(2,1)}, u32[]{:S(2)}, u32[]{:S(2)}) %collective-permute-start.4) | collective-permute-done | bytes 1048608 | tf_op jit(solution)/shard_map/ppermute | solution.py:69
  277.8 23.2 %collective-permute-done.5 = bf16[128,2048]{1,0:T(8,128)(2,1)} collective-permute-done((bf16[128,2048]{1,0:T(8,128)(2,1)}, bf16[128,2048]{1,0:T(8,128)(2,1)}, u32[]{:S(2)}, u32[]{:S(2)}) %collective-permute-start.5) | collective-permute-done | bytes 524320 | tf_op jit(solution)/shard_map/ppermute | solution.py:69
  302.6 25.5 %collective-permute-done.6 = bf16[128,2048]{1,0:T(8,128)(2,1)S(1)} collective-permute-done((bf16[128,2048]{1,0:T(8,128)(2,1)S(1)}, bf16[128,2048]{1,0:T(8,128)(2,1)S(1)}, u32[]{:S(2)}, u32[]{:S(2)}) %collective-permute-start.6) | collective-permute-done | bytes 524320 | tf_op jit(solution)/shard_map/ppermute | solution.py:74
  331.3 5.9 fusion.110
  337.3 18.2 %collective-permute-done.7 = bf16[256,2048]{1,0:T(8,128)(2,1)} collective-permute-done((bf16[256,2048]{1,0:T(8,128)(2,1)}, bf16[256,2048]{1,0:T(8,128)(2,1)}, u32[]{:S(2)}, u32[]{:S(2)}) %collective-permute-start.7) | collective-permute-done | bytes 1048608 | tf_op jit(solution)/shard_map/ppermute | solution.py:74
  359.4 3.4 multiply_reduce_fusion.4
  362.8 3.9 convert_add_fusion.1
  370.9 4.6 fusion.42
  375.4 5.6 fusion.44
  381.1 4.7 fusion.54
  385.9 22.0 %multiply_reduce_fusion.2 = (f32[512]{0:T(512)S(1)}, f32[512]{0:T(512)S(1)}, f32[512]{0:T(512)S(1)}, f32[512]{0:T(512)}, f32[512,4096]{1,0:T(8,128)}) fusion(f32[512,4096]{1,0:T(8,128)S(1)} %bitcast.52, f32[512]{0:T(512)S(1)} %copy-done.80, s32[512]{0:T(512)S(1)} %copy-done.75, pred[4096]{0:T(1024)(128)(4,1)S(1)} %bitcast.96, s32[512]{0:T(512)S(1)} %copy-done.72, ...), kind=kOutput, calls=%fused_computation.7 | convolution fusion | flops 578811904 | bytes 68329472 | tf_op jit(solution)/shard_map/dot_general | solution.py:45
  407.8 18.6 %multiply_convert_fusion.2 = (bf16[512,4096]{1,0:T(8,128)(2,1)}, bf16[512,4096]{1,0:T(8,128)(2,1)}, bf16[512,4096]{1,0:T(8,128)(2,1)}) fusion(f32[512,4096]{1,0:T(8,128)} %get-tuple-element.109, f32[512]{0:T(512)S(1)} %get-tuple-element.51, f32[512,4096]{1,0:T(8,128)S(1)} %bitcast.52, f32[512]{0:T(512)S(1)} %copy-done.80, s32[512]{0:T(512)S(1)} %copy-done.75, ...), kind=kLoop, calls=%fused_computation.6 | loop fusion | flops 39845888 | bytes 62951424 | tf_op jit(solution)/shard_map/convert_element_type | solution.py:236
  426.5 3.4 fusion.77
  434.1 10.4 %multiply_convert_fusion = bf16[512,4096]{1,0:T(8,128)(2,1)} fusion(f32[512,4096]{1,0:T(8,128)} %fusion.42, f32[512]{0:T(512)S(1)} %copy-done.90, f32[512,4096]{1,0:T(8,128)} %copy-done.10, f32[512]{0:T(512)S(1)} %copy-done.87, s32[512]{0:T(512)S(1)} %copy-done.76, pred[4096]{0:T(1024)(128)(4,1)S(1)} %bitcast.98, s32[512]{0:T(512)S(1)} %copy-done.73, ...), kind=kLoop, calls=%fused_computation | loop fusion | flops 18874368 | bytes 21000192 | tf_op jit(solution)/shard_map/convert_element_type | solution.py:236
  444.6 3.0 fusion.13
  447.7 4.9 fusion.24
  452.6 3.6 fusion.21
  456.3 3.7 fusion.10
  460.0 3.9 fusion.11
  466.2 4.2 convolution_multiply_fusion.2
  476.8 20.7 %collective-permute-done.9 = bf16[128,2048]{1,0:T(8,128)(2,1)S(1)} collective-permute-done((bf16[128,2048]{1,0:T(8,128)(2,1)S(1)}, bf16[128,2048]{1,0:T(8,128)(2,1)S(1)}, u32[]{:S(2)}, u32[]{:S(2)}) %collective-permute-start.9) | collective-permute-done | bytes 524320 | tf_op jit(solution)/shard_map/ppermute | solution.py:69
  499.4 23.4 %collective-permute-done.10 = bf16[128,2048]{1,0:T(8,128)(2,1)S(1)} collective-permute-done((bf16[128,2048]{1,0:T(8,128)(2,1)S(1)}, bf16[128,2048]{1,0:T(8,128)(2,1)S(1)}, u32[]{:S(2)}, u32[]{:S(2)}) %collective-permute-start.10) | collective-permute-done | bytes 524320 | tf_op jit(solution)/shard_map/ppermute | solution.py:74
  523.5 2.8 fusion.92
  526.3 2.7 fusion.82
  529.0 19.2 %collective-permute-done.11 = bf16[256,2048]{1,0:T(8,128)(2,1)S(1)} collective-permute-done((bf16[256,2048]{1,0:T(8,128)(2,1)S(1)}, bf16[256,2048]{1,0:T(8,128)(2,1)S(1)}, u32[]{:S(2)}, u32[]{:S(2)}) %collective-permute-start.11) | collective-permute-done | bytes 1048608 | tf_op jit(solution)/shard_map/ppermute | solution.py:74
  553.4 55.0 %reduce-scatter.2.cloned.1.call-done = bf16[512,512]{0,1:T(8,128)(2,1)} async-done(((bf16[4096,512]{0,1:T(8,128)(2,1)}), bf16[512,512]{0,1:T(8,128)(2,1)}) %reduce-scatter.2.cloned.1.call-update) | async-done | bytes 524304 | tf_op jit(solution)/shard_map/reduce_scatter | solution.py:247
  611.6 2.8 fusion.80
  622.8 23.3 %collective-permute-done.12 = bf16[256,2048]{1,0:T(8,128)(2,1)S(1)} collective-permute-done((bf16[256,2048]{1,0:T(8,128)(2,1)S(1)}, bf16[256,2048]{1,0:T(8,128)(2,1)S(1)}, u32[]{:S(2)}, u32[]{:S(2)}) %collective-permute-start.12) | collective-permute-done | bytes 1048608 | tf_op jit(solution)/shard_map/ppermute | solution.py:69
  648.9 22.4 %collective-permute-done.13 = bf16[128,2048]{1,0:T(8,128)(2,1)S(1)} collective-permute-done((bf16[128,2048]{1,0:T(8,128)(2,1)S(1)}, bf16[128,2048]{1,0:T(8,128)(2,1)S(1)}, u32[]{:S(2)}, u32[]{:S(2)}) %collective-permute-start.13) | collective-permute-done | bytes 524320 | tf_op jit(solution)/shard_map/ppermute | solution.py:69
  671.5 25.0 %collective-permute-done.14 = bf16[128,2048]{1,0:T(8,128)(2,1)S(1)} collective-permute-done((bf16[128,2048]{1,0:T(8,128)(2,1)S(1)}, bf16[128,2048]{1,0:T(8,128)(2,1)S(1)}, u32[]{:S(2)}, u32[]{:S(2)}) %collective-permute-start.14) | collective-permute-done | bytes 524320 | tf_op jit(solution)/shard_map/ppermute | solution.py:74
  703.5 16.8 %collective-permute-done.15 = bf16[256,2048]{1,0:T(8,128)(2,1)S(1)} collective-permute-done((bf16[256,2048]{1,0:T(8,128)(2,1)S(1)}, bf16[256,2048]{1,0:T(8,128)(2,1)S(1)}, u32[]{:S(2)}, u32[]{:S(2)}) %collective-permute-start.15) | collective-permute-done | bytes 1048608 | tf_op jit(solution)/shard_map/ppermute | solution.py:74
  722.9 5.8 convert_element_type.291
  728.7 5.2 convert_element_type.292
  734.0 6.0 convert_element_type.293
  740.0 36.4 %all-reduce.8.cloned.1.call-done = (bf16[2048,512]{1,0:T(8,128)(2,1)}, bf16[2048,256]{1,0:T(8,128)(2,1)}, bf16[2048,256]{1,0:T(8,128)(2,1)}, bf16[512,2048]{1,0:T(8,128)(2,1)}) async-done(((bf16[2048,512]{1,0:T(8,128)(2,1)}, bf16[2048,256]{1,0:T(8,128)(2,1)}, bf16[2048,256]{1,0:T(8,128)(2,1)}, bf16[512,2048]{1,0:T(8,128)(2,1)}), (bf16[2048,512]{1,0:T(8,128)(2,1)}, bf16[2048,256]{1,0:T(8,128)(2,1)}, ...) | async-done | bytes 6291472 | tf_op jit(solution)/shard_map/psum | solution.py:193
  776.4 4.3 convert_element_type.284
  791.4 7.4 fusion.17
  (368 shorter events, 110.1 us)
Async XLA Ops:
  7.2 92.6 %copy-start = (bf16[512,2048]{1,0:T(8,128)(2,1)S(1)}, bf16[512,2048]{1,0:T(8,128)(2,1)}, u32[]{:S(2)}) copy-start(bf16[512,2048]{1,0:T(8,128)(2,1)} %param.20) | copy-start | bytes 6291460
  7.2 52.1 %all-gather.3.cloned.1.call-start = ((), (), s32[]{:S(2)}) async-start(), calls=%async_computation.1 | async-start | bytes 4718592 | tf_op jit(solution)/shard_map/all_gather | solution.py:158
  10.4 19.5 %copy-start.84 = (f32[512]{0:T(512)}, f32[512]{0:T(512)S(1)}, u32[]{:S(2)}) copy-start(f32[512]{0:T(512)S(1)} %fusion.85) | copy-start | bytes 6148
  11.1 18.8 %copy-start.67 = (f32[2048]{0:T(1024)}, f32[2048]{0:T(1024)S(1)}, u32[]{:S(2)}) copy-start(f32[2048]{0:T(1024)S(1)} %convert_element_type.226) | copy-start | bytes 24580
  11.2 68.3 %copy-start.65 = (s32[2,2,8,128]{3,1,2,0:T(2,128)}, s32[2,2,8,128]{3,1,2,0:T(2,128)S(1)}, u32[]{:S(2)}) copy-start(s32[2,2,8,128]{3,1,2,0:T(2,128)S(1)} %copy.24) | copy-start | bytes 49156
  15.8 63.6 %copy-start.71 = (s32[512]{0:T(512)}, s32[512]{0:T(512)S(1)}, u32[]{:S(2)}) copy-start(s32[512]{0:T(512)S(1)} %get-tuple-element.63) | copy-start | bytes 6148
  17.1 16.6 %copy-start.43 = (f32[512,64]{0,1:T(8,128)}, f32[512,64]{0,1:T(8,128)S(1)}, u32[]{:S(2)}) copy-start(f32[512,64]{0,1:T(8,128)S(1)} %get-tuple-element.98) | copy-start | bytes 393220
  19.1 183.0 %all-reduce.6.cloned.1.call-start = ((), (), s32[]{:S(2)}) async-start(), calls=%async_computation.2 | async-start | bytes 2097152 | tf_op jit(solution)/shard_map/psum | solution.py:179
  29.9 49.6 %copy-start.69 = (pred[1,4,8,128]{3,1,2,0:T(4,128)(4,1)}, pred[1,4,8,128]{3,1,2,0:T(4,128)(4,1)S(1)}, u32[]{:S(2)}) copy-start(pred[1,4,8,128]{3,1,2,0:T(4,128)(4,1)S(1)} %copy.25) | copy-start | bytes 12292
  29.9 49.6 %copy-start.74 = (s32[512]{0:T(512)}, s32[512]{0:T(512)S(1)}, u32[]{:S(2)}) copy-start(s32[512]{0:T(512)S(1)} %iota_add_fusion) | copy-start | bytes 6148
  33.9 45.6 %copy-start.46 = (bf16[512,4,128]{0,2,1:T(8,128)(2,1)}, bf16[512,4,128]{0,2,1:T(8,128)(2,1)S(1)}, u32[]{:S(2)}) copy-start(bf16[512,4,128]{0,2,1:T(8,128)(2,1)S(1)} %pad_maximum_fusion.6) | copy-start | bytes 1572868
  73.2 20.3 %copy-start.7 = (f32[512,4096]{1,0:T(8,128)}, f32[512,4096]{1,0:T(8,128)S(1)}, u32[]{:S(2)}) copy-start(f32[512,4096]{1,0:T(8,128)S(1)} %get-tuple-element.104) | copy-start | bytes 25165828
  78.2 17.2 %copy-start.8 = (f32[512,4096]{1,0:T(8,128)}, f32[512,4096]{1,0:T(8,128)S(1)}, u32[]{:S(2)}) copy-start(f32[512,4096]{1,0:T(8,128)S(1)} %get-tuple-element.106) | copy-start | bytes 25165828
  85.0 12.7 %copy-start.9 = (f32[512,4096]{1,0:T(8,128)}, f32[512,4096]{1,0:T(8,128)S(1)}, u32[]{:S(2)}) copy-start(f32[512,4096]{1,0:T(8,128)S(1)} %get-tuple-element.108) | copy-start | bytes 25165828
  103.1 32.8 %copy-start.91 = (bf16[2048]{0:T(1024)(128)(2,1)S(1)}, bf16[2048]{0:T(1024)(128)(2,1)}, u32[]{:S(2)}) copy-start(bf16[2048]{0:T(1024)(128)(2,1)} %param.21) | copy-start | bytes 12292
  104.7 14.2 %collective-permute-start = (bf16[128,2048]{1,0:T(8,128)(2,1)S(1)}, bf16[128,2048]{1,0:T(8,128)(2,1)}, u32[]{:S(2)}, u32[]{:S(2)}) collective-permute-start(bf16[128,2048]{1,0:T(8,128)(2,1)S(1)} %dynamic-slice_convert_fusion.6), channel_id=1, source_target_pairs={{0,1},{1,0},{2,3},{3,2},{4,5},{5,4},{6,7},{7,6},{8,9},{9,8},{10,11... | collective-permute-start | bytes 1572872 | tf_op jit(solution)/shard_map/ppermute | solution.py:69
  120.5 14.3 %collective-permute-start.1 = (bf16[64,2048]{1,0:T(8,128)(2,1)S(1)}, bf16[64,2048]{1,0:T(8,128)(2,1)}, u32[]{:S(2)}, u32[]{:S(2)}) collective-permute-start(bf16[64,2048]{1,0:T(8,128)(2,1)S(1)} %dynamic-slice_convert_fusion.7), channel_id=1, source_target_pairs={{0,2},{1,3},{2,0},{3,1},{4,6},{5,7},{6,4},{7,5},{8,10},{9,11},{10,... | collective-permute-start | bytes 786440 | tf_op jit(solution)/shard_map/ppermute | solution.py:69
  135.8 21.9 %collective-permute-start.2 = (bf16[64,2048]{1,0:T(8,128)(2,1)S(1)}, bf16[64,2048]{1,0:T(8,128)(2,1)S(1)}, u32[]{:S(2)}, u32[]{:S(2)}) collective-permute-start(bf16[64,2048]{1,0:T(8,128)(2,1)S(1)} %add_convert_fusion.5), channel_id=1, source_target_pairs={{0,2},{1,3},{2,0},{3,1},{4,6},{5,7},{6,4},{7,5},{8,10},{9,11},{10,... | collective-permute-start | bytes 786440 | tf_op jit(solution)/shard_map/ppermute | solution.py:74
  138.7 414.7 %all-reduce.10.cloned.1.call-start = ((), (), s32[]{:S(2)}) async-start(), calls=%async_computation.5 | async-start | bytes 34603008 | tf_op jit(solution)/shard_map/psum | solution.py:193
  157.8 20.0 %collective-permute-start.3 = (bf16[128,2048]{1,0:T(8,128)(2,1)S(1)}, bf16[128,2048]{1,0:T(8,128)(2,1)S(1)}, u32[]{:S(2)}, u32[]{:S(2)}) collective-permute-start(bf16[128,2048]{1,0:T(8,128)(2,1)S(1)} %pad_maximum_fusion.9), channel_id=1, source_target_pairs={{0,1},{1,0},{2,3},{3,2},{4,5},{5,4},{6,7},{7,6},{8,9},{9,8},{10,11... | collective-permute-start | bytes 1572872 | tf_op jit(solution)/shard_map/ppermute | solution.py:74
  219.6 19.6 %copy-start.95 = (bf16[512,1408]{1,0:T(8,128)(2,1)}, bf16[512,1408]{1,0:T(8,128)(2,1)S(1)}, u32[]{:S(2)}) copy-start(bf16[512,1408]{1,0:T(8,128)(2,1)S(1)} %get-tuple-element.66) | copy-start | bytes 4325380
  223.0 11.1 %slice-start.16 = ((s8[5767168]{0:T(1024)(128)(4,1)}), s8[4194304]{0:T(1024)(128)(4,1)S(1)}, s32[]{:S(2)}) async-start(s8[5767168]{0:T(1024)(128)(4,1)} %bitcast.106), calls=%async_computation.22 | async-start | bytes 8388608
  247.0 25.3 %collective-permute-start.4 = (bf16[256,2048]{1,0:T(8,128)(2,1)}, bf16[256,2048]{1,0:T(8,128)(2,1)}, u32[]{:S(2)}, u32[]{:S(2)}) collective-permute-start(bf16[256,2048]{1,0:T(8,128)(2,1)} %dynamic-slice_convert_fusion.2), channel_id=1, source_target_pairs={{0,1},{1,0},{2,3},{3,2},{4,5},{5,4},{6,7},{7,6},{8,9},{9,8},{10,11... | collective-permute-start | bytes 3145736 | tf_op jit(solution)/shard_map/ppermute | solution.py:69
  276.7 24.3 %collective-permute-start.5 = (bf16[128,2048]{1,0:T(8,128)(2,1)}, bf16[128,2048]{1,0:T(8,128)(2,1)}, u32[]{:S(2)}, u32[]{:S(2)}) collective-permute-start(bf16[128,2048]{1,0:T(8,128)(2,1)} %dynamic-slice_convert_fusion.5), channel_id=1, source_target_pairs={{0,2},{1,3},{2,0},{3,1},{4,6},{5,7},{6,4},{7,5},{8,10},{9,11},{10,... | collective-permute-start | bytes 1572872 | tf_op jit(solution)/shard_map/ppermute | solution.py:69
  302.5 25.6 %collective-permute-start.6 = (bf16[128,2048]{1,0:T(8,128)(2,1)S(1)}, bf16[128,2048]{1,0:T(8,128)(2,1)S(1)}, u32[]{:S(2)}, u32[]{:S(2)}) collective-permute-start(bf16[128,2048]{1,0:T(8,128)(2,1)S(1)} %add_convert_fusion.3), channel_id=1, source_target_pairs={{0,2},{1,3},{2,0},{3,1},{4,6},{5,7},{6,4},{7,5},{8,10},{9,11},{10,... | collective-permute-start | bytes 1572872 | tf_op jit(solution)/shard_map/ppermute | solution.py:74
  330.1 25.4 %collective-permute-start.7 = (bf16[256,2048]{1,0:T(8,128)(2,1)}, bf16[256,2048]{1,0:T(8,128)(2,1)}, u32[]{:S(2)}, u32[]{:S(2)}) collective-permute-start(bf16[256,2048]{1,0:T(8,128)(2,1)} %pad_maximum_fusion.2), channel_id=1, source_target_pairs={{0,1},{1,0},{2,3},{3,2},{4,5},{5,4},{6,7},{7,6},{8,9},{9,8},{10,11... | collective-permute-start | bytes 3145736 | tf_op jit(solution)/shard_map/ppermute | solution.py:74
  331.2 277.1 %reduce-scatter.2.cloned.1.call-start = ((), (), s32[]{:S(2)}) async-start(), calls=%async_computation.3 | async-start | bytes 4718592 | tf_op jit(solution)/shard_map/reduce_scatter | solution.py:247
  331.3 24.2 %copy-start.35 = (bf16[128,2048]{1,0:T(8,128)(2,1)S(1)}, bf16[128,2048]{1,0:T(8,128)(2,1)}, u32[]{:S(2)}) copy-start(bf16[128,2048]{1,0:T(8,128)(2,1)} %copy-done.34) | copy-start | bytes 1572868
  331.3 24.2 %copy-start.37 = (bf16[128,2048]{1,0:T(8,128)(2,1)S(1)}, bf16[128,2048]{1,0:T(8,128)(2,1)}, u32[]{:S(2)}) copy-start(bf16[128,2048]{1,0:T(8,128)(2,1)} %copy-done.36) | copy-start | bytes 1572868
  337.3 30.8 %copy-start.45 = (f32[512,2048]{1,0:T(8,128)}, f32[512,2048]{1,0:T(8,128)S(1)}, u32[]{:S(2)}) copy-start(f32[512,2048]{1,0:T(8,128)S(1)} %fusion.110) | copy-start | bytes 12582916
  369.4 101.1 %collective-permute-start.8 = (bf16[256,2048]{1,0:T(8,128)(2,1)}, bf16[256,2048]{1,0:T(8,128)(2,1)}, u32[]{:S(2)}, u32[]{:S(2)}) collective-permute-start(bf16[256,2048]{1,0:T(8,128)(2,1)} %dynamic-slice_convert_fusion.1), channel_id=1, source_target_pairs={{0,1},{1,0},{2,3},{3,2},{4,5},{5,4},{6,7},{7,6},{8,9},{9,8},{10,11... | collective-permute-start | bytes 3145736 | tf_op jit(solution)/shard_map/ppermute | solution.py:69
  370.9 14.9 %slice-start.2 = ((s8[8388608]{0:T(1024)(128)(4,1)}), s8[4194304]{0:T(1024)(128)(4,1)S(1)}, s32[]{:S(2)}) async-start(s8[8388608]{0:T(1024)(128)(4,1)} %bitcast.51), calls=%async_computation.8 | async-start | bytes 8388608
  375.4 10.3 %slice-start = ((s8[8388608]{0:T(1024)(128)(4,1)}), s8[4194304]{0:T(1024)(128)(4,1)S(1)}, s32[]{:S(2)}) async-start(s8[8388608]{0:T(1024)(128)(4,1)} %bitcast.49), calls=%async_computation.6 | async-start | bytes 8388608
  375.4 10.3 %slice-start.3 = ((s8[8388608]{0:T(1024)(128)(4,1)}), s8[4194304]{0:T(1024)(128)(4,1)S(1)}, s32[]{:S(2)}) async-start(s8[8388608]{0:T(1024)(128)(4,1)} %bitcast.51), calls=%async_computation.9 | async-start | bytes 8388608
  407.8 18.6 %copy-start.47 = (bf16[512,4,128]{0,2,1:T(8,128)(2,1)S(1)}, bf16[512,4,128]{0,2,1:T(8,128)(2,1)}, u32[]{:S(2)}) copy-start(bf16[512,4,128]{0,2,1:T(8,128)(2,1)} %copy-done.46) | copy-start | bytes 1572868
  432.4 15.3 %slice-start.4 = ((s8[8388608]{0:T(1024)(128)(4,1)}), s8[4194304]{0:T(1024)(128)(4,1)S(1)}, s32[]{:S(2)}) async-start(s8[8388608]{0:T(1024)(128)(4,1)} %bitcast.53), calls=%async_computation.10 | async-start | bytes 8388608
  434.1 13.5 %slice-start.5 = ((s8[8388608]{0:T(1024)(128)(4,1)}), s8[4194304]{0:T(1024)(128)(4,1)S(1)}, s32[]{:S(2)}) async-start(s8[8388608]{0:T(1024)(128)(4,1)} %bitcast.53), calls=%async_computation.11 | async-start | bytes 8388608
  447.7 12.3 %slice-start.6 = ((s8[8388608]{0:T(1024)(128)(4,1)}), s8[4194304]{0:T(1024)(128)(4,1)S(1)}, s32[]{:S(2)}) async-start(s8[8388608]{0:T(1024)(128)(4,1)} %bitcast.55), calls=%async_computation.12 | async-start | bytes 8388608
  466.2 310.2 %all-reduce.8.cloned.1.call-start = ((), (), s32[]{:S(2)}) async-start(), calls=%async_computation.4 | async-start | bytes 12582912 | tf_op jit(solution)/shard_map/psum | solution.py:193
  472.9 24.5 %collective-permute-start.9 = (bf16[128,2048]{1,0:T(8,128)(2,1)S(1)}, bf16[128,2048]{1,0:T(8,128)(2,1)S(1)}, u32[]{:S(2)}, u32[]{:S(2)}) collective-permute-start(bf16[128,2048]{1,0:T(8,128)(2,1)S(1)} %dynamic-slice_convert_fusion.4), channel_id=1, source_target_pairs={{0,2},{1,3},{2,0},{3,1},{4,6},{5,7},{6,4},{7,5},{8,10},{9,11},{10,... | collective-permute-start | bytes 1572872 | tf_op jit(solution)/shard_map/ppermute | solution.py:69
  475.2 22.5 %copy-start.26 = (bf16[512,4096]{1,0:T(8,128)(2,1)S(1)}, bf16[512,4096]{1,0:T(8,128)(2,1)}, u32[]{:S(2)}) copy-start(bf16[512,4096]{1,0:T(8,128)(2,1)} %multiply_convert_fusion) | copy-start | bytes 12582916
  497.6 25.2 %collective-permute-start.10 = (bf16[128,2048]{1,0:T(8,128)(2,1)S(1)}, bf16[128,2048]{1,0:T(8,128)(2,1)S(1)}, u32[]{:S(2)}, u32[]{:S(2)}) collective-permute-start(bf16[128,2048]{1,0:T(8,128)(2,1)S(1)} %add_convert_fusion.2), channel_id=1, source_target_pairs={{0,2},{1,3},{2,0},{3,1},{4,6},{5,7},{6,4},{7,5},{8,10},{9,11},{10,... | collective-permute-start | bytes 1572872 | tf_op jit(solution)/shard_map/ppermute | solution.py:74
  499.2 23.9 %copy-start.44 = (f32[512,64]{0,1:T(8,128)S(1)}, f32[512,64]{0,1:T(8,128)}, u32[]{:S(2)}) copy-start(f32[512,64]{0,1:T(8,128)} %copy-done.43) | copy-start | bytes 393220
  499.2 23.9 %copy-start.52 = (f32[512,64]{0,1:T(8,128)S(1)}, f32[512,64]{0,1:T(8,128)}, u32[]{:S(2)}) copy-start(f32[512,64]{0,1:T(8,128)} %get-tuple-element.96) | copy-start | bytes 393220
  499.3 24.1 %copy-start.5 = (bf16[512,2048]{1,0:T(8,128)(2,1)S(1)}, bf16[512,2048]{1,0:T(8,128)(2,1)}, u32[]{:S(2)}) copy-start(bf16[512,2048]{1,0:T(8,128)(2,1)} %param.13) | copy-start | bytes 6291460
  499.3 24.1 %copy-start.68 = (f32[2048]{0:T(1024)S(1)}, f32[2048]{0:T(1024)}, u32[]{:S(2)}) copy-start(f32[2048]{0:T(1024)} %copy-done.67) | copy-start | bytes 24580
  499.3 24.1 %copy-start.85 = (f32[512]{0:T(512)S(1)}, f32[512]{0:T(512)}, u32[]{:S(2)}) copy-start(f32[512]{0:T(512)} %copy-done.84) | copy-start | bytes 6148
  523.1 25.2 %collective-permute-start.11 = (bf16[256,2048]{1,0:T(8,128)(2,1)S(1)}, bf16[256,2048]{1,0:T(8,128)(2,1)S(1)}, u32[]{:S(2)}, u32[]{:S(2)}) collective-permute-start(bf16[256,2048]{1,0:T(8,128)(2,1)S(1)} %pad_maximum_fusion.3), channel_id=1, source_target_pairs={{0,1},{1,0},{2,3},{3,2},{4,5},{5,4},{6,7},{7,6},{8,9},{9,8},{10,11... | collective-permute-start | bytes 3145736 | tf_op jit(solution)/shard_map/ppermute | solution.py:74
  621.3 24.8 %collective-permute-start.12 = (bf16[256,2048]{1,0:T(8,128)(2,1)S(1)}, bf16[256,2048]{1,0:T(8,128)(2,1)S(1)}, u32[]{:S(2)}, u32[]{:S(2)}) collective-permute-start(bf16[256,2048]{1,0:T(8,128)(2,1)S(1)} %dynamic-slice_convert_fusion), channel_id=1, source_target_pairs={{0,1},{1,0},{2,3},{3,2},{4,5},{5,4},{6,7},{7,6},{8,9},{9,8},{10,11... | collective-permute-start | bytes 3145736 | tf_op jit(solution)/shard_map/ppermute | solution.py:69
  646.4 24.8 %collective-permute-start.13 = (bf16[128,2048]{1,0:T(8,128)(2,1)S(1)}, bf16[128,2048]{1,0:T(8,128)(2,1)S(1)}, u32[]{:S(2)}, u32[]{:S(2)}) collective-permute-start(bf16[128,2048]{1,0:T(8,128)(2,1)S(1)} %dynamic-slice_convert_fusion.3), channel_id=1, source_target_pairs={{0,2},{1,3},{2,0},{3,1},{4,6},{5,7},{6,4},{7,5},{8,10},{9,11},{10,... | collective-permute-start | bytes 1572872 | tf_op jit(solution)/shard_map/ppermute | solution.py:69
  671.4 25.4 %copy-start.77 = (f32[2048]{0:T(1024)S(1)}, f32[2048]{0:T(1024)}, u32[]{:S(2)}) copy-start(f32[2048]{0:T(1024)} %get-tuple-element.47) | copy-start | bytes 24580
  671.4 25.1 %collective-permute-start.14 = (bf16[128,2048]{1,0:T(8,128)(2,1)S(1)}, bf16[128,2048]{1,0:T(8,128)(2,1)S(1)}, u32[]{:S(2)}, u32[]{:S(2)}) collective-permute-start(bf16[128,2048]{1,0:T(8,128)(2,1)S(1)} %add_convert_fusion.1), channel_id=1, source_target_pairs={{0,2},{1,3},{2,0},{3,1},{4,6},{5,7},{6,4},{7,5},{8,10},{9,11},{10,... | collective-permute-start | bytes 1572872 | tf_op jit(solution)/shard_map/ppermute | solution.py:74
  696.6 26.3 %slice-start.12 = ((s8[5767168]{0:T(1024)(128)(4,1)}), s8[4194304]{0:T(1024)(128)(4,1)S(1)}, s32[]{:S(2)}) async-start(s8[5767168]{0:T(1024)(128)(4,1)} %bitcast.61), calls=%async_computation.18 | async-start | bytes 8388608
  696.7 23.5 %collective-permute-start.15 = (bf16[256,2048]{1,0:T(8,128)(2,1)S(1)}, bf16[256,2048]{1,0:T(8,128)(2,1)S(1)}, u32[]{:S(2)}, u32[]{:S(2)}) collective-permute-start(bf16[256,2048]{1,0:T(8,128)(2,1)S(1)} %pad_maximum_fusion.5), channel_id=1, source_target_pairs={{0,1},{1,0},{2,3},{3,2},{4,5},{5,4},{6,7},{7,6},{8,9},{9,8},{10,11... | collective-permute-start | bytes 3145736 | tf_op jit(solution)/shard_map/ppermute | solution.py:74
  696.8 1.2 collective-permute-start.19
  698.0 4.0 collective-permute-start.20
  702.0 20.9 %slice-start.13 = ((s8[5767168]{0:T(1024)(128)(4,1)}), s8[1572864]{0:T(1024)(128)(4,1)S(1)}, s32[]{:S(2)}) async-start(s8[5767168]{0:T(1024)(128)(4,1)} %bitcast.61), calls=%async_computation.19 | async-start | bytes 3145728
  702.0 20.3 %collective-permute-start.21 = (f32[2048]{0:T(1024)S(1)}, f32[2048]{0:T(1024)S(1)}, u32[]{:S(2)}, u32[]{:S(2)}) collective-permute-start(f32[2048]{0:T(1024)S(1)} %add.276), channel_id=1, source_target_pairs={{0,16},{4,20},{8,24},{12,28},{16,0},{20,4},{24,8},{28,12},{1,17},{... | collective-permute-start | bytes 24584 | tf_op jit(solution)/shard_map/ppermute | solution.py:88
  722.2 64.2 %collective-permute-start.16 = (f32[2048]{0:T(1024)S(1)}, f32[2048]{0:T(1024)S(1)}, u32[]{:S(2)}, u32[]{:S(2)}) collective-permute-start(f32[2048]{0:T(1024)S(1)} %get-tuple-element.49), channel_id=1, source_target_pairs={{0,4},{4,0},{8,12},{12,8},{16,20},{20,16},{24,28},{28,24},{1,5},{5... | collective-permute-start | bytes 24584 | tf_op jit(solution)/shard_map/ppermute | solution.py:88
  722.9 11.0 %slice-start.8 = ((s8[5767168]{0:T(1024)(128)(4,1)}), s8[4194304]{0:T(1024)(128)(4,1)S(1)}, s32[]{:S(2)}) async-start(s8[5767168]{0:T(1024)(128)(4,1)} %bitcast.57), calls=%async_computation.14 | async-start | bytes 8388608
  776.4 15.0 %copy-start.31 = (bf16[256,2048]{1,0:T(8,128)(2,1)S(1)}, bf16[256,2048]{1,0:T(8,128)(2,1)}, u32[]{:S(2)}) copy-start(bf16[256,2048]{1,0:T(8,128)(2,1)} %copy-done.30) | copy-start | bytes 3145732
  780.7 10.6 %copy-start.27 = (f32[512,2048]{1,0:T(8,128)S(1)}, f32[512,2048]{1,0:T(8,128)}, u32[]{:S(2)}) copy-start(f32[512,2048]{1,0:T(8,128)} %maximum_convert_fusion.1) | copy-start | bytes 12582916
  786.4 3.7 collective-permute-start.17
  790.1 8.8 %collective-permute-start.18 = (f32[2048]{0:T(1024)S(1)}, f32[2048]{0:T(1024)S(1)}, u32[]{:S(2)}, u32[]{:S(2)}) collective-permute-start(f32[2048]{0:T(1024)S(1)} %add.273), channel_id=1, source_target_pairs={{0,16},{4,20},{8,24},{12,28},{16,0},{20,4},{24,8},{28,12},{1,17},{... | collective-permute-start | bytes 24584 | tf_op jit(solution)/shard_map/ppermute | solution.py:88
  (77 other events, 339.2 us)
Sparse Core Ops, SparseCore 0:
  19.2 40.0 all-gather.2
  138.8 63.2 all-reduce.5
  331.4 221.9 all-reduce.9
  557.1 51.1 reduce-scatter.1
  671.7 104.6 all-reduce.7

commit v3 on v2

--- a/solution.py
+++ b/solution.py
@@ -1,6 +1,10 @@
+import functools
+
 import jax
 import jax.numpy as jnp
 from jax import lax
+from jax.experimental import pallas as pl
+from jax.experimental.pallas import tpu as pltpu
 from jax.sharding import PartitionSpec as P
 
 
@@ -45,6 +49,252 @@
     return lax.dot_general(
         left, right, (((1,), (1,)), ((), ())), preferred_element_type=jnp.float32
     )
+
+
+def _allowed(qpos, own, kpos, kalive, start, width):
+    slots = lax.broadcasted_iota(jnp.int32, (1, width), 1) + start
+    return (kpos <= qpos) & ((kalive > 0) | (slots == own))
+
+
+def _attn_fwd_kernel(
+    chunk_ref, qblock_ref, q_ref, k_ref, v_ref, qpos_ref, own_ref, kpos_ref, kalive_ref,
+    o_ref, lse_ref, m_ref, l_ref, acc_ref, *, heads, halves, chunk, chunks, scale,
+):
+    rows = q_ref.shape[0] // halves
+    for head in range(heads):
+        for half in range(halves):
+            row_sl = pl.ds(half * rows, rows)
+            col_sl = pl.ds(head * HEAD_DIM, HEAD_DIM)
+            q = q_ref[row_sl, col_sl]
+            qpos = qpos_ref[row_sl, :]
+            own = own_ref[row_sl, :]
+            limit = qblock_ref[half]
+
+            def scores(c):
+                start = pl.multiple_of(c * chunk, chunk)
+                k = k_ref[pl.ds(start, chunk), :]
+                s = lax.dot_general(
+                    q, k, (((1,), (1,)), ((), ())), preferred_element_type=jnp.float32
+                ) * scale
+                ok = _allowed(
+                    qpos, own, kpos_ref[:, pl.ds(start, chunk)],
+                    kalive_ref[:, pl.ds(start, chunk)], start, chunk,
+                )
+                return jnp.where(ok, s, MASKED_SCORE), start
+
+            m_ref[...] = jnp.full(m_ref.shape, -jnp.inf, jnp.float32)
+            l_ref[...] = jnp.zeros(l_ref.shape, jnp.float32)
+
+            def stats(c, carry):
+                @pl.when(chunk_ref[c] <= limit)
+                def _():
+                    s, _ = scores(c)
+                    m_old = m_ref[...]
+                    m_new = jnp.maximum(m_old, jnp.max(s, axis=1, keepdims=True))
+                    l_ref[...] = l_ref[...] * jnp.exp(m_old - m_new) + jnp.sum(
+                        jnp.exp(s - m_new), axis=1, keepdims=True
+                    )
+                    m_ref[...] = m_new
+
+                return carry
+
+            lax.fori_loop(0, chunks, stats, 0)
+            lse = m_ref[...] + jnp.log(l_ref[...])
+            acc_ref[...] = jnp.zeros(acc_ref.shape, jnp.float32)
+
+            def accumulate(c, carry):
+                @pl.when(chunk_ref[c] <= limit)
+                def _():
+                    s, start = scores(c)
+                    p = jnp.exp(s - lse).astype(jnp.bfloat16)
+                    v = v_ref[pl.ds(start, chunk), :]
+                    acc_ref[...] += jnp.dot(p, v, preferred_element_type=jnp.float32)
+
+                return carry
+
+            lax.fori_loop(0, chunks, accumulate, 0)
+            o_ref[row_sl, col_sl] = acc_ref[...].astype(o_ref.dtype)
+            lse_ref[head, row_sl, :] = lse
+
+
+def _attn_bwd_kernel(
+    chunk_ref, qblock_ref, q_ref, k_ref, v_ref, do_ref, lse_ref, qpos_ref, own_ref, kpos_ref,
+    kalive_ref, dq_ref, dk_ref, dv_ref, delta_ref, dqacc_ref, *, heads, halves, chunk, chunks,
+    scale,
+):
+    rows = q_ref.shape[0] // halves
+    dk_ref[...] = jnp.zeros(dk_ref.shape, jnp.float32)
+    dv_ref[...] = jnp.zeros(dv_ref.shape, jnp.float32)
+    for head in range(heads):
+        for half in range(halves):
+            row_sl = pl.ds(half * rows, rows)
+            col_sl = pl.ds(head * HEAD_DIM, HEAD_DIM)
+            q = q_ref[row_sl, col_sl]
+            do = do_ref[row_sl, col_sl]
+            lse = lse_ref[head, row_sl, :]
+            qpos = qpos_ref[row_sl, :]
+            own = own_ref[row_sl, :]
+            limit = qblock_ref[half]
+
+            def probs_of(c):
+                start = pl.multiple_of(c * chunk, chunk)
+                k = k_ref[pl.ds(start, chunk), :]
+                v = v_ref[pl.ds(start, chunk), :]
+                s = lax.dot_general(
+                    q, k, (((1,), (1,)), ((), ())), preferred_element_type=jnp.float32
+                ) * scale
+                ok = _allowed(
+                    qpos, own, kpos_ref[:, pl.ds(start, chunk)],
+                    kalive_ref[:, pl.ds(start, chunk)], start, chunk,
+                )
+                p = jnp.where(ok, jnp.exp(jnp.where(ok, s, MASKED_SCORE) - lse), 0.0)
+                dp = lax.dot_general(
+                    do, v, (((1,), (1,)), ((), ())), preferred_element_type=jnp.float32
+                )
+                return p, dp, k, start
+
+            delta_ref[...] = jnp.zeros(delta_ref.shape, jnp.float32)
+
+            def deltas(c, carry):
+                @pl.when(chunk_ref[c] <= limit)
+                def _():
+                    p, dp, _, _ = probs_of(c)
+                    delta_ref[...] += jnp.sum(p * dp, axis=1, keepdims=True)
+
+                return carry
+
+            lax.fori_loop(0, chunks, deltas, 0)
+            delta = delta_ref[...]
+            dqacc_ref[...] = jnp.zeros(dqacc_ref.shape, jnp.float32)
+
+            def grads(c, carry):
+                @pl.when(chunk_ref[c] <= limit)
+                def _():
+                    p, dp, k, start = probs_of(c)
+                    ds = (p * (dp - delta)).astype(jnp.bfloat16)
+                    dqacc_ref[...] += jnp.dot(ds, k, preferred_element_type=jnp.float32)
+                    key_sl = pl.ds(start, chunk)
+                    dk_ref[key_sl, :] += lax.dot_general(
+                        ds, q, (((0,), (0,)), ((), ())), preferred_element_type=jnp.float32
+                    ) * scale
+                    dv_ref[key_sl, :] += lax.dot_general(
+                        p.astype(jnp.bfloat16), do, (((0,), (0,)), ((), ())),
+                        preferred_element_type=jnp.float32,
+                    )
+
+                return carry
+
+            lax.fori_loop(0, chunks, grads, 0)
+            dq_ref[row_sl, col_sl] = dqacc_ref[...] * scale
+
+
+def _common(query_low, all_kv, local_groups):
+    rows = query_low.shape[0]
+    length = all_kv.shape[0]
+    heads = query_low.shape[1] // HEAD_DIM // local_groups
+    return rows, length, heads
+
+
+def attention_forward(query_low, all_kv, chunk_blocks, query_blocks, query_pos, own_ids,
+                      key_pos, key_alive, *, local_groups, chunk):
+    rows, length, heads = _common(query_low, all_kv, local_groups)
+    halves = 2
+    chunks = length // chunk
+    kernel = functools.partial(
+        _attn_fwd_kernel, heads=heads, halves=halves, chunk=chunk, chunks=chunks,
+        scale=HEAD_DIM ** (-0.5),
+    )
+    group_cols = heads * HEAD_DIM
+    grid_spec = pltpu.PrefetchScalarGridSpec(
+        num_scalar_prefetch=2,
+        grid=(local_groups,),
+        in_specs=[
+            pl.BlockSpec((rows, group_cols), lambda g, *_: (0, g)),
+            pl.BlockSpec((length, HEAD_DIM), lambda g, *_: (0, g)),
+            pl.BlockSpec((length, HEAD_DIM), lambda g, *_: (0, local_groups + g)),
+            pl.BlockSpec((rows, 1), lambda g, *_: (0, 0)),
+            pl.BlockSpec((rows, 1), lambda g, *_: (0, 0)),
+            pl.BlockSpec((1, length), lambda g, *_: (0, 0)),
+            pl.BlockSpec((1, length), lambda g, *_: (0, 0)),
+        ],
+        out_specs=[
+            pl.BlockSpec((rows, group_cols), lambda g, *_: (0, g)),
+            pl.BlockSpec((heads, rows, 1), lambda g, *_: (g, 0, 0)),
+        ],
+        scratch_shapes=[
+            pltpu.VMEM((rows // halves, 1), jnp.float32),
+            pltpu.VMEM((rows // halves, 1), jnp.float32),
+            pltpu.VMEM((rows // halves, HEAD_DIM), jnp.float32),
+        ],
+    )
+    flops = 4 * rows * length * HEAD_DIM * heads * local_groups
+    return pl.pallas_call(
+        kernel,
+        grid_spec=grid_spec,
+        out_shape=[
+            jax.ShapeDtypeStruct((rows, heads * local_groups * HEAD_DIM), jnp.bfloat16),
+            jax.ShapeDtypeStruct((heads * local_groups, rows, 1), jnp.float32),
+        ],
+        compiler_params=pltpu.CompilerParams(vmem_limit_bytes=48 * 1024 * 1024),
+        cost_estimate=pl.CostEstimate(
+            flops=flops, transcendentals=rows * length * heads * local_groups,
+            bytes_accessed=2 * length * 4 * HEAD_DIM * local_groups,
+        ),
+    )(chunk_blocks, query_blocks, query_low, all_kv, all_kv, query_pos, own_ids, key_pos,
+      key_alive)
+
+
+def attention_backward(query_low, all_kv, d_attended, lse, chunk_blocks, query_blocks,
+                       query_pos, own_ids, key_pos, key_alive, *, local_groups, chunk):
+    rows, length, heads = _common(query_low, all_kv, local_groups)
+    halves = 2
+    chunks = length // chunk
+    kernel = functools.partial(
+        _attn_bwd_kernel, heads=heads, halves=halves, chunk=chunk, chunks=chunks,
+        scale=HEAD_DIM ** (-0.5),
+    )
+    group_cols = heads * HEAD_DIM
+    grid_spec = pltpu.PrefetchScalarGridSpec(
+        num_scalar_prefetch=2,
+        grid=(local_groups,),
+        in_specs=[
+            pl.BlockSpec((rows, group_cols), lambda g, *_: (0, g)),
+            pl.BlockSpec((length, HEAD_DIM), lambda g, *_: (0, g)),
+            pl.BlockSpec((length, HEAD_DIM), lambda g, *_: (0, local_groups + g)),
+            pl.BlockSpec((rows, group_cols), lambda g, *_: (0, g)),
+            pl.BlockSpec((heads, rows, 1), lambda g, *_: (g, 0, 0)),
+            pl.BlockSpec((rows, 1), lambda g, *_: (0, 0)),
+            pl.BlockSpec((rows, 1), lambda g, *_: (0, 0)),
+            pl.BlockSpec((1, length), lambda g, *_: (0, 0)),
+            pl.BlockSpec((1, length), lambda g, *_: (0, 0)),
+        ],
+        out_specs=[
+            pl.BlockSpec((rows, group_cols), lambda g, *_: (0, g)),
+            pl.BlockSpec((length, HEAD_DIM), lambda g, *_: (0, g)),
+            pl.BlockSpec((length, HEAD_DIM), lambda g, *_: (0, g)),
+        ],
+        scratch_shapes=[
+            pltpu.VMEM((rows // halves, 1), jnp.float32),
+            pltpu.VMEM((rows // halves, HEAD_DIM), jnp.float32),
+        ],
+    )
+    flops = 10 * rows * length * HEAD_DIM * heads * local_groups
+    kv_width = local_groups * HEAD_DIM
+    return pl.pallas_call(
+        kernel,
+        grid_spec=grid_spec,
+        out_shape=[
+            jax.ShapeDtypeStruct((rows, heads * local_groups * HEAD_DIM), jnp.float32),
+            jax.ShapeDtypeStruct((length, kv_width), jnp.float32),
+            jax.ShapeDtypeStruct((length, kv_width), jnp.float32),
+        ],
+        compiler_params=pltpu.CompilerParams(vmem_limit_bytes=48 * 1024 * 1024),
+        cost_estimate=pl.CostEstimate(
+            flops=flops, transcendentals=2 * rows * length * heads * local_groups,
+            bytes_accessed=2 * length * 4 * HEAD_DIM * local_groups * 3,
+        ),
+    )(chunk_blocks, query_blocks, query_low, all_kv, all_kv, d_attended, lse, query_pos,
+      own_ids, key_pos, key_alive)
 
 
 def partner_perm(axis_size, mask):
@@ -107,10 +357,8 @@
     row_count = inputs.shape[0]
     local_heads = w_query.shape[1] // HEAD_DIM
     local_groups = w_key.shape[1] // HEAD_DIM
-    group_size = local_heads // local_groups
     half_rows = row_count // 2
     length = row_count * lax.axis_size("dp")
-    score_scale = HEAD_DIM ** (-0.5)
     key_pos = (
         block_table[:, None] * half_rows + jnp.arange(half_rows, dtype=jnp.int32)[None, :]
     ).reshape(length)
@@ -142,39 +390,22 @@
     )
     alive_low = active.astype(jnp.bfloat16)
 
-    def allowed_of(alive_all):
-        return (key_pos[None, :] <= query_pos[:, None]) & (
-            (alive_all[None, :] > 0) | (slot_ids[None, :] == own_ids[:, None])
-        )
-
-    def head_scores(head_index, keys_all, allowed):
-        query_part = query_low[:, head_index * HEAD_DIM : (head_index + 1) * HEAD_DIM]
-        group_index = head_index // group_size
-        key_part = keys_all[:, group_index * HEAD_DIM : (group_index + 1) * HEAD_DIM]
-        raw_scores = right_trans(query_part, key_part) * score_scale
-        return jnp.where(allowed, raw_scores, MASKED_SCORE)
-
     kv_width = local_groups * HEAD_DIM
     all_kv = lax.all_gather(
         jnp.concatenate([key_low, value_low], axis=1), "dp", axis=0, tiled=True
     )
-    all_keys = all_kv[:, :kv_width]
-    all_values = all_kv[:, kv_width:]
     all_alive = lax.all_gather(alive_low, "dp", axis=0, tiled=True)
-    allowed_fwd = allowed_of(all_alive)
-    mixed_parts = []
-    lse_parts = []
-    for head_index in range(local_heads):
-        masked = head_scores(head_index, all_keys, allowed_fwd)
-        row_max = jnp.max(masked, axis=1, keepdims=True)
-        shifted = jnp.exp(masked - row_max)
-        row_total = jnp.sum(shifted, axis=1, keepdims=True)
-        probs_low = (shifted / row_total).astype(jnp.bfloat16)
-        lse_parts.append(row_max + jnp.log(row_total))
-        group_index = head_index // group_size
-        value_part = all_values[:, group_index * HEAD_DIM : (group_index + 1) * HEAD_DIM]
-        mixed_parts.append(jnp.dot(probs_low, value_part, preferred_element_type=jnp.float32))
-    attended = jnp.concatenate(mixed_parts, axis=1).astype(jnp.bfloat16)
+    mask_args = dict(
+        chunk_blocks=block_table,
+        query_blocks=lax.dynamic_slice_in_dim(block_table, 2 * lax.axis_index("dp"), 2),
+        query_pos=query_pos[:, None],
+        own_ids=own_ids[:, None],
+        key_pos=key_pos[None, :],
+        key_alive=(all_alive > 0).astype(jnp.int32)[None, :],
+    )
+    attended, lse = attention_forward(
+        query_low, all_kv, local_groups=local_groups, chunk=half_rows, **mask_args
+    )
     branch_part = jnp.dot(attended, w_out, preferred_element_type=jnp.float32)
     branch_top = lax.psum(branch_part[:half_rows].astype(jnp.bfloat16), "tensor")
     (branch_bottom,) = permute_sum([branch_part[half_rows:]], [0], "tensor")
@@ -217,32 +448,10 @@
         (grad_w_gate, grad_w_up, grad_w_down, grad_w_out)
     )
     d_attended = right_trans(d_branch, w_out).astype(jnp.bfloat16)
-    back_keys, back_values = all_keys, all_values
-    allowed_back = allowed_fwd
-    d_query_parts = []
-    d_key_parts = [jnp.zeros((length, HEAD_DIM), jnp.float32) for _ in range(local_groups)]
-    d_value_parts = [jnp.zeros((length, HEAD_DIM), jnp.float32) for _ in range(local_groups)]
-    for head_index in range(local_heads):
-        group_index = head_index // group_size
-        masked = head_scores(head_index, back_keys, allowed_back)
-        probs = jnp.where(allowed_back, jnp.exp(masked - lse_parts[head_index]), 0.0)
-        probs_low = probs.astype(jnp.bfloat16)
-        d_out_part = d_attended[:, head_index * HEAD_DIM : (head_index + 1) * HEAD_DIM]
-        key_part = back_keys[:, group_index * HEAD_DIM : (group_index + 1) * HEAD_DIM]
-        value_part = back_values[:, group_index * HEAD_DIM : (group_index + 1) * HEAD_DIM]
-        query_part = query_low[:, head_index * HEAD_DIM : (head_index + 1) * HEAD_DIM]
-        d_probs = right_trans(d_out_part, value_part)
-        row_delta = jnp.sum(probs * d_probs, axis=1, keepdims=True)
-        d_scores = (probs * (d_probs - row_delta)).astype(jnp.bfloat16)
-        d_query_parts.append(
-            jnp.dot(d_scores, key_part, preferred_element_type=jnp.float32) * score_scale
-        )
-        d_key_parts[group_index] = (
-            d_key_parts[group_index] + left_trans(d_scores, query_part) * score_scale
-        )
-        d_value_parts[group_index] = d_value_parts[group_index] + left_trans(probs_low, d_out_part)
-    d_key_all = jnp.concatenate(d_key_parts, axis=1)
-    d_value_all = jnp.concatenate(d_value_parts, axis=1)
+    d_queries, d_key_all, d_value_all = attention_backward(
+        query_low, all_kv, d_attended, lse, local_groups=local_groups, chunk=half_rows,
+        **mask_args,
+    )
     d_kv_cat = jnp.concatenate([d_key_all, d_value_all], axis=1).astype(jnp.bfloat16)
     d_kv_own = lax.psum_scatter(
         d_kv_cat,
@@ -253,7 +462,7 @@
     d_kv_own, grad_w_out = lax.optimization_barrier((d_kv_own, grad_w_out))
     d_key_own = d_kv_own[:, :kv_width]
     d_value_own = d_kv_own[:, kv_width:]
-    d_queries = jnp.concatenate(d_query_parts, axis=1).reshape(row_count, local_heads, HEAD_DIM)
+    d_queries = d_queries.reshape(row_count, local_heads, HEAD_DIM)
     d_query_low = (
         rotate(d_queries, cos_table, -sin_table)
         .reshape(row_count, local_heads * HEAD_DIM)

time: 810 us -> 778 us (0.960)
  Pallas kernels: 0 us -> 128 us
  matrix products: 178 us -> 78.4 us
  waiting for transfers between devices: 445 us -> 402 us
  other arithmetic: 116 us -> 90.7 us
    pallas_call x0 -> x2, Pallas kernels: none -> 128 us  [the longest x1 69 us: attention_backward(): pl.pallas_call(kernel, grid_spec=grid_spec, out_shape=[jax.ShapeDtypeStru...]
    reduce_scatter x1, waiting for transfers between devices: 55 us -> 0.01 us  [on_device(): lax.psum_scatter(d_kv_cat, 'dp', scatter_dimension=0, tiled=True)]
    dot_general x15 -> x7, matrix products: 78.8 us -> 26.1 us  [right_trans(): lax.dot_general(left, right, (((1,), (1,)), ((), ())), preferred_element_...]
    ppermute x8, waiting for transfers between devices: 138 us -> 169 us  [permute_sum(): got = lax.ppermute(send, axis, partner_perm(size, 1 << step))]
    convert_element_type x2 -> x0, other arithmetic: 29.1 us -> none  [on_device(): d_scores = (probs * (d_probs - row_delta)).astype(jnp.bfloat16)]
    dot_general x15 -> x7, matrix products: 50.7 us -> 25.2 us  [left_trans(): lax.dot_general(left, right, (((0,), (0,)), ((), ())), preferred_element_...]
    dot_general x8 -> x0, matrix products: 22.1 us -> none  [the longest x4 13.3 us: on_device(): jnp.dot(probs_low, value_part, preferred_element_type=jnp.float32)]
    all_gather x1, waiting for transfers between devices: 25.4 us -> 16.4 us  [on_device(): lax.all_gather(jnp.concatenate([key_low, value_low], axis=1), 'dp', axis=...]
  transfers between devices with their start and end apart: 27 -> 27, of which waited for: 23 -> 22; matrix products, arithmetic and copies ran while one was open for 23% -> 14% of each run, Pallas kernels for 0% -> 9%
where the time goes in v3:
time: 778 us; the launch traced here: 771 us
  waiting for transfers between devices  402 us (52%)
  Pallas kernels  128 us (16%)
  other arithmetic  90.7 us (12%)
  matrix products  78.4 us (10%)
  local copies, waits for them, and re-layouts  30.3 us (4%)
  between operations  15.3 us (2%)
  starting transfers between devices  14.5 us (2%)
  blocking collectives  10.8 us (1%)
    ppermute x8, waiting for transfers between devices, permute_sum(): got = lax.ppermute(send, axis, partner_perm(size, 1 << step))  169 us
    ppermute x8, waiting for transfers between devices, permute_sum(): got = lax.ppermute(pieces, axis, partner_perm(size, 1 << step))  155 us
    pallas_call x1, Pallas kernels, attention_backward(): pl.pallas_call(kernel, grid_spec=grid_spec, out_shape=[jax.ShapeDtypeStru...  69 us
    pallas_call x1, Pallas kernels, attention_forward(): pl.pallas_call(kernel, grid_spec=grid_spec, out_shape=[jax.ShapeDtypeStru...  59.4 us
    psum x2, waiting for transfers between devices, dp_sum(): return [lax.psum(grad.astype(jnp.bfloat16), 'dp') for grad in grads]  35.4 us
    convert_element_type x7, other arithmetic, on_device(): grad.astype(jnp.float32)  27 us
    dot_general x7, matrix products, right_trans(): lax.dot_general(left, right, (((1,), (1,)), ((), ())), preferred_element_...  26.1 us
    dot_general x7, matrix products, left_trans(): lax.dot_general(left, right, (((0,), (0,)), ((), ())), preferred_element_...  25.2 us
  transfers between devices with their start and end apart: 27, of which 22 were waited for; matrix products, arithmetic and copies ran while one was open for 14% of the time, Pallas kernels for 9%

profile of v3, /device:TPU:0, one launch (start us, length us, event | category | flops | bytes accessed | tf_op | source)
XLA Modules:
  0.0 770.8 jit_solution(5653404258013631829)
XLA Ops:
  8.1 2.3 fusion.6
  11.2 2.6 convolution_convert_fusion.1
  21.6 3.6 fusion.41
  26.1 2.4 copy.45
  29.8 2.3 subtract_convert_fusion.1
  32.9 10.8 %all-gather = bf16[8,1,512]{2,1,0:T(2,128)(2,1)S(1)} all-gather(bf16[1,1,512]{2,1,0:T(2,128)(2,1)S(1)} %reshape.197), channel_id=1, replica_groups=mesh['dp'=8,'tensor'=4] {'dp'}, dimensions={0}, use_global_device_ids=true | all-gather | bytes 9216 | tf_op jit(solution)/shard_map/all_gather | solution.py:397
  44.4 16.4 %all-gather.3.cloned.1.call-done.k_ref.v_ref = bf16[4096,512]{1,0:T(8,128)(2,1)} async-done(((bf16[512,512]{1,0:T(8,128)(2,1)}), bf16[4096,512]{1,0:T(8,128)(2,1)}) %all-gather.3.cloned.1.call-update) | async-done | bytes 4194320 | tf_op jit(solution)/shard_map/all_gather | solution.py:394
  61.7 59.4 %shard_map.212 = (bf16[512,512]{1,0:T(8,128)(2,1)S(1)}, f32[4,512,1]{2,1,0:T(8,128)S(1)}) custom-call(s32[16]{0:T(128)S(1)} %copy-done.4, s32[2]{0:T(128)S(1)} %dynamic_slice.54.qblock_ref, bf16[512,512]{1,0:T(8,128)(2,1)S(1)} %bitcast.57, bf16[4096,512]{1,0:T(8,128)(2,1)} %all-gather.3.cloned.1.call-done.k_ref.v_ref, ...), custom_call_target="tpu_custom_call" | custom-call | flops 4294967296 | bytes 8388608 | tf_op jit(solution)/shard_map/pallas_call | solution.py:231
  126.8 12.9 %collective-permute-done = bf16[128,2048]{1,0:T(8,128)(2,1)} collective-permute-done((bf16[128,2048]{1,0:T(8,128)(2,1)}, bf16[128,2048]{1,0:T(8,128)(2,1)}, u32[]{:S(2)}, u32[]{:S(2)}) %collective-permute-start) | collective-permute-done | bytes 524320 | tf_op jit(solution)/shard_map/ppermute | solution.py:319
  142.9 2.4 collective-permute-start.1
  145.3 12.0 %collective-permute-done.1 = bf16[64,2048]{1,0:T(8,128)(2,1)} collective-permute-done((bf16[64,2048]{1,0:T(8,128)(2,1)}, bf16[64,2048]{1,0:T(8,128)(2,1)}, u32[]{:S(2)}, u32[]{:S(2)}) %collective-permute-start.1) | collective-permute-done | bytes 262176 | tf_op jit(solution)/shard_map/ppermute | solution.py:319
  157.3 1.9 add_convert_fusion.7
  159.2 2.7 slice.73
  162.0 19.9 %collective-permute-done.2 = bf16[64,2048]{1,0:T(8,128)(2,1)} collective-permute-done((bf16[64,2048]{1,0:T(8,128)(2,1)}, bf16[64,2048]{1,0:T(8,128)(2,1)}, u32[]{:S(2)}, u32[]{:S(2)}) %collective-permute-start.2) | collective-permute-done | bytes 262176 | tf_op jit(solution)/shard_map/ppermute | solution.py:324
  183.1 8.4 %fusion.14 = f32[512,1408]{1,0:T(8,128)} fusion(bf16[1408,2048]{1,0:T(8,128)(2,1)} %param.24, bf16[512,2048]{1,0:T(8,128)(2,1)} %param.25, f32[512]{0:T(512)S(1)} %get-tuple-element.106), kind=kOutput, calls=%fused_computation.70 | convolution fusion | flops 2955935744 | bytes 10749952 | tf_op jit(solution)/shard_map/dot_general | solution.py:49
  191.5 9.9 %collective-permute-done.3 = bf16[128,2048]{1,0:T(8,128)(2,1)S(1)} collective-permute-done((bf16[128,2048]{1,0:T(8,128)(2,1)S(1)}, bf16[128,2048]{1,0:T(8,128)(2,1)S(1)}, u32[]{:S(2)}, u32[]{:S(2)}) %collective-permute-start.3) | collective-permute-done | bytes 524320 | tf_op jit(solution)/shard_map/ppermute | solution.py:324
  202.6 21.4 %all-reduce.6.cloned.1.call-done = bf16[256,2048]{1,0:T(8,128)(2,1)} async-done(((bf16[256,2048]{1,0:T(8,128)(2,1)}), bf16[256,2048]{1,0:T(8,128)(2,1)}) %all-reduce.6.cloned.1.call-update) | async-done | bytes 1048592 | tf_op jit(solution)/shard_map/psum | solution.py:410
  223.9 3.3 multiply_reduce_fusion.2
  227.3 3.8 multiply_convert_fusion.1
  231.1 5.9 fusion.48
  237.1 4.6 multiply_convert_fusion.2
  241.7 3.4 fusion.52
  245.2 5.3 fusion.50
  250.5 5.3 fusion.51
  255.9 5.0 convolution_add_fusion
  260.9 5.1 fusion.12
  266.0 2.7 dynamic-slice_convert_fusion.2
  270.1 23.9 %collective-permute-done.4 = bf16[256,2048]{1,0:T(8,128)(2,1)} collective-permute-done((bf16[256,2048]{1,0:T(8,128)(2,1)}, bf16[256,2048]{1,0:T(8,128)(2,1)}, u32[]{:S(2)}, u32[]{:S(2)}) %collective-permute-start.4) | collective-permute-done | bytes 1048608 | tf_op jit(solution)/shard_map/ppermute | solution.py:319
  294.0 2.2 convert_add_fusion.4
  299.5 23.3 %collective-permute-done.5 = bf16[128,2048]{1,0:T(8,128)(2,1)} collective-permute-done((bf16[128,2048]{1,0:T(8,128)(2,1)}, bf16[128,2048]{1,0:T(8,128)(2,1)}, u32[]{:S(2)}, u32[]{:S(2)}) %collective-permute-start.5) | collective-permute-done | bytes 524320 | tf_op jit(solution)/shard_map/ppermute | solution.py:319
  324.6 25.7 %collective-permute-done.6 = bf16[128,2048]{1,0:T(8,128)(2,1)S(1)} collective-permute-done((bf16[128,2048]{1,0:T(8,128)(2,1)S(1)}, bf16[128,2048]{1,0:T(8,128)(2,1)S(1)}, u32[]{:S(2)}, u32[]{:S(2)}) %collective-permute-start.6) | collective-permute-done | bytes 524320 | tf_op jit(solution)/shard_map/ppermute | solution.py:324
  350.5 8.0 %fusion.49 = f32[512,2048]{1,0:T(8,128)} fusion(bf16[512,1408]{1,0:T(8,128)(2,1)S(1)} %copy-done.52, bf16[1408,2048]{1,0:T(8,128)(2,1)} %param.24), kind=kOutput, calls=%fused_computation.134 | convolution fusion | flops 2952790016 | bytes 11403264 | tf_op jit(solution)/shard_map/dot_general | solution.py:420
  358.5 17.1 %collective-permute-done.7 = bf16[256,2048]{1,0:T(8,128)(2,1)S(1)} collective-permute-done((bf16[256,2048]{1,0:T(8,128)(2,1)S(1)}, bf16[256,2048]{1,0:T(8,128)(2,1)S(1)}, u32[]{:S(2)}, u32[]{:S(2)}) %collective-permute-start.7) | collective-permute-done | bytes 1048608 | tf_op jit(solution)/shard_map/ppermute | solution.py:324
  378.3 3.0 multiply_reduce_fusion
  381.3 4.1 convert_add_fusion.1
  388.0 69.0 %shard_map.213 = (f32[512,512]{1,0:T(8,128)S(1)}, f32[4096,256]{1,0:T(8,128)}, f32[4096,256]{1,0:T(8,128)}) custom-call(s32[16]{0:T(128)S(1)} %copy-done.4, s32[2]{0:T(128)S(1)} %dynamic_slice.54.qblock_ref, bf16[512,512]{1,0:T(8,128)(2,1)S(1)} %bitcast.58, bf16[4096,512]{1,0:T(8,128)(2,1)} %all-gather.3.cloned.1.call-done.k_ref.v_ref, ...), custom_call_target="tpu_custom_call" | custom-call | flops 10737418240 | bytes 25165824 | tf_op jit(solution)/shard_map/pallas_call | solution.py:283
  457.0 2.7 convert.45
  460.9 2.3 pad_maximum_fusion
  463.5 1.9 dynamic-slice_convert_fusion.1
  465.5 24.5 %collective-permute-done.8 = bf16[256,2048]{1,0:T(8,128)(2,1)S(1)} collective-permute-done((bf16[256,2048]{1,0:T(8,128)(2,1)S(1)}, bf16[256,2048]{1,0:T(8,128)(2,1)S(1)}, u32[]{:S(2)}, u32[]{:S(2)}) %collective-permute-start.8) | collective-permute-done | bytes 1048608 | tf_op jit(solution)/shard_map/ppermute | solution.py:319
  492.2 24.5 %collective-permute-done.9 = bf16[128,2048]{1,0:T(8,128)(2,1)S(1)} collective-permute-done((bf16[128,2048]{1,0:T(8,128)(2,1)S(1)}, bf16[128,2048]{1,0:T(8,128)(2,1)S(1)}, u32[]{:S(2)}, u32[]{:S(2)}) %collective-permute-start.9) | collective-permute-done | bytes 524320 | tf_op jit(solution)/shard_map/ppermute | solution.py:319
  518.2 22.7 %collective-permute-done.10 = bf16[128,2048]{1,0:T(8,128)(2,1)S(1)} collective-permute-done((bf16[128,2048]{1,0:T(8,128)(2,1)S(1)}, bf16[128,2048]{1,0:T(8,128)(2,1)S(1)}, u32[]{:S(2)}, u32[]{:S(2)}) %collective-permute-start.10) | collective-permute-done | bytes 524320 | tf_op jit(solution)/shard_map/ppermute | solution.py:324
  543.6 2.8 fusion.16
  546.4 2.7 fusion.34
  549.1 17.1 %collective-permute-done.11 = bf16[256,2048]{1,0:T(8,128)(2,1)S(1)} collective-permute-done((bf16[256,2048]{1,0:T(8,128)(2,1)S(1)}, bf16[256,2048]{1,0:T(8,128)(2,1)S(1)}, u32[]{:S(2)}, u32[]{:S(2)}) %collective-permute-start.11) | collective-permute-done | bytes 1048608 | tf_op jit(solution)/shard_map/ppermute | solution.py:324
  566.7 2.6 maximum_convert_fusion.1
  571.4 2.0 fusion.28
  573.4 2.8 fusion.27
  579.0 2.0 fusion.21
  581.0 2.1 fusion.23
  583.6 3.2 add_add_fusion.2
  587.3 23.9 %collective-permute-done.12 = bf16[256,2048]{1,0:T(8,128)(2,1)S(1)} collective-permute-done((bf16[256,2048]{1,0:T(8,128)(2,1)S(1)}, bf16[256,2048]{1,0:T(8,128)(2,1)S(1)}, u32[]{:S(2)}, u32[]{:S(2)}) %collective-permute-start.12) | collective-permute-done | bytes 1048608 | tf_op jit(solution)/shard_map/ppermute | solution.py:319
  612.3 23.6 %collective-permute-done.13 = bf16[128,2048]{1,0:T(8,128)(2,1)S(1)} collective-permute-done((bf16[128,2048]{1,0:T(8,128)(2,1)S(1)}, bf16[128,2048]{1,0:T(8,128)(2,1)S(1)}, u32[]{:S(2)}, u32[]{:S(2)}) %collective-permute-start.13) | collective-permute-done | bytes 524320 | tf_op jit(solution)/shard_map/ppermute | solution.py:319
  636.2 24.0 %collective-permute-done.14 = bf16[128,2048]{1,0:T(8,128)(2,1)S(1)} collective-permute-done((bf16[128,2048]{1,0:T(8,128)(2,1)S(1)}, bf16[128,2048]{1,0:T(8,128)(2,1)S(1)}, u32[]{:S(2)}, u32[]{:S(2)}) %collective-permute-start.14) | collective-permute-done | bytes 524320 | tf_op jit(solution)/shard_map/ppermute | solution.py:324
  663.3 2.4 collective-permute-done.20
  667.1 18.4 %collective-permute-done.15 = bf16[256,2048]{1,0:T(8,128)(2,1)S(1)} collective-permute-done((bf16[256,2048]{1,0:T(8,128)(2,1)S(1)}, bf16[256,2048]{1,0:T(8,128)(2,1)S(1)}, u32[]{:S(2)}, u32[]{:S(2)}) %collective-permute-start.15) | collective-permute-done | bytes 1048608 | tf_op jit(solution)/shard_map/ppermute | solution.py:324
  688.3 5.8 convert_element_type.242
  694.1 5.2 convert_element_type.243
  699.3 6.0 convert_element_type.244
  705.3 35.4 %all-reduce.8.cloned.1.call-done = (bf16[2048,512]{1,0:T(8,128)(2,1)}, bf16[2048,256]{1,0:T(8,128)(2,1)}, bf16[2048,256]{1,0:T(8,128)(2,1)}, bf16[512,2048]{1,0:T(8,128)(2,1)}) async-done(((bf16[2048,512]{1,0:T(8,128)(2,1)}, bf16[2048,256]{1,0:T(8,128)(2,1)}, bf16[2048,256]{1,0:T(8,128)(2,1)}, bf16[512,2048]{1,0:T(8,128)(2,1)}), (bf16[2048,512]{1,0:T(8,128)(2,1)}, bf16[2048,256]{1,0:T(8,128)(2,1)}, ...) | async-done | bytes 6291472 | tf_op jit(solution)/shard_map/psum | solution.py:424
  740.8 4.3 convert_element_type.235
  748.1 2.7 convert_element_type.241
  752.3 2.2 collective-permute-done.17
  755.8 7.5 fusion.5
  (245 shorter events, 66.3 us)
Async XLA Ops:
  7.2 113.9 %copy-start = (bf16[512,2048]{1,0:T(8,128)(2,1)S(1)}, bf16[512,2048]{1,0:T(8,128)(2,1)}, u32[]{:S(2)}) copy-start(bf16[512,2048]{1,0:T(8,128)(2,1)} %param.20) | copy-start | bytes 6291460
  7.2 6.6 copy-start.45
  7.2 53.6 %all-gather.3.cloned.1.call-start = ((), (), s32[]{:S(2)}) async-start(), calls=%async_computation.1 | async-start | bytes 4718592 | tf_op jit(solution)/shard_map/all_gather | solution.py:394
  7.3 6.5 copy-start.7
  10.4 4.4 copy-start.46
  14.8 6.5 copy-start.4
  14.8 6.6 copy-start.49
  17.9 11.9 %copy-start.30 = (f32[512,64]{1,0:T(8,128)}, f32[512,64]{1,0:T(8,128)S(1)}, u32[]{:S(2)}) copy-start(f32[512,64]{1,0:T(8,128)S(1)} %get-tuple-element.105) | copy-start | bytes 393220
  21.3 202.7 %all-reduce.6.cloned.1.call-start = ((), (), s32[]{:S(2)}) async-start(), calls=%async_computation.2 | async-start | bytes 2097152 | tf_op jit(solution)/shard_map/psum | solution.py:410
  122.4 36.8 %copy-start.48 = (bf16[2048]{0:T(1024)(128)(2,1)S(1)}, bf16[2048]{0:T(1024)(128)(2,1)}, u32[]{:S(2)}) copy-start(bf16[2048]{0:T(1024)(128)(2,1)} %param.21) | copy-start | bytes 12292
  125.3 14.4 %collective-permute-start = (bf16[128,2048]{1,0:T(8,128)(2,1)}, bf16[128,2048]{1,0:T(8,128)(2,1)}, u32[]{:S(2)}, u32[]{:S(2)}) collective-permute-start(bf16[128,2048]{1,0:T(8,128)(2,1)} %dynamic-slice_convert_fusion.6), channel_id=1, source_target_pairs={{0,1},{1,0},{2,3},{3,2},{4,5},{5,4},{6,7},{7,6},{8,9},{9,8},{10,11... | collective-permute-start | bytes 1572872 | tf_op jit(solution)/shard_map/ppermute | solution.py:319
  142.9 14.4 %collective-permute-start.1 = (bf16[64,2048]{1,0:T(8,128)(2,1)}, bf16[64,2048]{1,0:T(8,128)(2,1)}, u32[]{:S(2)}, u32[]{:S(2)}) collective-permute-start(bf16[64,2048]{1,0:T(8,128)(2,1)} %dynamic-slice_convert_fusion.7), channel_id=1, source_target_pairs={{0,2},{1,3},{2,0},{3,1},{4,6},{5,7},{6,4},{7,5},{8,10},{9,11},{10,... | collective-permute-start | bytes 786440 | tf_op jit(solution)/shard_map/ppermute | solution.py:319
  159.2 22.7 %collective-permute-start.2 = (bf16[64,2048]{1,0:T(8,128)(2,1)}, bf16[64,2048]{1,0:T(8,128)(2,1)}, u32[]{:S(2)}, u32[]{:S(2)}) collective-permute-start(bf16[64,2048]{1,0:T(8,128)(2,1)} %add_convert_fusion.7), channel_id=1, source_target_pairs={{0,2},{1,3},{2,0},{3,1},{4,6},{5,7},{6,4},{7,5},{8,10},{9,11},{10,... | collective-permute-start | bytes 786440 | tf_op jit(solution)/shard_map/ppermute | solution.py:324
  162.0 407.3 %all-reduce.10.cloned.1.call-start = ((), (), s32[]{:S(2)}) async-start(), calls=%async_computation.5 | async-start | bytes 34603008 | tf_op jit(solution)/shard_map/psum | solution.py:424
  183.0 18.3 %collective-permute-start.3 = (bf16[128,2048]{1,0:T(8,128)(2,1)S(1)}, bf16[128,2048]{1,0:T(8,128)(2,1)S(1)}, u32[]{:S(2)}, u32[]{:S(2)}) collective-permute-start(bf16[128,2048]{1,0:T(8,128)(2,1)S(1)} %pad_maximum_fusion.7), channel_id=1, source_target_pairs={{0,1},{1,0},{2,3},{3,2},{4,5},{5,4},{6,7},{7,6},{8,9},{9,8},{10,11... | collective-permute-start | bytes 1572872 | tf_op jit(solution)/shard_map/ppermute | solution.py:324
  227.3 9.7 %slice-start.6 = ((s8[5767168]{0:T(1024)(128)(4,1)}), s8[4194304]{0:T(1024)(128)(4,1)S(1)}, s32[]{:S(2)}) async-start(s8[5767168]{0:T(1024)(128)(4,1)} %bitcast.80), calls=%async_computation.12 | async-start | bytes 8388608
  231.1 6.0 slice-start.7
  231.1 5.9 copy-start.50
  241.7 19.1 %copy-start.51 = (bf16[512,1408]{1,0:T(8,128)(2,1)}, bf16[512,1408]{1,0:T(8,128)(2,1)S(1)}, u32[]{:S(2)}) copy-start(bf16[512,1408]{1,0:T(8,128)(2,1)S(1)} %get-tuple-element.72) | copy-start | bytes 4325380
  245.2 10.7 %slice-start.8 = ((s8[5767168]{0:T(1024)(128)(4,1)}), s8[4194304]{0:T(1024)(128)(4,1)S(1)}, s32[]{:S(2)}) async-start(s8[5767168]{0:T(1024)(128)(4,1)} %bitcast.82), calls=%async_computation.14 | async-start | bytes 8388608
  250.5 5.3 slice-start.9
  255.9 5.0 copy-start.38
  268.7 25.3 %collective-permute-start.4 = (bf16[256,2048]{1,0:T(8,128)(2,1)}, bf16[256,2048]{1,0:T(8,128)(2,1)}, u32[]{:S(2)}, u32[]{:S(2)}) collective-permute-start(bf16[256,2048]{1,0:T(8,128)(2,1)} %dynamic-slice_convert_fusion.2), channel_id=1, source_target_pairs={{0,1},{1,0},{2,3},{3,2},{4,5},{5,4},{6,7},{7,6},{8,9},{9,8},{10,11... | collective-permute-start | bytes 3145736 | tf_op jit(solution)/shard_map/ppermute | solution.py:319
  270.1 299.2 %reduce-scatter.2.cloned.1.call-start = ((), (), s32[]{:S(2)}) async-start(), calls=%async_computation.3 | async-start | bytes 4718592 | tf_op jit(solution)/shard_map/reduce_scatter | solution.py:456
  298.4 24.4 %collective-permute-start.5 = (bf16[128,2048]{1,0:T(8,128)(2,1)}, bf16[128,2048]{1,0:T(8,128)(2,1)}, u32[]{:S(2)}, u32[]{:S(2)}) collective-permute-start(bf16[128,2048]{1,0:T(8,128)(2,1)} %dynamic-slice_convert_fusion.5), channel_id=1, source_target_pairs={{0,2},{1,3},{2,0},{3,1},{4,6},{5,7},{6,4},{7,5},{8,10},{9,11},{10,... | collective-permute-start | bytes 1572872 | tf_op jit(solution)/shard_map/ppermute | solution.py:319
  299.5 51.0 %copy-start.52 = (bf16[512,1408]{1,0:T(8,128)(2,1)S(1)}, bf16[512,1408]{1,0:T(8,128)(2,1)}, u32[]{:S(2)}) copy-start(bf16[512,1408]{1,0:T(8,128)(2,1)} %copy-done.51) | copy-start | bytes 4325380
  324.5 25.8 %collective-permute-start.6 = (bf16[128,2048]{1,0:T(8,128)(2,1)S(1)}, bf16[128,2048]{1,0:T(8,128)(2,1)S(1)}, u32[]{:S(2)}, u32[]{:S(2)}) collective-permute-start(bf16[128,2048]{1,0:T(8,128)(2,1)S(1)} %add_convert_fusion.4), channel_id=1, source_target_pairs={{0,2},{1,3},{2,0},{3,1},{4,6},{5,7},{6,4},{7,5},{8,10},{9,11},{10,... | collective-permute-start | bytes 1572872 | tf_op jit(solution)/shard_map/ppermute | solution.py:324
  350.4 25.1 %collective-permute-start.7 = (bf16[256,2048]{1,0:T(8,128)(2,1)S(1)}, bf16[256,2048]{1,0:T(8,128)(2,1)S(1)}, u32[]{:S(2)}, u32[]{:S(2)}) collective-permute-start(bf16[256,2048]{1,0:T(8,128)(2,1)S(1)} %pad_maximum_fusion.2), channel_id=1, source_target_pairs={{0,1},{1,0},{2,3},{3,2},{4,5},{5,4},{6,7},{7,6},{8,9},{9,8},{10,11... | collective-permute-start | bytes 3145736 | tf_op jit(solution)/shard_map/ppermute | solution.py:324
  385.5 71.5 %copy-start.23 = (f32[512,2048]{1,0:T(8,128)}, f32[512,2048]{1,0:T(8,128)S(1)}, u32[]{:S(2)}) copy-start(f32[512,2048]{1,0:T(8,128)S(1)} %convert_add_fusion.1) | copy-start | bytes 12582916
  463.3 277.5 %all-reduce.8.cloned.1.call-start = ((), (), s32[]{:S(2)}) async-start(), calls=%async_computation.4 | async-start | bytes 12582912 | tf_op jit(solution)/shard_map/psum | solution.py:424
  465.5 24.6 %collective-permute-start.8 = (bf16[256,2048]{1,0:T(8,128)(2,1)S(1)}, bf16[256,2048]{1,0:T(8,128)(2,1)S(1)}, u32[]{:S(2)}, u32[]{:S(2)}) collective-permute-start(bf16[256,2048]{1,0:T(8,128)(2,1)S(1)} %dynamic-slice_convert_fusion.1), channel_id=1, source_target_pairs={{0,1},{1,0},{2,3},{3,2},{4,5},{5,4},{6,7},{7,6},{8,9},{9,8},{10,11... | collective-permute-start | bytes 3145736 | tf_op jit(solution)/shard_map/ppermute | solution.py:319
  492.0 49.2 %copy-start.31 = (f32[512,64]{1,0:T(8,128)S(1)}, f32[512,64]{1,0:T(8,128)}, u32[]{:S(2)}) copy-start(f32[512,64]{1,0:T(8,128)} %copy-done.30) | copy-start | bytes 393220
  492.0 49.2 %copy-start.36 = (f32[512,64]{1,0:T(8,128)S(1)}, f32[512,64]{1,0:T(8,128)}, u32[]{:S(2)}) copy-start(f32[512,64]{1,0:T(8,128)} %get-tuple-element.103) | copy-start | bytes 393220
  492.0 24.7 %collective-permute-start.9 = (bf16[128,2048]{1,0:T(8,128)(2,1)S(1)}, bf16[128,2048]{1,0:T(8,128)(2,1)S(1)}, u32[]{:S(2)}, u32[]{:S(2)}) collective-permute-start(bf16[128,2048]{1,0:T(8,128)(2,1)S(1)} %dynamic-slice_convert_fusion.4), channel_id=1, source_target_pairs={{0,2},{1,3},{2,0},{3,1},{4,6},{5,7},{6,4},{7,5},{8,10},{9,11},{10,... | collective-permute-start | bytes 1572872 | tf_op jit(solution)/shard_map/ppermute | solution.py:319
  516.8 24.0 %collective-permute-start.10 = (bf16[128,2048]{1,0:T(8,128)(2,1)S(1)}, bf16[128,2048]{1,0:T(8,128)(2,1)S(1)}, u32[]{:S(2)}, u32[]{:S(2)}) collective-permute-start(bf16[128,2048]{1,0:T(8,128)(2,1)S(1)} %add_convert_fusion.3), channel_id=1, source_target_pairs={{0,2},{1,3},{2,0},{3,1},{4,6},{5,7},{6,4},{7,5},{8,10},{9,11},{10,... | collective-permute-start | bytes 1572872 | tf_op jit(solution)/shard_map/ppermute | solution.py:324
  518.2 23.0 %copy-start.29 = (f32[512,4,128]{2,1,0:T(4,128)S(1)}, f32[512,4,128]{2,1,0:T(4,128)}, u32[]{:S(2)}) copy-start(f32[512,4,128]{2,1,0:T(4,128)} %reshape.194) | copy-start | bytes 3145732
  541.1 25.2 %collective-permute-start.11 = (bf16[256,2048]{1,0:T(8,128)(2,1)S(1)}, bf16[256,2048]{1,0:T(8,128)(2,1)S(1)}, u32[]{:S(2)}, u32[]{:S(2)}) collective-permute-start(bf16[256,2048]{1,0:T(8,128)(2,1)S(1)} %pad_maximum_fusion.3), channel_id=1, source_target_pairs={{0,1},{1,0},{2,3},{3,2},{4,5},{5,4},{6,7},{7,6},{8,9},{9,8},{10,11... | collective-permute-start | bytes 3145736 | tf_op jit(solution)/shard_map/ppermute | solution.py:324
  587.0 24.3 %collective-permute-start.12 = (bf16[256,2048]{1,0:T(8,128)(2,1)S(1)}, bf16[256,2048]{1,0:T(8,128)(2,1)S(1)}, u32[]{:S(2)}, u32[]{:S(2)}) collective-permute-start(bf16[256,2048]{1,0:T(8,128)(2,1)S(1)} %dynamic-slice_convert_fusion), channel_id=1, source_target_pairs={{0,1},{1,0},{2,3},{3,2},{4,5},{5,4},{6,7},{7,6},{8,9},{9,8},{10,11... | collective-permute-start | bytes 3145736 | tf_op jit(solution)/shard_map/ppermute | solution.py:319
  611.6 24.3 %collective-permute-start.13 = (bf16[128,2048]{1,0:T(8,128)(2,1)S(1)}, bf16[128,2048]{1,0:T(8,128)(2,1)S(1)}, u32[]{:S(2)}, u32[]{:S(2)}) collective-permute-start(bf16[128,2048]{1,0:T(8,128)(2,1)S(1)} %dynamic-slice_convert_fusion.3), channel_id=1, source_target_pairs={{0,2},{1,3},{2,0},{3,1},{4,6},{5,7},{6,4},{7,5},{8,10},{9,11},{10,... | collective-permute-start | bytes 1572872 | tf_op jit(solution)/shard_map/ppermute | solution.py:319
  636.1 24.1 %collective-permute-start.14 = (bf16[128,2048]{1,0:T(8,128)(2,1)S(1)}, bf16[128,2048]{1,0:T(8,128)(2,1)S(1)}, u32[]{:S(2)}, u32[]{:S(2)}) collective-permute-start(bf16[128,2048]{1,0:T(8,128)(2,1)S(1)} %add_convert_fusion.1), channel_id=1, source_target_pairs={{0,2},{1,3},{2,0},{3,1},{4,6},{5,7},{6,4},{7,5},{8,10},{9,11},{10,... | collective-permute-start | bytes 1572872 | tf_op jit(solution)/shard_map/ppermute | solution.py:324
  660.3 27.9 %slice-start.4 = ((s8[5767168]{0:T(1024)(128)(4,1)}), s8[4194304]{0:T(1024)(128)(4,1)S(1)}, s32[]{:S(2)}) async-start(s8[5767168]{0:T(1024)(128)(4,1)} %bitcast.67), calls=%async_computation.10 | async-start | bytes 8388608
  660.4 25.1 %collective-permute-start.15 = (bf16[256,2048]{1,0:T(8,128)(2,1)S(1)}, bf16[256,2048]{1,0:T(8,128)(2,1)S(1)}, u32[]{:S(2)}, u32[]{:S(2)}) collective-permute-start(bf16[256,2048]{1,0:T(8,128)(2,1)S(1)} %pad_maximum_fusion.4), channel_id=1, source_target_pairs={{0,1},{1,0},{2,3},{3,2},{4,5},{5,4},{6,7},{7,6},{8,9},{9,8},{10,11... | collective-permute-start | bytes 3145736 | tf_op jit(solution)/shard_map/ppermute | solution.py:324
  660.5 1.2 collective-permute-start.19
  661.7 3.9 collective-permute-start.20
  665.7 22.6 %slice-start.5 = ((s8[5767168]{0:T(1024)(128)(4,1)}), s8[1572864]{0:T(1024)(128)(4,1)S(1)}, s32[]{:S(2)}) async-start(s8[5767168]{0:T(1024)(128)(4,1)} %bitcast.67), calls=%async_computation.11 | async-start | bytes 3145728
  665.7 22.0 %collective-permute-start.21 = (f32[2048]{0:T(1024)S(1)}, f32[2048]{0:T(1024)S(1)}, u32[]{:S(2)}, u32[]{:S(2)}) collective-permute-start(f32[2048]{0:T(1024)S(1)} %add.238), channel_id=1, source_target_pairs={{0,16},{4,20},{8,24},{12,28},{16,0},{20,4},{24,8},{28,12},{1,17},{... | collective-permute-start | bytes 24584 | tf_op jit(solution)/shard_map/ppermute | solution.py:338
  686.0 8.1 %slice-start.2 = ((s8[5767168]{0:T(1024)(128)(4,1)}), s8[4194304]{0:T(1024)(128)(4,1)S(1)}, s32[]{:S(2)}) async-start(s8[5767168]{0:T(1024)(128)(4,1)} %bitcast.65), calls=%async_computation.8 | async-start | bytes 8388608
  687.6 63.2 %collective-permute-start.16 = (f32[2048]{0:T(1024)S(1)}, f32[2048]{0:T(1024)S(1)}, u32[]{:S(2)}, u32[]{:S(2)}) collective-permute-start(f32[2048]{0:T(1024)S(1)} %get-tuple-element.59), channel_id=1, source_target_pairs={{0,4},{4,0},{8,12},{12,8},{16,20},{20,16},{24,28},{28,24},{1,5},{5... | collective-permute-start | bytes 24584 | tf_op jit(solution)/shard_map/ppermute | solution.py:338
  688.3 5.9 slice-start.3
  688.3 11.0 %slice-start = ((s8[5767168]{0:T(1024)(128)(4,1)}), s8[4194304]{0:T(1024)(128)(4,1)S(1)}, s32[]{:S(2)}) async-start(s8[5767168]{0:T(1024)(128)(4,1)} %bitcast.63), calls=%async_computation.6 | async-start | bytes 8388608
  694.1 5.2 slice-start.1
  740.7 5.8 copy-start.42
  740.7 7.4 copy-start.37
  740.7 15.0 %copy-start.28 = (bf16[256,2048]{1,0:T(8,128)(2,1)S(1)}, bf16[256,2048]{1,0:T(8,128)(2,1)}, u32[]{:S(2)}) copy-start(bf16[256,2048]{1,0:T(8,128)(2,1)} %copy-done.27) | copy-start | bytes 3145732
  745.1 10.6 %copy-start.25 = (f32[512,2048]{1,0:T(8,128)S(1)}, f32[512,2048]{1,0:T(8,128)}, u32[]{:S(2)}) copy-start(f32[512,2048]{1,0:T(8,128)} %copy-done.23) | copy-start | bytes 12582916
  746.6 5.7 copy-start.47
  746.6 9.1 %copy-start.11 = (bf16[512,2048]{1,0:T(8,128)(2,1)S(1)}, bf16[512,2048]{1,0:T(8,128)(2,1)}, u32[]{:S(2)}) copy-start(bf16[512,2048]{1,0:T(8,128)(2,1)} %param.13) | copy-start | bytes 6291460
  746.6 9.1 %copy-start.14 = (bf16[256,2048]{1,0:T(8,128)(2,1)S(1)}, bf16[256,2048]{1,0:T(8,128)(2,1)}, u32[]{:S(2)}) copy-start(bf16[256,2048]{1,0:T(8,128)(2,1)} %all-reduce.6.cloned.1.call-done) | copy-start | bytes 3145732
  746.6 9.1 %copy-start.17 = (bf16[128,2048]{1,0:T(8,128)(2,1)S(1)}, bf16[128,2048]{1,0:T(8,128)(2,1)}, u32[]{:S(2)}) copy-start(bf16[128,2048]{1,0:T(8,128)(2,1)} %get-tuple-element.95) | copy-start | bytes 1572868
  746.6 9.1 %copy-start.20 = (bf16[128,2048]{1,0:T(8,128)(2,1)S(1)}, bf16[128,2048]{1,0:T(8,128)(2,1)}, u32[]{:S(2)}) copy-start(bf16[128,2048]{1,0:T(8,128)(2,1)} %get-tuple-element.96) | copy-start | bytes 1572868
  746.6 9.1 %copy-start.21 = (f32[512,2048]{1,0:T(8,128)S(1)}, f32[512,2048]{1,0:T(8,128)}, u32[]{:S(2)}) copy-start(f32[512,2048]{1,0:T(8,128)} %maximum_convert_fusion.1) | copy-start | bytes 12582916
  750.8 3.7 collective-permute-start.17
  754.4 8.8 %collective-permute-start.18 = (f32[2048]{0:T(1024)S(1)}, f32[2048]{0:T(1024)S(1)}, u32[]{:S(2)}, u32[]{:S(2)}) collective-permute-start(f32[2048]{0:T(1024)S(1)} %add.235), channel_id=1, source_target_pairs={{0,16},{4,20},{8,24},{12,28},{16,0},{20,4},{24,8},{28,12},{1,17},{... | collective-permute-start | bytes 24584 | tf_op jit(solution)/shard_map/ppermute | solution.py:338
  755.8 8.1 %copy-start.1 = (bf16[512,2048]{1,0:T(8,128)(2,1)S(1)}, bf16[512,2048]{1,0:T(8,128)(2,1)}, u32[]{:S(2)}) copy-start(bf16[512,2048]{1,0:T(8,128)(2,1)} %param.20) | copy-start | bytes 6291460
  (26 other events, 62.4 us)
Sparse Core Ops, SparseCore 0:
  21.4 39.3 all-gather.2
  162.1 61.7 all-reduce.5
  270.2 221.5 all-reduce.9
  495.5 51.2 reduce-scatter.1
  636.3 104.3 all-reduce.7

commit v4 on v3

--- a/solution.py
+++ b/solution.py
@@ -54,67 +54,6 @@
 def _allowed(qpos, own, kpos, kalive, start, width):
     slots = lax.broadcasted_iota(jnp.int32, (1, width), 1) + start
     return (kpos <= qpos) & ((kalive > 0) | (slots == own))
-
-
-def _attn_fwd_kernel(
-    chunk_ref, qblock_ref, q_ref, k_ref, v_ref, qpos_ref, own_ref, kpos_ref, kalive_ref,
-    o_ref, lse_ref, m_ref, l_ref, acc_ref, *, heads, halves, chunk, chunks, scale,
-):
-    rows = q_ref.shape[0] // halves
-    for head in range(heads):
-        for half in range(halves):
-            row_sl = pl.ds(half * rows, rows)
-            col_sl = pl.ds(head * HEAD_DIM, HEAD_DIM)
-            q = q_ref[row_sl, col_sl]
-            qpos = qpos_ref[row_sl, :]
-            own = own_ref[row_sl, :]
-            limit = qblock_ref[half]
-
-            def scores(c):
-                start = pl.multiple_of(c * chunk, chunk)
-                k = k_ref[pl.ds(start, chunk), :]
-                s = lax.dot_general(
-                    q, k, (((1,), (1,)), ((), ())), preferred_element_type=jnp.float32
-                ) * scale
-                ok = _allowed(
-                    qpos, own, kpos_ref[:, pl.ds(start, chunk)],
-                    kalive_ref[:, pl.ds(start, chunk)], start, chunk,
-                )
-                return jnp.where(ok, s, MASKED_SCORE), start
-
-            m_ref[...] = jnp.full(m_ref.shape, -jnp.inf, jnp.float32)
-            l_ref[...] = jnp.zeros(l_ref.shape, jnp.float32)
-
-            def stats(c, carry):
-                @pl.when(chunk_ref[c] <= limit)
-                def _():
-                    s, _ = scores(c)
-                    m_old = m_ref[...]
-                    m_new = jnp.maximum(m_old, jnp.max(s, axis=1, keepdims=True))
-                    l_ref[...] = l_ref[...] * jnp.exp(m_old - m_new) + jnp.sum(
-                        jnp.exp(s - m_new), axis=1, keepdims=True
-                    )
-                    m_ref[...] = m_new
-
-                return carry
-
-            lax.fori_loop(0, chunks, stats, 0)
-            lse = m_ref[...] + jnp.log(l_ref[...])
-            acc_ref[...] = jnp.zeros(acc_ref.shape, jnp.float32)
-
-            def accumulate(c, carry):
-                @pl.when(chunk_ref[c] <= limit)
-                def _():
-                    s, start = scores(c)
-                    p = jnp.exp(s - lse).astype(jnp.bfloat16)
-                    v = v_ref[pl.ds(start, chunk), :]
-                    acc_ref[...] += jnp.dot(p, v, preferred_element_type=jnp.float32)
-
-                return carry
-
-            lax.fori_loop(0, chunks, accumulate, 0)
-            o_ref[row_sl, col_sl] = acc_ref[...].astype(o_ref.dtype)
-            lse_ref[head, row_sl, :] = lse
 
 
 def _attn_bwd_kernel(
@@ -193,55 +132,6 @@
     length = all_kv.shape[0]
     heads = query_low.shape[1] // HEAD_DIM // local_groups
     return rows, length, heads
-
-
-def attention_forward(query_low, all_kv, chunk_blocks, query_blocks, query_pos, own_ids,
-                      key_pos, key_alive, *, local_groups, chunk):
-    rows, length, heads = _common(query_low, all_kv, local_groups)
-    halves = 2
-    chunks = length // chunk
-    kernel = functools.partial(
-        _attn_fwd_kernel, heads=heads, halves=halves, chunk=chunk, chunks=chunks,
-        scale=HEAD_DIM ** (-0.5),
-    )
-    group_cols = heads * HEAD_DIM
-    grid_spec = pltpu.PrefetchScalarGridSpec(
-        num_scalar_prefetch=2,
-        grid=(local_groups,),
-        in_specs=[
-            pl.BlockSpec((rows, group_cols), lambda g, *_: (0, g)),
-            pl.BlockSpec((length, HEAD_DIM), lambda g, *_: (0, g)),
-            pl.BlockSpec((length, HEAD_DIM), lambda g, *_: (0, local_groups + g)),
-            pl.BlockSpec((rows, 1), lambda g, *_: (0, 0)),
-            pl.BlockSpec((rows, 1), lambda g, *_: (0, 0)),
-            pl.BlockSpec((1, length), lambda g, *_: (0, 0)),
-            pl.BlockSpec((1, length), lambda g, *_: (0, 0)),
-        ],
-        out_specs=[
-            pl.BlockSpec((rows, group_cols), lambda g, *_: (0, g)),
-            pl.BlockSpec((heads, rows, 1), lambda g, *_: (g, 0, 0)),
-        ],
-        scratch_shapes=[
-            pltpu.VMEM((rows // halves, 1), jnp.float32),
-            pltpu.VMEM((rows // halves, 1), jnp.float32),
-            pltpu.VMEM((rows // halves, HEAD_DIM), jnp.float32),
-        ],
-    )
-    flops = 4 * rows * length * HEAD_DIM * heads * local_groups
-    return pl.pallas_call(
-        kernel,
-        grid_spec=grid_spec,
-        out_shape=[
-            jax.ShapeDtypeStruct((rows, heads * local_groups * HEAD_DIM), jnp.bfloat16),
-            jax.ShapeDtypeStruct((heads * local_groups, rows, 1), jnp.float32),
-        ],
-        compiler_params=pltpu.CompilerParams(vmem_limit_bytes=48 * 1024 * 1024),
-        cost_estimate=pl.CostEstimate(
-            flops=flops, transcendentals=rows * length * heads * local_groups,
-            bytes_accessed=2 * length * 4 * HEAD_DIM * local_groups,
-        ),
-    )(chunk_blocks, query_blocks, query_low, all_kv, all_kv, query_pos, own_ids, key_pos,
-      key_alive)
 
 
 def attention_backward(query_low, all_kv, d_attended, lse, chunk_blocks, query_blocks,
@@ -357,8 +247,10 @@
     row_count = inputs.shape[0]
     local_heads = w_query.shape[1] // HEAD_DIM
     local_groups = w_key.shape[1] // HEAD_DIM
+    group_size = local_heads // local_groups
     half_rows = row_count // 2
     length = row_count * lax.axis_size("dp")
+    score_scale = HEAD_DIM ** (-0.5)
     key_pos = (
         block_table[:, None] * half_rows + jnp.arange(half_rows, dtype=jnp.int32)[None, :]
     ).reshape(length)
@@ -403,9 +295,36 @@
         key_pos=key_pos[None, :],
         key_alive=(all_alive > 0).astype(jnp.int32)[None, :],
     )
-    attended, lse = attention_forward(
-        query_low, all_kv, local_groups=local_groups, chunk=half_rows, **mask_args
-    )
+
+    def allowed_of(alive_all):
+        return (key_pos[None, :] <= query_pos[:, None]) & (
+            (alive_all[None, :] > 0) | (slot_ids[None, :] == own_ids[:, None])
+        )
+
+    def head_scores(head_index, keys_all, allowed):
+        query_part = query_low[:, head_index * HEAD_DIM : (head_index + 1) * HEAD_DIM]
+        group_index = head_index // group_size
+        key_part = keys_all[:, group_index * HEAD_DIM : (group_index + 1) * HEAD_DIM]
+        raw_scores = right_trans(query_part, key_part) * score_scale
+        return jnp.where(allowed, raw_scores, MASKED_SCORE)
+
+    all_keys = all_kv[:, :kv_width]
+    all_values = all_kv[:, kv_width:]
+    allowed_fwd = allowed_of(all_alive)
+    mixed_parts = []
+    lse_parts = []
+    for head_index in range(local_heads):
+        masked = head_scores(head_index, all_keys, allowed_fwd)
+        row_max = jnp.max(masked, axis=1, keepdims=True)
+        shifted = jnp.exp(masked - row_max)
+        row_total = jnp.sum(shifted, axis=1, keepdims=True)
+        probs_low = (shifted / row_total).astype(jnp.bfloat16)
+        lse_parts.append(row_max + jnp.log(row_total))
+        group_index = head_index // group_size
+        value_part = all_values[:, group_index * HEAD_DIM : (group_index + 1) * HEAD_DIM]
+        mixed_parts.append(jnp.dot(probs_low, value_part, preferred_element_type=jnp.float32))
+    attended = jnp.concatenate(mixed_parts, axis=1).astype(jnp.bfloat16)
+    lse = jnp.stack(lse_parts)
     branch_part = jnp.dot(attended, w_out, preferred_element_type=jnp.float32)
     branch_top = lax.psum(branch_part[:half_rows].astype(jnp.bfloat16), "tensor")
     (branch_bottom,) = permute_sum([branch_part[half_rows:]], [0], "tensor")

time: 778 us -> 765 us (0.983)
  Pallas kernels: 128 us -> 68.6 us
  matrix products: 78.4 us -> 115 us
  other arithmetic: 90.7 us -> 104 us
    pallas_call x1 -> x0, Pallas kernels: 59.4 us -> none  [attention_forward(): pl.pallas_call(kernel, grid_spec=grid_spec, out_shape=[jax.ShapeDtypeStru...]
    dot_general x7 -> x11, matrix products: 26.1 us -> 46.7 us  [right_trans(): lax.dot_general(left, right, (((1,), (1,)), ((), ())), preferred_element_...]
    dot_general x0 -> x4, matrix products: none -> 10.9 us  [on_device(): jnp.dot(probs_low, value_part, preferred_element_type=jnp.float32)]
    reduce_sum x0 -> x4, other arithmetic: none -> 8.89 us  [on_device(): row_total = jnp.sum(shifted, axis=1, keepdims=True)]
  transfers between devices with their start and end apart: 27 -> 27, of which waited for: 22 -> 22; matrix products, arithmetic and copies ran while one was open for 14% -> 15% of each run, Pallas kernels for 9% -> 9%
where the time goes in v4:
time: 765 us; the launch traced here: 760 us
  waiting for transfers between devices  399 us (52%)
  matrix products  115 us (15%)
  other arithmetic  104 us (14%)
  Pallas kernels  68.6 us (9%)
  local copies, waits for them, and re-layouts  32 us (4%)
  starting transfers between devices  15.4 us (2%)
  between operations  15.3 us (2%)
  blocking collectives  10.6 us (1%)
    ppermute x8, waiting for transfers between devices, permute_sum(): got = lax.ppermute(send, axis, partner_perm(size, 1 << step))  166 us
    ppermute x8, waiting for transfers between devices, permute_sum(): got = lax.ppermute(pieces, axis, partner_perm(size, 1 << step))  153 us
    pallas_call x1, Pallas kernels, attention_backward(): pl.pallas_call(kernel, grid_spec=grid_spec, out_shape=[jax.ShapeDtypeStru...  68.6 us
    dot_general x11, matrix products, right_trans(): lax.dot_general(left, right, (((1,), (1,)), ((), ())), preferred_element_...  46.7 us
    psum x2, waiting for transfers between devices, dp_sum(): return [lax.psum(grad.astype(jnp.bfloat16), 'dp') for grad in grads]  34.1 us
    dot_general x7, matrix products, left_trans(): lax.dot_general(left, right, (((0,), (0,)), ((), ())), preferred_element_...  28.6 us
    convert_element_type x7, other arithmetic, on_device(): grad.astype(jnp.float32)  27.3 us
    psum x1, waiting for transfers between devices, on_device(): lax.psum(branch_part[:half_rows].astype(jnp.bfloat16), 'tensor')  23.1 us
  transfers between devices with their start and end apart: 27, of which 22 were waited for; matrix products, arithmetic and copies ran while one was open for 15% of the time, Pallas kernels for 9%

profile of v4, /device:TPU:0, one launch (start us, length us, event | category | flops | bytes accessed | tf_op | source)
XLA Modules:
  0.0 760.2 jit_solution(7561616691007156359)
XLA Ops:
  12.3 3.3 convolution_convert_fusion.1
  22.0 10.6 %all-gather = bf16[8,1,512]{2,1,0:T(2,128)(2,1)S(1)} all-gather(bf16[1,1,512]{2,1,0:T(2,128)(2,1)S(1)} %reshape.291), channel_id=1, replica_groups=mesh['dp'=8,'tensor'=4] {'dp'}, dimensions={0}, use_global_device_ids=true | all-gather | bytes 9216 | tf_op jit(solution)/shard_map/all_gather | solution.py:289
  32.6 3.7 fusion.70
  38.9 2.4 copy.61
  43.9 17.4 %all-gather.3.cloned.1.call-done.k_ref.v_ref = bf16[4096,512]{1,0:T(8,128)(2,1)} async-done(((bf16[512,512]{1,0:T(8,128)(2,1)}), bf16[4096,512]{1,0:T(8,128)(2,1)}) %all-gather.3.cloned.1.call-update) | async-done | bytes 4194320 | tf_op jit(solution)/shard_map/all_gather | solution.py:286
  61.3 4.6 fusion.76
  67.2 4.6 fusion.77
  73.5 4.6 fusion.78
  79.3 6.9 fusion.79
  86.2 4.6 fusion.2
  90.9 3.4 fusion.22
  94.3 3.4 fusion.23
  108.4 12.7 %collective-permute-done = bf16[128,2048]{1,0:T(8,128)(2,1)} collective-permute-done((bf16[128,2048]{1,0:T(8,128)(2,1)S(1)}, bf16[128,2048]{1,0:T(8,128)(2,1)}, u32[]{:S(2)}, u32[]{:S(2)}) %collective-permute-start) | collective-permute-done | bytes 524320 | tf_op jit(solution)/shard_map/ppermute | solution.py:209
  122.7 2.5 collective-permute-start.1
  125.1 11.8 %collective-permute-done.1 = bf16[64,2048]{1,0:T(8,128)(2,1)} collective-permute-done((bf16[64,2048]{1,0:T(8,128)(2,1)S(1)}, bf16[64,2048]{1,0:T(8,128)(2,1)}, u32[]{:S(2)}, u32[]{:S(2)}) %collective-permute-start.1) | collective-permute-done | bytes 262176 | tf_op jit(solution)/shard_map/ppermute | solution.py:209
  138.1 2.7 slice.147
  141.0 18.8 %collective-permute-done.2 = bf16[64,2048]{1,0:T(8,128)(2,1)S(1)} collective-permute-done((bf16[64,2048]{1,0:T(8,128)(2,1)S(1)}, bf16[64,2048]{1,0:T(8,128)(2,1)S(1)}, u32[]{:S(2)}, u32[]{:S(2)}) %collective-permute-start.2) | collective-permute-done | bytes 262176 | tf_op jit(solution)/shard_map/ppermute | solution.py:214
  160.0 8.4 %fusion.36 = f32[512,1408]{1,0:T(8,128)} fusion(bf16[1408,2048]{1,0:T(8,128)(2,1)} %param.24, bf16[512,2048]{1,0:T(8,128)(2,1)} %param.25, f32[512]{0:T(512)S(1)} %get-tuple-element.102), kind=kOutput, calls=%fused_computation.106 | convolution fusion | flops 2955935744 | bytes 10749952 | tf_op jit(solution)/shard_map/dot_general | solution.py:49
  168.3 11.6 %collective-permute-done.3 = bf16[128,2048]{1,0:T(8,128)(2,1)S(1)} collective-permute-done((bf16[128,2048]{1,0:T(8,128)(2,1)S(1)}, bf16[128,2048]{1,0:T(8,128)(2,1)S(1)}, u32[]{:S(2)}, u32[]{:S(2)}) %collective-permute-start.3) | collective-permute-done | bytes 524320 | tf_op jit(solution)/shard_map/ppermute | solution.py:214
  181.1 23.1 %all-reduce.6.cloned.1.call-done = bf16[256,2048]{1,0:T(8,128)(2,1)} async-done(((bf16[256,2048]{1,0:T(8,128)(2,1)}), bf16[256,2048]{1,0:T(8,128)(2,1)}) %all-reduce.6.cloned.1.call-update) | async-done | bytes 1048592 | tf_op jit(solution)/shard_map/psum | solution.py:329
  204.2 3.3 multiply_reduce_fusion.2
  207.6 3.2 multiply_convert_fusion.1
  210.9 5.9 fusion.80
  216.9 4.6 multiply_convert_fusion.2
  221.5 3.4 fusion.84
  225.0 5.3 fusion.82
  230.3 5.5 fusion.83
  235.8 5.0 convolution_add_fusion
  240.8 5.1 fusion.34
  246.0 2.7 dynamic-slice_convert_fusion.2
  250.1 23.9 %collective-permute-done.4 = bf16[256,2048]{1,0:T(8,128)(2,1)} collective-permute-done((bf16[256,2048]{1,0:T(8,128)(2,1)}, bf16[256,2048]{1,0:T(8,128)(2,1)}, u32[]{:S(2)}, u32[]{:S(2)}) %collective-permute-start.4) | collective-permute-done | bytes 1048608 | tf_op jit(solution)/shard_map/ppermute | solution.py:209
  280.5 22.3 %collective-permute-done.5 = bf16[128,2048]{1,0:T(8,128)(2,1)} collective-permute-done((bf16[128,2048]{1,0:T(8,128)(2,1)}, bf16[128,2048]{1,0:T(8,128)(2,1)}, u32[]{:S(2)}, u32[]{:S(2)}) %collective-permute-start.5) | collective-permute-done | bytes 524320 | tf_op jit(solution)/shard_map/ppermute | solution.py:209
  302.8 2.5 add_convert_fusion.4
  307.9 23.4 %collective-permute-done.6 = bf16[128,2048]{1,0:T(8,128)(2,1)} collective-permute-done((bf16[128,2048]{1,0:T(8,128)(2,1)}, bf16[128,2048]{1,0:T(8,128)(2,1)}, u32[]{:S(2)}, u32[]{:S(2)}) %collective-permute-start.6) | collective-permute-done | bytes 524320 | tf_op jit(solution)/shard_map/ppermute | solution.py:214
  336.6 8.6 %fusion.81 = f32[512,2048]{1,0:T(8,128)} fusion(bf16[512,1408]{1,0:T(8,128)(2,1)} %copy-done.68, bf16[1408,2048]{1,0:T(8,128)(2,1)} %param.24), kind=kOutput, calls=%fused_computation.186 | convolution fusion | flops 2952790016 | bytes 11403264 | tf_op jit(solution)/shard_map/dot_general | solution.py:339
  345.2 14.6 %collective-permute-done.7 = bf16[256,2048]{1,0:T(8,128)(2,1)} collective-permute-done((bf16[256,2048]{1,0:T(8,128)(2,1)}, bf16[256,2048]{1,0:T(8,128)(2,1)}, u32[]{:S(2)}, u32[]{:S(2)}) %collective-permute-start.7) | collective-permute-done | bytes 1048608 | tf_op jit(solution)/shard_map/ppermute | solution.py:214
  363.5 3.2 multiply_reduce_fusion
  366.7 3.9 convert_add_fusion.1
  372.3 68.6 %shard_map.212 = (f32[512,512]{1,0:T(8,128)S(1)}, f32[4096,256]{1,0:T(8,128)}, f32[4096,256]{1,0:T(8,128)}) custom-call(s32[16]{0:T(128)S(1)} %copy-done.4, s32[2]{0:T(128)S(1)} %dynamic_slice.67.qblock_ref, bf16[512,512]{1,0:T(8,128)(2,1)S(1)} %bitcast.65, bf16[4096,512]{1,0:T(8,128)(2,1)} %all-gather.3.cloned.1.call-done.k_ref.v_ref, ...), custom_call_target="tpu_custom_call" | custom-call | flops 10737418240 | bytes 25165824 | tf_op jit(solution)/shard_map/pallas_call | solution.py:173
  441.0 2.6 convert.61
  444.8 2.3 pad_maximum_fusion
  449.4 24.2 %collective-permute-done.8 = bf16[256,2048]{1,0:T(8,128)(2,1)S(1)} collective-permute-done((bf16[256,2048]{1,0:T(8,128)(2,1)S(1)}, bf16[256,2048]{1,0:T(8,128)(2,1)S(1)}, u32[]{:S(2)}, u32[]{:S(2)}) %collective-permute-start.8) | collective-permute-done | bytes 1048608 | tf_op jit(solution)/shard_map/ppermute | solution.py:209
  476.2 23.7 %collective-permute-done.9 = bf16[128,2048]{1,0:T(8,128)(2,1)S(1)} collective-permute-done((bf16[128,2048]{1,0:T(8,128)(2,1)S(1)}, bf16[128,2048]{1,0:T(8,128)(2,1)S(1)}, u32[]{:S(2)}, u32[]{:S(2)}) %collective-permute-start.9) | collective-permute-done | bytes 524320 | tf_op jit(solution)/shard_map/ppermute | solution.py:209
  502.2 23.8 %collective-permute-done.10 = bf16[128,2048]{1,0:T(8,128)(2,1)} collective-permute-done((bf16[128,2048]{1,0:T(8,128)(2,1)}, bf16[128,2048]{1,0:T(8,128)(2,1)}, u32[]{:S(2)}, u32[]{:S(2)}) %collective-permute-start.10) | collective-permute-done | bytes 524320 | tf_op jit(solution)/shard_map/ppermute | solution.py:214
  529.5 2.7 fusion.55
  532.2 2.8 fusion.38
  535.0 17.5 %collective-permute-done.11 = bf16[256,2048]{1,0:T(8,128)(2,1)S(1)} collective-permute-done((bf16[256,2048]{1,0:T(8,128)(2,1)S(1)}, bf16[256,2048]{1,0:T(8,128)(2,1)S(1)}, u32[]{:S(2)}, u32[]{:S(2)}) %collective-permute-start.11) | collective-permute-done | bytes 1048608 | tf_op jit(solution)/shard_map/ppermute | solution.py:214
  553.1 2.6 maximum_convert_fusion.1
  557.8 3.6 fusion.54
  561.4 2.8 fusion.53
  567.0 3.6 fusion.43
  573.2 3.2 add_add_fusion.2
  576.9 23.9 %collective-permute-done.12 = bf16[256,2048]{1,0:T(8,128)(2,1)S(1)} collective-permute-done((bf16[256,2048]{1,0:T(8,128)(2,1)S(1)}, bf16[256,2048]{1,0:T(8,128)(2,1)S(1)}, u32[]{:S(2)}, u32[]{:S(2)}) %collective-permute-start.12) | collective-permute-done | bytes 1048608 | tf_op jit(solution)/shard_map/ppermute | solution.py:209
  602.5 23.0 %collective-permute-done.13 = bf16[128,2048]{1,0:T(8,128)(2,1)S(1)} collective-permute-done((bf16[128,2048]{1,0:T(8,128)(2,1)S(1)}, bf16[128,2048]{1,0:T(8,128)(2,1)S(1)}, u32[]{:S(2)}, u32[]{:S(2)}) %collective-permute-start.13) | collective-permute-done | bytes 524320 | tf_op jit(solution)/shard_map/ppermute | solution.py:209
  625.8 25.1 %collective-permute-done.14 = bf16[128,2048]{1,0:T(8,128)(2,1)S(1)} collective-permute-done((bf16[128,2048]{1,0:T(8,128)(2,1)S(1)}, bf16[128,2048]{1,0:T(8,128)(2,1)S(1)}, u32[]{:S(2)}, u32[]{:S(2)}) %collective-permute-start.14) | collective-permute-done | bytes 524320 | tf_op jit(solution)/shard_map/ppermute | solution.py:214
  653.8 2.5 collective-permute-done.20
  657.7 18.5 %collective-permute-done.15 = bf16[256,2048]{1,0:T(8,128)(2,1)S(1)} collective-permute-done((bf16[256,2048]{1,0:T(8,128)(2,1)S(1)}, bf16[256,2048]{1,0:T(8,128)(2,1)S(1)}, u32[]{:S(2)}, u32[]{:S(2)}) %collective-permute-start.15) | collective-permute-done | bytes 1048608 | tf_op jit(solution)/shard_map/ppermute | solution.py:214
  678.9 6.1 convert_element_type.259
  685.1 5.2 convert_element_type.260
  690.2 6.0 convert_element_type.261
  696.2 34.1 %all-reduce.8.cloned.1.call-done = (bf16[2048,512]{1,0:T(8,128)(2,1)}, bf16[2048,256]{1,0:T(8,128)(2,1)}, bf16[2048,256]{1,0:T(8,128)(2,1)}, bf16[512,2048]{1,0:T(8,128)(2,1)}) async-done(((bf16[2048,512]{1,0:T(8,128)(2,1)}, bf16[2048,256]{1,0:T(8,128)(2,1)}, bf16[2048,256]{1,0:T(8,128)(2,1)}, bf16[512,2048]{1,0:T(8,128)(2,1)}), (bf16[2048,512]{1,0:T(8,128)(2,1)}, bf16[2048,256]{1,0:T(8,128)(2,1)}, ...) | async-done | bytes 6291472 | tf_op jit(solution)/shard_map/psum | solution.py:343
  730.3 4.3 convert_element_type.252
  737.7 2.7 convert_element_type.258
  745.4 7.4 fusion.11
  (305 shorter events, 94.4 us)
Async XLA Ops:
  7.2 94.7 %copy-start = (bf16[512,2048]{1,0:T(8,128)(2,1)S(1)}, bf16[512,2048]{1,0:T(8,128)(2,1)}, u32[]{:S(2)}) copy-start(bf16[512,2048]{1,0:T(8,128)(2,1)} %param.20) | copy-start | bytes 6291460
  7.2 8.4 %copy-start.47 = (bf16[2048,256]{1,0:T(8,128)(2,1)S(1)}, bf16[2048,256]{1,0:T(8,128)(2,1)}, u32[]{:S(2)}) copy-start(bf16[2048,256]{1,0:T(8,128)(2,1)} %param.18) | copy-start | bytes 3145732
  7.2 54.1 %all-gather.3.cloned.1.call-start = ((), (), s32[]{:S(2)}) async-start(), calls=%async_computation.1 | async-start | bytes 4718592 | tf_op jit(solution)/shard_map/all_gather | solution.py:286
  7.3 8.4 %copy-start.5 = (bf16[512,2048]{1,0:T(8,128)(2,1)S(1)}, bf16[512,2048]{1,0:T(8,128)(2,1)}, u32[]{:S(2)}) copy-start(bf16[512,2048]{1,0:T(8,128)(2,1)} %param.13) | copy-start | bytes 6291460
  10.9 21.7 %copy-start.60 = (f32[512]{0:T(512)}, f32[512]{0:T(512)S(1)}, u32[]{:S(2)}) copy-start(f32[512]{0:T(512)S(1)} %fusion.60) | copy-start | bytes 6148
  11.6 21.0 %copy-start.57 = (f32[2048]{0:T(1024)}, f32[2048]{0:T(1024)S(1)}, u32[]{:S(2)}) copy-start(f32[2048]{0:T(1024)S(1)} %convert_element_type.202) | copy-start | bytes 24580
  19.0 22.3 %copy-start.28 = (f32[512,64]{1,0:T(8,128)}, f32[512,64]{1,0:T(8,128)S(1)}, u32[]{:S(2)}) copy-start(f32[512,64]{1,0:T(8,128)S(1)} %get-tuple-element.101) | copy-start | bytes 393220
  21.9 182.3 %all-reduce.6.cloned.1.call-start = ((), (), s32[]{:S(2)}) async-start(), calls=%async_computation.2 | async-start | bytes 2097152 | tf_op jit(solution)/shard_map/psum | solution.py:329
  43.9 35.5 %copy-start.1 = (bf16[64,8,4,128]{3,1,2,0:T(8,128)(2,1)}, bf16[64,8,4,128]{3,1,2,0:T(8,128)(2,1)S(1)}, u32[]{:S(2)}) copy-start(bf16[64,8,4,128]{3,1,2,0:T(8,128)(2,1)S(1)} %copy.90) | copy-start | bytes 1572868
  90.9 8.9 %slice-start = ((s8[8388608]{0:T(1024)(128)(4,1)}), s8[4194304]{0:T(1024)(128)(4,1)S(1)}, s32[]{:S(2)}) async-start(s8[8388608]{0:T(1024)(128)(4,1)} %bitcast.68), calls=%async_computation.6 | async-start | bytes 8388608
  94.3 7.6 %copy-start.48 = (bf16[512,128]{0,1:T(8,128)(2,1)}, bf16[512,128]{0,1:T(8,128)(2,1)S(1)}, u32[]{:S(2)}) copy-start(bf16[512,128]{0,1:T(8,128)(2,1)S(1)} %fusion.22) | copy-start | bytes 393220
  105.2 32.8 %copy-start.64 = (bf16[2048]{0:T(1024)(128)(2,1)S(1)}, bf16[2048]{0:T(1024)(128)(2,1)}, u32[]{:S(2)}) copy-start(bf16[2048]{0:T(1024)(128)(2,1)} %param.21) | copy-start | bytes 12292
  106.9 14.2 %collective-permute-start = (bf16[128,2048]{1,0:T(8,128)(2,1)S(1)}, bf16[128,2048]{1,0:T(8,128)(2,1)}, u32[]{:S(2)}, u32[]{:S(2)}) collective-permute-start(bf16[128,2048]{1,0:T(8,128)(2,1)S(1)} %dynamic-slice_convert_fusion.6), channel_id=1, source_target_pairs={{0,1},{1,0},{2,3},{3,2},{4,5},{5,4},{6,7},{7,6},{8,9},{9,8},{10,11... | collective-permute-start | bytes 1572872 | tf_op jit(solution)/shard_map/ppermute | solution.py:209
  122.7 14.3 %collective-permute-start.1 = (bf16[64,2048]{1,0:T(8,128)(2,1)S(1)}, bf16[64,2048]{1,0:T(8,128)(2,1)}, u32[]{:S(2)}, u32[]{:S(2)}) collective-permute-start(bf16[64,2048]{1,0:T(8,128)(2,1)S(1)} %dynamic-slice_convert_fusion.7), channel_id=1, source_target_pairs={{0,2},{1,3},{2,0},{3,1},{4,6},{5,7},{6,4},{7,5},{8,10},{9,11},{10,... | collective-permute-start | bytes 786440 | tf_op jit(solution)/shard_map/ppermute | solution.py:209
  137.9 21.9 %collective-permute-start.2 = (bf16[64,2048]{1,0:T(8,128)(2,1)S(1)}, bf16[64,2048]{1,0:T(8,128)(2,1)S(1)}, u32[]{:S(2)}, u32[]{:S(2)}) collective-permute-start(bf16[64,2048]{1,0:T(8,128)(2,1)S(1)} %add_convert_fusion.7), channel_id=1, source_target_pairs={{0,2},{1,3},{2,0},{3,1},{4,6},{5,7},{6,4},{7,5},{8,10},{9,11},{10,... | collective-permute-start | bytes 786440 | tf_op jit(solution)/shard_map/ppermute | solution.py:214
  140.8 414.9 %all-reduce.10.cloned.1.call-start = ((), (), s32[]{:S(2)}) async-start(), calls=%async_computation.5 | async-start | bytes 34603008 | tf_op jit(solution)/shard_map/psum | solution.py:343
  159.9 20.0 %collective-permute-start.3 = (bf16[128,2048]{1,0:T(8,128)(2,1)S(1)}, bf16[128,2048]{1,0:T(8,128)(2,1)S(1)}, u32[]{:S(2)}, u32[]{:S(2)}) collective-permute-start(bf16[128,2048]{1,0:T(8,128)(2,1)S(1)} %pad_maximum_fusion.9), channel_id=1, source_target_pairs={{0,1},{1,0},{2,3},{3,2},{4,5},{5,4},{6,7},{7,6},{8,9},{9,8},{10,11... | collective-permute-start | bytes 1572872 | tf_op jit(solution)/shard_map/ppermute | solution.py:214
  207.6 9.2 %slice-start.8 = ((s8[5767168]{0:T(1024)(128)(4,1)}), s8[4194304]{0:T(1024)(128)(4,1)S(1)}, s32[]{:S(2)}) async-start(s8[5767168]{0:T(1024)(128)(4,1)} %bitcast.101), calls=%async_computation.14 | async-start | bytes 8388608
  210.9 6.0 slice-start.9
  210.9 6.0 copy-start.67
  221.5 19.3 %copy-start.68 = (bf16[512,1408]{1,0:T(8,128)(2,1)}, bf16[512,1408]{1,0:T(8,128)(2,1)S(1)}, u32[]{:S(2)}) copy-start(bf16[512,1408]{1,0:T(8,128)(2,1)S(1)} %get-tuple-element.68) | copy-start | bytes 4325380
  225.0 10.9 %slice-start.10 = ((s8[5767168]{0:T(1024)(128)(4,1)}), s8[4194304]{0:T(1024)(128)(4,1)S(1)}, s32[]{:S(2)}) async-start(s8[5767168]{0:T(1024)(128)(4,1)} %bitcast.103), calls=%async_computation.16 | async-start | bytes 8388608
  248.7 25.3 %collective-permute-start.4 = (bf16[256,2048]{1,0:T(8,128)(2,1)}, bf16[256,2048]{1,0:T(8,128)(2,1)}, u32[]{:S(2)}, u32[]{:S(2)}) collective-permute-start(bf16[256,2048]{1,0:T(8,128)(2,1)} %dynamic-slice_convert_fusion.2), channel_id=1, source_target_pairs={{0,1},{1,0},{2,3},{3,2},{4,5},{5,4},{6,7},{7,6},{8,9},{9,8},{10,11... | collective-permute-start | bytes 3145736 | tf_op jit(solution)/shard_map/ppermute | solution.py:209
  250.1 29.4 %copy-start.4 = (s32[16]{0:T(128)S(1)}, s32[16]{0:T(128)}, u32[]{:S(2)}) copy-start(s32[16]{0:T(128)} %chunk_ref.1) | copy-start | bytes 196
  250.1 29.5 %copy-start.59 = (s32[1,1,16,256]{3,2,1,0:T(8,128)S(1)}, s32[1,1,16,256]{3,2,1,0:T(8,128)}, u32[]{:S(2)}) copy-start(s32[1,1,16,256]{3,2,1,0:T(8,128)} %get-tuple-element.104) | copy-start | bytes 49156
  250.1 305.6 %reduce-scatter.2.cloned.1.call-start = ((), (), s32[]{:S(2)}) async-start(), calls=%async_computation.3 | async-start | bytes 4718592 | tf_op jit(solution)/shard_map/reduce_scatter | solution.py:375
  278.4 24.4 %collective-permute-start.5 = (bf16[128,2048]{1,0:T(8,128)(2,1)}, bf16[128,2048]{1,0:T(8,128)(2,1)}, u32[]{:S(2)}, u32[]{:S(2)}) collective-permute-start(bf16[128,2048]{1,0:T(8,128)(2,1)} %dynamic-slice_convert_fusion.5), channel_id=1, source_target_pairs={{0,2},{1,3},{2,0},{3,1},{4,6},{5,7},{6,4},{7,5},{8,10},{9,11},{10,... | collective-permute-start | bytes 1572872 | tf_op jit(solution)/shard_map/ppermute | solution.py:209
  305.3 26.0 %collective-permute-start.6 = (bf16[128,2048]{1,0:T(8,128)(2,1)}, bf16[128,2048]{1,0:T(8,128)(2,1)}, u32[]{:S(2)}, u32[]{:S(2)}) collective-permute-start(bf16[128,2048]{1,0:T(8,128)(2,1)} %add_convert_fusion.4), channel_id=1, source_target_pairs={{0,2},{1,3},{2,0},{3,1},{4,6},{5,7},{6,4},{7,5},{8,10},{9,11},{10,... | collective-permute-start | bytes 1572872 | tf_op jit(solution)/shard_map/ppermute | solution.py:214
  334.4 25.4 %collective-permute-start.7 = (bf16[256,2048]{1,0:T(8,128)(2,1)}, bf16[256,2048]{1,0:T(8,128)(2,1)}, u32[]{:S(2)}, u32[]{:S(2)}) collective-permute-start(bf16[256,2048]{1,0:T(8,128)(2,1)} %pad_maximum_fusion.2), channel_id=1, source_target_pairs={{0,1},{1,0},{2,3},{3,2},{4,5},{5,4},{6,7},{7,6},{8,9},{9,8},{10,11... | collective-permute-start | bytes 3145736 | tf_op jit(solution)/shard_map/ppermute | solution.py:214
  336.5 23.2 %copy-start.33 = (bf16[128,2048]{1,0:T(8,128)(2,1)S(1)}, bf16[128,2048]{1,0:T(8,128)(2,1)}, u32[]{:S(2)}) copy-start(bf16[128,2048]{1,0:T(8,128)(2,1)} %copy-done.32) | copy-start | bytes 1572868
  336.5 23.2 %copy-start.35 = (bf16[128,2048]{1,0:T(8,128)(2,1)S(1)}, bf16[128,2048]{1,0:T(8,128)(2,1)}, u32[]{:S(2)}) copy-start(bf16[128,2048]{1,0:T(8,128)(2,1)} %copy-done.34) | copy-start | bytes 1572868
  370.6 70.3 %copy-start.11 = (f32[512,2048]{1,0:T(8,128)}, f32[512,2048]{1,0:T(8,128)S(1)}, u32[]{:S(2)}) copy-start(f32[512,2048]{1,0:T(8,128)S(1)} %convert_add_fusion.1) | copy-start | bytes 12582916
  447.2 283.1 %all-reduce.8.cloned.1.call-start = ((), (), s32[]{:S(2)}) async-start(), calls=%async_computation.4 | async-start | bytes 12582912 | tf_op jit(solution)/shard_map/psum | solution.py:343
  449.3 24.3 %collective-permute-start.8 = (bf16[256,2048]{1,0:T(8,128)(2,1)S(1)}, bf16[256,2048]{1,0:T(8,128)(2,1)S(1)}, u32[]{:S(2)}, u32[]{:S(2)}) collective-permute-start(bf16[256,2048]{1,0:T(8,128)(2,1)S(1)} %dynamic-slice_convert_fusion.1), channel_id=1, source_target_pairs={{0,1},{1,0},{2,3},{3,2},{4,5},{5,4},{6,7},{7,6},{8,9},{9,8},{10,11... | collective-permute-start | bytes 3145736 | tf_op jit(solution)/shard_map/ppermute | solution.py:209
  475.6 51.9 %copy-start.29 = (f32[512,64]{1,0:T(8,128)S(1)}, f32[512,64]{1,0:T(8,128)}, u32[]{:S(2)}) copy-start(f32[512,64]{1,0:T(8,128)} %copy-done.28) | copy-start | bytes 393220
  475.6 24.3 %collective-permute-start.9 = (bf16[128,2048]{1,0:T(8,128)(2,1)S(1)}, bf16[128,2048]{1,0:T(8,128)(2,1)S(1)}, u32[]{:S(2)}, u32[]{:S(2)}) collective-permute-start(bf16[128,2048]{1,0:T(8,128)(2,1)S(1)} %dynamic-slice_convert_fusion.4), channel_id=1, source_target_pairs={{0,2},{1,3},{2,0},{3,1},{4,6},{5,7},{6,4},{7,5},{8,10},{9,11},{10,... | collective-permute-start | bytes 1572872 | tf_op jit(solution)/shard_map/ppermute | solution.py:209
  500.9 25.1 %collective-permute-start.10 = (bf16[128,2048]{1,0:T(8,128)(2,1)}, bf16[128,2048]{1,0:T(8,128)(2,1)}, u32[]{:S(2)}, u32[]{:S(2)}) collective-permute-start(bf16[128,2048]{1,0:T(8,128)(2,1)} %add_convert_fusion.3), channel_id=1, source_target_pairs={{0,2},{1,3},{2,0},{3,1},{4,6},{5,7},{6,4},{7,5},{8,10},{9,11},{10,... | collective-permute-start | bytes 1572872 | tf_op jit(solution)/shard_map/ppermute | solution.py:214
  502.2 25.3 %copy-start.27 = (f32[512,4,128]{2,1,0:T(4,128)S(1)}, f32[512,4,128]{2,1,0:T(4,128)}, u32[]{:S(2)}) copy-start(f32[512,4,128]{2,1,0:T(4,128)} %reshape.288) | copy-start | bytes 3145732
  502.2 25.3 %copy-start.37 = (f32[512,64]{1,0:T(8,128)S(1)}, f32[512,64]{1,0:T(8,128)}, u32[]{:S(2)}) copy-start(f32[512,64]{1,0:T(8,128)} %get-tuple-element.99) | copy-start | bytes 393220
  527.4 25.1 %collective-permute-start.11 = (bf16[256,2048]{1,0:T(8,128)(2,1)S(1)}, bf16[256,2048]{1,0:T(8,128)(2,1)S(1)}, u32[]{:S(2)}, u32[]{:S(2)}) collective-permute-start(bf16[256,2048]{1,0:T(8,128)(2,1)S(1)} %pad_maximum_fusion.3), channel_id=1, source_target_pairs={{0,1},{1,0},{2,3},{3,2},{4,5},{5,4},{6,7},{7,6},{8,9},{9,8},{10,11... | collective-permute-start | bytes 3145736 | tf_op jit(solution)/shard_map/ppermute | solution.py:214
  576.5 24.3 %collective-permute-start.12 = (bf16[256,2048]{1,0:T(8,128)(2,1)S(1)}, bf16[256,2048]{1,0:T(8,128)(2,1)S(1)}, u32[]{:S(2)}, u32[]{:S(2)}) collective-permute-start(bf16[256,2048]{1,0:T(8,128)(2,1)S(1)} %dynamic-slice_convert_fusion), channel_id=1, source_target_pairs={{0,1},{1,0},{2,3},{3,2},{4,5},{5,4},{6,7},{7,6},{8,9},{9,8},{10,11... | collective-permute-start | bytes 3145736 | tf_op jit(solution)/shard_map/ppermute | solution.py:209
  601.2 24.3 %collective-permute-start.13 = (bf16[128,2048]{1,0:T(8,128)(2,1)S(1)}, bf16[128,2048]{1,0:T(8,128)(2,1)S(1)}, u32[]{:S(2)}, u32[]{:S(2)}) collective-permute-start(bf16[128,2048]{1,0:T(8,128)(2,1)S(1)} %dynamic-slice_convert_fusion.3), channel_id=1, source_target_pairs={{0,2},{1,3},{2,0},{3,1},{4,6},{5,7},{6,4},{7,5},{8,10},{9,11},{10,... | collective-permute-start | bytes 1572872 | tf_op jit(solution)/shard_map/ppermute | solution.py:209
  625.6 25.2 %collective-permute-start.14 = (bf16[128,2048]{1,0:T(8,128)(2,1)S(1)}, bf16[128,2048]{1,0:T(8,128)(2,1)S(1)}, u32[]{:S(2)}, u32[]{:S(2)}) collective-permute-start(bf16[128,2048]{1,0:T(8,128)(2,1)S(1)} %add_convert_fusion.1), channel_id=1, source_target_pairs={{0,2},{1,3},{2,0},{3,1},{4,6},{5,7},{6,4},{7,5},{8,10},{9,11},{10,... | collective-permute-start | bytes 1572872 | tf_op jit(solution)/shard_map/ppermute | solution.py:214
  625.7 50.9 %copy-start.9 = (bf16[512,2048]{1,0:T(8,128)(2,1)S(1)}, bf16[512,2048]{1,0:T(8,128)(2,1)}, u32[]{:S(2)}) copy-start(bf16[512,2048]{1,0:T(8,128)(2,1)} %param.13) | copy-start | bytes 6291460
  650.9 28.0 %slice-start.6 = ((s8[5767168]{0:T(1024)(128)(4,1)}), s8[4194304]{0:T(1024)(128)(4,1)S(1)}, s32[]{:S(2)}) async-start(s8[5767168]{0:T(1024)(128)(4,1)} %bitcast.74), calls=%async_computation.12 | async-start | bytes 8388608
  651.1 25.1 %collective-permute-start.15 = (bf16[256,2048]{1,0:T(8,128)(2,1)S(1)}, bf16[256,2048]{1,0:T(8,128)(2,1)S(1)}, u32[]{:S(2)}, u32[]{:S(2)}) collective-permute-start(bf16[256,2048]{1,0:T(8,128)(2,1)S(1)} %pad_maximum_fusion.5), channel_id=1, source_target_pairs={{0,1},{1,0},{2,3},{3,2},{4,5},{5,4},{6,7},{7,6},{8,9},{9,8},{10,11... | collective-permute-start | bytes 3145736 | tf_op jit(solution)/shard_map/ppermute | solution.py:214
  651.1 1.2 collective-permute-start.19
  652.4 3.9 collective-permute-start.20
  656.3 22.6 %slice-start.7 = ((s8[5767168]{0:T(1024)(128)(4,1)}), s8[1572864]{0:T(1024)(128)(4,1)S(1)}, s32[]{:S(2)}) async-start(s8[5767168]{0:T(1024)(128)(4,1)} %bitcast.74), calls=%async_computation.13 | async-start | bytes 3145728
  656.3 22.0 %collective-permute-start.21 = (f32[2048]{0:T(1024)S(1)}, f32[2048]{0:T(1024)S(1)}, u32[]{:S(2)}, u32[]{:S(2)}) collective-permute-start(f32[2048]{0:T(1024)S(1)} %add.314), channel_id=1, source_target_pairs={{0,16},{4,20},{8,24},{12,28},{16,0},{20,4},{24,8},{28,12},{1,17},{... | collective-permute-start | bytes 24584 | tf_op jit(solution)/shard_map/ppermute | solution.py:228
  676.6 8.4 %slice-start.4 = ((s8[5767168]{0:T(1024)(128)(4,1)}), s8[4194304]{0:T(1024)(128)(4,1)S(1)}, s32[]{:S(2)}) async-start(s8[5767168]{0:T(1024)(128)(4,1)} %bitcast.72), calls=%async_computation.10 | async-start | bytes 8388608
  678.2 62.2 %collective-permute-start.16 = (f32[2048]{0:T(1024)S(1)}, f32[2048]{0:T(1024)S(1)}, u32[]{:S(2)}, u32[]{:S(2)}) collective-permute-start(f32[2048]{0:T(1024)S(1)} %get-tuple-element.55), channel_id=1, source_target_pairs={{0,4},{4,0},{8,12},{12,8},{16,20},{20,16},{24,28},{28,24},{1,5},{5... | collective-permute-start | bytes 24584 | tf_op jit(solution)/shard_map/ppermute | solution.py:228
  678.9 6.1 slice-start.5
  678.9 11.3 %slice-start.2 = ((s8[5767168]{0:T(1024)(128)(4,1)}), s8[4194304]{0:T(1024)(128)(4,1)S(1)}, s32[]{:S(2)}) async-start(s8[5767168]{0:T(1024)(128)(4,1)} %bitcast.70), calls=%async_computation.8 | async-start | bytes 8388608
  730.3 7.4 copy-start.39
  730.3 15.0 %copy-start.26 = (bf16[256,2048]{1,0:T(8,128)(2,1)S(1)}, bf16[256,2048]{1,0:T(8,128)(2,1)}, u32[]{:S(2)}) copy-start(bf16[256,2048]{1,0:T(8,128)(2,1)} %copy-done.25) | copy-start | bytes 3145732
  734.7 10.6 %copy-start.22 = (f32[512,2048]{1,0:T(8,128)S(1)}, f32[512,2048]{1,0:T(8,128)}, u32[]{:S(2)}) copy-start(f32[512,2048]{1,0:T(8,128)} %maximum_convert_fusion.1) | copy-start | bytes 12582916
  736.2 9.2 %copy-start.10 = (bf16[512,2048]{1,0:T(8,128)(2,1)S(1)}, bf16[512,2048]{1,0:T(8,128)(2,1)}, u32[]{:S(2)}) copy-start(bf16[512,2048]{1,0:T(8,128)(2,1)} %param.13) | copy-start | bytes 6291460
  736.2 9.2 %copy-start.13 = (f32[512,2048]{1,0:T(8,128)S(1)}, f32[512,2048]{1,0:T(8,128)}, u32[]{:S(2)}) copy-start(f32[512,2048]{1,0:T(8,128)} %copy-done.11) | copy-start | bytes 12582916
  736.2 9.2 %copy-start.15 = (bf16[256,2048]{1,0:T(8,128)(2,1)S(1)}, bf16[256,2048]{1,0:T(8,128)(2,1)}, u32[]{:S(2)}) copy-start(bf16[256,2048]{1,0:T(8,128)(2,1)} %all-reduce.6.cloned.1.call-done) | copy-start | bytes 3145732
  736.2 9.2 %copy-start.18 = (bf16[128,2048]{1,0:T(8,128)(2,1)S(1)}, bf16[128,2048]{1,0:T(8,128)(2,1)}, u32[]{:S(2)}) copy-start(bf16[128,2048]{1,0:T(8,128)(2,1)} %get-tuple-element.91) | copy-start | bytes 1572868
  736.2 9.2 %copy-start.21 = (bf16[128,2048]{1,0:T(8,128)(2,1)S(1)}, bf16[128,2048]{1,0:T(8,128)(2,1)}, u32[]{:S(2)}) copy-start(bf16[128,2048]{1,0:T(8,128)(2,1)} %get-tuple-element.92) | copy-start | bytes 1572868
  740.4 3.7 collective-permute-start.17
  744.0 8.8 %collective-permute-start.18 = (f32[2048]{0:T(1024)S(1)}, f32[2048]{0:T(1024)S(1)}, u32[]{:S(2)}, u32[]{:S(2)}) collective-permute-start(f32[2048]{0:T(1024)S(1)} %add.311), channel_id=1, source_target_pairs={{0,16},{4,20},{8,24},{12,28},{16,0},{20,4},{24,8},{28,12},{1,17},{... | collective-permute-start | bytes 24584 | tf_op jit(solution)/shard_map/ppermute | solution.py:228
  (44 other events, 136.8 us)
Sparse Core Ops, SparseCore 0:
  22.0 39.3 all-gather.2
  140.9 63.2 all-reduce.5
  250.2 221.4 all-reduce.9
  475.5 51.2 reduce-scatter.1
  625.9 104.4 all-reduce.7

commit v5 on v4

--- a/solution.py
+++ b/solution.py
@@ -326,8 +326,9 @@
     attended = jnp.concatenate(mixed_parts, axis=1).astype(jnp.bfloat16)
     lse = jnp.stack(lse_parts)
     branch_part = jnp.dot(attended, w_out, preferred_element_type=jnp.float32)
-    branch_top = lax.psum(branch_part[:half_rows].astype(jnp.bfloat16), "tensor")
-    (branch_bottom,) = permute_sum([branch_part[half_rows:]], [0], "tensor")
+    sc_rows = row_count * 5 // 8
+    branch_top = lax.psum(branch_part[:sc_rows].astype(jnp.bfloat16), "tensor")
+    (branch_bottom,) = permute_sum([branch_part[sc_rows:]], [0], "tensor")
     branch = jnp.concatenate([branch_top.astype(jnp.float32), branch_bottom], axis=0)
     middle = source + keep_rows * branch
     normed_two_full, norm_two_back = jax.vjp(rms_norm, middle, gain_two.astype(jnp.float32))

time: 765 us -> 767 us (level)
    psum x1, waiting for transfers between devices: 23.1 us -> 31 us  [on_device(): branch_top = lax.psum(branch_part[:sc_rows].astype(jnp.bfloat16), 'tensor')]
  transfers between devices with their start and end apart: 27 -> 27, of which waited for: 22 -> 22; matrix products, arithmetic and copies ran while one was open for 15% -> 16% of each run, Pallas kernels for 9% -> 9%
where the time goes in v5:
time: 767 us; the launch traced here: 762 us
  waiting for transfers between devices  399 us (52%)
  matrix products  117 us (15%)
  other arithmetic  104 us (14%)
  Pallas kernels  68.7 us (9%)
  local copies, waits for them, and re-layouts  31.3 us (4%)
  starting transfers between devices  16.9 us (2%)
  between operations  15.3 us (2%)
  blocking collectives  10.6 us (1%)
    ppermute x8, waiting for transfers between devices, permute_sum(): got = lax.ppermute(send, axis, partner_perm(size, 1 << step))  159 us
    ppermute x8, waiting for transfers between devices, permute_sum(): got = lax.ppermute(pieces, axis, partner_perm(size, 1 << step))  150 us
    pallas_call x1, Pallas kernels, attention_backward(): pl.pallas_call(kernel, grid_spec=grid_spec, out_shape=[jax.ShapeDtypeStru...  68.7 us
    dot_general x11, matrix products, right_trans(): lax.dot_general(left, right, (((1,), (1,)), ((), ())), preferred_element_...  46.7 us
    psum x2, waiting for transfers between devices, dp_sum(): return [lax.psum(grad.astype(jnp.bfloat16), 'dp') for grad in grads]  34.5 us
    psum x1, waiting for transfers between devices, on_device(): branch_top = lax.psum(branch_part[:sc_rows].astype(jnp.bfloat16), 'tensor')  31 us
    dot_general x7, matrix products, left_trans(): lax.dot_general(left, right, (((0,), (0,)), ((), ())), preferred_element_...  28.6 us
    convert_element_type x7, other arithmetic, on_device(): grad.astype(jnp.float32)  27.2 us
  transfers between devices with their start and end apart: 27, of which 22 were waited for; matrix products, arithmetic and copies ran while one was open for 16% of the time, Pallas kernels for 9%

profile of v5, /device:TPU:0, one launch (start us, length us, event | category | flops | bytes accessed | tf_op | source)
XLA Modules:
  0.0 762.3 jit_solution(7657333394165803955)
XLA Ops:
  12.4 3.3 convolution_convert_fusion.1
  22.0 10.6 %all-gather = bf16[8,1,512]{2,1,0:T(2,128)(2,1)S(1)} all-gather(bf16[1,1,512]{2,1,0:T(2,128)(2,1)S(1)} %reshape.291), channel_id=1, replica_groups=mesh['dp'=8,'tensor'=4] {'dp'}, dimensions={0}, use_global_device_ids=true | all-gather | bytes 9216 | tf_op jit(solution)/shard_map/all_gather | solution.py:289
  32.7 3.7 fusion.70
  44.0 17.4 %all-gather.3.cloned.1.call-done.k_ref.v_ref = bf16[4096,512]{1,0:T(8,128)(2,1)} async-done(((bf16[512,512]{1,0:T(8,128)(2,1)}), bf16[4096,512]{1,0:T(8,128)(2,1)}) %all-gather.3.cloned.1.call-update) | async-done | bytes 4194320 | tf_op jit(solution)/shard_map/all_gather | solution.py:286
  61.4 4.6 fusion.76
  67.3 4.6 fusion.77
  73.5 4.6 fusion.78
  79.4 6.9 fusion.79
  86.3 4.6 fusion.2
  90.9 3.2 fusion.22
  94.2 3.4 fusion.23
  102.1 3.3 fusion.56
  109.6 9.8 %collective-permute-done = bf16[96,2048]{1,0:T(8,128)(2,1)S(1)} collective-permute-done((bf16[96,2048]{1,0:T(8,128)(2,1)S(1)}, bf16[96,2048]{1,0:T(8,128)(2,1)S(1)}, u32[]{:S(2)}, u32[]{:S(2)}) %collective-permute-start) | collective-permute-done | bytes 393248 | tf_op jit(solution)/shard_map/ppermute | solution.py:209
  120.7 2.5 collective-permute-start.1
  123.1 8.9 %collective-permute-done.1 = bf16[48,2048]{1,0:T(8,128)(2,1)S(1)} collective-permute-done((bf16[48,2048]{1,0:T(8,128)(2,1)S(1)}, bf16[48,2048]{1,0:T(8,128)(2,1)S(1)}, u32[]{:S(2)}, u32[]{:S(2)}) %collective-permute-start.1) | collective-permute-done | bytes 196640 | tf_op jit(solution)/shard_map/ppermute | solution.py:209
  132.2 3.0 slice.147
  135.4 7.8 %collective-permute-done.2 = bf16[48,2048]{1,0:T(8,128)(2,1)S(1)} collective-permute-done((bf16[48,2048]{1,0:T(8,128)(2,1)S(1)}, bf16[48,2048]{1,0:T(8,128)(2,1)S(1)}, u32[]{:S(2)}, u32[]{:S(2)}) %collective-permute-start.2) | collective-permute-done | bytes 196640 | tf_op jit(solution)/shard_map/ppermute | solution.py:214
  143.3 8.3 %fusion.36 = f32[512,1408]{1,0:T(8,128)} fusion(bf16[1408,2048]{1,0:T(8,128)(2,1)} %param.24, bf16[512,2048]{1,0:T(8,128)(2,1)} %param.25, f32[512]{0:T(512)S(1)} %get-tuple-element.102), kind=kOutput, calls=%fused_computation.104 | convolution fusion | flops 2955935744 | bytes 10749952 | tf_op jit(solution)/shard_map/dot_general | solution.py:49
  151.6 20.5 %collective-permute-done.3 = bf16[96,2048]{1,0:T(8,128)(2,1)} collective-permute-done((bf16[96,2048]{1,0:T(8,128)(2,1)S(1)}, bf16[96,2048]{1,0:T(8,128)(2,1)}, u32[]{:S(2)}, u32[]{:S(2)}) %collective-permute-start.3) | collective-permute-done | bytes 393248 | tf_op jit(solution)/shard_map/ppermute | solution.py:214
  173.3 31.0 %all-reduce.6.cloned.1.call-done = bf16[320,2048]{1,0:T(8,128)(2,1)} async-done(((bf16[320,2048]{1,0:T(8,128)(2,1)}), bf16[320,2048]{1,0:T(8,128)(2,1)}) %all-reduce.6.cloned.1.call-update) | async-done | bytes 1310736 | tf_op jit(solution)/shard_map/psum | solution.py:330
  204.3 3.1 multiply_reduce_fusion.2
  207.5 3.3 multiply_convert_fusion.1
  210.8 5.9 fusion.80
  216.8 4.7 multiply_convert_fusion.2
  221.5 3.4 fusion.84
  224.9 5.3 fusion.82
  230.3 5.5 fusion.83
  235.8 5.0 convolution_add_fusion
  240.8 5.1 fusion.34
  246.0 2.7 dynamic-slice_convert_fusion.2
  250.2 23.8 %collective-permute-done.4 = bf16[256,2048]{1,0:T(8,128)(2,1)} collective-permute-done((bf16[256,2048]{1,0:T(8,128)(2,1)}, bf16[256,2048]{1,0:T(8,128)(2,1)}, u32[]{:S(2)}, u32[]{:S(2)}) %collective-permute-start.4) | collective-permute-done | bytes 1048608 | tf_op jit(solution)/shard_map/ppermute | solution.py:209
  274.0 3.6 convert_add_fusion.4
  282.4 22.5 %collective-permute-done.5 = bf16[128,2048]{1,0:T(8,128)(2,1)} collective-permute-done((bf16[128,2048]{1,0:T(8,128)(2,1)}, bf16[128,2048]{1,0:T(8,128)(2,1)}, u32[]{:S(2)}, u32[]{:S(2)}) %collective-permute-start.5) | collective-permute-done | bytes 524320 | tf_op jit(solution)/shard_map/ppermute | solution.py:209
  304.9 2.6 add_convert_fusion.4
  309.4 22.7 %collective-permute-done.6 = bf16[128,2048]{1,0:T(8,128)(2,1)} collective-permute-done((bf16[128,2048]{1,0:T(8,128)(2,1)}, bf16[128,2048]{1,0:T(8,128)(2,1)}, u32[]{:S(2)}, u32[]{:S(2)}) %collective-permute-start.6) | collective-permute-done | bytes 524320 | tf_op jit(solution)/shard_map/ppermute | solution.py:214
  337.4 8.6 %fusion.81 = f32[512,2048]{1,0:T(8,128)} fusion(bf16[512,1408]{1,0:T(8,128)(2,1)} %copy-done.65, bf16[1408,2048]{1,0:T(8,128)(2,1)} %param.24), kind=kOutput, calls=%fused_computation.186 | convolution fusion | flops 2952790016 | bytes 11403264 | tf_op jit(solution)/shard_map/dot_general | solution.py:340
  346.0 14.7 %collective-permute-done.7 = bf16[256,2048]{1,0:T(8,128)(2,1)} collective-permute-done((bf16[256,2048]{1,0:T(8,128)(2,1)}, bf16[256,2048]{1,0:T(8,128)(2,1)}, u32[]{:S(2)}, u32[]{:S(2)}) %collective-permute-start.7) | collective-permute-done | bytes 1048608 | tf_op jit(solution)/shard_map/ppermute | solution.py:214
  364.5 3.2 multiply_reduce_fusion
  367.8 3.8 convert_add_fusion.1
  373.3 68.7 %shard_map.212 = (f32[512,512]{1,0:T(8,128)S(1)}, f32[4096,256]{1,0:T(8,128)}, f32[4096,256]{1,0:T(8,128)}) custom-call(s32[16]{0:T(128)S(1)} %copy-done.4, s32[2]{0:T(128)S(1)} %dynamic_slice.67.qblock_ref, bf16[512,512]{1,0:T(8,128)(2,1)S(1)} %bitcast.65, bf16[4096,512]{1,0:T(8,128)(2,1)} %all-gather.3.cloned.1.call-done.k_ref.v_ref, ...), custom_call_target="tpu_custom_call" | custom-call | flops 10737418240 | bytes 25165824 | tf_op jit(solution)/shard_map/pallas_call | solution.py:173
  442.0 2.6 convert.61
  450.7 24.1 %collective-permute-done.8 = bf16[256,2048]{1,0:T(8,128)(2,1)S(1)} collective-permute-done((bf16[256,2048]{1,0:T(8,128)(2,1)S(1)}, bf16[256,2048]{1,0:T(8,128)(2,1)S(1)}, u32[]{:S(2)}, u32[]{:S(2)}) %collective-permute-start.8) | collective-permute-done | bytes 1048608 | tf_op jit(solution)/shard_map/ppermute | solution.py:209
  478.3 22.7 %collective-permute-done.9 = bf16[128,2048]{1,0:T(8,128)(2,1)S(1)} collective-permute-done((bf16[128,2048]{1,0:T(8,128)(2,1)S(1)}, bf16[128,2048]{1,0:T(8,128)(2,1)S(1)}, u32[]{:S(2)}, u32[]{:S(2)}) %collective-permute-start.9) | collective-permute-done | bytes 524320 | tf_op jit(solution)/shard_map/ppermute | solution.py:209
  503.3 24.4 %collective-permute-done.10 = bf16[128,2048]{1,0:T(8,128)(2,1)} collective-permute-done((bf16[128,2048]{1,0:T(8,128)(2,1)}, bf16[128,2048]{1,0:T(8,128)(2,1)}, u32[]{:S(2)}, u32[]{:S(2)}) %collective-permute-start.10) | collective-permute-done | bytes 524320 | tf_op jit(solution)/shard_map/ppermute | solution.py:214
  531.2 2.7 fusion.55
  533.9 2.8 fusion.38
  536.7 17.5 %collective-permute-done.11 = bf16[256,2048]{1,0:T(8,128)(2,1)S(1)} collective-permute-done((bf16[256,2048]{1,0:T(8,128)(2,1)S(1)}, bf16[256,2048]{1,0:T(8,128)(2,1)S(1)}, u32[]{:S(2)}, u32[]{:S(2)}) %collective-permute-start.11) | collective-permute-done | bytes 1048608 | tf_op jit(solution)/shard_map/ppermute | solution.py:214
  554.8 2.6 maximum_convert_fusion.1
  559.5 3.6 fusion.54
  563.1 2.8 fusion.53
  568.6 3.6 fusion.43
  574.9 3.2 add_add_fusion.2
  578.6 23.9 %collective-permute-done.12 = bf16[256,2048]{1,0:T(8,128)(2,1)S(1)} collective-permute-done((bf16[256,2048]{1,0:T(8,128)(2,1)S(1)}, bf16[256,2048]{1,0:T(8,128)(2,1)S(1)}, u32[]{:S(2)}, u32[]{:S(2)}) %collective-permute-start.12) | collective-permute-done | bytes 1048608 | tf_op jit(solution)/shard_map/ppermute | solution.py:209
  603.7 23.5 %collective-permute-done.13 = bf16[128,2048]{1,0:T(8,128)(2,1)S(1)} collective-permute-done((bf16[128,2048]{1,0:T(8,128)(2,1)S(1)}, bf16[128,2048]{1,0:T(8,128)(2,1)S(1)}, u32[]{:S(2)}, u32[]{:S(2)}) %collective-permute-start.13) | collective-permute-done | bytes 524320 | tf_op jit(solution)/shard_map/ppermute | solution.py:209
  627.4 24.7 %collective-permute-done.14 = bf16[128,2048]{1,0:T(8,128)(2,1)S(1)} collective-permute-done((bf16[128,2048]{1,0:T(8,128)(2,1)S(1)}, bf16[128,2048]{1,0:T(8,128)(2,1)S(1)}, u32[]{:S(2)}, u32[]{:S(2)}) %collective-permute-start.14) | collective-permute-done | bytes 524320 | tf_op jit(solution)/shard_map/ppermute | solution.py:214
  655.0 2.6 collective-permute-done.20
  659.3 18.2 %collective-permute-done.15 = bf16[256,2048]{1,0:T(8,128)(2,1)S(1)} collective-permute-done((bf16[256,2048]{1,0:T(8,128)(2,1)S(1)}, bf16[256,2048]{1,0:T(8,128)(2,1)S(1)}, u32[]{:S(2)}, u32[]{:S(2)}) %collective-permute-start.15) | collective-permute-done | bytes 1048608 | tf_op jit(solution)/shard_map/ppermute | solution.py:214
  680.2 6.0 convert_element_type.259
  686.2 5.2 convert_element_type.260
  691.4 6.0 convert_element_type.261
  697.4 34.5 %all-reduce.8.cloned.1.call-done = (bf16[2048,512]{1,0:T(8,128)(2,1)}, bf16[2048,256]{1,0:T(8,128)(2,1)}, bf16[2048,256]{1,0:T(8,128)(2,1)}, bf16[512,2048]{1,0:T(8,128)(2,1)}) async-done(((bf16[2048,512]{1,0:T(8,128)(2,1)}, bf16[2048,256]{1,0:T(8,128)(2,1)}, bf16[2048,256]{1,0:T(8,128)(2,1)}, bf16[512,2048]{1,0:T(8,128)(2,1)}), (bf16[2048,512]{1,0:T(8,128)(2,1)}, bf16[2048,256]{1,0:T(8,128)(2,1)}, ...) | async-done | bytes 6291472 | tf_op jit(solution)/shard_map/psum | solution.py:344
  731.9 4.3 convert_element_type.252
  739.3 2.7 convert_element_type.258
  747.0 7.9 %fusion.11 = (f32[512,2048]{1,0:T(8,128)}, bf16[512,2048]{1,0:T(8,128)(2,1)}) fusion(f32[512,2048]{1,0:T(8,128)S(1)} %copy-done.13, bf16[512,2048]{1,0:T(8,128)(2,1)S(1)} %copy-done.10, f32[512]{0:T(512)S(1)} %multiply_multiply_fusion, f32[2048]{0:T(1024)S(1)} %copy-done.55, f32[512]{0:T(512)S(1)} %copy-done.58, bf16[256,2048]{1,0:T(8,128)(2,1)S(1)} %copy-done.24, ...), kind=kLoop, calls=%fused_computation.36 | loop fusion | flops 23068672 | bytes 20985856 | tf_op jit(solution)/shard_map/add | solution.py:424
  (299 shorter events, 94.6 us)
Async XLA Ops:
  7.2 94.9 %copy-start = (bf16[512,2048]{1,0:T(8,128)(2,1)S(1)}, bf16[512,2048]{1,0:T(8,128)(2,1)}, u32[]{:S(2)}) copy-start(bf16[512,2048]{1,0:T(8,128)(2,1)} %param.20) | copy-start | bytes 6291460
  7.2 8.5 %copy-start.44 = (bf16[2048,256]{1,0:T(8,128)(2,1)S(1)}, bf16[2048,256]{1,0:T(8,128)(2,1)}, u32[]{:S(2)}) copy-start(bf16[2048,256]{1,0:T(8,128)(2,1)} %param.18) | copy-start | bytes 3145732
  7.2 54.2 %all-gather.3.cloned.1.call-start = ((), (), s32[]{:S(2)}) async-start(), calls=%async_computation.1 | async-start | bytes 4718592 | tf_op jit(solution)/shard_map/all_gather | solution.py:286
  7.3 8.4 %copy-start.5 = (bf16[512,2048]{1,0:T(8,128)(2,1)S(1)}, bf16[512,2048]{1,0:T(8,128)(2,1)}, u32[]{:S(2)}) copy-start(bf16[512,2048]{1,0:T(8,128)(2,1)} %param.13) | copy-start | bytes 6291460
  11.0 21.7 %copy-start.57 = (f32[512]{0:T(512)}, f32[512]{0:T(512)S(1)}, u32[]{:S(2)}) copy-start(f32[512]{0:T(512)S(1)} %fusion.60) | copy-start | bytes 6148
  11.7 21.0 %copy-start.54 = (f32[2048]{0:T(1024)}, f32[2048]{0:T(1024)S(1)}, u32[]{:S(2)}) copy-start(f32[2048]{0:T(1024)S(1)} %convert_element_type.202) | copy-start | bytes 24580
  19.0 22.3 %copy-start.26 = (f32[512,64]{1,0:T(8,128)}, f32[512,64]{1,0:T(8,128)S(1)}, u32[]{:S(2)}) copy-start(f32[512,64]{1,0:T(8,128)S(1)} %get-tuple-element.101) | copy-start | bytes 393220
  21.9 182.4 %all-reduce.6.cloned.1.call-start = ((), (), s32[]{:S(2)}) async-start(), calls=%async_computation.2 | async-start | bytes 2621440 | tf_op jit(solution)/shard_map/psum | solution.py:330
  43.9 35.5 %copy-start.1 = (bf16[64,8,4,128]{3,1,2,0:T(8,128)(2,1)}, bf16[64,8,4,128]{3,1,2,0:T(8,128)(2,1)S(1)}, u32[]{:S(2)}) copy-start(bf16[64,8,4,128]{3,1,2,0:T(8,128)(2,1)S(1)} %copy.90) | copy-start | bytes 1572868
  94.2 7.8 %copy-start.45 = (bf16[512,128]{0,1:T(8,128)(2,1)}, bf16[512,128]{0,1:T(8,128)(2,1)S(1)}, u32[]{:S(2)}) copy-start(bf16[512,128]{0,1:T(8,128)(2,1)S(1)} %fusion.22) | copy-start | bytes 393220
  108.1 11.3 %collective-permute-start = (bf16[96,2048]{1,0:T(8,128)(2,1)S(1)}, bf16[96,2048]{1,0:T(8,128)(2,1)S(1)}, u32[]{:S(2)}, u32[]{:S(2)}) collective-permute-start(bf16[96,2048]{1,0:T(8,128)(2,1)S(1)} %dynamic-slice_convert_fusion.6), channel_id=1, source_target_pairs={{0,1},{1,0},{2,3},{3,2},{4,5},{5,4},{6,7},{7,6},{8,9},{9,8},{10,11... | collective-permute-start | bytes 1179656 | tf_op jit(solution)/shard_map/ppermute | solution.py:209
  120.7 11.4 %collective-permute-start.1 = (bf16[48,2048]{1,0:T(8,128)(2,1)S(1)}, bf16[48,2048]{1,0:T(8,128)(2,1)S(1)}, u32[]{:S(2)}, u32[]{:S(2)}) collective-permute-start(bf16[48,2048]{1,0:T(8,128)(2,1)S(1)} %dynamic-slice_convert_fusion.7), channel_id=1, source_target_pairs={{0,2},{1,3},{2,0},{3,1},{4,6},{5,7},{6,4},{7,5},{8,10},{9,11},{10,... | collective-permute-start | bytes 589832 | tf_op jit(solution)/shard_map/ppermute | solution.py:209
  132.1 11.1 %collective-permute-start.2 = (bf16[48,2048]{1,0:T(8,128)(2,1)S(1)}, bf16[48,2048]{1,0:T(8,128)(2,1)S(1)}, u32[]{:S(2)}, u32[]{:S(2)}) collective-permute-start(bf16[48,2048]{1,0:T(8,128)(2,1)S(1)} %add_convert_fusion.8), channel_id=1, source_target_pairs={{0,2},{1,3},{2,0},{3,1},{4,6},{5,7},{6,4},{7,5},{8,10},{9,11},{10,... | collective-permute-start | bytes 589832 | tf_op jit(solution)/shard_map/ppermute | solution.py:214
  135.2 422.2 %all-reduce.10.cloned.1.call-start = ((), (), s32[]{:S(2)}) async-start(), calls=%async_computation.5 | async-start | bytes 34603008 | tf_op jit(solution)/shard_map/psum | solution.py:344
  143.2 29.0 %collective-permute-start.3 = (bf16[96,2048]{1,0:T(8,128)(2,1)S(1)}, bf16[96,2048]{1,0:T(8,128)(2,1)}, u32[]{:S(2)}, u32[]{:S(2)}) collective-permute-start(bf16[96,2048]{1,0:T(8,128)(2,1)S(1)} %pad_maximum_fusion.10), channel_id=1, source_target_pairs={{0,1},{1,0},{2,3},{3,2},{4,5},{5,4},{6,7},{7,6},{8,9},{9,8},{10,11... | collective-permute-start | bytes 1179656 | tf_op jit(solution)/shard_map/ppermute | solution.py:214
  143.3 8.3 %copy-start.61 = (bf16[2048]{0:T(1024)(128)(2,1)S(1)}, bf16[2048]{0:T(1024)(128)(2,1)}, u32[]{:S(2)}) copy-start(bf16[2048]{0:T(1024)(128)(2,1)} %param.21) | copy-start | bytes 12292
  173.3 194.4 %copy-start.19 = (bf16[96,2048]{1,0:T(8,128)(2,1)}, bf16[96,2048]{1,0:T(8,128)(2,1)S(1)}, u32[]{:S(2)}) copy-start(bf16[96,2048]{1,0:T(8,128)(2,1)S(1)} %get-tuple-element.93) | copy-start | bytes 1179652
  173.3 194.4 %copy-start.21 = (bf16[96,2048]{1,0:T(8,128)(2,1)}, bf16[96,2048]{1,0:T(8,128)(2,1)S(1)}, u32[]{:S(2)}) copy-start(bf16[96,2048]{1,0:T(8,128)(2,1)S(1)} %get-tuple-element.94) | copy-start | bytes 1179652
  207.5 9.3 %slice-start.8 = ((s8[5767168]{0:T(1024)(128)(4,1)}), s8[4194304]{0:T(1024)(128)(4,1)S(1)}, s32[]{:S(2)}) async-start(s8[5767168]{0:T(1024)(128)(4,1)} %bitcast.101), calls=%async_computation.14 | async-start | bytes 8388608
  210.8 6.0 slice-start.9
  221.5 19.3 %copy-start.65 = (bf16[512,1408]{1,0:T(8,128)(2,1)}, bf16[512,1408]{1,0:T(8,128)(2,1)S(1)}, u32[]{:S(2)}) copy-start(bf16[512,1408]{1,0:T(8,128)(2,1)S(1)} %get-tuple-element.68) | copy-start | bytes 4325380
  224.9 10.9 %slice-start.10 = ((s8[5767168]{0:T(1024)(128)(4,1)}), s8[4194304]{0:T(1024)(128)(4,1)S(1)}, s32[]{:S(2)}) async-start(s8[5767168]{0:T(1024)(128)(4,1)} %bitcast.103), calls=%async_computation.16 | async-start | bytes 8388608
  248.7 25.4 %collective-permute-start.4 = (bf16[256,2048]{1,0:T(8,128)(2,1)}, bf16[256,2048]{1,0:T(8,128)(2,1)}, u32[]{:S(2)}, u32[]{:S(2)}) collective-permute-start(bf16[256,2048]{1,0:T(8,128)(2,1)} %dynamic-slice_convert_fusion.2), channel_id=1, source_target_pairs={{0,1},{1,0},{2,3},{3,2},{4,5},{5,4},{6,7},{7,6},{8,9},{9,8},{10,11... | collective-permute-start | bytes 3145736 | tf_op jit(solution)/shard_map/ppermute | solution.py:209
  250.2 31.2 %copy-start.4 = (s32[16]{0:T(128)S(1)}, s32[16]{0:T(128)}, u32[]{:S(2)}) copy-start(s32[16]{0:T(128)} %chunk_ref.1) | copy-start | bytes 196
  250.2 31.3 %copy-start.56 = (s32[1,1,16,256]{3,2,1,0:T(8,128)S(1)}, s32[1,1,16,256]{3,2,1,0:T(8,128)}, u32[]{:S(2)}) copy-start(s32[1,1,16,256]{3,2,1,0:T(8,128)} %get-tuple-element.104) | copy-start | bytes 49156
  250.2 307.2 %reduce-scatter.2.cloned.1.call-start = ((), (), s32[]{:S(2)}) async-start(), calls=%async_computation.3 | async-start | bytes 4718592 | tf_op jit(solution)/shard_map/reduce_scatter | solution.py:376
  280.0 24.9 %collective-permute-start.5 = (bf16[128,2048]{1,0:T(8,128)(2,1)}, bf16[128,2048]{1,0:T(8,128)(2,1)}, u32[]{:S(2)}, u32[]{:S(2)}) collective-permute-start(bf16[128,2048]{1,0:T(8,128)(2,1)} %dynamic-slice_convert_fusion.5), channel_id=1, source_target_pairs={{0,2},{1,3},{2,0},{3,1},{4,6},{5,7},{6,4},{7,5},{8,10},{9,11},{10,... | collective-permute-start | bytes 1572872 | tf_op jit(solution)/shard_map/ppermute | solution.py:209
  307.5 24.7 %collective-permute-start.6 = (bf16[128,2048]{1,0:T(8,128)(2,1)}, bf16[128,2048]{1,0:T(8,128)(2,1)}, u32[]{:S(2)}, u32[]{:S(2)}) collective-permute-start(bf16[128,2048]{1,0:T(8,128)(2,1)} %add_convert_fusion.4), channel_id=1, source_target_pairs={{0,2},{1,3},{2,0},{3,1},{4,6},{5,7},{6,4},{7,5},{8,10},{9,11},{10,... | collective-permute-start | bytes 1572872 | tf_op jit(solution)/shard_map/ppermute | solution.py:214
  335.3 25.4 %collective-permute-start.7 = (bf16[256,2048]{1,0:T(8,128)(2,1)}, bf16[256,2048]{1,0:T(8,128)(2,1)}, u32[]{:S(2)}, u32[]{:S(2)}) collective-permute-start(bf16[256,2048]{1,0:T(8,128)(2,1)} %pad_maximum_fusion.2), channel_id=1, source_target_pairs={{0,1},{1,0},{2,3},{3,2},{4,5},{5,4},{6,7},{7,6},{8,9},{9,8},{10,11... | collective-permute-start | bytes 3145736 | tf_op jit(solution)/shard_map/ppermute | solution.py:214
  337.4 23.3 %copy-start.30 = (bf16[128,2048]{1,0:T(8,128)(2,1)S(1)}, bf16[128,2048]{1,0:T(8,128)(2,1)}, u32[]{:S(2)}) copy-start(bf16[128,2048]{1,0:T(8,128)(2,1)} %copy-done.29) | copy-start | bytes 1572868
  337.4 23.3 %copy-start.32 = (bf16[128,2048]{1,0:T(8,128)(2,1)S(1)}, bf16[128,2048]{1,0:T(8,128)(2,1)}, u32[]{:S(2)}) copy-start(bf16[128,2048]{1,0:T(8,128)(2,1)} %copy-done.31) | copy-start | bytes 1572868
  371.6 70.4 %copy-start.11 = (f32[512,2048]{1,0:T(8,128)}, f32[512,2048]{1,0:T(8,128)S(1)}, u32[]{:S(2)}) copy-start(f32[512,2048]{1,0:T(8,128)S(1)} %convert_add_fusion.1) | copy-start | bytes 12582916
  448.4 283.5 %all-reduce.8.cloned.1.call-start = ((), (), s32[]{:S(2)}) async-start(), calls=%async_computation.4 | async-start | bytes 12582912 | tf_op jit(solution)/shard_map/psum | solution.py:344
  450.4 24.3 %collective-permute-start.8 = (bf16[256,2048]{1,0:T(8,128)(2,1)S(1)}, bf16[256,2048]{1,0:T(8,128)(2,1)S(1)}, u32[]{:S(2)}, u32[]{:S(2)}) collective-permute-start(bf16[256,2048]{1,0:T(8,128)(2,1)S(1)} %dynamic-slice_convert_fusion.1), channel_id=1, source_target_pairs={{0,1},{1,0},{2,3},{3,2},{4,5},{5,4},{6,7},{7,6},{8,9},{9,8},{10,11... | collective-permute-start | bytes 3145736 | tf_op jit(solution)/shard_map/ppermute | solution.py:209
  476.7 52.5 %copy-start.27 = (f32[512,64]{1,0:T(8,128)S(1)}, f32[512,64]{1,0:T(8,128)}, u32[]{:S(2)}) copy-start(f32[512,64]{1,0:T(8,128)} %copy-done.26) | copy-start | bytes 393220
  476.7 24.3 %collective-permute-start.9 = (bf16[128,2048]{1,0:T(8,128)(2,1)S(1)}, bf16[128,2048]{1,0:T(8,128)(2,1)S(1)}, u32[]{:S(2)}, u32[]{:S(2)}) collective-permute-start(bf16[128,2048]{1,0:T(8,128)(2,1)S(1)} %dynamic-slice_convert_fusion.4), channel_id=1, source_target_pairs={{0,2},{1,3},{2,0},{3,1},{4,6},{5,7},{6,4},{7,5},{8,10},{9,11},{10,... | collective-permute-start | bytes 1572872 | tf_op jit(solution)/shard_map/ppermute | solution.py:209
  502.0 25.7 %collective-permute-start.10 = (bf16[128,2048]{1,0:T(8,128)(2,1)}, bf16[128,2048]{1,0:T(8,128)(2,1)}, u32[]{:S(2)}, u32[]{:S(2)}) collective-permute-start(bf16[128,2048]{1,0:T(8,128)(2,1)} %add_convert_fusion.3), channel_id=1, source_target_pairs={{0,2},{1,3},{2,0},{3,1},{4,6},{5,7},{6,4},{7,5},{8,10},{9,11},{10,... | collective-permute-start | bytes 1572872 | tf_op jit(solution)/shard_map/ppermute | solution.py:214
  503.3 25.9 %copy-start.25 = (f32[512,4,128]{2,1,0:T(4,128)S(1)}, f32[512,4,128]{2,1,0:T(4,128)}, u32[]{:S(2)}) copy-start(f32[512,4,128]{2,1,0:T(4,128)} %reshape.288) | copy-start | bytes 3145732
  503.3 25.9 %copy-start.34 = (f32[512,64]{1,0:T(8,128)S(1)}, f32[512,64]{1,0:T(8,128)}, u32[]{:S(2)}) copy-start(f32[512,64]{1,0:T(8,128)} %get-tuple-element.99) | copy-start | bytes 393220
  529.1 25.1 %collective-permute-start.11 = (bf16[256,2048]{1,0:T(8,128)(2,1)S(1)}, bf16[256,2048]{1,0:T(8,128)(2,1)S(1)}, u32[]{:S(2)}, u32[]{:S(2)}) collective-permute-start(bf16[256,2048]{1,0:T(8,128)(2,1)S(1)} %pad_maximum_fusion.3), channel_id=1, source_target_pairs={{0,1},{1,0},{2,3},{3,2},{4,5},{5,4},{6,7},{7,6},{8,9},{9,8},{10,11... | collective-permute-start | bytes 3145736 | tf_op jit(solution)/shard_map/ppermute | solution.py:214
  578.2 24.3 %collective-permute-start.12 = (bf16[256,2048]{1,0:T(8,128)(2,1)S(1)}, bf16[256,2048]{1,0:T(8,128)(2,1)S(1)}, u32[]{:S(2)}, u32[]{:S(2)}) collective-permute-start(bf16[256,2048]{1,0:T(8,128)(2,1)S(1)} %dynamic-slice_convert_fusion), channel_id=1, source_target_pairs={{0,1},{1,0},{2,3},{3,2},{4,5},{5,4},{6,7},{7,6},{8,9},{9,8},{10,11... | collective-permute-start | bytes 3145736 | tf_op jit(solution)/shard_map/ppermute | solution.py:209
  602.8 24.3 %collective-permute-start.13 = (bf16[128,2048]{1,0:T(8,128)(2,1)S(1)}, bf16[128,2048]{1,0:T(8,128)(2,1)S(1)}, u32[]{:S(2)}, u32[]{:S(2)}) collective-permute-start(bf16[128,2048]{1,0:T(8,128)(2,1)S(1)} %dynamic-slice_convert_fusion.3), channel_id=1, source_target_pairs={{0,2},{1,3},{2,0},{3,1},{4,6},{5,7},{6,4},{7,5},{8,10},{9,11},{10,... | collective-permute-start | bytes 1572872 | tf_op jit(solution)/shard_map/ppermute | solution.py:209
  627.3 24.8 %collective-permute-start.14 = (bf16[128,2048]{1,0:T(8,128)(2,1)S(1)}, bf16[128,2048]{1,0:T(8,128)(2,1)S(1)}, u32[]{:S(2)}, u32[]{:S(2)}) collective-permute-start(bf16[128,2048]{1,0:T(8,128)(2,1)S(1)} %add_convert_fusion.1), channel_id=1, source_target_pairs={{0,2},{1,3},{2,0},{3,1},{4,6},{5,7},{6,4},{7,5},{8,10},{9,11},{10,... | collective-permute-start | bytes 1572872 | tf_op jit(solution)/shard_map/ppermute | solution.py:214
  627.4 50.4 %copy-start.9 = (bf16[512,2048]{1,0:T(8,128)(2,1)S(1)}, bf16[512,2048]{1,0:T(8,128)(2,1)}, u32[]{:S(2)}) copy-start(bf16[512,2048]{1,0:T(8,128)(2,1)} %param.13) | copy-start | bytes 6291460
  652.2 28.0 %slice-start.6 = ((s8[5767168]{0:T(1024)(128)(4,1)}), s8[4194304]{0:T(1024)(128)(4,1)S(1)}, s32[]{:S(2)}) async-start(s8[5767168]{0:T(1024)(128)(4,1)} %bitcast.74), calls=%async_computation.12 | async-start | bytes 8388608
  652.3 25.1 %collective-permute-start.15 = (bf16[256,2048]{1,0:T(8,128)(2,1)S(1)}, bf16[256,2048]{1,0:T(8,128)(2,1)S(1)}, u32[]{:S(2)}, u32[]{:S(2)}) collective-permute-start(bf16[256,2048]{1,0:T(8,128)(2,1)S(1)} %pad_maximum_fusion.5), channel_id=1, source_target_pairs={{0,1},{1,0},{2,3},{3,2},{4,5},{5,4},{6,7},{7,6},{8,9},{9,8},{10,11... | collective-permute-start | bytes 3145736 | tf_op jit(solution)/shard_map/ppermute | solution.py:214
  652.4 1.2 collective-permute-start.19
  653.6 4.0 collective-permute-start.20
  657.6 22.6 %slice-start.7 = ((s8[5767168]{0:T(1024)(128)(4,1)}), s8[1572864]{0:T(1024)(128)(4,1)S(1)}, s32[]{:S(2)}) async-start(s8[5767168]{0:T(1024)(128)(4,1)} %bitcast.74), calls=%async_computation.13 | async-start | bytes 3145728
  657.6 22.0 %collective-permute-start.21 = (f32[2048]{0:T(1024)S(1)}, f32[2048]{0:T(1024)S(1)}, u32[]{:S(2)}, u32[]{:S(2)}) collective-permute-start(f32[2048]{0:T(1024)S(1)} %add.314), channel_id=1, source_target_pairs={{0,16},{4,20},{8,24},{12,28},{16,0},{20,4},{24,8},{28,12},{1,17},{... | collective-permute-start | bytes 24584 | tf_op jit(solution)/shard_map/ppermute | solution.py:228
  677.9 8.3 %slice-start.4 = ((s8[5767168]{0:T(1024)(128)(4,1)}), s8[4194304]{0:T(1024)(128)(4,1)S(1)}, s32[]{:S(2)}) async-start(s8[5767168]{0:T(1024)(128)(4,1)} %bitcast.72), calls=%async_computation.10 | async-start | bytes 8388608
  679.5 62.5 %collective-permute-start.16 = (f32[2048]{0:T(1024)S(1)}, f32[2048]{0:T(1024)S(1)}, u32[]{:S(2)}, u32[]{:S(2)}) collective-permute-start(f32[2048]{0:T(1024)S(1)} %get-tuple-element.55), channel_id=1, source_target_pairs={{0,4},{4,0},{8,12},{12,8},{16,20},{20,16},{24,28},{28,24},{1,5},{5... | collective-permute-start | bytes 24584 | tf_op jit(solution)/shard_map/ppermute | solution.py:228
  680.2 6.0 slice-start.5
  680.2 11.2 %slice-start.2 = ((s8[5767168]{0:T(1024)(128)(4,1)}), s8[4194304]{0:T(1024)(128)(4,1)S(1)}, s32[]{:S(2)}) async-start(s8[5767168]{0:T(1024)(128)(4,1)} %bitcast.70), calls=%async_computation.8 | async-start | bytes 8388608
  731.9 7.4 copy-start.36
  731.9 15.0 %copy-start.24 = (bf16[256,2048]{1,0:T(8,128)(2,1)S(1)}, bf16[256,2048]{1,0:T(8,128)(2,1)}, u32[]{:S(2)}) copy-start(bf16[256,2048]{1,0:T(8,128)(2,1)} %copy-done.23) | copy-start | bytes 3145732
  736.3 10.6 %copy-start.17 = (f32[512,2048]{1,0:T(8,128)S(1)}, f32[512,2048]{1,0:T(8,128)}, u32[]{:S(2)}) copy-start(f32[512,2048]{1,0:T(8,128)} %maximum_convert_fusion.1) | copy-start | bytes 12582916
  737.8 9.2 %copy-start.10 = (bf16[512,2048]{1,0:T(8,128)(2,1)S(1)}, bf16[512,2048]{1,0:T(8,128)(2,1)}, u32[]{:S(2)}) copy-start(bf16[512,2048]{1,0:T(8,128)(2,1)} %param.13) | copy-start | bytes 6291460
  737.8 9.2 %copy-start.13 = (f32[512,2048]{1,0:T(8,128)S(1)}, f32[512,2048]{1,0:T(8,128)}, u32[]{:S(2)}) copy-start(f32[512,2048]{1,0:T(8,128)} %copy-done.11) | copy-start | bytes 12582916
  737.8 9.2 %copy-start.16 = (bf16[320,2048]{1,0:T(8,128)(2,1)S(1)}, bf16[320,2048]{1,0:T(8,128)(2,1)}, u32[]{:S(2)}) copy-start(bf16[320,2048]{1,0:T(8,128)(2,1)} %all-reduce.6.cloned.1.call-done) | copy-start | bytes 3932164
  737.8 9.2 %copy-start.20 = (bf16[96,2048]{1,0:T(8,128)(2,1)S(1)}, bf16[96,2048]{1,0:T(8,128)(2,1)}, u32[]{:S(2)}) copy-start(bf16[96,2048]{1,0:T(8,128)(2,1)} %copy-done.19) | copy-start | bytes 1179652
  737.8 9.2 %copy-start.22 = (bf16[96,2048]{1,0:T(8,128)(2,1)S(1)}, bf16[96,2048]{1,0:T(8,128)(2,1)}, u32[]{:S(2)}) copy-start(bf16[96,2048]{1,0:T(8,128)(2,1)} %copy-done.21) | copy-start | bytes 1179652
  742.0 3.7 collective-permute-start.17
  745.6 9.2 %collective-permute-start.18 = (f32[2048]{0:T(1024)S(1)}, f32[2048]{0:T(1024)S(1)}, u32[]{:S(2)}, u32[]{:S(2)}) collective-permute-start(f32[2048]{0:T(1024)S(1)} %add.311), channel_id=1, source_target_pairs={{0,16},{4,20},{8,24},{12,28},{16,0},{20,4},{24,8},{28,12},{1,17},{... | collective-permute-start | bytes 24584 | tf_op jit(solution)/shard_map/ppermute | solution.py:228
  (41 other events, 134.5 us)
Sparse Core Ops, SparseCore 0:
  22.1 39.2 all-gather.2
  135.3 68.9 all-reduce.5
  250.3 221.6 all-reduce.9
  475.8 51.2 reduce-scatter.1
  627.5 104.3 all-reduce.7

commit v6 on v5

--- a/solution.py
+++ b/solution.py
@@ -219,6 +219,29 @@
             for mine, theirs, dim in zip(pieces, got, dims)
         ]
     return [piece.astype(jnp.float32) for piece in pieces]
+
+
+def permute_scatter(value, axis):
+    size = lax.axis_size(axis)
+    steps = size.bit_length() - 1
+    assert 1 << steps == size
+    block = value.shape[0] // size
+
+    def reverse(index):
+        return int(format(index, f"0{steps}b")[::-1], 2) if steps else 0
+
+    value = jnp.concatenate(
+        [value[reverse(place) * block : (reverse(place) + 1) * block] for place in range(size)], axis=0
+    )
+    me = lax.axis_index(axis)
+    for step in range(steps):
+        bit = (me >> step) & 1
+        half = value.shape[0] // 2
+        keep = lax.dynamic_slice_in_dim(value, bit * half, half, axis=0)
+        send = lax.dynamic_slice_in_dim(value, (1 - bit) * half, half, axis=0).astype(jnp.bfloat16)
+        got = lax.ppermute(send, axis, partner_perm(size, 1 << step))
+        value = keep.astype(jnp.float32) + got.astype(jnp.float32)
+    return value
 
 
 def permute_allsum(value, axis):
@@ -372,13 +395,7 @@
         query_low, all_kv, d_attended, lse, local_groups=local_groups, chunk=half_rows,
         **mask_args,
     )
-    d_kv_cat = jnp.concatenate([d_key_all, d_value_all], axis=1).astype(jnp.bfloat16)
-    d_kv_own = lax.psum_scatter(
-        d_kv_cat,
-        "dp",
-        scatter_dimension=0,
-        tiled=True,
-    ).astype(jnp.float32)
+    d_kv_own = permute_scatter(jnp.concatenate([d_key_all, d_value_all], axis=1), "dp")
     d_kv_own, grad_w_out = lax.optimization_barrier((d_kv_own, grad_w_out))
     d_key_own = d_kv_own[:, :kv_width]
     d_value_own = d_kv_own[:, kv_width:]

time: 767 us -> 793 us (1.034)
  waiting for transfers between devices: 399 us -> 416 us
  local copies, waits for them, and re-layouts: 31.3 us -> 40.2 us
    psum x2, waiting for transfers between devices: 34.5 us -> 68.9 us  [dp_sum(): return [lax.psum(grad.astype(jnp.bfloat16), 'dp') for grad in grads]]
    ppermute x0 -> x3, waiting for transfers between devices: none -> 33 us  [permute_scatter(): got = lax.ppermute(send, axis, partner_perm(size, 1 << step))]
    ppermute x8, waiting for transfers between devices: 159 us -> 127 us  [permute_sum(): got = lax.ppermute(send, axis, partner_perm(size, 1 << step))]
    ppermute x8, waiting for transfers between devices: 150 us -> 133 us  [permute_sum(): got = lax.ppermute(pieces, axis, partner_perm(size, 1 << step))]
    unnamed x166 -> x182, local copies, waits for them, and re-layouts: 12.1 us -> 20.2 us
  transfers between devices with their start and end apart: 27 -> 29, of which waited for: 22 -> 24; matrix products, arithmetic and copies ran while one was open for 16% -> 14% of each run, Pallas kernels for 9% -> 9%
where the time goes in v6:
time: 793 us; the launch traced here: 788 us
  waiting for transfers between devices  416 us (52%)
  matrix products  117 us (15%)
  other arithmetic  96.5 us (12%)
  Pallas kernels  68.5 us (9%)
  local copies, waits for them, and re-layouts  40.2 us (5%)
  starting transfers between devices  23.6 us (3%)
  between operations  15.5 us (2%)
  blocking collectives  10.6 us (1%)
    ppermute x8, waiting for transfers between devices, permute_sum(): got = lax.ppermute(pieces, axis, partner_perm(size, 1 << step))  133 us
    ppermute x8, waiting for transfers between devices, permute_sum(): got = lax.ppermute(send, axis, partner_perm(size, 1 << step))  127 us
    psum x2, waiting for transfers between devices, dp_sum(): return [lax.psum(grad.astype(jnp.bfloat16), 'dp') for grad in grads]  68.9 us
    pallas_call x1, Pallas kernels, attention_backward(): pl.pallas_call(kernel, grid_spec=grid_spec, out_shape=[jax.ShapeDtypeStru...  68.5 us
    dot_general x11, matrix products, right_trans(): lax.dot_general(left, right, (((1,), (1,)), ((), ())), preferred_element_...  46.5 us
    ppermute x3, waiting for transfers between devices, permute_scatter(): got = lax.ppermute(send, axis, partner_perm(size, 1 << step))  33 us
    dot_general x7, matrix products, left_trans(): lax.dot_general(left, right, (((0,), (0,)), ((), ())), preferred_element_...  31.8 us
    psum x1, waiting for transfers between devices, on_device(): branch_top = lax.psum(branch_part[:sc_rows].astype(jnp.bfloat16), 'tensor')  31 us
  transfers between devices with their start and end apart: 29, of which 24 were waited for; matrix products, arithmetic and copies ran while one was open for 14% of the time, Pallas kernels for 9%

profile of v6, /device:TPU:0, one launch (start us, length us, event | category | flops | bytes accessed | tf_op | source)
XLA Modules:
  0.0 787.6 jit_solution(7347112657102768523)
XLA Ops:
  12.3 3.3 convolution_convert_fusion.1
  21.9 10.6 %all-gather = bf16[8,1,512]{2,1,0:T(2,128)(2,1)S(1)} all-gather(bf16[1,1,512]{2,1,0:T(2,128)(2,1)S(1)} %reshape.291), channel_id=1, replica_groups=mesh['dp'=8,'tensor'=4] {'dp'}, dimensions={0}, use_global_device_ids=true | all-gather | bytes 9216 | tf_op jit(solution)/shard_map/all_gather | solution.py:312
  32.6 3.7 fusion.70
  43.9 17.5 %all-gather.3.cloned.1.call-done.k_ref.v_ref = bf16[4096,512]{1,0:T(8,128)(2,1)} async-done(((bf16[512,512]{1,0:T(8,128)(2,1)}), bf16[4096,512]{1,0:T(8,128)(2,1)}) %all-gather.3.cloned.1.call-update) | async-done | bytes 4194320 | tf_op jit(solution)/shard_map/all_gather | solution.py:309
  61.3 4.6 fusion.76
  67.2 4.6 fusion.77
  73.5 4.6 fusion.78
  79.3 6.9 fusion.79
  86.2 4.6 fusion.2
  90.9 3.2 fusion.22
  94.1 3.4 fusion.23
  102.0 3.3 fusion.56
  109.6 9.8 %collective-permute-done = bf16[96,2048]{1,0:T(8,128)(2,1)S(1)} collective-permute-done((bf16[96,2048]{1,0:T(8,128)(2,1)S(1)}, bf16[96,2048]{1,0:T(8,128)(2,1)S(1)}, u32[]{:S(2)}, u32[]{:S(2)}) %collective-permute-start) | collective-permute-done | bytes 393248 | tf_op jit(solution)/shard_map/ppermute | solution.py:209
  123.1 8.9 %collective-permute-done.1 = bf16[48,2048]{1,0:T(8,128)(2,1)S(1)} collective-permute-done((bf16[48,2048]{1,0:T(8,128)(2,1)S(1)}, bf16[48,2048]{1,0:T(8,128)(2,1)S(1)}, u32[]{:S(2)}, u32[]{:S(2)}) %collective-permute-start.1) | collective-permute-done | bytes 196640 | tf_op jit(solution)/shard_map/ppermute | solution.py:209
  132.1 3.0 slice.195
  135.3 7.8 collective-permute-done.2
  143.3 8.3 %fusion.36 = f32[512,1408]{1,0:T(8,128)} fusion(bf16[1408,2048]{1,0:T(8,128)(2,1)} %param.24, bf16[512,2048]{1,0:T(8,128)(2,1)} %param.25, f32[512]{0:T(512)S(1)} %get-tuple-element.102), kind=kOutput, calls=%fused_computation.117 | convolution fusion | flops 2955935744 | bytes 10749952 | tf_op jit(solution)/shard_map/dot_general | solution.py:49
  151.6 20.5 %collective-permute-done.3 = bf16[96,2048]{1,0:T(8,128)(2,1)} collective-permute-done((bf16[96,2048]{1,0:T(8,128)(2,1)S(1)}, bf16[96,2048]{1,0:T(8,128)(2,1)}, u32[]{:S(2)}, u32[]{:S(2)}) %collective-permute-start.3) | collective-permute-done | bytes 393248 | tf_op jit(solution)/shard_map/ppermute | solution.py:214
  173.3 31.0 %all-reduce.6.cloned.1.call-done = bf16[320,2048]{1,0:T(8,128)(2,1)} async-done(((bf16[320,2048]{1,0:T(8,128)(2,1)}), bf16[320,2048]{1,0:T(8,128)(2,1)}) %all-reduce.6.cloned.1.call-update) | async-done | bytes 1310736 | tf_op jit(solution)/shard_map/psum | solution.py:353
  204.3 3.1 multiply_reduce_fusion.2
  207.4 3.3 multiply_convert_fusion.1
  210.8 5.9 fusion.80
  216.7 4.7 multiply_convert_fusion.2
  221.4 3.4 fusion.84
  224.9 5.3 fusion.82
  230.2 5.5 fusion.83
  235.7 5.0 convolution_add_fusion
  240.8 5.2 fusion.34
  245.9 2.7 dynamic-slice_convert_fusion.4
  250.1 23.9 %collective-permute-done.4 = bf16[256,2048]{1,0:T(8,128)(2,1)} collective-permute-done((bf16[256,2048]{1,0:T(8,128)(2,1)}, bf16[256,2048]{1,0:T(8,128)(2,1)}, u32[]{:S(2)}, u32[]{:S(2)}) %collective-permute-start.4) | collective-permute-done | bytes 1048608 | tf_op jit(solution)/shard_map/ppermute | solution.py:209
  281.1 22.3 %collective-permute-done.5 = bf16[128,2048]{1,0:T(8,128)(2,1)} collective-permute-done((bf16[128,2048]{1,0:T(8,128)(2,1)}, bf16[128,2048]{1,0:T(8,128)(2,1)}, u32[]{:S(2)}, u32[]{:S(2)}) %collective-permute-start.5) | collective-permute-done | bytes 524320 | tf_op jit(solution)/shard_map/ppermute | solution.py:209
  304.9 24.4 %collective-permute-done.6 = bf16[128,2048]{1,0:T(8,128)(2,1)S(1)} collective-permute-done((bf16[128,2048]{1,0:T(8,128)(2,1)S(1)}, bf16[128,2048]{1,0:T(8,128)(2,1)S(1)}, u32[]{:S(2)}, u32[]{:S(2)}) %collective-permute-start.6) | collective-permute-done | bytes 524320 | tf_op jit(solution)/shard_map/ppermute | solution.py:214
  336.3 6.3 fusion.81
  342.5 14.1 %collective-permute-done.7 = bf16[256,2048]{1,0:T(8,128)(2,1)} collective-permute-done((bf16[256,2048]{1,0:T(8,128)(2,1)}, bf16[256,2048]{1,0:T(8,128)(2,1)}, u32[]{:S(2)}, u32[]{:S(2)}) %collective-permute-start.7) | collective-permute-done | bytes 1048608 | tf_op jit(solution)/shard_map/ppermute | solution.py:214
  360.3 2.8 multiply_reduce_fusion
  363.2 3.8 convert_add_fusion.1
  370.0 68.5 %shard_map.212 = (f32[512,512]{1,0:T(8,128)S(1)}, f32[4096,256]{1,0:T(8,128)}, f32[4096,256]{1,0:T(8,128)}) custom-call(s32[16]{0:T(128)S(1)} %copy-done.5, s32[2]{0:T(128)S(1)} %dynamic_slice.85.qblock_ref, bf16[512,512]{1,0:T(8,128)(2,1)S(1)} %bitcast.65, bf16[4096,512]{1,0:T(8,128)(2,1)} %all-gather.3.cloned.1.call-done.k_ref.v_ref, ...), custom_call_target="tpu_custom_call" | custom-call | flops 10737418240 | bytes 25165824 | tf_op jit(solution)/shard_map/pallas_call | solution.py:173
  438.5 3.1 constant_dynamic-update-slice_fusion.1
  445.4 3.1 copy-done.39
  453.9 5.7 fusion.55
  459.6 16.0 %collective-permute-done.9 = bf16[128,2048]{1,0:T(8,128)(2,1)} collective-permute-done((bf16[128,2048]{1,0:T(8,128)(2,1)}, bf16[128,2048]{1,0:T(8,128)(2,1)}, u32[]{:S(2)}, u32[]{:S(2)}) %collective-permute-start.9) | collective-permute-done | bytes 524320 | tf_op jit(solution)/shard_map/ppermute | solution.py:209
  479.8 2.9 collective-permute-start.13
  482.7 20.0 %collective-permute-done.10 = bf16[128,2048]{1,0:T(8,128)(2,1)S(1)} collective-permute-done((bf16[128,2048]{1,0:T(8,128)(2,1)S(1)}, bf16[128,2048]{1,0:T(8,128)(2,1)S(1)}, u32[]{:S(2)}, u32[]{:S(2)}) %collective-permute-start.10) | collective-permute-done | bytes 524320 | tf_op jit(solution)/shard_map/ppermute | solution.py:214
  504.6 2.8 fusion.38
  507.4 16.7 %collective-permute-done.13 = bf16[1024,512]{1,0:T(8,128)(2,1)S(1)} collective-permute-done((bf16[1024,512]{1,0:T(8,128)(2,1)S(1)}, bf16[1024,512]{1,0:T(8,128)(2,1)S(1)}, u32[]{:S(2)}, u32[]{:S(2)}) %collective-permute-start.13) | collective-permute-done | bytes 1048608 | tf_op jit(solution)/shard_map/ppermute | solution.py:242
  528.4 2.6 maximum_convert_fusion.1
  530.9 16.3 %collective-permute-done.14 = bf16[512,512]{1,0:T(8,128)(2,1)S(1)} collective-permute-done((bf16[512,512]{1,0:T(8,128)(2,1)S(1)}, bf16[512,512]{1,0:T(8,128)(2,1)S(1)}, u32[]{:S(2)}, u32[]{:S(2)}) %collective-permute-start.14) | collective-permute-done | bytes 524320 | tf_op jit(solution)/shard_map/ppermute | solution.py:242
  547.4 35.3 %all-reduce.10.cloned.1.call-done = (bf16[2048,1408]{1,0:T(8,128)(2,1)}, bf16[2048,1408]{1,0:T(8,128)(2,1)}, bf16[1408,2048]{1,0:T(8,128)(2,1)}) async-done(((bf16[2048,1408]{1,0:T(8,128)(2,1)}, bf16[2048,1408]{1,0:T(8,128)(2,1)}, bf16[1408,2048]{1,0:T(8,128)(2,1)}), (bf16[2048,1408]{1,0:T(8,128)(2,1)}, bf16[2048,1408]{1,0:T(8,128)(2,1)}, bf16[1408,2048]{1,0:T(8,128)(2,1)})) %all-reduce.10.cloned.1.call-update) | async-done | bytes 17301520 | tf_op jit(solution)/shard_map/psum | solution.py:367
  583.5 3.5 fusion.54
  587.0 2.8 fusion.53
  593.6 3.7 fusion.43
  600.0 3.0 add_add_fusion.2
  604.7 23.2 %collective-permute-done.15 = bf16[256,2048]{1,0:T(8,128)(2,1)S(1)} collective-permute-done((bf16[256,2048]{1,0:T(8,128)(2,1)S(1)}, bf16[256,2048]{1,0:T(8,128)(2,1)S(1)}, u32[]{:S(2)}, u32[]{:S(2)}) %collective-permute-start.15) | collective-permute-done | bytes 1048608 | tf_op jit(solution)/shard_map/ppermute | solution.py:209
  630.6 22.4 %collective-permute-done.16 = bf16[128,2048]{1,0:T(8,128)(2,1)S(1)} collective-permute-done((bf16[128,2048]{1,0:T(8,128)(2,1)S(1)}, bf16[128,2048]{1,0:T(8,128)(2,1)S(1)}, u32[]{:S(2)}, u32[]{:S(2)}) %collective-permute-start.16) | collective-permute-done | bytes 524320 | tf_op jit(solution)/shard_map/ppermute | solution.py:209
  653.3 24.6 %collective-permute-done.17 = bf16[128,2048]{1,0:T(8,128)(2,1)S(1)} collective-permute-done((bf16[128,2048]{1,0:T(8,128)(2,1)S(1)}, bf16[128,2048]{1,0:T(8,128)(2,1)S(1)}, u32[]{:S(2)}, u32[]{:S(2)}) %collective-permute-start.17) | collective-permute-done | bytes 524320 | tf_op jit(solution)/shard_map/ppermute | solution.py:214
  680.6 2.8 collective-permute-done.23
  684.1 19.2 %collective-permute-done.18 = bf16[256,2048]{1,0:T(8,128)(2,1)S(1)} collective-permute-done((bf16[256,2048]{1,0:T(8,128)(2,1)S(1)}, bf16[256,2048]{1,0:T(8,128)(2,1)S(1)}, u32[]{:S(2)}, u32[]{:S(2)}) %collective-permute-start.18) | collective-permute-done | bytes 1048608 | tf_op jit(solution)/shard_map/ppermute | solution.py:214
  706.0 6.2 convert_element_type.278
  712.2 5.2 convert_element_type.279
  717.3 6.0 convert_element_type.280
  723.4 33.7 %all-reduce.8.cloned.1.call-done = (bf16[2048,512]{1,0:T(8,128)(2,1)}, bf16[2048,256]{1,0:T(8,128)(2,1)}, bf16[2048,256]{1,0:T(8,128)(2,1)}, bf16[512,2048]{1,0:T(8,128)(2,1)}) async-done(((bf16[2048,512]{1,0:T(8,128)(2,1)}, bf16[2048,256]{1,0:T(8,128)(2,1)}, bf16[2048,256]{1,0:T(8,128)(2,1)}, bf16[512,2048]{1,0:T(8,128)(2,1)}), (bf16[2048,512]{1,0:T(8,128)(2,1)}, bf16[2048,256]{1,0:T(8,128)(2,1)}, ...) | async-done | bytes 6291472 | tf_op jit(solution)/shard_map/psum | solution.py:367
  757.0 4.3 convert_element_type.271
  764.4 2.7 convert_element_type.277
  772.1 8.2 %fusion.11 = (f32[512,2048]{1,0:T(8,128)}, bf16[512,2048]{1,0:T(8,128)(2,1)}) fusion(f32[512,2048]{1,0:T(8,128)S(1)} %copy-done.13, bf16[512,2048]{1,0:T(8,128)(2,1)S(1)} %copy-done.11, f32[512]{0:T(512)S(1)} %multiply_multiply_fusion, f32[2048]{0:T(1024)S(1)} %copy-done.59, f32[512]{0:T(512)S(1)} %copy-done.62, bf16[256,2048]{1,0:T(8,128)(2,1)S(1)} %copy-done.24, ...), kind=kLoop, calls=%fused_computation.36 | loop fusion | flops 23068672 | bytes 20985856 | tf_op jit(solution)/shard_map/add | solution.py:441
  (322 shorter events, 106.6 us)
Async XLA Ops:
  7.2 94.8 %copy-start = (bf16[512,2048]{1,0:T(8,128)(2,1)S(1)}, bf16[512,2048]{1,0:T(8,128)(2,1)}, u32[]{:S(2)}) copy-start(bf16[512,2048]{1,0:T(8,128)(2,1)} %param.20) | copy-start | bytes 6291460
  7.2 8.4 %copy-start.50 = (bf16[2048,256]{1,0:T(8,128)(2,1)S(1)}, bf16[2048,256]{1,0:T(8,128)(2,1)}, u32[]{:S(2)}) copy-start(bf16[2048,256]{1,0:T(8,128)(2,1)} %param.18) | copy-start | bytes 3145732
  7.2 54.1 %all-gather.3.cloned.1.call-start = ((), (), s32[]{:S(2)}) async-start(), calls=%async_computation | async-start | bytes 4718592 | tf_op jit(solution)/shard_map/all_gather | solution.py:309
  7.3 8.3 %copy-start.6 = (bf16[512,2048]{1,0:T(8,128)(2,1)S(1)}, bf16[512,2048]{1,0:T(8,128)(2,1)}, u32[]{:S(2)}) copy-start(bf16[512,2048]{1,0:T(8,128)(2,1)} %param.13) | copy-start | bytes 6291460
  10.9 21.7 %copy-start.61 = (f32[512]{0:T(512)}, f32[512]{0:T(512)S(1)}, u32[]{:S(2)}) copy-start(f32[512]{0:T(512)S(1)} %fusion.60) | copy-start | bytes 6148
  11.6 21.0 %copy-start.58 = (f32[2048]{0:T(1024)}, f32[2048]{0:T(1024)S(1)}, u32[]{:S(2)}) copy-start(f32[2048]{0:T(1024)S(1)} %convert_element_type.216) | copy-start | bytes 24580
  18.9 22.3 %copy-start.26 = (f32[512,64]{1,0:T(8,128)}, f32[512,64]{1,0:T(8,128)S(1)}, u32[]{:S(2)}) copy-start(f32[512,64]{1,0:T(8,128)S(1)} %get-tuple-element.101) | copy-start | bytes 393220
  21.8 182.4 %all-reduce.6.cloned.1.call-start = ((), (), s32[]{:S(2)}) async-start(), calls=%async_computation.1 | async-start | bytes 2621440 | tf_op jit(solution)/shard_map/psum | solution.py:353
  43.9 35.5 %copy-start.2 = (bf16[64,8,4,128]{3,1,2,0:T(8,128)(2,1)}, bf16[64,8,4,128]{3,1,2,0:T(8,128)(2,1)S(1)}, u32[]{:S(2)}) copy-start(bf16[64,8,4,128]{3,1,2,0:T(8,128)(2,1)S(1)} %copy.90) | copy-start | bytes 1572868
  108.0 11.3 %collective-permute-start = (bf16[96,2048]{1,0:T(8,128)(2,1)S(1)}, bf16[96,2048]{1,0:T(8,128)(2,1)S(1)}, u32[]{:S(2)}, u32[]{:S(2)}) collective-permute-start(bf16[96,2048]{1,0:T(8,128)(2,1)S(1)} %dynamic-slice_convert_fusion.9), channel_id=1, source_target_pairs={{0,1},{1,0},{2,3},{3,2},{4,5},{5,4},{6,7},{7,6},{8,9},{9,8},{10,11... | collective-permute-start | bytes 1179656 | tf_op jit(solution)/shard_map/ppermute | solution.py:209
  120.6 11.4 %collective-permute-start.1 = (bf16[48,2048]{1,0:T(8,128)(2,1)S(1)}, bf16[48,2048]{1,0:T(8,128)(2,1)S(1)}, u32[]{:S(2)}, u32[]{:S(2)}) collective-permute-start(bf16[48,2048]{1,0:T(8,128)(2,1)S(1)} %dynamic-slice_convert_fusion.10), channel_id=1, source_target_pairs={{0,2},{1,3},{2,0},{3,1},{4,6},{5,7},{6,4},{7,5},{8,10},{9,11},{10,... | collective-permute-start | bytes 589832 | tf_op jit(solution)/shard_map/ppermute | solution.py:209
  132.0 11.1 %collective-permute-start.2 = (bf16[48,2048]{1,0:T(8,128)(2,1)S(1)}, bf16[48,2048]{1,0:T(8,128)(2,1)S(1)}, u32[]{:S(2)}, u32[]{:S(2)}) collective-permute-start(bf16[48,2048]{1,0:T(8,128)(2,1)S(1)} %add_convert_fusion.8), channel_id=1, source_target_pairs={{0,2},{1,3},{2,0},{3,1},{4,6},{5,7},{6,4},{7,5},{8,10},{9,11},{10,... | collective-permute-start | bytes 589832 | tf_op jit(solution)/shard_map/ppermute | solution.py:214
  135.1 447.6 %all-reduce.10.cloned.1.call-start = ((), (), s32[]{:S(2)}) async-start(), calls=%async_computation.3 | async-start | bytes 34603008 | tf_op jit(solution)/shard_map/psum | solution.py:367
  143.2 28.9 %collective-permute-start.3 = (bf16[96,2048]{1,0:T(8,128)(2,1)S(1)}, bf16[96,2048]{1,0:T(8,128)(2,1)}, u32[]{:S(2)}, u32[]{:S(2)}) collective-permute-start(bf16[96,2048]{1,0:T(8,128)(2,1)S(1)} %pad_maximum_fusion.9), channel_id=1, source_target_pairs={{0,1},{1,0},{2,3},{3,2},{4,5},{5,4},{6,7},{7,6},{8,9},{9,8},{10,11... | collective-permute-start | bytes 1179656 | tf_op jit(solution)/shard_map/ppermute | solution.py:214
  173.3 189.9 %copy-start.19 = (bf16[96,2048]{1,0:T(8,128)(2,1)}, bf16[96,2048]{1,0:T(8,128)(2,1)S(1)}, u32[]{:S(2)}) copy-start(bf16[96,2048]{1,0:T(8,128)(2,1)S(1)} %get-tuple-element.93) | copy-start | bytes 1179652
  173.3 189.9 %copy-start.21 = (bf16[96,2048]{1,0:T(8,128)(2,1)}, bf16[96,2048]{1,0:T(8,128)(2,1)S(1)}, u32[]{:S(2)}) copy-start(bf16[96,2048]{1,0:T(8,128)(2,1)S(1)} %get-tuple-element.94) | copy-start | bytes 1179652
  207.4 9.3 %slice-start.8 = ((s8[5767168]{0:T(1024)(128)(4,1)}), s8[4194304]{0:T(1024)(128)(4,1)S(1)}, s32[]{:S(2)}) async-start(s8[5767168]{0:T(1024)(128)(4,1)} %bitcast.101), calls=%async_computation.12 | async-start | bytes 8388608
  221.4 19.3 %copy-start.69 = (bf16[512,1408]{1,0:T(8,128)(2,1)}, bf16[512,1408]{1,0:T(8,128)(2,1)S(1)}, u32[]{:S(2)}) copy-start(bf16[512,1408]{1,0:T(8,128)(2,1)S(1)} %get-tuple-element.68) | copy-start | bytes 4325380
  224.9 10.9 %slice-start.10 = ((s8[5767168]{0:T(1024)(128)(4,1)}), s8[4194304]{0:T(1024)(128)(4,1)S(1)}, s32[]{:S(2)}) async-start(s8[5767168]{0:T(1024)(128)(4,1)} %bitcast.103), calls=%async_computation.14 | async-start | bytes 8388608
  245.9 34.1 %copy-start.5 = (s32[16]{0:T(128)S(1)}, s32[16]{0:T(128)}, u32[]{:S(2)}) copy-start(s32[16]{0:T(128)} %chunk_ref.1) | copy-start | bytes 196
  245.9 34.2 %copy-start.60 = (s32[1,1,16,256]{3,2,1,0:T(8,128)S(1)}, s32[1,1,16,256]{3,2,1,0:T(8,128)}, u32[]{:S(2)}) copy-start(s32[1,1,16,256]{3,2,1,0:T(8,128)} %get-tuple-element.104) | copy-start | bytes 49156
  248.7 25.4 %collective-permute-start.4 = (bf16[256,2048]{1,0:T(8,128)(2,1)}, bf16[256,2048]{1,0:T(8,128)(2,1)}, u32[]{:S(2)}, u32[]{:S(2)}) collective-permute-start(bf16[256,2048]{1,0:T(8,128)(2,1)} %dynamic-slice_convert_fusion.4), channel_id=1, source_target_pairs={{0,1},{1,0},{2,3},{3,2},{4,5},{5,4},{6,7},{7,6},{8,9},{9,8},{10,11... | collective-permute-start | bytes 3145736 | tf_op jit(solution)/shard_map/ppermute | solution.py:209
  278.4 24.9 %collective-permute-start.5 = (bf16[128,2048]{1,0:T(8,128)(2,1)}, bf16[128,2048]{1,0:T(8,128)(2,1)}, u32[]{:S(2)}, u32[]{:S(2)}) collective-permute-start(bf16[128,2048]{1,0:T(8,128)(2,1)} %dynamic-slice_convert_fusion.8), channel_id=1, source_target_pairs={{0,2},{1,3},{2,0},{3,1},{4,6},{5,7},{6,4},{7,5},{8,10},{9,11},{10,... | collective-permute-start | bytes 1572872 | tf_op jit(solution)/shard_map/ppermute | solution.py:209
  304.8 24.5 %collective-permute-start.6 = (bf16[128,2048]{1,0:T(8,128)(2,1)S(1)}, bf16[128,2048]{1,0:T(8,128)(2,1)S(1)}, u32[]{:S(2)}, u32[]{:S(2)}) collective-permute-start(bf16[128,2048]{1,0:T(8,128)(2,1)S(1)} %add_convert_fusion.4), channel_id=1, source_target_pairs={{0,2},{1,3},{2,0},{3,1},{4,6},{5,7},{6,4},{7,5},{8,10},{9,11},{10,... | collective-permute-start | bytes 1572872 | tf_op jit(solution)/shard_map/ppermute | solution.py:214
  331.3 25.4 %collective-permute-start.7 = (bf16[256,2048]{1,0:T(8,128)(2,1)}, bf16[256,2048]{1,0:T(8,128)(2,1)}, u32[]{:S(2)}, u32[]{:S(2)}) collective-permute-start(bf16[256,2048]{1,0:T(8,128)(2,1)} %pad_maximum_fusion.1), channel_id=1, source_target_pairs={{0,1},{1,0},{2,3},{3,2},{4,5},{5,4},{6,7},{7,6},{8,9},{9,8},{10,11... | collective-permute-start | bytes 3145736 | tf_op jit(solution)/shard_map/ppermute | solution.py:214
  336.2 420.8 %all-reduce.8.cloned.1.call-start = ((), (), s32[]{:S(2)}) async-start(), calls=%async_computation.2 | async-start | bytes 12582912 | tf_op jit(solution)/shard_map/psum | solution.py:367
  336.2 20.4 %copy-start.34 = (bf16[128,2048]{1,0:T(8,128)(2,1)S(1)}, bf16[128,2048]{1,0:T(8,128)(2,1)}, u32[]{:S(2)}) copy-start(bf16[128,2048]{1,0:T(8,128)(2,1)} %copy-done.33) | copy-start | bytes 1572868
  336.3 20.4 %copy-start.36 = (bf16[128,2048]{1,0:T(8,128)(2,1)S(1)}, bf16[128,2048]{1,0:T(8,128)(2,1)}, u32[]{:S(2)}) copy-start(bf16[128,2048]{1,0:T(8,128)(2,1)} %copy-done.35) | copy-start | bytes 1572868
  342.5 25.8 %copy-start.38 = (f32[512,2048]{1,0:T(8,128)}, f32[512,2048]{1,0:T(8,128)S(1)}, u32[]{:S(2)}) copy-start(f32[512,2048]{1,0:T(8,128)S(1)} %fusion.81) | copy-start | bytes 12582916
  369.3 76.1 %collective-permute-start.8 = (bf16[256,2048]{1,0:T(8,128)(2,1)S(1)}, bf16[256,2048]{1,0:T(8,128)(2,1)S(1)}, u32[]{:S(2)}, u32[]{:S(2)}) collective-permute-start(bf16[256,2048]{1,0:T(8,128)(2,1)S(1)} %dynamic-slice_convert_fusion.3), channel_id=1, source_target_pairs={{0,1},{1,0},{2,3},{3,2},{4,5},{5,4},{6,7},{7,6},{8,9},{9,8},{10,11... | collective-permute-start | bytes 3145736 | tf_op jit(solution)/shard_map/ppermute | solution.py:209
  445.4 8.5 %copy-start.52 = (bf16[512,128]{0,1:T(8,128)(2,1)S(1)}, bf16[512,128]{0,1:T(8,128)(2,1)}, u32[]{:S(2)}) copy-start(bf16[512,128]{0,1:T(8,128)(2,1)} %copy-done.51) | copy-start | bytes 393220
  445.4 8.5 %copy-start.54 = (bf16[512,128]{0,1:T(8,128)(2,1)S(1)}, bf16[512,128]{0,1:T(8,128)(2,1)}, u32[]{:S(2)}) copy-start(bf16[512,128]{0,1:T(8,128)(2,1)} %copy-done.53) | copy-start | bytes 393220
  445.4 31.8 %collective-permute-start.12 = (bf16[2048,512]{1,0:T(8,128)(2,1)}, bf16[2048,512]{1,0:T(8,128)(2,1)}, u32[]{:S(2)}, u32[]{:S(2)}) collective-permute-start(bf16[2048,512]{1,0:T(8,128)(2,1)} %dynamic-slice_convert_fusion), channel_id=1, source_target_pairs={{0,4},{4,0},{8,12},{12,8},{16,20},{20,16},{24,28},{28,24},{1,5},{5... | collective-permute-start | bytes 6291464 | tf_op jit(solution)/shard_map/ppermute | solution.py:242
  450.3 25.4 %collective-permute-start.9 = (bf16[128,2048]{1,0:T(8,128)(2,1)}, bf16[128,2048]{1,0:T(8,128)(2,1)}, u32[]{:S(2)}, u32[]{:S(2)}) collective-permute-start(bf16[128,2048]{1,0:T(8,128)(2,1)} %dynamic-slice_convert_fusion.7), channel_id=1, source_target_pairs={{0,2},{1,3},{2,0},{3,1},{4,6},{5,7},{6,4},{7,5},{8,10},{9,11},{10,... | collective-permute-start | bytes 1572872 | tf_op jit(solution)/shard_map/ppermute | solution.py:209
  453.9 23.3 %copy-start.29 = (f32[4096,512]{1,0:T(8,128)S(1)}, f32[4096,512]{1,0:T(8,128)}, u32[]{:S(2)}) copy-start(f32[4096,512]{1,0:T(8,128)} %copy-done.28) | copy-start | bytes 25165828
  477.1 25.6 %collective-permute-start.10 = (bf16[128,2048]{1,0:T(8,128)(2,1)S(1)}, bf16[128,2048]{1,0:T(8,128)(2,1)S(1)}, u32[]{:S(2)}, u32[]{:S(2)}) collective-permute-start(bf16[128,2048]{1,0:T(8,128)(2,1)S(1)} %add_convert_fusion.3), channel_id=1, source_target_pairs={{0,2},{1,3},{2,0},{3,1},{4,6},{5,7},{6,4},{7,5},{8,10},{9,11},{10,... | collective-permute-start | bytes 1572872 | tf_op jit(solution)/shard_map/ppermute | solution.py:214
  479.6 23.3 %copy-start.25 = (f32[512,4,128]{2,1,0:T(4,128)S(1)}, f32[512,4,128]{2,1,0:T(4,128)}, u32[]{:S(2)}) copy-start(f32[512,4,128]{2,1,0:T(4,128)} %reshape.288) | copy-start | bytes 3145732
  479.6 23.3 %copy-start.27 = (f32[512,64]{1,0:T(8,128)S(1)}, f32[512,64]{1,0:T(8,128)}, u32[]{:S(2)}) copy-start(f32[512,64]{1,0:T(8,128)} %copy-done.26) | copy-start | bytes 393220
  479.6 23.3 %copy-start.40 = (f32[512,64]{1,0:T(8,128)S(1)}, f32[512,64]{1,0:T(8,128)}, u32[]{:S(2)}) copy-start(f32[512,64]{1,0:T(8,128)} %get-tuple-element.99) | copy-start | bytes 393220
  479.8 44.2 %collective-permute-start.13 = (bf16[1024,512]{1,0:T(8,128)(2,1)S(1)}, bf16[1024,512]{1,0:T(8,128)(2,1)S(1)}, u32[]{:S(2)}, u32[]{:S(2)}) collective-permute-start(bf16[1024,512]{1,0:T(8,128)(2,1)S(1)} %dynamic-slice_convert_fusion.2), channel_id=1, source_target_pairs={{0,8},{4,12},{8,0},{12,4},{16,24},{20,28},{24,16},{28,20},{1,9},{5... | collective-permute-start | bytes 3145736 | tf_op jit(solution)/shard_map/ppermute | solution.py:242
  502.9 24.9 %collective-permute-start.11 = (bf16[256,2048]{1,0:T(8,128)(2,1)S(1)}, bf16[256,2048]{1,0:T(8,128)(2,1)S(1)}, u32[]{:S(2)}, u32[]{:S(2)}) collective-permute-start(bf16[256,2048]{1,0:T(8,128)(2,1)S(1)} %pad_maximum_fusion.2), channel_id=1, source_target_pairs={{0,1},{1,0},{2,3},{3,2},{4,5},{5,4},{6,7},{7,6},{8,9},{9,8},{10,11... | collective-permute-start | bytes 3145736 | tf_op jit(solution)/shard_map/ppermute | solution.py:214
  524.4 22.8 %collective-permute-start.14 = (bf16[512,512]{1,0:T(8,128)(2,1)S(1)}, bf16[512,512]{1,0:T(8,128)(2,1)S(1)}, u32[]{:S(2)}, u32[]{:S(2)}) collective-permute-start(bf16[512,512]{1,0:T(8,128)(2,1)S(1)} %dynamic-slice_convert_fusion.6), channel_id=1, source_target_pairs={{0,16},{4,20},{8,24},{12,28},{16,0},{20,4},{24,8},{28,12},{1,17},{... | collective-permute-start | bytes 1572872 | tf_op jit(solution)/shard_map/ppermute | solution.py:242
  603.1 24.8 %collective-permute-start.15 = (bf16[256,2048]{1,0:T(8,128)(2,1)S(1)}, bf16[256,2048]{1,0:T(8,128)(2,1)S(1)}, u32[]{:S(2)}, u32[]{:S(2)}) collective-permute-start(bf16[256,2048]{1,0:T(8,128)(2,1)S(1)} %dynamic-slice_convert_fusion.1), channel_id=1, source_target_pairs={{0,1},{1,0},{2,3},{3,2},{4,5},{5,4},{6,7},{7,6},{8,9},{9,8},{10,11... | collective-permute-start | bytes 3145736 | tf_op jit(solution)/shard_map/ppermute | solution.py:209
  628.2 24.8 %collective-permute-start.16 = (bf16[128,2048]{1,0:T(8,128)(2,1)S(1)}, bf16[128,2048]{1,0:T(8,128)(2,1)S(1)}, u32[]{:S(2)}, u32[]{:S(2)}) collective-permute-start(bf16[128,2048]{1,0:T(8,128)(2,1)S(1)} %dynamic-slice_convert_fusion.5), channel_id=1, source_target_pairs={{0,2},{1,3},{2,0},{3,1},{4,6},{5,7},{6,4},{7,5},{8,10},{9,11},{10,... | collective-permute-start | bytes 1572872 | tf_op jit(solution)/shard_map/ppermute | solution.py:209
  653.2 24.8 %collective-permute-start.17 = (bf16[128,2048]{1,0:T(8,128)(2,1)S(1)}, bf16[128,2048]{1,0:T(8,128)(2,1)S(1)}, u32[]{:S(2)}, u32[]{:S(2)}) collective-permute-start(bf16[128,2048]{1,0:T(8,128)(2,1)S(1)} %add_convert_fusion.1), channel_id=1, source_target_pairs={{0,2},{1,3},{2,0},{3,1},{4,6},{5,7},{6,4},{7,5},{8,10},{9,11},{10,... | collective-permute-start | bytes 1572872 | tf_op jit(solution)/shard_map/ppermute | solution.py:214
  653.3 50.4 %copy-start.10 = (bf16[512,2048]{1,0:T(8,128)(2,1)S(1)}, bf16[512,2048]{1,0:T(8,128)(2,1)}, u32[]{:S(2)}) copy-start(bf16[512,2048]{1,0:T(8,128)(2,1)} %param.13) | copy-start | bytes 6291460
  678.0 28.0 %slice-start.6 = ((s8[5767168]{0:T(1024)(128)(4,1)}), s8[4194304]{0:T(1024)(128)(4,1)S(1)}, s32[]{:S(2)}) async-start(s8[5767168]{0:T(1024)(128)(4,1)} %bitcast.74), calls=%async_computation.10 | async-start | bytes 8388608
  678.1 25.1 %collective-permute-start.18 = (bf16[256,2048]{1,0:T(8,128)(2,1)S(1)}, bf16[256,2048]{1,0:T(8,128)(2,1)S(1)}, u32[]{:S(2)}, u32[]{:S(2)}) collective-permute-start(bf16[256,2048]{1,0:T(8,128)(2,1)S(1)} %pad_maximum_fusion.4), channel_id=1, source_target_pairs={{0,1},{1,0},{2,3},{3,2},{4,5},{5,4},{6,7},{7,6},{8,9},{9,8},{10,11... | collective-permute-start | bytes 3145736 | tf_op jit(solution)/shard_map/ppermute | solution.py:214
  678.2 1.2 collective-permute-start.22
  679.4 4.0 collective-permute-start.23
  683.4 22.6 %slice-start.7 = ((s8[5767168]{0:T(1024)(128)(4,1)}), s8[1572864]{0:T(1024)(128)(4,1)S(1)}, s32[]{:S(2)}) async-start(s8[5767168]{0:T(1024)(128)(4,1)} %bitcast.74), calls=%async_computation.11 | async-start | bytes 3145728
  683.4 22.0 %collective-permute-start.24 = (f32[2048]{0:T(1024)S(1)}, f32[2048]{0:T(1024)S(1)}, u32[]{:S(2)}, u32[]{:S(2)}) collective-permute-start(f32[2048]{0:T(1024)S(1)} %add.348), channel_id=1, source_target_pairs={{0,16},{4,20},{8,24},{12,28},{16,0},{20,4},{24,8},{28,12},{1,17},{... | collective-permute-start | bytes 24584 | tf_op jit(solution)/shard_map/ppermute | solution.py:251
  703.7 8.5 %slice-start.4 = ((s8[5767168]{0:T(1024)(128)(4,1)}), s8[4194304]{0:T(1024)(128)(4,1)S(1)}, s32[]{:S(2)}) async-start(s8[5767168]{0:T(1024)(128)(4,1)} %bitcast.72), calls=%async_computation.8 | async-start | bytes 8388608
  705.3 61.8 %collective-permute-start.19 = (f32[2048]{0:T(1024)S(1)}, f32[2048]{0:T(1024)S(1)}, u32[]{:S(2)}, u32[]{:S(2)}) collective-permute-start(f32[2048]{0:T(1024)S(1)} %get-tuple-element.55), channel_id=1, source_target_pairs={{0,4},{4,0},{8,12},{12,8},{16,20},{20,16},{24,28},{28,24},{1,5},{5... | collective-permute-start | bytes 24584 | tf_op jit(solution)/shard_map/ppermute | solution.py:251
  706.0 11.3 %slice-start.2 = ((s8[5767168]{0:T(1024)(128)(4,1)}), s8[4194304]{0:T(1024)(128)(4,1)S(1)}, s32[]{:S(2)}) async-start(s8[5767168]{0:T(1024)(128)(4,1)} %bitcast.70), calls=%async_computation.6 | async-start | bytes 8388608
  757.0 15.0 %copy-start.24 = (bf16[256,2048]{1,0:T(8,128)(2,1)S(1)}, bf16[256,2048]{1,0:T(8,128)(2,1)}, u32[]{:S(2)}) copy-start(bf16[256,2048]{1,0:T(8,128)(2,1)} %copy-done.23) | copy-start | bytes 3145732
  761.4 10.6 %copy-start.17 = (f32[512,2048]{1,0:T(8,128)S(1)}, f32[512,2048]{1,0:T(8,128)}, u32[]{:S(2)}) copy-start(f32[512,2048]{1,0:T(8,128)} %maximum_convert_fusion.1) | copy-start | bytes 12582916
  762.9 9.2 %copy-start.11 = (bf16[512,2048]{1,0:T(8,128)(2,1)S(1)}, bf16[512,2048]{1,0:T(8,128)(2,1)}, u32[]{:S(2)}) copy-start(bf16[512,2048]{1,0:T(8,128)(2,1)} %param.13) | copy-start | bytes 6291460
  762.9 9.2 %copy-start.13 = (f32[512,2048]{1,0:T(8,128)S(1)}, f32[512,2048]{1,0:T(8,128)}, u32[]{:S(2)}) copy-start(f32[512,2048]{1,0:T(8,128)} %copy-done.12) | copy-start | bytes 12582916
  762.9 9.2 %copy-start.16 = (bf16[320,2048]{1,0:T(8,128)(2,1)S(1)}, bf16[320,2048]{1,0:T(8,128)(2,1)}, u32[]{:S(2)}) copy-start(bf16[320,2048]{1,0:T(8,128)(2,1)} %all-reduce.6.cloned.1.call-done) | copy-start | bytes 3932164
  762.9 9.2 %copy-start.20 = (bf16[96,2048]{1,0:T(8,128)(2,1)S(1)}, bf16[96,2048]{1,0:T(8,128)(2,1)}, u32[]{:S(2)}) copy-start(bf16[96,2048]{1,0:T(8,128)(2,1)} %copy-done.19) | copy-start | bytes 1179652
  762.9 9.2 %copy-start.22 = (bf16[96,2048]{1,0:T(8,128)(2,1)S(1)}, bf16[96,2048]{1,0:T(8,128)(2,1)}, u32[]{:S(2)}) copy-start(bf16[96,2048]{1,0:T(8,128)(2,1)} %copy-done.21) | copy-start | bytes 1179652
  767.1 3.7 collective-permute-start.20
  770.7 9.5 %collective-permute-start.21 = (f32[2048]{0:T(1024)S(1)}, f32[2048]{0:T(1024)S(1)}, u32[]{:S(2)}, u32[]{:S(2)}) collective-permute-start(f32[2048]{0:T(1024)S(1)} %add.345), channel_id=1, source_target_pairs={{0,16},{4,20},{8,24},{12,28},{16,0},{20,4},{24,8},{28,12},{1,17},{... | collective-permute-start | bytes 24584 | tf_op jit(solution)/shard_map/ppermute | solution.py:251
  (47 other events, 168.4 us)
Sparse Core Ops, SparseCore 0:
  22.0 39.3 all-gather.2
  135.2 68.9 all-reduce.5
  336.3 246.3 all-reduce.9
  653.4 103.5 all-reduce.7

commit v7 on v6

--- a/solution.py
+++ b/solution.py
@@ -135,8 +135,11 @@
 
 
 def attention_backward(query_low, all_kv, d_attended, lse, chunk_blocks, query_blocks,
-                       query_pos, own_ids, key_pos, key_alive, *, local_groups, chunk):
+                       query_pos, own_ids, key_pos, key_alive, *, local_groups, chunk,
+                       first_group=0, groups=None):
     rows, length, heads = _common(query_low, all_kv, local_groups)
+    groups = local_groups if groups is None else groups
+    at = first_group
     halves = 2
     chunks = length // chunk
     kernel = functools.partial(
@@ -146,13 +149,13 @@
     group_cols = heads * HEAD_DIM
     grid_spec = pltpu.PrefetchScalarGridSpec(
         num_scalar_prefetch=2,
-        grid=(local_groups,),
+        grid=(groups,),
         in_specs=[
-            pl.BlockSpec((rows, group_cols), lambda g, *_: (0, g)),
-            pl.BlockSpec((length, HEAD_DIM), lambda g, *_: (0, g)),
-            pl.BlockSpec((length, HEAD_DIM), lambda g, *_: (0, local_groups + g)),
-            pl.BlockSpec((rows, group_cols), lambda g, *_: (0, g)),
-            pl.BlockSpec((heads, rows, 1), lambda g, *_: (g, 0, 0)),
+            pl.BlockSpec((rows, group_cols), lambda g, *_: (0, at + g)),
+            pl.BlockSpec((length, HEAD_DIM), lambda g, *_: (0, at + g)),
+            pl.BlockSpec((length, HEAD_DIM), lambda g, *_: (0, local_groups + at + g)),
+            pl.BlockSpec((rows, group_cols), lambda g, *_: (0, at + g)),
+            pl.BlockSpec((heads, rows, 1), lambda g, *_: (at + g, 0, 0)),
             pl.BlockSpec((rows, 1), lambda g, *_: (0, 0)),
             pl.BlockSpec((rows, 1), lambda g, *_: (0, 0)),
             pl.BlockSpec((1, length), lambda g, *_: (0, 0)),
@@ -168,20 +171,20 @@
             pltpu.VMEM((rows // halves, HEAD_DIM), jnp.float32),
         ],
     )
-    flops = 10 * rows * length * HEAD_DIM * heads * local_groups
-    kv_width = local_groups * HEAD_DIM
+    flops = 10 * rows * length * HEAD_DIM * heads * groups
+    kv_width = groups * HEAD_DIM
     return pl.pallas_call(
         kernel,
         grid_spec=grid_spec,
         out_shape=[
-            jax.ShapeDtypeStruct((rows, heads * local_groups * HEAD_DIM), jnp.float32),
+            jax.ShapeDtypeStruct((rows, heads * groups * HEAD_DIM), jnp.float32),
             jax.ShapeDtypeStruct((length, kv_width), jnp.float32),
             jax.ShapeDtypeStruct((length, kv_width), jnp.float32),
         ],
         compiler_params=pltpu.CompilerParams(vmem_limit_bytes=48 * 1024 * 1024),
         cost_estimate=pl.CostEstimate(
-            flops=flops, transcendentals=2 * rows * length * heads * local_groups,
-            bytes_accessed=2 * length * 4 * HEAD_DIM * local_groups * 3,
+            flops=flops, transcendentals=2 * rows * length * heads * groups,
+            bytes_accessed=2 * length * 4 * HEAD_DIM * groups * 3,
         ),
     )(chunk_blocks, query_blocks, query_low, all_kv, all_kv, d_attended, lse, query_pos,
       own_ids, key_pos, key_alive)
@@ -391,10 +394,17 @@
         (grad_w_gate, grad_w_up, grad_w_down, grad_w_out)
     )
     d_attended = right_trans(d_branch, w_out).astype(jnp.bfloat16)
-    d_queries, d_key_all, d_value_all = attention_backward(
-        query_low, all_kv, d_attended, lse, local_groups=local_groups, chunk=half_rows,
-        **mask_args,
-    )
+    group_grads = []
+    for group_index in range(local_groups):
+        group_grads.append(
+            attention_backward(
+                query_low, all_kv, d_attended, lse, local_groups=local_groups,
+                chunk=half_rows, first_group=group_index, groups=1, **mask_args,
+            )
+        )
+    d_queries, d_key_all, d_value_all = [
+        jnp.concatenate(parts, axis=1) for parts in zip(*group_grads)
+    ]
     d_kv_own = permute_scatter(jnp.concatenate([d_key_all, d_value_all], axis=1), "dp")
     d_kv_own, grad_w_out = lax.optimization_barrier((d_kv_own, grad_w_out))
     d_key_own = d_kv_own[:, :kv_width]

time: 793 us -> 793 us (level)
    pallas_call x1 -> x2, Pallas kernels: 68.5 us -> 71.2 us  [attention_backward(): pl.pallas_call(kernel, grid_spec=grid_spec, out_shape=[jax.ShapeDtypeStru...]
    unnamed x182 -> x198, local copies, waits for them, and re-layouts: 20.2 us -> 20.5 us
  transfers between devices with their start and end apart: 29 -> 29, of which waited for: 24 -> 23; matrix products, arithmetic and copies ran while one was open for 14% -> 14% of each run, Pallas kernels for 9% -> 9%
where the time goes in v7:
time: 793 us; the launch traced here: 788 us
  waiting for transfers between devices  413 us (52%)
  matrix products  114 us (14%)
  other arithmetic  98.4 us (12%)
  Pallas kernels  71.2 us (9%)
  local copies, waits for them, and re-layouts  38.4 us (5%)
  starting transfers between devices  25.7 us (3%)
  between operations  15.6 us (2%)
  blocking collectives  10.6 us (1%)
    ppermute x8, waiting for transfers between devices, permute_sum(): got = lax.ppermute(pieces, axis, partner_perm(size, 1 << step))  130 us
    ppermute x8, waiting for transfers between devices, permute_sum(): got = lax.ppermute(send, axis, partner_perm(size, 1 << step))  126 us
    pallas_call x2, Pallas kernels, attention_backward(): pl.pallas_call(kernel, grid_spec=grid_spec, out_shape=[jax.ShapeDtypeStru...  71.2 us
    psum x2, waiting for transfers between devices, dp_sum(): return [lax.psum(grad.astype(jnp.bfloat16), 'dp') for grad in grads]  67.5 us
    dot_general x11, matrix products, right_trans(): lax.dot_general(left, right, (((1,), (1,)), ((), ())), preferred_element_...  46.5 us
    ppermute x3, waiting for transfers between devices, permute_scatter(): got = lax.ppermute(send, axis, partner_perm(size, 1 << step))  36.5 us
    dot_general x7, matrix products, left_trans(): lax.dot_general(left, right, (((0,), (0,)), ((), ())), preferred_element_...  31.2 us
    psum x1, waiting for transfers between devices, on_device(): branch_top = lax.psum(branch_part[:sc_rows].astype(jnp.bfloat16), 'tensor')  31 us
  transfers between devices with their start and end apart: 29, of which 23 were waited for; matrix products, arithmetic and copies ran while one was open for 14% of the time, Pallas kernels for 9%

profile of v7, /device:TPU:0, one launch (start us, length us, event | category | flops | bytes accessed | tf_op | source)
XLA Modules:
  0.0 787.6 jit_solution(11746541016405875947)
XLA Ops:
  12.4 3.3 convolution_convert_fusion.1
  22.0 10.6 %all-gather = bf16[8,1,512]{2,1,0:T(2,128)(2,1)S(1)} all-gather(bf16[1,1,512]{2,1,0:T(2,128)(2,1)S(1)} %reshape.291), channel_id=1, replica_groups=mesh['dp'=8,'tensor'=4] {'dp'}, dimensions={0}, use_global_device_ids=true | all-gather | bytes 9216 | tf_op jit(solution)/shard_map/all_gather | solution.py:315
  32.7 3.7 fusion.70
  43.9 17.5 %all-gather.3.cloned.1.call-done.k_ref.v_ref = bf16[4096,512]{1,0:T(8,128)(2,1)} async-done(((bf16[512,512]{1,0:T(8,128)(2,1)}), bf16[4096,512]{1,0:T(8,128)(2,1)}) %all-gather.3.cloned.1.call-update) | async-done | bytes 4194320 | tf_op jit(solution)/shard_map/all_gather | solution.py:312
  61.4 4.6 fusion.76
  67.2 4.6 fusion.77
  73.5 4.6 fusion.78
  79.4 6.9 fusion.79
  86.3 4.6 fusion.2
  90.9 3.2 fusion.22
  94.2 3.4 fusion.23
  108.3 9.8 %collective-permute-done = bf16[96,2048]{1,0:T(8,128)(2,1)S(1)} collective-permute-done((bf16[96,2048]{1,0:T(8,128)(2,1)S(1)}, bf16[96,2048]{1,0:T(8,128)(2,1)S(1)}, u32[]{:S(2)}, u32[]{:S(2)}) %collective-permute-start) | collective-permute-done | bytes 393248 | tf_op jit(solution)/shard_map/ppermute | solution.py:212
  119.3 2.5 collective-permute-start.1
  121.8 8.9 %collective-permute-done.1 = bf16[48,2048]{1,0:T(8,128)(2,1)S(1)} collective-permute-done((bf16[48,2048]{1,0:T(8,128)(2,1)S(1)}, bf16[48,2048]{1,0:T(8,128)(2,1)S(1)}, u32[]{:S(2)}, u32[]{:S(2)}) %collective-permute-start.1) | collective-permute-done | bytes 196640 | tf_op jit(solution)/shard_map/ppermute | solution.py:212
  130.8 3.0 slice.195
  134.1 7.8 collective-permute-done.2
  142.0 8.3 %fusion.36 = f32[512,1408]{1,0:T(8,128)} fusion(bf16[1408,2048]{1,0:T(8,128)(2,1)} %param.24, bf16[512,2048]{1,0:T(8,128)(2,1)} %param.25, f32[512]{0:T(512)S(1)} %get-tuple-element.108), kind=kOutput, calls=%fused_computation.118 | convolution fusion | flops 2955935744 | bytes 10749952 | tf_op jit(solution)/shard_map/dot_general | solution.py:49
  150.3 20.5 %collective-permute-done.3 = bf16[96,2048]{1,0:T(8,128)(2,1)} collective-permute-done((bf16[96,2048]{1,0:T(8,128)(2,1)S(1)}, bf16[96,2048]{1,0:T(8,128)(2,1)}, u32[]{:S(2)}, u32[]{:S(2)}) %collective-permute-start.3) | collective-permute-done | bytes 393248 | tf_op jit(solution)/shard_map/ppermute | solution.py:217
  172.0 31.0 %all-reduce.6.cloned.1.call-done = bf16[320,2048]{1,0:T(8,128)(2,1)} async-done(((bf16[320,2048]{1,0:T(8,128)(2,1)}), bf16[320,2048]{1,0:T(8,128)(2,1)}) %all-reduce.6.cloned.1.call-update) | async-done | bytes 1310736 | tf_op jit(solution)/shard_map/psum | solution.py:356
  203.0 3.1 multiply_reduce_fusion.2
  206.1 3.3 multiply_convert_fusion.1
  209.4 5.9 fusion.80
  215.4 4.7 multiply_convert_fusion.2
  220.1 3.4 fusion.84
  223.6 5.3 fusion.82
  228.9 5.7 fusion.83
  234.6 5.0 convolution_add_fusion
  239.6 5.2 fusion.34
  248.1 23.7 %collective-permute-done.4 = bf16[256,2048]{1,0:T(8,128)(2,1)} collective-permute-done((bf16[256,2048]{1,0:T(8,128)(2,1)S(1)}, bf16[256,2048]{1,0:T(8,128)(2,1)}, u32[]{:S(2)}, u32[]{:S(2)}) %collective-permute-start.4) | collective-permute-done | bytes 1048608 | tf_op jit(solution)/shard_map/ppermute | solution.py:212
  278.1 22.0 %collective-permute-done.5 = bf16[128,2048]{1,0:T(8,128)(2,1)S(1)} collective-permute-done((bf16[128,2048]{1,0:T(8,128)(2,1)S(1)}, bf16[128,2048]{1,0:T(8,128)(2,1)S(1)}, u32[]{:S(2)}, u32[]{:S(2)}) %collective-permute-start.5) | collective-permute-done | bytes 524320 | tf_op jit(solution)/shard_map/ppermute | solution.py:212
  301.5 24.4 %collective-permute-done.6 = bf16[128,2048]{1,0:T(8,128)(2,1)S(1)} collective-permute-done((bf16[128,2048]{1,0:T(8,128)(2,1)S(1)}, bf16[128,2048]{1,0:T(8,128)(2,1)S(1)}, u32[]{:S(2)}, u32[]{:S(2)}) %collective-permute-start.6) | collective-permute-done | bytes 524320 | tf_op jit(solution)/shard_map/ppermute | solution.py:217
  332.7 5.9 fusion.81
  338.6 14.6 %collective-permute-done.7 = bf16[256,2048]{1,0:T(8,128)(2,1)} collective-permute-done((bf16[256,2048]{1,0:T(8,128)(2,1)}, bf16[256,2048]{1,0:T(8,128)(2,1)}, u32[]{:S(2)}, u32[]{:S(2)}) %collective-permute-start.7) | collective-permute-done | bytes 1048608 | tf_op jit(solution)/shard_map/ppermute | solution.py:217
  357.3 2.8 multiply_reduce_fusion
  360.1 3.8 convert_add_fusion.1
  366.7 35.6 %shard_map.212 = (f32[512,256]{1,0:T(8,128)S(1)}, f32[4096,128]{1,0:T(8,128)S(1)}, f32[4096,128]{1,0:T(8,128)}) custom-call(s32[16]{0:T(128)S(1)} %copy-done.8, s32[2]{0:T(128)S(1)} %dynamic_slice.85.qblock_ref, bf16[512,512]{1,0:T(8,128)(2,1)S(1)} %bitcast.65, bf16[4096,512]{1,0:T(8,128)(2,1)} %all-gather.3.cloned.1.call-done.k_ref.v_ref, ...), custom_call_target="tpu_custom_call" | custom-call | flops 5368709120 | bytes 12582912 | tf_op jit(solution)/shard_map/pallas_call | solution.py:176
  402.6 35.6 %shard_map.213 = (f32[512,256]{1,0:T(8,128)S(1)}, f32[4096,128]{1,0:T(8,128)S(1)}, f32[4096,128]{1,0:T(8,128)}) custom-call(s32[16]{0:T(128)S(1)} %copy-done.8, s32[2]{0:T(128)S(1)} %dynamic_slice.85.qblock_ref, bf16[512,512]{1,0:T(8,128)(2,1)S(1)} %bitcast.66, bf16[4096,512]{1,0:T(8,128)(2,1)} %all-gather.3.cloned.1.call-done.k_ref.v_ref, ...), custom_call_target="tpu_custom_call" | custom-call | flops 5368709120 | bytes 12582912 | tf_op jit(solution)/shard_map/pallas_call | solution.py:176
  443.3 3.0 copy-done.43
  449.8 2.7 collective-permute-start.9
  455.3 5.1 fusion.55
  460.4 14.9 %collective-permute-done.9 = bf16[128,2048]{1,0:T(8,128)(2,1)} collective-permute-done((bf16[128,2048]{1,0:T(8,128)(2,1)}, bf16[128,2048]{1,0:T(8,128)(2,1)}, u32[]{:S(2)}, u32[]{:S(2)}) %collective-permute-start.9) | collective-permute-done | bytes 524320 | tf_op jit(solution)/shard_map/ppermute | solution.py:212
  476.9 2.4 convert_add_fusion.2
  481.7 20.2 %collective-permute-done.10 = bf16[128,2048]{1,0:T(8,128)(2,1)S(1)} collective-permute-done((bf16[128,2048]{1,0:T(8,128)(2,1)S(1)}, bf16[128,2048]{1,0:T(8,128)(2,1)S(1)}, u32[]{:S(2)}, u32[]{:S(2)}) %collective-permute-start.10) | collective-permute-done | bytes 524320 | tf_op jit(solution)/shard_map/ppermute | solution.py:217
  503.9 2.8 fusion.38
  506.7 18.5 %collective-permute-done.13 = bf16[1024,512]{1,0:T(8,128)(2,1)S(1)} collective-permute-done((bf16[1024,512]{1,0:T(8,128)(2,1)S(1)}, bf16[1024,512]{1,0:T(8,128)(2,1)S(1)}, u32[]{:S(2)}, u32[]{:S(2)}) %collective-permute-start.13) | collective-permute-done | bytes 1048608 | tf_op jit(solution)/shard_map/ppermute | solution.py:245
  527.8 2.5 maximum_convert_fusion.1
  530.4 18.0 %collective-permute-done.14 = bf16[512,512]{1,0:T(8,128)(2,1)S(1)} collective-permute-done((bf16[512,512]{1,0:T(8,128)(2,1)S(1)}, bf16[512,512]{1,0:T(8,128)(2,1)S(1)}, u32[]{:S(2)}, u32[]{:S(2)}) %collective-permute-start.14) | collective-permute-done | bytes 524320 | tf_op jit(solution)/shard_map/ppermute | solution.py:245
  548.6 32.5 %all-reduce.10.cloned.1.call-done = (bf16[2048,1408]{1,0:T(8,128)(2,1)}, bf16[2048,1408]{1,0:T(8,128)(2,1)}, bf16[1408,2048]{1,0:T(8,128)(2,1)}) async-done(((bf16[2048,1408]{1,0:T(8,128)(2,1)}, bf16[2048,1408]{1,0:T(8,128)(2,1)}, bf16[1408,2048]{1,0:T(8,128)(2,1)}), (bf16[2048,1408]{1,0:T(8,128)(2,1)}, bf16[2048,1408]{1,0:T(8,128)(2,1)}, bf16[1408,2048]{1,0:T(8,128)(2,1)})) %all-reduce.10.cloned.1.call-update) | async-done | bytes 17301520 | tf_op jit(solution)/shard_map/psum | solution.py:370
  581.8 3.5 fusion.54
  585.4 2.8 fusion.53
  592.1 3.6 fusion.43
  598.4 3.0 add_add_fusion.2
  601.5 3.1 collective-permute-start.15
  604.5 22.8 %collective-permute-done.15 = bf16[256,2048]{1,0:T(8,128)(2,1)S(1)} collective-permute-done((bf16[256,2048]{1,0:T(8,128)(2,1)S(1)}, bf16[256,2048]{1,0:T(8,128)(2,1)S(1)}, u32[]{:S(2)}, u32[]{:S(2)}) %collective-permute-start.15) | collective-permute-done | bytes 1048608 | tf_op jit(solution)/shard_map/ppermute | solution.py:212
  628.8 23.7 %collective-permute-done.16 = bf16[128,2048]{1,0:T(8,128)(2,1)S(1)} collective-permute-done((bf16[128,2048]{1,0:T(8,128)(2,1)S(1)}, bf16[128,2048]{1,0:T(8,128)(2,1)S(1)}, u32[]{:S(2)}, u32[]{:S(2)}) %collective-permute-start.16) | collective-permute-done | bytes 524320 | tf_op jit(solution)/shard_map/ppermute | solution.py:212
  652.8 23.8 %collective-permute-done.17 = bf16[128,2048]{1,0:T(8,128)(2,1)S(1)} collective-permute-done((bf16[128,2048]{1,0:T(8,128)(2,1)S(1)}, bf16[128,2048]{1,0:T(8,128)(2,1)S(1)}, u32[]{:S(2)}, u32[]{:S(2)}) %collective-permute-start.17) | collective-permute-done | bytes 524320 | tf_op jit(solution)/shard_map/ppermute | solution.py:217
  683.5 18.5 %collective-permute-done.18 = bf16[256,2048]{1,0:T(8,128)(2,1)S(1)} collective-permute-done((bf16[256,2048]{1,0:T(8,128)(2,1)S(1)}, bf16[256,2048]{1,0:T(8,128)(2,1)S(1)}, u32[]{:S(2)}, u32[]{:S(2)}) %collective-permute-start.18) | collective-permute-done | bytes 1048608 | tf_op jit(solution)/shard_map/ppermute | solution.py:217
  704.8 5.9 convert_element_type.278
  710.7 5.2 convert_element_type.279
  715.9 6.0 convert_element_type.280
  721.9 35.1 %all-reduce.8.cloned.1.call-done = (bf16[2048,512]{1,0:T(8,128)(2,1)}, bf16[2048,256]{1,0:T(8,128)(2,1)}, bf16[2048,256]{1,0:T(8,128)(2,1)}, bf16[512,2048]{1,0:T(8,128)(2,1)}) async-done(((bf16[2048,512]{1,0:T(8,128)(2,1)}, bf16[2048,256]{1,0:T(8,128)(2,1)}, bf16[2048,256]{1,0:T(8,128)(2,1)}, bf16[512,2048]{1,0:T(8,128)(2,1)}), (bf16[2048,512]{1,0:T(8,128)(2,1)}, bf16[2048,256]{1,0:T(8,128)(2,1)}, ...) | async-done | bytes 6291472 | tf_op jit(solution)/shard_map/psum | solution.py:370
  757.0 4.3 convert_element_type.271
  764.3 2.7 convert_element_type.277
  772.0 8.2 %fusion.11 = (f32[512,2048]{1,0:T(8,128)}, bf16[512,2048]{1,0:T(8,128)(2,1)}) fusion(f32[512,2048]{1,0:T(8,128)S(1)} %copy-done.16, bf16[512,2048]{1,0:T(8,128)(2,1)S(1)} %copy-done.14, f32[512]{0:T(512)S(1)} %multiply_multiply_fusion, f32[2048]{0:T(1024)S(1)} %copy-done.66, f32[512]{0:T(512)S(1)} %copy-done.69, bf16[256,2048]{1,0:T(8,128)(2,1)S(1)} %copy-done.30, ...), kind=kLoop, calls=%fused_computation.36 | loop fusion | flops 23068672 | bytes 20985856 | tf_op jit(solution)/shard_map/add | solution.py:451
  (340 shorter events, 108.5 us)
Async XLA Ops:
  7.2 94.8 %copy-start = (bf16[512,2048]{1,0:T(8,128)(2,1)S(1)}, bf16[512,2048]{1,0:T(8,128)(2,1)}, u32[]{:S(2)}) copy-start(bf16[512,2048]{1,0:T(8,128)(2,1)} %param.20) | copy-start | bytes 6291460
  7.2 54.2 %all-gather.3.cloned.1.call-start = ((), (), s32[]{:S(2)}) async-start(), calls=%async_computation | async-start | bytes 4718592 | tf_op jit(solution)/shard_map/all_gather | solution.py:312
  11.0 21.7 %copy-start.68 = (f32[512]{0:T(512)}, f32[512]{0:T(512)S(1)}, u32[]{:S(2)}) copy-start(f32[512]{0:T(512)S(1)} %fusion.60) | copy-start | bytes 6148
  11.7 21.0 %copy-start.65 = (f32[2048]{0:T(1024)}, f32[2048]{0:T(1024)S(1)}, u32[]{:S(2)}) copy-start(f32[2048]{0:T(1024)S(1)} %convert_element_type.216) | copy-start | bytes 24580
  19.0 22.3 %copy-start.31 = (f32[512,64]{1,0:T(8,128)}, f32[512,64]{1,0:T(8,128)S(1)}, u32[]{:S(2)}) copy-start(f32[512,64]{1,0:T(8,128)S(1)} %get-tuple-element.107) | copy-start | bytes 393220
  21.9 181.1 %all-reduce.6.cloned.1.call-start = ((), (), s32[]{:S(2)}) async-start(), calls=%async_computation.1 | async-start | bytes 2621440 | tf_op jit(solution)/shard_map/psum | solution.py:356
  43.9 35.5 %copy-start.1 = (bf16[64,8,4,128]{3,1,2,0:T(8,128)(2,1)}, bf16[64,8,4,128]{3,1,2,0:T(8,128)(2,1)S(1)}, u32[]{:S(2)}) copy-start(bf16[64,8,4,128]{3,1,2,0:T(8,128)(2,1)S(1)} %copy.94) | copy-start | bytes 1572868
  106.7 11.3 %collective-permute-start = (bf16[96,2048]{1,0:T(8,128)(2,1)S(1)}, bf16[96,2048]{1,0:T(8,128)(2,1)S(1)}, u32[]{:S(2)}, u32[]{:S(2)}) collective-permute-start(bf16[96,2048]{1,0:T(8,128)(2,1)S(1)} %dynamic-slice_convert_fusion.9), channel_id=1, source_target_pairs={{0,1},{1,0},{2,3},{3,2},{4,5},{5,4},{6,7},{7,6},{8,9},{9,8},{10,11... | collective-permute-start | bytes 1179656 | tf_op jit(solution)/shard_map/ppermute | solution.py:212
  119.3 11.4 %collective-permute-start.1 = (bf16[48,2048]{1,0:T(8,128)(2,1)S(1)}, bf16[48,2048]{1,0:T(8,128)(2,1)S(1)}, u32[]{:S(2)}, u32[]{:S(2)}) collective-permute-start(bf16[48,2048]{1,0:T(8,128)(2,1)S(1)} %dynamic-slice_convert_fusion.10), channel_id=1, source_target_pairs={{0,2},{1,3},{2,0},{3,1},{4,6},{5,7},{6,4},{7,5},{8,10},{9,11},{10,... | collective-permute-start | bytes 589832 | tf_op jit(solution)/shard_map/ppermute | solution.py:212
  130.7 11.1 %collective-permute-start.2 = (bf16[48,2048]{1,0:T(8,128)(2,1)S(1)}, bf16[48,2048]{1,0:T(8,128)(2,1)S(1)}, u32[]{:S(2)}, u32[]{:S(2)}) collective-permute-start(bf16[48,2048]{1,0:T(8,128)(2,1)S(1)} %add_convert_fusion.8), channel_id=1, source_target_pairs={{0,2},{1,3},{2,0},{3,1},{4,6},{5,7},{6,4},{7,5},{8,10},{9,11},{10,... | collective-permute-start | bytes 589832 | tf_op jit(solution)/shard_map/ppermute | solution.py:217
  133.8 447.2 %all-reduce.10.cloned.1.call-start = ((), (), s32[]{:S(2)}) async-start(), calls=%async_computation.3 | async-start | bytes 34603008 | tf_op jit(solution)/shard_map/psum | solution.py:370
  141.9 28.9 %collective-permute-start.3 = (bf16[96,2048]{1,0:T(8,128)(2,1)S(1)}, bf16[96,2048]{1,0:T(8,128)(2,1)}, u32[]{:S(2)}, u32[]{:S(2)}) collective-permute-start(bf16[96,2048]{1,0:T(8,128)(2,1)S(1)} %pad_maximum_fusion.10), channel_id=1, source_target_pairs={{0,1},{1,0},{2,3},{3,2},{4,5},{5,4},{6,7},{7,6},{8,9},{9,8},{10,11... | collective-permute-start | bytes 1179656 | tf_op jit(solution)/shard_map/ppermute | solution.py:217
  172.0 37.4 %copy-start.22 = (bf16[96,2048]{1,0:T(8,128)(2,1)}, bf16[96,2048]{1,0:T(8,128)(2,1)S(1)}, u32[]{:S(2)}) copy-start(bf16[96,2048]{1,0:T(8,128)(2,1)S(1)} %get-tuple-element.99) | copy-start | bytes 1179652
  172.0 37.4 %copy-start.25 = (bf16[96,2048]{1,0:T(8,128)(2,1)}, bf16[96,2048]{1,0:T(8,128)(2,1)S(1)}, u32[]{:S(2)}) copy-start(bf16[96,2048]{1,0:T(8,128)(2,1)S(1)} %get-tuple-element.100) | copy-start | bytes 1179652
  206.1 9.3 %slice-start.8 = ((s8[5767168]{0:T(1024)(128)(4,1)}), s8[4194304]{0:T(1024)(128)(4,1)S(1)}, s32[]{:S(2)}) async-start(s8[5767168]{0:T(1024)(128)(4,1)} %bitcast.104), calls=%async_computation.12 | async-start | bytes 8388608
  220.1 19.5 %copy-start.76 = (bf16[512,1408]{1,0:T(8,128)(2,1)}, bf16[512,1408]{1,0:T(8,128)(2,1)S(1)}, u32[]{:S(2)}) copy-start(bf16[512,1408]{1,0:T(8,128)(2,1)S(1)} %get-tuple-element.74) | copy-start | bytes 4325380
  223.6 11.1 %slice-start.10 = ((s8[5767168]{0:T(1024)(128)(4,1)}), s8[4194304]{0:T(1024)(128)(4,1)S(1)}, s32[]{:S(2)}) async-start(s8[5767168]{0:T(1024)(128)(4,1)} %bitcast.106), calls=%async_computation.14 | async-start | bytes 8388608
  244.8 32.3 %copy-start.8 = (s32[16]{0:T(128)S(1)}, s32[16]{0:T(128)}, u32[]{:S(2)}) copy-start(s32[16]{0:T(128)} %chunk_ref.3) | copy-start | bytes 196
  244.8 32.4 %copy-start.67 = (s32[1,1,16,256]{3,2,1,0:T(8,128)S(1)}, s32[1,1,16,256]{3,2,1,0:T(8,128)}, u32[]{:S(2)}) copy-start(s32[1,1,16,256]{3,2,1,0:T(8,128)} %get-tuple-element.110) | copy-start | bytes 49156
  246.6 25.2 %collective-permute-start.4 = (bf16[256,2048]{1,0:T(8,128)(2,1)S(1)}, bf16[256,2048]{1,0:T(8,128)(2,1)}, u32[]{:S(2)}, u32[]{:S(2)}) collective-permute-start(bf16[256,2048]{1,0:T(8,128)(2,1)S(1)} %dynamic-slice_convert_fusion.4), channel_id=1, source_target_pairs={{0,1},{1,0},{2,3},{3,2},{4,5},{5,4},{6,7},{7,6},{8,9},{9,8},{10,11... | collective-permute-start | bytes 3145736 | tf_op jit(solution)/shard_map/ppermute | solution.py:212
  275.4 24.7 %collective-permute-start.5 = (bf16[128,2048]{1,0:T(8,128)(2,1)S(1)}, bf16[128,2048]{1,0:T(8,128)(2,1)S(1)}, u32[]{:S(2)}, u32[]{:S(2)}) collective-permute-start(bf16[128,2048]{1,0:T(8,128)(2,1)S(1)} %dynamic-slice_convert_fusion.8), channel_id=1, source_target_pairs={{0,2},{1,3},{2,0},{3,1},{4,6},{5,7},{6,4},{7,5},{8,10},{9,11},{10,... | collective-permute-start | bytes 1572872 | tf_op jit(solution)/shard_map/ppermute | solution.py:212
  301.4 24.5 %collective-permute-start.6 = (bf16[128,2048]{1,0:T(8,128)(2,1)S(1)}, bf16[128,2048]{1,0:T(8,128)(2,1)S(1)}, u32[]{:S(2)}, u32[]{:S(2)}) collective-permute-start(bf16[128,2048]{1,0:T(8,128)(2,1)S(1)} %add_convert_fusion.4), channel_id=1, source_target_pairs={{0,2},{1,3},{2,0},{3,1},{4,6},{5,7},{6,4},{7,5},{8,10},{9,11},{10,... | collective-permute-start | bytes 1572872 | tf_op jit(solution)/shard_map/ppermute | solution.py:217
  327.9 25.4 %collective-permute-start.7 = (bf16[256,2048]{1,0:T(8,128)(2,1)}, bf16[256,2048]{1,0:T(8,128)(2,1)}, u32[]{:S(2)}, u32[]{:S(2)}) collective-permute-start(bf16[256,2048]{1,0:T(8,128)(2,1)} %pad_maximum_fusion.1), channel_id=1, source_target_pairs={{0,1},{1,0},{2,3},{3,2},{4,5},{5,4},{6,7},{7,6},{8,9},{9,8},{10,11... | collective-permute-start | bytes 3145736 | tf_op jit(solution)/shard_map/ppermute | solution.py:217
  332.6 424.4 %all-reduce.8.cloned.1.call-start = ((), (), s32[]{:S(2)}) async-start(), calls=%async_computation.2 | async-start | bytes 12582912 | tf_op jit(solution)/shard_map/psum | solution.py:370
  332.6 20.6 %copy-start.39 = (bf16[128,2048]{1,0:T(8,128)(2,1)S(1)}, bf16[128,2048]{1,0:T(8,128)(2,1)}, u32[]{:S(2)}) copy-start(bf16[128,2048]{1,0:T(8,128)(2,1)} %copy-done.38) | copy-start | bytes 1572868
  332.7 20.6 %copy-start.41 = (bf16[128,2048]{1,0:T(8,128)(2,1)S(1)}, bf16[128,2048]{1,0:T(8,128)(2,1)}, u32[]{:S(2)}) copy-start(bf16[128,2048]{1,0:T(8,128)(2,1)} %copy-done.40) | copy-start | bytes 1572868
  338.6 26.6 %copy-start.42 = (f32[512,2048]{1,0:T(8,128)}, f32[512,2048]{1,0:T(8,128)S(1)}, u32[]{:S(2)}) copy-start(f32[512,2048]{1,0:T(8,128)S(1)} %fusion.81) | copy-start | bytes 12582916
  366.4 76.9 %collective-permute-start.8 = (bf16[256,2048]{1,0:T(8,128)(2,1)}, bf16[256,2048]{1,0:T(8,128)(2,1)}, u32[]{:S(2)}, u32[]{:S(2)}) collective-permute-start(bf16[256,2048]{1,0:T(8,128)(2,1)} %dynamic-slice_convert_fusion.3), channel_id=1, source_target_pairs={{0,1},{1,0},{2,3},{3,2},{4,5},{5,4},{6,7},{7,6},{8,9},{9,8},{10,11... | collective-permute-start | bytes 3145736 | tf_op jit(solution)/shard_map/ppermute | solution.py:212
  402.3 35.9 %copy-start.3 = (f32[512,256]{1,0:T(8,128)}, f32[512,256]{1,0:T(8,128)S(1)}, u32[]{:S(2)}) copy-start(f32[512,256]{1,0:T(8,128)S(1)} %get-tuple-element.38) | copy-start | bytes 1572868
  443.2 9.4 %copy-start.4 = (f32[512,256]{1,0:T(8,128)S(1)}, f32[512,256]{1,0:T(8,128)}, u32[]{:S(2)}) copy-start(f32[512,256]{1,0:T(8,128)} %copy-done.3) | copy-start | bytes 1572868
  443.2 9.4 %copy-start.6 = (f32[512,256]{1,0:T(8,128)S(1)}, f32[512,256]{1,0:T(8,128)}, u32[]{:S(2)}) copy-start(f32[512,256]{1,0:T(8,128)} %copy-done.5) | copy-start | bytes 1572868
  443.2 12.1 %copy-start.58 = (bf16[512,128]{0,1:T(8,128)(2,1)S(1)}, bf16[512,128]{0,1:T(8,128)(2,1)}, u32[]{:S(2)}) copy-start(bf16[512,128]{0,1:T(8,128)(2,1)} %copy-done.57) | copy-start | bytes 393220
  443.2 12.1 %copy-start.60 = (bf16[512,128]{0,1:T(8,128)(2,1)S(1)}, bf16[512,128]{0,1:T(8,128)(2,1)}, u32[]{:S(2)}) copy-start(bf16[512,128]{0,1:T(8,128)(2,1)} %copy-done.59) | copy-start | bytes 393220
  443.2 12.1 %copy-start.62 = (bf16[512,128]{0,1:T(8,128)(2,1)S(1)}, bf16[512,128]{0,1:T(8,128)(2,1)}, u32[]{:S(2)}) copy-start(bf16[512,128]{0,1:T(8,128)(2,1)} %copy-done.61) | copy-start | bytes 393220
  443.2 33.7 %collective-permute-start.12 = (bf16[2048,512]{1,0:T(8,128)(2,1)}, bf16[2048,512]{1,0:T(8,128)(2,1)}, u32[]{:S(2)}, u32[]{:S(2)}) collective-permute-start(bf16[2048,512]{1,0:T(8,128)(2,1)} %dynamic-slice_convert_fusion), channel_id=1, source_target_pairs={{0,4},{4,0},{8,12},{12,8},{16,20},{20,16},{24,28},{28,24},{1,5},{5... | collective-permute-start | bytes 6291464 | tf_op jit(solution)/shard_map/ppermute | solution.py:245
  449.8 25.5 %collective-permute-start.9 = (bf16[128,2048]{1,0:T(8,128)(2,1)}, bf16[128,2048]{1,0:T(8,128)(2,1)}, u32[]{:S(2)}, u32[]{:S(2)}) collective-permute-start(bf16[128,2048]{1,0:T(8,128)(2,1)} %dynamic-slice_convert_fusion.7), channel_id=1, source_target_pairs={{0,2},{1,3},{2,0},{3,1},{4,6},{5,7},{6,4},{7,5},{8,10},{9,11},{10,... | collective-permute-start | bytes 1572872 | tf_op jit(solution)/shard_map/ppermute | solution.py:212
  455.3 21.6 %copy-start.34 = (f32[4096,512]{1,0:T(8,128)S(1)}, f32[4096,512]{1,0:T(8,128)}, u32[]{:S(2)}) copy-start(f32[4096,512]{1,0:T(8,128)} %copy-done.33) | copy-start | bytes 25165828
  476.8 25.2 %collective-permute-start.10 = (bf16[128,2048]{1,0:T(8,128)(2,1)S(1)}, bf16[128,2048]{1,0:T(8,128)(2,1)S(1)}, u32[]{:S(2)}, u32[]{:S(2)}) collective-permute-start(bf16[128,2048]{1,0:T(8,128)(2,1)S(1)} %add_convert_fusion.3), channel_id=1, source_target_pairs={{0,2},{1,3},{2,0},{3,1},{4,6},{5,7},{6,4},{7,5},{8,10},{9,11},{10,... | collective-permute-start | bytes 1572872 | tf_op jit(solution)/shard_map/ppermute | solution.py:217
  479.3 23.0 %copy-start.32 = (f32[512,64]{1,0:T(8,128)S(1)}, f32[512,64]{1,0:T(8,128)}, u32[]{:S(2)}) copy-start(f32[512,64]{1,0:T(8,128)} %copy-done.31) | copy-start | bytes 393220
  479.3 23.0 %copy-start.44 = (f32[512,64]{1,0:T(8,128)S(1)}, f32[512,64]{1,0:T(8,128)}, u32[]{:S(2)}) copy-start(f32[512,64]{1,0:T(8,128)} %get-tuple-element.105) | copy-start | bytes 393220
  479.5 45.7 %collective-permute-start.13 = (bf16[1024,512]{1,0:T(8,128)(2,1)S(1)}, bf16[1024,512]{1,0:T(8,128)(2,1)S(1)}, u32[]{:S(2)}, u32[]{:S(2)}) collective-permute-start(bf16[1024,512]{1,0:T(8,128)(2,1)S(1)} %dynamic-slice_convert_fusion.2), channel_id=1, source_target_pairs={{0,8},{4,12},{8,0},{12,4},{16,24},{20,28},{24,16},{28,20},{1,9},{5... | collective-permute-start | bytes 3145736 | tf_op jit(solution)/shard_map/ppermute | solution.py:245
  502.2 25.0 %collective-permute-start.11 = (bf16[256,2048]{1,0:T(8,128)(2,1)S(1)}, bf16[256,2048]{1,0:T(8,128)(2,1)S(1)}, u32[]{:S(2)}, u32[]{:S(2)}) collective-permute-start(bf16[256,2048]{1,0:T(8,128)(2,1)S(1)} %pad_maximum_fusion.2), channel_id=1, source_target_pairs={{0,1},{1,0},{2,3},{3,2},{4,5},{5,4},{6,7},{7,6},{8,9},{9,8},{10,11... | collective-permute-start | bytes 3145736 | tf_op jit(solution)/shard_map/ppermute | solution.py:217
  525.6 22.8 %collective-permute-start.14 = (bf16[512,512]{1,0:T(8,128)(2,1)S(1)}, bf16[512,512]{1,0:T(8,128)(2,1)S(1)}, u32[]{:S(2)}, u32[]{:S(2)}) collective-permute-start(bf16[512,512]{1,0:T(8,128)(2,1)S(1)} %dynamic-slice_convert_fusion.6), channel_id=1, source_target_pairs={{0,16},{4,20},{8,24},{12,28},{16,0},{20,4},{24,8},{28,12},{1,17},{... | collective-permute-start | bytes 1572872 | tf_op jit(solution)/shard_map/ppermute | solution.py:245
  601.5 25.8 %collective-permute-start.15 = (bf16[256,2048]{1,0:T(8,128)(2,1)S(1)}, bf16[256,2048]{1,0:T(8,128)(2,1)S(1)}, u32[]{:S(2)}, u32[]{:S(2)}) collective-permute-start(bf16[256,2048]{1,0:T(8,128)(2,1)S(1)} %dynamic-slice_convert_fusion.1), channel_id=1, source_target_pairs={{0,1},{1,0},{2,3},{3,2},{4,5},{5,4},{6,7},{7,6},{8,9},{9,8},{10,11... | collective-permute-start | bytes 3145736 | tf_op jit(solution)/shard_map/ppermute | solution.py:212
  627.7 24.9 %collective-permute-start.16 = (bf16[128,2048]{1,0:T(8,128)(2,1)S(1)}, bf16[128,2048]{1,0:T(8,128)(2,1)S(1)}, u32[]{:S(2)}, u32[]{:S(2)}) collective-permute-start(bf16[128,2048]{1,0:T(8,128)(2,1)S(1)} %dynamic-slice_convert_fusion.5), channel_id=1, source_target_pairs={{0,2},{1,3},{2,0},{3,1},{4,6},{5,7},{6,4},{7,5},{8,10},{9,11},{10,... | collective-permute-start | bytes 1572872 | tf_op jit(solution)/shard_map/ppermute | solution.py:212
  652.7 23.9 %collective-permute-start.17 = (bf16[128,2048]{1,0:T(8,128)(2,1)S(1)}, bf16[128,2048]{1,0:T(8,128)(2,1)S(1)}, u32[]{:S(2)}, u32[]{:S(2)}) collective-permute-start(bf16[128,2048]{1,0:T(8,128)(2,1)S(1)} %add_convert_fusion.1), channel_id=1, source_target_pairs={{0,2},{1,3},{2,0},{3,1},{4,6},{5,7},{6,4},{7,5},{8,10},{9,11},{10,... | collective-permute-start | bytes 1572872 | tf_op jit(solution)/shard_map/ppermute | solution.py:217
  652.8 49.6 %copy-start.13 = (bf16[512,2048]{1,0:T(8,128)(2,1)S(1)}, bf16[512,2048]{1,0:T(8,128)(2,1)}, u32[]{:S(2)}) copy-start(bf16[512,2048]{1,0:T(8,128)(2,1)} %param.13) | copy-start | bytes 6291460
  676.7 28.0 %slice-start.6 = ((s8[5767168]{0:T(1024)(128)(4,1)}), s8[4194304]{0:T(1024)(128)(4,1)S(1)}, s32[]{:S(2)}) async-start(s8[5767168]{0:T(1024)(128)(4,1)} %bitcast.77), calls=%async_computation.10 | async-start | bytes 8388608
  676.9 25.1 %collective-permute-start.18 = (bf16[256,2048]{1,0:T(8,128)(2,1)S(1)}, bf16[256,2048]{1,0:T(8,128)(2,1)S(1)}, u32[]{:S(2)}, u32[]{:S(2)}) collective-permute-start(bf16[256,2048]{1,0:T(8,128)(2,1)S(1)} %pad_maximum_fusion.5), channel_id=1, source_target_pairs={{0,1},{1,0},{2,3},{3,2},{4,5},{5,4},{6,7},{7,6},{8,9},{9,8},{10,11... | collective-permute-start | bytes 3145736 | tf_op jit(solution)/shard_map/ppermute | solution.py:217
  676.9 1.2 collective-permute-start.22
  678.2 4.3 collective-permute-start.23
  682.5 22.2 %slice-start.7 = ((s8[5767168]{0:T(1024)(128)(4,1)}), s8[1572864]{0:T(1024)(128)(4,1)S(1)}, s32[]{:S(2)}) async-start(s8[5767168]{0:T(1024)(128)(4,1)} %bitcast.77), calls=%async_computation.11 | async-start | bytes 3145728
  682.5 21.6 %collective-permute-start.24 = (f32[2048]{0:T(1024)S(1)}, f32[2048]{0:T(1024)S(1)}, u32[]{:S(2)}, u32[]{:S(2)}) collective-permute-start(f32[2048]{0:T(1024)S(1)} %add.348), channel_id=1, source_target_pairs={{0,16},{4,20},{8,24},{12,28},{16,0},{20,4},{24,8},{28,12},{1,17},{... | collective-permute-start | bytes 24584 | tf_op jit(solution)/shard_map/ppermute | solution.py:254
  704.0 63.0 %collective-permute-start.19 = (f32[2048]{0:T(1024)S(1)}, f32[2048]{0:T(1024)S(1)}, u32[]{:S(2)}, u32[]{:S(2)}) collective-permute-start(f32[2048]{0:T(1024)S(1)} %get-tuple-element.61), channel_id=1, source_target_pairs={{0,4},{4,0},{8,12},{12,8},{16,20},{20,16},{24,28},{28,24},{1,5},{5... | collective-permute-start | bytes 24584 | tf_op jit(solution)/shard_map/ppermute | solution.py:254
  704.7 11.1 %slice-start.2 = ((s8[5767168]{0:T(1024)(128)(4,1)}), s8[4194304]{0:T(1024)(128)(4,1)S(1)}, s32[]{:S(2)}) async-start(s8[5767168]{0:T(1024)(128)(4,1)} %bitcast.73), calls=%async_computation.6 | async-start | bytes 8388608
  757.0 15.0 %copy-start.30 = (bf16[256,2048]{1,0:T(8,128)(2,1)S(1)}, bf16[256,2048]{1,0:T(8,128)(2,1)}, u32[]{:S(2)}) copy-start(bf16[256,2048]{1,0:T(8,128)(2,1)} %copy-done.29) | copy-start | bytes 3145732
  761.3 10.6 %copy-start.20 = (f32[512,2048]{1,0:T(8,128)S(1)}, f32[512,2048]{1,0:T(8,128)}, u32[]{:S(2)}) copy-start(f32[512,2048]{1,0:T(8,128)} %maximum_convert_fusion.1) | copy-start | bytes 12582916
  762.8 9.2 %copy-start.14 = (bf16[512,2048]{1,0:T(8,128)(2,1)S(1)}, bf16[512,2048]{1,0:T(8,128)(2,1)}, u32[]{:S(2)}) copy-start(bf16[512,2048]{1,0:T(8,128)(2,1)} %param.13) | copy-start | bytes 6291460
  762.8 9.2 %copy-start.16 = (f32[512,2048]{1,0:T(8,128)S(1)}, f32[512,2048]{1,0:T(8,128)}, u32[]{:S(2)}) copy-start(f32[512,2048]{1,0:T(8,128)} %copy-done.15) | copy-start | bytes 12582916
  762.8 9.2 %copy-start.19 = (bf16[320,2048]{1,0:T(8,128)(2,1)S(1)}, bf16[320,2048]{1,0:T(8,128)(2,1)}, u32[]{:S(2)}) copy-start(bf16[320,2048]{1,0:T(8,128)(2,1)} %all-reduce.6.cloned.1.call-done) | copy-start | bytes 3932164
  762.8 9.2 %copy-start.24 = (bf16[96,2048]{1,0:T(8,128)(2,1)S(1)}, bf16[96,2048]{1,0:T(8,128)(2,1)}, u32[]{:S(2)}) copy-start(bf16[96,2048]{1,0:T(8,128)(2,1)} %copy-done.22) | copy-start | bytes 1179652
  762.8 9.2 %copy-start.27 = (bf16[96,2048]{1,0:T(8,128)(2,1)S(1)}, bf16[96,2048]{1,0:T(8,128)(2,1)}, u32[]{:S(2)}) copy-start(bf16[96,2048]{1,0:T(8,128)(2,1)} %copy-done.25) | copy-start | bytes 1179652
  767.0 3.7 collective-permute-start.20
  770.7 9.5 %collective-permute-start.21 = (f32[2048]{0:T(1024)S(1)}, f32[2048]{0:T(1024)S(1)}, u32[]{:S(2)}, u32[]{:S(2)}) collective-permute-start(f32[2048]{0:T(1024)S(1)} %add.345), channel_id=1, source_target_pairs={{0,16},{4,20},{8,24},{12,28},{16,0},{20,4},{24,8},{28,12},{1,17},{... | collective-permute-start | bytes 24584 | tf_op jit(solution)/shard_map/ppermute | solution.py:254
  (54 other events, 200.7 us)
Sparse Core Ops, SparseCore 0:
  22.0 39.3 all-gather.2
  134.0 68.9 all-reduce.5
  332.7 248.2 all-reduce.9
  652.9 103.9 all-reduce.7

commit v8 on v6

--- a/solution.py
+++ b/solution.py
@@ -429,9 +429,8 @@
     ) = lax.optimization_barrier(
         (down_sum, d_normed_part, grad_w_out, grad_w_query, grad_w_key, grad_w_value)
     )
-    grad_w_out, grad_w_query, grad_w_key, grad_w_value = dp_sum(
-        [grad_w_out, grad_w_query, grad_w_key, grad_w_value]
-    )
+    grad_w_out, grad_w_query = dp_sum([grad_w_out, grad_w_query])
+    grad_w_key, grad_w_value = permute_sum([grad_w_key, grad_w_value], [0, 0], "dp")
     grad_w_gate, grad_w_up, grad_w_down = [
         grad.astype(jnp.float32) for grad in (grad_w_gate, grad_w_up, grad_w_down)
     ]
@@ -441,9 +440,7 @@
     grad_input = grad_middle + d_source_norm
     grad_gain_one = permute_allsum(grad_gain_one, "dp")
     grad_gain_two = permute_allsum(grad_gain_two, "dp")
-    grad_w_out, grad_w_query, grad_w_key, grad_w_value = [
-        grad.astype(jnp.float32) for grad in (grad_w_out, grad_w_query, grad_w_key, grad_w_value)
-    ]
+    grad_w_out, grad_w_query = [grad.astype(jnp.float32) for grad in (grad_w_out, grad_w_query)]
     return (
         output,
         grad_input,

time: 793 us -> 802 us (1.011)
  waiting for transfers between devices: 416 us -> 390 us
  other arithmetic: 96.5 us -> 115 us
  starting transfers between devices: 23.6 us -> 33.1 us
  local copies, waits for them, and re-layouts: 40.2 us -> 48.8 us
    ppermute x8 -> x14, waiting for transfers between devices: 133 us -> 108 us  [permute_sum(): got = lax.ppermute(pieces, axis, partner_perm(size, 1 << step))]
    ppermute x8 -> x14, waiting for transfers between devices: 127 us -> 117 us  [permute_sum(): got = lax.ppermute(send, axis, partner_perm(size, 1 << step))]
    ppermute x8 -> x14, starting transfers between devices: 13.7 us -> 18.7 us  [permute_sum(): got = lax.ppermute(send, axis, partner_perm(size, 1 << step))]
    unnamed x182 -> x186, local copies, waits for them, and re-layouts: 20.2 us -> 24.8 us
    convert_element_type x7 -> x5, other arithmetic: 27.3 us -> 31 us  [on_device(): grad.astype(jnp.float32)]
  transfers between devices with their start and end apart: 29 -> 41, of which waited for: 24 -> 26; matrix products, arithmetic and copies ran while one was open for 14% -> 17% of each run, Pallas kernels for 9% -> 9%
where the time goes in v8:
time: 802 us; the launch traced here: 797 us
  waiting for transfers between devices  390 us (49%)
  other arithmetic  115 us (14%)
  matrix products  115 us (14%)
  Pallas kernels  68.6 us (9%)
  local copies, waits for them, and re-layouts  48.8 us (6%)
  starting transfers between devices  33.1 us (4%)
  between operations  15.6 us (2%)
  blocking collectives  10.6 us (1%)
    ppermute x14, waiting for transfers between devices, permute_sum(): got = lax.ppermute(send, axis, partner_perm(size, 1 << step))  117 us
    ppermute x14, waiting for transfers between devices, permute_sum(): got = lax.ppermute(pieces, axis, partner_perm(size, 1 << step))  108 us
    psum x2, waiting for transfers between devices, dp_sum(): return [lax.psum(grad.astype(jnp.bfloat16), 'dp') for grad in grads]  71.8 us
    pallas_call x1, Pallas kernels, attention_backward(): pl.pallas_call(kernel, grid_spec=grid_spec, out_shape=[jax.ShapeDtypeStru...  68.6 us
    dot_general x11, matrix products, right_trans(): lax.dot_general(left, right, (((1,), (1,)), ((), ())), preferred_element_...  45.5 us
    ppermute x3, waiting for transfers between devices, permute_scatter(): got = lax.ppermute(send, axis, partner_perm(size, 1 << step))  36 us
    dot_general x7, matrix products, left_trans(): lax.dot_general(left, right, (((0,), (0,)), ((), ())), preferred_element_...  32.6 us
    psum x1, waiting for transfers between devices, on_device(): branch_top = lax.psum(branch_part[:sc_rows].astype(jnp.bfloat16), 'tensor')  31 us
  transfers between devices with their start and end apart: 41, of which 26 were waited for; matrix products, arithmetic and copies ran while one was open for 17% of the time, Pallas kernels for 9%

profile of v8, /device:TPU:0, one launch (start us, length us, event | category | flops | bytes accessed | tf_op | source)
XLA Modules:
  0.0 797.1 jit_solution(9209051359579991084)
XLA Ops:
  12.4 3.3 convolution_convert_fusion.1
  22.0 10.6 %all-gather = bf16[8,1,512]{2,1,0:T(2,128)(2,1)S(1)} all-gather(bf16[1,1,512]{2,1,0:T(2,128)(2,1)S(1)} %reshape.291), channel_id=1, replica_groups=mesh['dp'=8,'tensor'=4] {'dp'}, dimensions={0}, use_global_device_ids=true | all-gather | bytes 9216 | tf_op jit(solution)/shard_map/all_gather | solution.py:312
  32.7 3.7 fusion.70
  44.0 17.4 %all-gather.3.cloned.1.call-done.k_ref.v_ref = bf16[4096,512]{1,0:T(8,128)(2,1)} async-done(((bf16[512,512]{1,0:T(8,128)(2,1)}), bf16[4096,512]{1,0:T(8,128)(2,1)}) %all-gather.3.cloned.1.call-update) | async-done | bytes 4194320 | tf_op jit(solution)/shard_map/all_gather | solution.py:309
  61.4 4.6 fusion.76
  67.3 4.6 fusion.77
  73.5 4.6 fusion.78
  79.4 6.9 fusion.79
  86.3 4.6 fusion.2
  90.9 3.2 fusion.22
  94.2 3.4 fusion.23
  108.3 9.8 %collective-permute-done = bf16[96,2048]{1,0:T(8,128)(2,1)S(1)} collective-permute-done((bf16[96,2048]{1,0:T(8,128)(2,1)S(1)}, bf16[96,2048]{1,0:T(8,128)(2,1)S(1)}, u32[]{:S(2)}, u32[]{:S(2)}) %collective-permute-start) | collective-permute-done | bytes 393248 | tf_op jit(solution)/shard_map/ppermute | solution.py:209
  121.8 8.9 %collective-permute-done.1 = bf16[48,2048]{1,0:T(8,128)(2,1)S(1)} collective-permute-done((bf16[48,2048]{1,0:T(8,128)(2,1)S(1)}, bf16[48,2048]{1,0:T(8,128)(2,1)S(1)}, u32[]{:S(2)}, u32[]{:S(2)}) %collective-permute-start.1) | collective-permute-done | bytes 196640 | tf_op jit(solution)/shard_map/ppermute | solution.py:209
  130.8 3.0 slice.195
  134.1 7.8 collective-permute-done.2
  142.0 8.3 %fusion.36 = f32[512,1408]{1,0:T(8,128)} fusion(bf16[1408,2048]{1,0:T(8,128)(2,1)} %param.24, bf16[512,2048]{1,0:T(8,128)(2,1)} %param.25, f32[512]{0:T(512)S(1)} %get-tuple-element.112), kind=kOutput, calls=%fused_computation.123 | convolution fusion | flops 2955935744 | bytes 10749952 | tf_op jit(solution)/shard_map/dot_general | solution.py:49
  150.3 20.5 %collective-permute-done.3 = bf16[96,2048]{1,0:T(8,128)(2,1)} collective-permute-done((bf16[96,2048]{1,0:T(8,128)(2,1)S(1)}, bf16[96,2048]{1,0:T(8,128)(2,1)}, u32[]{:S(2)}, u32[]{:S(2)}) %collective-permute-start.3) | collective-permute-done | bytes 393248 | tf_op jit(solution)/shard_map/ppermute | solution.py:214
  172.0 31.0 %all-reduce.6.cloned.1.call-done = bf16[320,2048]{1,0:T(8,128)(2,1)} async-done(((bf16[320,2048]{1,0:T(8,128)(2,1)}), bf16[320,2048]{1,0:T(8,128)(2,1)}) %all-reduce.6.cloned.1.call-update) | async-done | bytes 1310736 | tf_op jit(solution)/shard_map/psum | solution.py:353
  203.0 3.1 multiply_reduce_fusion.2
  206.1 3.3 multiply_convert_fusion.1
  209.5 5.9 fusion.80
  215.4 4.7 multiply_convert_fusion.2
  220.1 3.4 fusion.84
  223.6 5.3 fusion.82
  228.9 5.5 fusion.83
  234.5 5.0 convolution_add_fusion
  239.5 5.2 fusion.34
  244.6 2.7 dynamic-slice_convert_fusion.4
  248.8 23.9 %collective-permute-done.4 = bf16[256,2048]{1,0:T(8,128)(2,1)} collective-permute-done((bf16[256,2048]{1,0:T(8,128)(2,1)}, bf16[256,2048]{1,0:T(8,128)(2,1)}, u32[]{:S(2)}, u32[]{:S(2)}) %collective-permute-start.4) | collective-permute-done | bytes 1048608 | tf_op jit(solution)/shard_map/ppermute | solution.py:209
  279.8 22.4 %collective-permute-done.5 = bf16[128,2048]{1,0:T(8,128)(2,1)} collective-permute-done((bf16[128,2048]{1,0:T(8,128)(2,1)}, bf16[128,2048]{1,0:T(8,128)(2,1)}, u32[]{:S(2)}, u32[]{:S(2)}) %collective-permute-start.5) | collective-permute-done | bytes 524320 | tf_op jit(solution)/shard_map/ppermute | solution.py:209
  303.7 24.5 %collective-permute-done.6 = bf16[128,2048]{1,0:T(8,128)(2,1)S(1)} collective-permute-done((bf16[128,2048]{1,0:T(8,128)(2,1)S(1)}, bf16[128,2048]{1,0:T(8,128)(2,1)S(1)}, u32[]{:S(2)}, u32[]{:S(2)}) %collective-permute-start.6) | collective-permute-done | bytes 524320 | tf_op jit(solution)/shard_map/ppermute | solution.py:214
  335.2 6.3 fusion.81
  341.5 14.1 %collective-permute-done.7 = bf16[256,2048]{1,0:T(8,128)(2,1)} collective-permute-done((bf16[256,2048]{1,0:T(8,128)(2,1)}, bf16[256,2048]{1,0:T(8,128)(2,1)}, u32[]{:S(2)}, u32[]{:S(2)}) %collective-permute-start.7) | collective-permute-done | bytes 1048608 | tf_op jit(solution)/shard_map/ppermute | solution.py:214
  359.2 2.8 multiply_reduce_fusion
  362.1 3.8 convert_add_fusion.1
  369.0 68.6 %shard_map.212 = (f32[512,512]{1,0:T(8,128)S(1)}, f32[4096,256]{1,0:T(8,128)}, f32[4096,256]{1,0:T(8,128)}) custom-call(s32[16]{0:T(128)S(1)} %copy-done.5, s32[2]{0:T(128)S(1)} %dynamic_slice.121.qblock_ref, bf16[512,512]{1,0:T(8,128)(2,1)S(1)} %bitcast.65, bf16[4096,512]{1,0:T(8,128)(2,1)} %all-gather.3.cloned.1.call-done.k_ref.v_ref, ...), custom_call_target="tpu_custom_call" | custom-call | flops 10737418240 | bytes 25165824 | tf_op jit(solution)/shard_map/pallas_call | solution.py:173
  437.5 3.0 constant_dynamic-update-slice_fusion.1
  444.4 3.0 copy-done.45
  453.0 5.6 fusion.55
  458.6 16.0 %collective-permute-done.9 = bf16[128,2048]{1,0:T(8,128)(2,1)} collective-permute-done((bf16[128,2048]{1,0:T(8,128)(2,1)}, bf16[128,2048]{1,0:T(8,128)(2,1)}, u32[]{:S(2)}, u32[]{:S(2)}) %collective-permute-start.9) | collective-permute-done | bytes 524320 | tf_op jit(solution)/shard_map/ppermute | solution.py:209
  479.7 2.6 collective-permute-start.13
  482.3 19.3 %collective-permute-done.10 = bf16[128,2048]{1,0:T(8,128)(2,1)S(1)} collective-permute-done((bf16[128,2048]{1,0:T(8,128)(2,1)S(1)}, bf16[128,2048]{1,0:T(8,128)(2,1)S(1)}, u32[]{:S(2)}, u32[]{:S(2)}) %collective-permute-start.10) | collective-permute-done | bytes 524320 | tf_op jit(solution)/shard_map/ppermute | solution.py:214
  505.2 2.8 fusion.38
  508.0 17.1 %collective-permute-done.13 = bf16[1024,512]{1,0:T(8,128)(2,1)} collective-permute-done((bf16[1024,512]{1,0:T(8,128)(2,1)}, bf16[1024,512]{1,0:T(8,128)(2,1)}, u32[]{:S(2)}, u32[]{:S(2)}) %collective-permute-start.13) | collective-permute-done | bytes 1048608 | tf_op jit(solution)/shard_map/ppermute | solution.py:242
  525.1 2.6 convert_add_fusion.4
  533.0 18.9 %collective-permute-done.14 = bf16[512,512]{1,0:T(8,128)(2,1)S(1)} collective-permute-done((bf16[512,512]{1,0:T(8,128)(2,1)S(1)}, bf16[512,512]{1,0:T(8,128)(2,1)S(1)}, u32[]{:S(2)}, u32[]{:S(2)}) %collective-permute-start.14) | collective-permute-done | bytes 524320 | tf_op jit(solution)/shard_map/ppermute | solution.py:242
  552.1 32.4 %all-reduce.10.cloned.1.call-done = (bf16[2048,1408]{1,0:T(8,128)(2,1)}, bf16[2048,1408]{1,0:T(8,128)(2,1)}, bf16[1408,2048]{1,0:T(8,128)(2,1)}) async-done(((bf16[2048,1408]{1,0:T(8,128)(2,1)}, bf16[2048,1408]{1,0:T(8,128)(2,1)}, bf16[1408,2048]{1,0:T(8,128)(2,1)}), (bf16[2048,1408]{1,0:T(8,128)(2,1)}, bf16[2048,1408]{1,0:T(8,128)(2,1)}, bf16[1408,2048]{1,0:T(8,128)(2,1)})) %all-reduce.10.cloned.1.call-update) | async-done | bytes 17301520 | tf_op jit(solution)/shard_map/psum | solution.py:367
  585.3 4.0 fusion.54
  589.2 2.8 fusion.53
  595.8 4.2 fusion.43
  602.3 3.3 add_add_fusion.2
  615.9 6.9 collective-permute-done.29
  624.1 3.1 collective-permute-done.23
  629.5 3.6 collective-permute-done.24
  640.8 20.7 %collective-permute-done.16 = bf16[128,2048]{1,0:T(8,128)(2,1)S(1)} collective-permute-done((bf16[128,2048]{1,0:T(8,128)(2,1)S(1)}, bf16[128,2048]{1,0:T(8,128)(2,1)S(1)}, u32[]{:S(2)}, u32[]{:S(2)}) %collective-permute-start.16) | collective-permute-done | bytes 524320 | tf_op jit(solution)/shard_map/ppermute | solution.py:209
  664.2 22.1 %collective-permute-done.17 = bf16[128,2048]{1,0:T(8,128)(2,1)S(1)} collective-permute-done((bf16[128,2048]{1,0:T(8,128)(2,1)S(1)}, bf16[128,2048]{1,0:T(8,128)(2,1)S(1)}, u32[]{:S(2)}, u32[]{:S(2)}) %collective-permute-start.17) | collective-permute-done | bytes 524320 | tf_op jit(solution)/shard_map/ppermute | solution.py:214
  694.2 3.0 collective-permute-done.36
  697.8 8.1 %convert_element_type.326 = f32[2048,1408]{1,0:T(8,128)} convert(bf16[2048,1408]{1,0:T(8,128)(2,1)} %get-tuple-element.50) | non-fusion elementwise | flops 2883584 | bytes 17301504 | tf_op jit(solution)/shard_map/convert_element_type | solution.py:435
  705.9 8.0 %convert_element_type.327 = f32[2048,1408]{1,0:T(8,128)} convert(bf16[2048,1408]{1,0:T(8,128)(2,1)} %get-tuple-element.51) | non-fusion elementwise | flops 2883584 | bytes 17301504 | tf_op jit(solution)/shard_map/convert_element_type | solution.py:435
  713.9 6.0 convert_element_type.328
  728.8 39.4 %all-reduce.8.cloned.1.call-done = (bf16[2048,512]{1,0:T(8,128)(2,1)}, bf16[512,2048]{1,0:T(8,128)(2,1)}) async-done(((bf16[2048,512]{1,0:T(8,128)(2,1)}, bf16[512,2048]{1,0:T(8,128)(2,1)}), (bf16[2048,512]{1,0:T(8,128)(2,1)}, bf16[512,2048]{1,0:T(8,128)(2,1)})) %all-reduce.8.cloned.1.call-update) | async-done | bytes 4194320 | tf_op jit(solution)/shard_map/psum | solution.py:367
  768.3 4.3 convert_element_type.307
  772.6 4.5 convert_element_type.325
  782.2 7.5 fusion.11
  (370 shorter events, 139.8 us)
Async XLA Ops:
  7.2 94.9 %copy-start = (bf16[512,2048]{1,0:T(8,128)(2,1)S(1)}, bf16[512,2048]{1,0:T(8,128)(2,1)}, u32[]{:S(2)}) copy-start(bf16[512,2048]{1,0:T(8,128)(2,1)} %param.20) | copy-start | bytes 6291460
  7.2 54.2 %all-gather.3.cloned.1.call-start = ((), (), s32[]{:S(2)}) async-start(), calls=%async_computation | async-start | bytes 4718592 | tf_op jit(solution)/shard_map/all_gather | solution.py:309
  11.0 21.7 %copy-start.67 = (f32[512]{0:T(512)}, f32[512]{0:T(512)S(1)}, u32[]{:S(2)}) copy-start(f32[512]{0:T(512)S(1)} %fusion.60) | copy-start | bytes 6148
  11.7 21.0 %copy-start.64 = (f32[2048]{0:T(1024)}, f32[2048]{0:T(1024)S(1)}, u32[]{:S(2)}) copy-start(f32[2048]{0:T(1024)S(1)} %convert_element_type.252) | copy-start | bytes 24580
  19.0 22.3 %copy-start.28 = (f32[512,64]{1,0:T(8,128)}, f32[512,64]{1,0:T(8,128)S(1)}, u32[]{:S(2)}) copy-start(f32[512,64]{1,0:T(8,128)S(1)} %get-tuple-element.111) | copy-start | bytes 393220
  21.9 181.0 %all-reduce.6.cloned.1.call-start = ((), (), s32[]{:S(2)}) async-start(), calls=%async_computation.1 | async-start | bytes 2621440 | tf_op jit(solution)/shard_map/psum | solution.py:353
  43.9 35.5 %copy-start.2 = (bf16[64,8,4,128]{3,1,2,0:T(8,128)(2,1)}, bf16[64,8,4,128]{3,1,2,0:T(8,128)(2,1)S(1)}, u32[]{:S(2)}) copy-start(bf16[64,8,4,128]{3,1,2,0:T(8,128)(2,1)S(1)} %copy.90) | copy-start | bytes 1572868
  106.8 11.3 %collective-permute-start = (bf16[96,2048]{1,0:T(8,128)(2,1)S(1)}, bf16[96,2048]{1,0:T(8,128)(2,1)S(1)}, u32[]{:S(2)}, u32[]{:S(2)}) collective-permute-start(bf16[96,2048]{1,0:T(8,128)(2,1)S(1)} %dynamic-slice_convert_fusion.11), channel_id=1, source_target_pairs={{0,1},{1,0},{2,3},{3,2},{4,5},{5,4},{6,7},{7,6},{8,9},{9,8},{10,11... | collective-permute-start | bytes 1179656 | tf_op jit(solution)/shard_map/ppermute | solution.py:209
  119.3 11.4 %collective-permute-start.1 = (bf16[48,2048]{1,0:T(8,128)(2,1)S(1)}, bf16[48,2048]{1,0:T(8,128)(2,1)S(1)}, u32[]{:S(2)}, u32[]{:S(2)}) collective-permute-start(bf16[48,2048]{1,0:T(8,128)(2,1)S(1)} %dynamic-slice_convert_fusion.14), channel_id=1, source_target_pairs={{0,2},{1,3},{2,0},{3,1},{4,6},{5,7},{6,4},{7,5},{8,10},{9,11},{10,... | collective-permute-start | bytes 589832 | tf_op jit(solution)/shard_map/ppermute | solution.py:209
  130.8 11.1 %collective-permute-start.2 = (bf16[48,2048]{1,0:T(8,128)(2,1)S(1)}, bf16[48,2048]{1,0:T(8,128)(2,1)S(1)}, u32[]{:S(2)}, u32[]{:S(2)}) collective-permute-start(bf16[48,2048]{1,0:T(8,128)(2,1)S(1)} %add_convert_fusion.8), channel_id=1, source_target_pairs={{0,2},{1,3},{2,0},{3,1},{4,6},{5,7},{6,4},{7,5},{8,10},{9,11},{10,... | collective-permute-start | bytes 589832 | tf_op jit(solution)/shard_map/ppermute | solution.py:214
  133.9 450.6 %all-reduce.10.cloned.1.call-start = ((), (), s32[]{:S(2)}) async-start(), calls=%async_computation.3 | async-start | bytes 34603008 | tf_op jit(solution)/shard_map/psum | solution.py:367
  141.9 28.9 %collective-permute-start.3 = (bf16[96,2048]{1,0:T(8,128)(2,1)S(1)}, bf16[96,2048]{1,0:T(8,128)(2,1)}, u32[]{:S(2)}, u32[]{:S(2)}) collective-permute-start(bf16[96,2048]{1,0:T(8,128)(2,1)S(1)} %pad_maximum_fusion.11), channel_id=1, source_target_pairs={{0,1},{1,0},{2,3},{3,2},{4,5},{5,4},{6,7},{7,6},{8,9},{9,8},{10,11... | collective-permute-start | bytes 1179656 | tf_op jit(solution)/shard_map/ppermute | solution.py:214
  172.0 190.1 %copy-start.19 = (bf16[96,2048]{1,0:T(8,128)(2,1)}, bf16[96,2048]{1,0:T(8,128)(2,1)S(1)}, u32[]{:S(2)}) copy-start(bf16[96,2048]{1,0:T(8,128)(2,1)S(1)} %get-tuple-element.95) | copy-start | bytes 1179652
  172.0 190.1 %copy-start.21 = (bf16[96,2048]{1,0:T(8,128)(2,1)}, bf16[96,2048]{1,0:T(8,128)(2,1)S(1)}, u32[]{:S(2)}) copy-start(bf16[96,2048]{1,0:T(8,128)(2,1)S(1)} %get-tuple-element.96) | copy-start | bytes 1179652
  220.1 19.3 %copy-start.75 = (bf16[512,1408]{1,0:T(8,128)(2,1)}, bf16[512,1408]{1,0:T(8,128)(2,1)S(1)}, u32[]{:S(2)}) copy-start(bf16[512,1408]{1,0:T(8,128)(2,1)S(1)} %get-tuple-element.66) | copy-start | bytes 4325380
  244.6 34.1 %copy-start.5 = (s32[16]{0:T(128)S(1)}, s32[16]{0:T(128)}, u32[]{:S(2)}) copy-start(s32[16]{0:T(128)} %chunk_ref.1) | copy-start | bytes 196
  244.6 34.2 %copy-start.66 = (s32[1,1,16,256]{3,2,1,0:T(8,128)S(1)}, s32[1,1,16,256]{3,2,1,0:T(8,128)}, u32[]{:S(2)}) copy-start(s32[1,1,16,256]{3,2,1,0:T(8,128)} %get-tuple-element.114) | copy-start | bytes 49156
  247.4 25.4 %collective-permute-start.4 = (bf16[256,2048]{1,0:T(8,128)(2,1)}, bf16[256,2048]{1,0:T(8,128)(2,1)}, u32[]{:S(2)}, u32[]{:S(2)}) collective-permute-start(bf16[256,2048]{1,0:T(8,128)(2,1)} %dynamic-slice_convert_fusion.4), channel_id=1, source_target_pairs={{0,1},{1,0},{2,3},{3,2},{4,5},{5,4},{6,7},{7,6},{8,9},{9,8},{10,11... | collective-permute-start | bytes 3145736 | tf_op jit(solution)/shard_map/ppermute | solution.py:209
  277.1 25.0 %collective-permute-start.5 = (bf16[128,2048]{1,0:T(8,128)(2,1)}, bf16[128,2048]{1,0:T(8,128)(2,1)}, u32[]{:S(2)}, u32[]{:S(2)}) collective-permute-start(bf16[128,2048]{1,0:T(8,128)(2,1)} %dynamic-slice_convert_fusion.10), channel_id=1, source_target_pairs={{0,2},{1,3},{2,0},{3,1},{4,6},{5,7},{6,4},{7,5},{8,10},{9,11},{10,... | collective-permute-start | bytes 1572872 | tf_op jit(solution)/shard_map/ppermute | solution.py:209
  303.6 24.6 %collective-permute-start.6 = (bf16[128,2048]{1,0:T(8,128)(2,1)S(1)}, bf16[128,2048]{1,0:T(8,128)(2,1)S(1)}, u32[]{:S(2)}, u32[]{:S(2)}) collective-permute-start(bf16[128,2048]{1,0:T(8,128)(2,1)S(1)} %add_convert_fusion.4), channel_id=1, source_target_pairs={{0,2},{1,3},{2,0},{3,1},{4,6},{5,7},{6,4},{7,5},{8,10},{9,11},{10,... | collective-permute-start | bytes 1572872 | tf_op jit(solution)/shard_map/ppermute | solution.py:214
  330.2 25.4 %collective-permute-start.7 = (bf16[256,2048]{1,0:T(8,128)(2,1)}, bf16[256,2048]{1,0:T(8,128)(2,1)}, u32[]{:S(2)}, u32[]{:S(2)}) collective-permute-start(bf16[256,2048]{1,0:T(8,128)(2,1)} %pad_maximum_fusion.1), channel_id=1, source_target_pairs={{0,1},{1,0},{2,3},{3,2},{4,5},{5,4},{6,7},{7,6},{8,9},{9,8},{10,11... | collective-permute-start | bytes 3145736 | tf_op jit(solution)/shard_map/ppermute | solution.py:214
  335.1 433.2 %all-reduce.8.cloned.1.call-start = ((), (), s32[]{:S(2)}) async-start(), calls=%async_computation.2 | async-start | bytes 8388608 | tf_op jit(solution)/shard_map/psum | solution.py:367
  335.2 20.4 %copy-start.40 = (bf16[128,2048]{1,0:T(8,128)(2,1)S(1)}, bf16[128,2048]{1,0:T(8,128)(2,1)}, u32[]{:S(2)}) copy-start(bf16[128,2048]{1,0:T(8,128)(2,1)} %copy-done.39) | copy-start | bytes 1572868
  335.2 20.4 %copy-start.42 = (bf16[128,2048]{1,0:T(8,128)(2,1)S(1)}, bf16[128,2048]{1,0:T(8,128)(2,1)}, u32[]{:S(2)}) copy-start(bf16[128,2048]{1,0:T(8,128)(2,1)} %copy-done.41) | copy-start | bytes 1572868
  341.5 25.8 %copy-start.44 = (f32[512,2048]{1,0:T(8,128)}, f32[512,2048]{1,0:T(8,128)S(1)}, u32[]{:S(2)}) copy-start(f32[512,2048]{1,0:T(8,128)S(1)} %fusion.81) | copy-start | bytes 12582916
  368.2 76.1 %collective-permute-start.8 = (bf16[256,2048]{1,0:T(8,128)(2,1)S(1)}, bf16[256,2048]{1,0:T(8,128)(2,1)S(1)}, u32[]{:S(2)}, u32[]{:S(2)}) collective-permute-start(bf16[256,2048]{1,0:T(8,128)(2,1)S(1)} %dynamic-slice_convert_fusion.3), channel_id=1, source_target_pairs={{0,1},{1,0},{2,3},{3,2},{4,5},{5,4},{6,7},{7,6},{8,9},{9,8},{10,11... | collective-permute-start | bytes 3145736 | tf_op jit(solution)/shard_map/ppermute | solution.py:209
  444.4 31.8 %collective-permute-start.12 = (bf16[2048,512]{1,0:T(8,128)(2,1)}, bf16[2048,512]{1,0:T(8,128)(2,1)}, u32[]{:S(2)}, u32[]{:S(2)}) collective-permute-start(bf16[2048,512]{1,0:T(8,128)(2,1)} %dynamic-slice_convert_fusion), channel_id=1, source_target_pairs={{0,4},{4,0},{8,12},{12,8},{16,20},{20,16},{24,28},{28,24},{1,5},{5... | collective-permute-start | bytes 6291464 | tf_op jit(solution)/shard_map/ppermute | solution.py:242
  449.2 25.4 %collective-permute-start.9 = (bf16[128,2048]{1,0:T(8,128)(2,1)}, bf16[128,2048]{1,0:T(8,128)(2,1)}, u32[]{:S(2)}, u32[]{:S(2)}) collective-permute-start(bf16[128,2048]{1,0:T(8,128)(2,1)} %dynamic-slice_convert_fusion.9), channel_id=1, source_target_pairs={{0,2},{1,3},{2,0},{3,1},{4,6},{5,7},{6,4},{7,5},{8,10},{9,11},{10,... | collective-permute-start | bytes 1572872 | tf_op jit(solution)/shard_map/ppermute | solution.py:209
  453.0 23.2 %copy-start.31 = (f32[4096,512]{1,0:T(8,128)S(1)}, f32[4096,512]{1,0:T(8,128)}, u32[]{:S(2)}) copy-start(f32[4096,512]{1,0:T(8,128)} %copy-done.30) | copy-start | bytes 25165828
  476.1 25.6 %collective-permute-start.10 = (bf16[128,2048]{1,0:T(8,128)(2,1)S(1)}, bf16[128,2048]{1,0:T(8,128)(2,1)S(1)}, u32[]{:S(2)}, u32[]{:S(2)}) collective-permute-start(bf16[128,2048]{1,0:T(8,128)(2,1)S(1)} %add_convert_fusion.3), channel_id=1, source_target_pairs={{0,2},{1,3},{2,0},{3,1},{4,6},{5,7},{6,4},{7,5},{8,10},{9,11},{10,... | collective-permute-start | bytes 1572872 | tf_op jit(solution)/shard_map/ppermute | solution.py:214
  478.6 23.1 %copy-start.23 = (f32[2048,512]{1,0:T(8,128)}, f32[2048,512]{1,0:T(8,128)S(1)}, u32[]{:S(2)}) copy-start(f32[2048,512]{1,0:T(8,128)S(1)} %convert_add_fusion.2) | copy-start | bytes 12582916
  478.6 24.2 %copy-start.27 = (f32[512,4,128]{2,1,0:T(4,128)S(1)}, f32[512,4,128]{2,1,0:T(4,128)}, u32[]{:S(2)}) copy-start(f32[512,4,128]{2,1,0:T(4,128)} %reshape.288) | copy-start | bytes 3145732
  478.6 24.2 %copy-start.29 = (f32[512,64]{1,0:T(8,128)S(1)}, f32[512,64]{1,0:T(8,128)}, u32[]{:S(2)}) copy-start(f32[512,64]{1,0:T(8,128)} %copy-done.28) | copy-start | bytes 393220
  478.6 24.2 %copy-start.46 = (f32[512,64]{1,0:T(8,128)S(1)}, f32[512,64]{1,0:T(8,128)}, u32[]{:S(2)}) copy-start(f32[512,64]{1,0:T(8,128)} %get-tuple-element.109) | copy-start | bytes 393220
  479.7 45.4 %collective-permute-start.13 = (bf16[1024,512]{1,0:T(8,128)(2,1)}, bf16[1024,512]{1,0:T(8,128)(2,1)}, u32[]{:S(2)}, u32[]{:S(2)}) collective-permute-start(bf16[1024,512]{1,0:T(8,128)(2,1)} %dynamic-slice_convert_fusion.2), channel_id=1, source_target_pairs={{0,8},{4,12},{8,0},{12,4},{16,24},{20,28},{24,16},{28,20},{1,9},{5... | collective-permute-start | bytes 3145736 | tf_op jit(solution)/shard_map/ppermute | solution.py:242
  502.8 25.9 %collective-permute-start.11 = (bf16[256,2048]{1,0:T(8,128)(2,1)}, bf16[256,2048]{1,0:T(8,128)(2,1)}, u32[]{:S(2)}, u32[]{:S(2)}) collective-permute-start(bf16[256,2048]{1,0:T(8,128)(2,1)} %pad_maximum_fusion.2), channel_id=1, source_target_pairs={{0,1},{1,0},{2,3},{3,2},{4,5},{5,4},{6,7},{7,6},{8,9},{9,8},{10,11... | collective-permute-start | bytes 3145736 | tf_op jit(solution)/shard_map/ppermute | solution.py:214
  527.8 24.1 %collective-permute-start.14 = (bf16[512,512]{1,0:T(8,128)(2,1)S(1)}, bf16[512,512]{1,0:T(8,128)(2,1)S(1)}, u32[]{:S(2)}, u32[]{:S(2)}) collective-permute-start(bf16[512,512]{1,0:T(8,128)(2,1)S(1)} %dynamic-slice_convert_fusion.8), channel_id=1, source_target_pairs={{0,16},{4,20},{8,24},{12,28},{16,0},{20,4},{24,8},{28,12},{1,17},{... | collective-permute-start | bytes 1572872 | tf_op jit(solution)/shard_map/ppermute | solution.py:242
  606.9 5.2 collective-permute-start.28
  608.5 6.4 collective-permute-start.22
  610.7 25.2 %collective-permute-start.15 = (bf16[256,2048]{1,0:T(8,128)(2,1)S(1)}, bf16[256,2048]{1,0:T(8,128)(2,1)S(1)}, u32[]{:S(2)}, u32[]{:S(2)}) collective-permute-start(bf16[256,2048]{1,0:T(8,128)(2,1)S(1)} %dynamic-slice_convert_fusion.1), channel_id=1, source_target_pairs={{0,1},{1,0},{2,3},{3,2},{4,5},{5,4},{6,7},{7,6},{8,9},{9,8},{10,11... | collective-permute-start | bytes 3145736 | tf_op jit(solution)/shard_map/ppermute | solution.py:209
  613.5 22.4 %copy-start.24 = (f32[512,2048]{1,0:T(8,128)S(1)}, f32[512,2048]{1,0:T(8,128)}, u32[]{:S(2)}) copy-start(f32[512,2048]{1,0:T(8,128)} %add_add_fusion.2) | copy-start | bytes 12582916
  613.5 9.2 %collective-permute-start.29 = (bf16[512,256]{1,0:T(8,128)(2,1)S(1)}, bf16[512,256]{1,0:T(8,128)(2,1)S(1)}, u32[]{:S(2)}, u32[]{:S(2)}) collective-permute-start(bf16[512,256]{1,0:T(8,128)(2,1)S(1)} %dynamic-slice_convert_fusion.12), channel_id=1, source_target_pairs={{0,8},{4,12},{8,0},{12,4},{16,24},{20,28},{24,16},{28,20},{1,9},{5... | collective-permute-start | bytes 786440 | tf_op jit(solution)/shard_map/ppermute | solution.py:209
  615.0 12.2 %collective-permute-start.23 = (bf16[512,256]{1,0:T(8,128)(2,1)S(1)}, bf16[512,256]{1,0:T(8,128)(2,1)S(1)}, u32[]{:S(2)}, u32[]{:S(2)}) collective-permute-start(bf16[512,256]{1,0:T(8,128)(2,1)S(1)} %dynamic-slice_convert_fusion.13), channel_id=1, source_target_pairs={{0,8},{4,12},{8,0},{12,4},{16,24},{20,28},{24,16},{28,20},{1,9},{5... | collective-permute-start | bytes 786440 | tf_op jit(solution)/shard_map/ppermute | solution.py:209
  622.9 5.6 collective-permute-start.30
  627.3 5.8 collective-permute-start.24
  628.5 10.0 %collective-permute-start.31 = (bf16[256,256]{1,0:T(8,128)(2,1)S(1)}, bf16[256,256]{1,0:T(8,128)(2,1)S(1)}, u32[]{:S(2)}, u32[]{:S(2)}) collective-permute-start(bf16[256,256]{1,0:T(8,128)(2,1)S(1)} %add_convert_fusion.9), channel_id=1, source_target_pairs={{0,16},{4,20},{8,24},{12,28},{16,0},{20,4},{24,8},{28,12},{1,17},{... | collective-permute-start | bytes 393224 | tf_op jit(solution)/shard_map/ppermute | solution.py:214
  633.1 7.0 collective-permute-start.25
  636.3 25.2 %collective-permute-start.16 = (bf16[128,2048]{1,0:T(8,128)(2,1)S(1)}, bf16[128,2048]{1,0:T(8,128)(2,1)S(1)}, u32[]{:S(2)}, u32[]{:S(2)}) collective-permute-start(bf16[128,2048]{1,0:T(8,128)(2,1)S(1)} %dynamic-slice_convert_fusion.7), channel_id=1, source_target_pairs={{0,2},{1,3},{2,0},{3,1},{4,6},{5,7},{6,4},{7,5},{8,10},{9,11},{10,... | collective-permute-start | bytes 1572872 | tf_op jit(solution)/shard_map/ppermute | solution.py:209
  638.6 23.2 %collective-permute-start.32 = (bf16[512,256]{1,0:T(8,128)(2,1)S(1)}, bf16[512,256]{1,0:T(8,128)(2,1)S(1)}, u32[]{:S(2)}, u32[]{:S(2)}) collective-permute-start(bf16[512,256]{1,0:T(8,128)(2,1)S(1)} %pad_maximum_fusion.15), channel_id=1, source_target_pairs={{0,8},{4,12},{8,0},{12,4},{16,24},{20,28},{24,16},{28,20},{1,9},{5... | collective-permute-start | bytes 786440 | tf_op jit(solution)/shard_map/ppermute | solution.py:214
  640.2 22.6 %collective-permute-start.26 = (bf16[512,256]{1,0:T(8,128)(2,1)S(1)}, bf16[512,256]{1,0:T(8,128)(2,1)S(1)}, u32[]{:S(2)}, u32[]{:S(2)}) collective-permute-start(bf16[512,256]{1,0:T(8,128)(2,1)S(1)} %pad_maximum_fusion.14), channel_id=1, source_target_pairs={{0,8},{4,12},{8,0},{12,4},{16,24},{20,28},{24,16},{28,20},{1,9},{5... | collective-permute-start | bytes 786440 | tf_op jit(solution)/shard_map/ppermute | solution.py:214
  661.7 24.7 %collective-permute-start.17 = (bf16[128,2048]{1,0:T(8,128)(2,1)S(1)}, bf16[128,2048]{1,0:T(8,128)(2,1)S(1)}, u32[]{:S(2)}, u32[]{:S(2)}) collective-permute-start(bf16[128,2048]{1,0:T(8,128)(2,1)S(1)} %add_convert_fusion.1), channel_id=1, source_target_pairs={{0,2},{1,3},{2,0},{3,1},{4,6},{5,7},{6,4},{7,5},{8,10},{9,11},{10,... | collective-permute-start | bytes 1572872 | tf_op jit(solution)/shard_map/ppermute | solution.py:214
  662.8 57.1 %collective-permute-start.33 = (bf16[1024,256]{1,0:T(8,128)(2,1)}, bf16[1024,256]{1,0:T(8,128)(2,1)}, u32[]{:S(2)}, u32[]{:S(2)}) collective-permute-start(bf16[1024,256]{1,0:T(8,128)(2,1)} %pad_maximum_fusion.10), channel_id=1, source_target_pairs={{0,4},{4,0},{8,12},{12,8},{16,20},{20,16},{24,28},{28,24},{1,5},{5... | collective-permute-start | bytes 1572872 | tf_op jit(solution)/shard_map/ppermute | solution.py:214
  663.7 57.5 %collective-permute-start.27 = (bf16[1024,256]{1,0:T(8,128)(2,1)}, bf16[1024,256]{1,0:T(8,128)(2,1)}, u32[]{:S(2)}, u32[]{:S(2)}) collective-permute-start(bf16[1024,256]{1,0:T(8,128)(2,1)} %pad_maximum_fusion.9), channel_id=1, source_target_pairs={{0,4},{4,0},{8,12},{12,8},{16,20},{20,16},{24,28},{28,24},{1,5},{5... | collective-permute-start | bytes 1572872 | tf_op jit(solution)/shard_map/ppermute | solution.py:214
  688.3 35.7 %collective-permute-start.18 = (bf16[256,2048]{1,0:T(8,128)(2,1)}, bf16[256,2048]{1,0:T(8,128)(2,1)}, u32[]{:S(2)}, u32[]{:S(2)}) collective-permute-start(bf16[256,2048]{1,0:T(8,128)(2,1)} %pad_maximum_fusion.4), channel_id=1, source_target_pairs={{0,1},{1,0},{2,3},{3,2},{4,5},{5,4},{6,7},{7,6},{8,9},{9,8},{10,11... | collective-permute-start | bytes 3145736 | tf_op jit(solution)/shard_map/ppermute | solution.py:214
  688.4 1.2 collective-permute-start.34
  689.6 3.7 collective-permute-start.35
  693.3 4.0 collective-permute-start.36
  697.8 16.1 %slice-start.2 = ((s8[5767168]{0:T(1024)(128)(4,1)}), s8[4194304]{0:T(1024)(128)(4,1)S(1)}, s32[]{:S(2)}) async-start(s8[5767168]{0:T(1024)(128)(4,1)} %bitcast.70), calls=%async_computation.6 | async-start | bytes 8388608
  727.3 49.9 %collective-permute-start.19 = (f32[2048]{0:T(1024)S(1)}, f32[2048]{0:T(1024)S(1)}, u32[]{:S(2)}, u32[]{:S(2)}) collective-permute-start(f32[2048]{0:T(1024)S(1)} %get-tuple-element.55), channel_id=1, source_target_pairs={{0,4},{4,0},{8,12},{12,8},{16,20},{20,16},{24,28},{28,24},{1,5},{5... | collective-permute-start | bytes 24584 | tf_op jit(solution)/shard_map/ppermute | solution.py:251
  768.3 13.9 %copy-start.17 = (f32[512,2048]{1,0:T(8,128)S(1)}, f32[512,2048]{1,0:T(8,128)}, u32[]{:S(2)}) copy-start(f32[512,2048]{1,0:T(8,128)} %maximum_convert_fusion.1) | copy-start | bytes 12582916
  768.3 13.9 %copy-start.20 = (bf16[96,2048]{1,0:T(8,128)(2,1)S(1)}, bf16[96,2048]{1,0:T(8,128)(2,1)}, u32[]{:S(2)}) copy-start(bf16[96,2048]{1,0:T(8,128)(2,1)} %copy-done.19) | copy-start | bytes 1179652
  768.3 13.9 %copy-start.22 = (bf16[96,2048]{1,0:T(8,128)(2,1)S(1)}, bf16[96,2048]{1,0:T(8,128)(2,1)}, u32[]{:S(2)}) copy-start(bf16[96,2048]{1,0:T(8,128)(2,1)} %copy-done.21) | copy-start | bytes 1179652
  777.2 3.7 collective-permute-start.20
  780.8 8.9 %collective-permute-start.21 = (f32[2048]{0:T(1024)S(1)}, f32[2048]{0:T(1024)S(1)}, u32[]{:S(2)}, u32[]{:S(2)}) collective-permute-start(f32[2048]{0:T(1024)S(1)} %add.383), channel_id=1, source_target_pairs={{0,16},{4,20},{8,24},{12,28},{16,0},{20,4},{24,8},{28,12},{1,17},{... | collective-permute-start | bytes 24584 | tf_op jit(solution)/shard_map/ppermute | solution.py:251
  (61 other events, 269.1 us)
Sparse Core Ops, SparseCore 0:
  22.1 39.2 all-gather.2
  134.0 68.9 all-reduce.5
  335.2 249.1 all-reduce.9
  688.5 79.7 all-reduce.7

commit v9 on v5

--- a/solution.py
+++ b/solution.py
@@ -402,15 +402,18 @@
         + right_trans(d_key_low, w_key)
         + right_trans(d_value_low, w_value)
     )
+    unit_normed = source * lax.rsqrt(jnp.mean(source * source, axis=-1, keepdims=True) + EPS)
+    grad_gain_one = jnp.sum(d_normed_part * unit_normed, axis=0)
     (
         down_sum,
         d_normed_part,
+        grad_gain_one,
         grad_w_out,
         grad_w_query,
         grad_w_key,
         grad_w_value,
     ) = lax.optimization_barrier(
-        (down_sum, d_normed_part, grad_w_out, grad_w_query, grad_w_key, grad_w_value)
+        (down_sum, d_normed_part, grad_gain_one, grad_w_out, grad_w_query, grad_w_key, grad_w_value)
     )
     grad_w_out, grad_w_query, grad_w_key, grad_w_value = dp_sum(
         [grad_w_out, grad_w_query, grad_w_key, grad_w_value]
@@ -419,10 +422,10 @@
         grad.astype(jnp.float32) for grad in (grad_w_gate, grad_w_up, grad_w_down)
     ]
     output = (middle + keep_rows * down_sum).astype(jnp.bfloat16)
+    grad_gain_one = permute_allsum(permute_allsum(grad_gain_one, "dp"), "tensor")
     (d_normed,) = permute_sum([d_normed_part], [0], "tensor")
-    d_source_norm, grad_gain_one = norm_one_back(d_normed)
+    d_source_norm, _ = norm_one_back(d_normed)
     grad_input = grad_middle + d_source_norm
-    grad_gain_one = permute_allsum(grad_gain_one, "dp")
     grad_gain_two = permute_allsum(grad_gain_two, "dp")
     grad_w_out, grad_w_query, grad_w_key, grad_w_value = [
         grad.astype(jnp.float32) for grad in (grad_w_out, grad_w_query, grad_w_key, grad_w_value)

time: 767 us -> 744 us (0.970)
  waiting for transfers between devices: 399 us -> 363 us
    psum x2, waiting for transfers between devices: 34.5 us -> 6.78 us  [dp_sum(): return [lax.psum(grad.astype(jnp.bfloat16), 'dp') for grad in grads]]
    ppermute x8, waiting for transfers between devices: 150 us -> 133 us  [permute_sum(): got = lax.ppermute(pieces, axis, partner_perm(size, 1 << step))]
    ppermute x6 -> x8, waiting for transfers between devices: 5.89 us -> 16 us  [permute_allsum(): value = value + lax.ppermute(value, axis, partner_perm(size, 1 << step))]
  transfers between devices with their start and end apart: 27 -> 29, of which waited for: 22 -> 22; matrix products, arithmetic and copies ran while one was open for 16% -> 15% of each run, Pallas kernels for 9% -> 9%
where the time goes in v9:
time: 744 us; the launch traced here: 739 us
  waiting for transfers between devices  363 us (49%)
  matrix products  119 us (16%)
  other arithmetic  108 us (15%)
  Pallas kernels  68.6 us (9%)
  local copies, waits for them, and re-layouts  31.9 us (4%)
  starting transfers between devices  21.6 us (3%)
  between operations  15.3 us (2%)
  blocking collectives  10.6 us (1%)
    ppermute x8, waiting for transfers between devices, permute_sum(): got = lax.ppermute(send, axis, partner_perm(size, 1 << step))  159 us
    ppermute x8, waiting for transfers between devices, permute_sum(): got = lax.ppermute(pieces, axis, partner_perm(size, 1 << step))  133 us
    pallas_call x1, Pallas kernels, attention_backward(): pl.pallas_call(kernel, grid_spec=grid_spec, out_shape=[jax.ShapeDtypeStru...  68.6 us
    dot_general x11, matrix products, right_trans(): lax.dot_general(left, right, (((1,), (1,)), ((), ())), preferred_element_...  47.6 us
    psum x1, waiting for transfers between devices, on_device(): branch_top = lax.psum(branch_part[:sc_rows].astype(jnp.bfloat16), 'tensor')  31 us
    convert_element_type x7, other arithmetic, on_device(): grad.astype(jnp.float32)  29.6 us
    dot_general x7, matrix products, left_trans(): lax.dot_general(left, right, (((0,), (0,)), ((), ())), preferred_element_...  28.6 us
    all_gather x1, waiting for transfers between devices, on_device(): lax.all_gather(jnp.concatenate([key_low, value_low], axis=1), 'dp', axis=...  18.1 us
  transfers between devices with their start and end apart: 29, of which 22 were waited for; matrix products, arithmetic and copies ran while one was open for 15% of the time, Pallas kernels for 9%

profile of v9, /device:TPU:0, one launch (start us, length us, event | category | flops | bytes accessed | tf_op | source)
XLA Modules:
  0.0 739.1 jit_solution(1151870077007211238)
XLA Ops:
  12.3 3.3 convolution_convert_fusion.1
  22.0 10.6 %all-gather = bf16[8,1,512]{2,1,0:T(2,128)(2,1)S(1)} all-gather(bf16[1,1,512]{2,1,0:T(2,128)(2,1)S(1)} %reshape.288), channel_id=1, replica_groups=mesh['dp'=8,'tensor'=4] {'dp'}, dimensions={0}, use_global_device_ids=true | all-gather | bytes 9216 | tf_op jit(solution)/shard_map/all_gather | solution.py:289
  32.7 3.1 fusion.70
  43.3 18.1 %all-gather.3.cloned.1.call-done.k_ref.v_ref = bf16[4096,512]{1,0:T(8,128)(2,1)} async-done(((bf16[512,512]{1,0:T(8,128)(2,1)}), bf16[4096,512]{1,0:T(8,128)(2,1)}) %all-gather.3.cloned.1.call-update) | async-done | bytes 4194320 | tf_op jit(solution)/shard_map/all_gather | solution.py:286
  61.3 4.6 fusion.76
  67.2 4.6 fusion.77
  73.5 4.6 fusion.78
  79.4 6.9 fusion.79
  86.2 4.6 fusion.2
  90.9 3.2 fusion.22
  94.1 3.4 fusion.23
  97.6 3.4 fusion.24
  101.0 3.4 fusion.25
  104.4 3.3 fusion.56
  112.0 9.8 %collective-permute-done = bf16[96,2048]{1,0:T(8,128)(2,1)S(1)} collective-permute-done((bf16[96,2048]{1,0:T(8,128)(2,1)S(1)}, bf16[96,2048]{1,0:T(8,128)(2,1)S(1)}, u32[]{:S(2)}, u32[]{:S(2)}) %collective-permute-start) | collective-permute-done | bytes 393248 | tf_op jit(solution)/shard_map/ppermute | solution.py:209
  123.0 2.5 collective-permute-start.1
  125.5 8.9 %collective-permute-done.1 = bf16[48,2048]{1,0:T(8,128)(2,1)S(1)} collective-permute-done((bf16[48,2048]{1,0:T(8,128)(2,1)S(1)}, bf16[48,2048]{1,0:T(8,128)(2,1)S(1)}, u32[]{:S(2)}, u32[]{:S(2)}) %collective-permute-start.1) | collective-permute-done | bytes 196640 | tf_op jit(solution)/shard_map/ppermute | solution.py:209
  134.5 3.0 slice.147
  137.8 7.8 %collective-permute-done.2 = bf16[48,2048]{1,0:T(8,128)(2,1)S(1)} collective-permute-done((bf16[48,2048]{1,0:T(8,128)(2,1)S(1)}, bf16[48,2048]{1,0:T(8,128)(2,1)S(1)}, u32[]{:S(2)}, u32[]{:S(2)}) %collective-permute-start.2) | collective-permute-done | bytes 196640 | tf_op jit(solution)/shard_map/ppermute | solution.py:214
  145.7 8.3 %fusion.36 = f32[512,1408]{1,0:T(8,128)} fusion(bf16[1408,2048]{1,0:T(8,128)(2,1)} %param.24, bf16[512,2048]{1,0:T(8,128)(2,1)} %param.25, f32[512]{0:T(512)S(1)} %get-tuple-element.102), kind=kOutput, calls=%fused_computation.103 | convolution fusion | flops 2955935744 | bytes 10749952 | tf_op jit(solution)/shard_map/dot_general | solution.py:49
  154.0 20.5 %collective-permute-done.3 = bf16[96,2048]{1,0:T(8,128)(2,1)} collective-permute-done((bf16[96,2048]{1,0:T(8,128)(2,1)S(1)}, bf16[96,2048]{1,0:T(8,128)(2,1)}, u32[]{:S(2)}, u32[]{:S(2)}) %collective-permute-start.3) | collective-permute-done | bytes 393248 | tf_op jit(solution)/shard_map/ppermute | solution.py:214
  175.7 31.0 %all-reduce.6.cloned.1.call-done = bf16[320,2048]{1,0:T(8,128)(2,1)} async-done(((bf16[320,2048]{1,0:T(8,128)(2,1)}), bf16[320,2048]{1,0:T(8,128)(2,1)}) %all-reduce.6.cloned.1.call-update) | async-done | bytes 1310736 | tf_op jit(solution)/shard_map/psum | solution.py:330
  206.7 3.1 multiply_reduce_fusion.2
  209.9 3.3 multiply_convert_fusion.1
  213.2 5.9 fusion.80
  219.2 4.7 multiply_convert_fusion.2
  223.9 3.4 fusion.84
  227.4 5.3 fusion.82
  232.7 5.5 fusion.83
  238.2 5.0 convolution_add_fusion
  243.2 5.1 fusion.34
  248.4 2.7 dynamic-slice_convert_fusion.2
  252.6 23.8 %collective-permute-done.4 = bf16[256,2048]{1,0:T(8,128)(2,1)} collective-permute-done((bf16[256,2048]{1,0:T(8,128)(2,1)}, bf16[256,2048]{1,0:T(8,128)(2,1)}, u32[]{:S(2)}, u32[]{:S(2)}) %collective-permute-start.4) | collective-permute-done | bytes 1048608 | tf_op jit(solution)/shard_map/ppermute | solution.py:209
  283.5 22.4 %collective-permute-done.5 = bf16[128,2048]{1,0:T(8,128)(2,1)} collective-permute-done((bf16[128,2048]{1,0:T(8,128)(2,1)}, bf16[128,2048]{1,0:T(8,128)(2,1)}, u32[]{:S(2)}, u32[]{:S(2)}) %collective-permute-start.5) | collective-permute-done | bytes 524320 | tf_op jit(solution)/shard_map/ppermute | solution.py:209
  310.1 23.0 %collective-permute-done.6 = bf16[128,2048]{1,0:T(8,128)(2,1)} collective-permute-done((bf16[128,2048]{1,0:T(8,128)(2,1)}, bf16[128,2048]{1,0:T(8,128)(2,1)}, u32[]{:S(2)}, u32[]{:S(2)}) %collective-permute-start.6) | collective-permute-done | bytes 524320 | tf_op jit(solution)/shard_map/ppermute | solution.py:214
  338.3 8.6 %fusion.81 = f32[512,2048]{1,0:T(8,128)} fusion(bf16[512,1408]{1,0:T(8,128)(2,1)} %copy-done.65, bf16[1408,2048]{1,0:T(8,128)(2,1)} %param.24), kind=kOutput, calls=%fused_computation.185 | convolution fusion | flops 2952790016 | bytes 11403264 | tf_op jit(solution)/shard_map/dot_general | solution.py:340
  346.9 14.7 %collective-permute-done.7 = bf16[256,2048]{1,0:T(8,128)(2,1)} collective-permute-done((bf16[256,2048]{1,0:T(8,128)(2,1)}, bf16[256,2048]{1,0:T(8,128)(2,1)}, u32[]{:S(2)}, u32[]{:S(2)}) %collective-permute-start.7) | collective-permute-done | bytes 1048608 | tf_op jit(solution)/shard_map/ppermute | solution.py:214
  365.4 3.2 multiply_reduce_fusion
  368.7 3.8 convert_add_fusion.1
  374.3 68.6 %shard_map.212 = (f32[512,512]{1,0:T(8,128)S(1)}, f32[4096,256]{1,0:T(8,128)}, f32[4096,256]{1,0:T(8,128)}) custom-call(s32[16]{0:T(128)S(1)} %copy-done.4, s32[2]{0:T(128)S(1)} %dynamic_slice.67.qblock_ref, bf16[512,512]{1,0:T(8,128)(2,1)S(1)} %bitcast.67, bf16[4096,512]{1,0:T(8,128)(2,1)} %all-gather.3.cloned.1.call-done.k_ref.v_ref, ...), custom_call_target="tpu_custom_call" | custom-call | flops 10737418240 | bytes 25165824 | tf_op jit(solution)/shard_map/pallas_call | solution.py:173
  442.9 2.6 convert.61
  451.7 23.7 %collective-permute-done.8 = bf16[256,2048]{1,0:T(8,128)(2,1)S(1)} collective-permute-done((bf16[256,2048]{1,0:T(8,128)(2,1)S(1)}, bf16[256,2048]{1,0:T(8,128)(2,1)S(1)}, u32[]{:S(2)}, u32[]{:S(2)}) %collective-permute-start.8) | collective-permute-done | bytes 1048608 | tf_op jit(solution)/shard_map/ppermute | solution.py:209
  479.1 22.7 %collective-permute-done.9 = bf16[128,2048]{1,0:T(8,128)(2,1)S(1)} collective-permute-done((bf16[128,2048]{1,0:T(8,128)(2,1)S(1)}, bf16[128,2048]{1,0:T(8,128)(2,1)S(1)}, u32[]{:S(2)}, u32[]{:S(2)}) %collective-permute-start.9) | collective-permute-done | bytes 524320 | tf_op jit(solution)/shard_map/ppermute | solution.py:209
  504.1 24.7 %collective-permute-done.10 = bf16[128,2048]{1,0:T(8,128)(2,1)} collective-permute-done((bf16[128,2048]{1,0:T(8,128)(2,1)}, bf16[128,2048]{1,0:T(8,128)(2,1)}, u32[]{:S(2)}, u32[]{:S(2)}) %collective-permute-start.10) | collective-permute-done | bytes 524320 | tf_op jit(solution)/shard_map/ppermute | solution.py:214
  532.4 2.7 fusion.55
  535.1 2.8 fusion.38
  537.9 17.3 %collective-permute-done.11 = bf16[256,2048]{1,0:T(8,128)(2,1)S(1)} collective-permute-done((bf16[256,2048]{1,0:T(8,128)(2,1)S(1)}, bf16[256,2048]{1,0:T(8,128)(2,1)S(1)}, u32[]{:S(2)}, u32[]{:S(2)}) %collective-permute-start.11) | collective-permute-done | bytes 1048608 | tf_op jit(solution)/shard_map/ppermute | solution.py:214
  555.8 2.6 maximum_convert_fusion.1
  560.4 3.6 fusion.54
  564.0 2.8 fusion.53
  569.6 3.6 fusion.43
  575.3 4.0 fusion.9
  579.8 23.7 %collective-permute-done.12 = bf16[256,2048]{1,0:T(8,128)(2,1)S(1)} collective-permute-done((bf16[256,2048]{1,0:T(8,128)(2,1)S(1)}, bf16[256,2048]{1,0:T(8,128)(2,1)S(1)}, u32[]{:S(2)}, u32[]{:S(2)}) %collective-permute-start.12) | collective-permute-done | bytes 1048608 | tf_op jit(solution)/shard_map/ppermute | solution.py:209
  606.0 23.4 %collective-permute-done.13 = bf16[128,2048]{1,0:T(8,128)(2,1)S(1)} collective-permute-done((bf16[128,2048]{1,0:T(8,128)(2,1)S(1)}, bf16[128,2048]{1,0:T(8,128)(2,1)S(1)}, u32[]{:S(2)}, u32[]{:S(2)}) %collective-permute-start.13) | collective-permute-done | bytes 524320 | tf_op jit(solution)/shard_map/ppermute | solution.py:209
  630.8 24.8 %collective-permute-done.14 = bf16[128,2048]{1,0:T(8,128)(2,1)S(1)} collective-permute-done((bf16[128,2048]{1,0:T(8,128)(2,1)S(1)}, bf16[128,2048]{1,0:T(8,128)(2,1)S(1)}, u32[]{:S(2)}, u32[]{:S(2)}) %collective-permute-start.14) | collective-permute-done | bytes 524320 | tf_op jit(solution)/shard_map/ppermute | solution.py:214
  669.6 12.6 %collective-permute-done.19 = f32[2048]{0:T(1024)S(1)} collective-permute-done((f32[2048]{0:T(1024)S(1)}, f32[2048]{0:T(1024)S(1)}, u32[]{:S(2)}, u32[]{:S(2)}) %collective-permute-start.19) | collective-permute-done | bytes 8224 | tf_op jit(solution)/shard_map/ppermute | solution.py:228
  683.7 8.4 %convert_element_type.259 = f32[2048,1408]{1,0:T(8,128)} convert(bf16[2048,1408]{1,0:T(8,128)(2,1)} %get-tuple-element.52) | non-fusion elementwise | flops 2883584 | bytes 17301504 | tf_op jit(solution)/shard_map/convert_element_type | solution.py:422
  692.2 5.2 convert_element_type.260
  697.3 6.0 convert_element_type.261
  704.0 6.8 all-reduce.8.cloned.1.call-done
  710.7 4.3 convert_element_type.252
  718.1 2.7 convert_element_type.258
  720.8 2.5 broadcast_select_fusion.1
  724.5 7.9 %fusion.11 = (f32[512,2048]{1,0:T(8,128)}, bf16[512,2048]{1,0:T(8,128)(2,1)}) fusion(f32[512,2048]{1,0:T(8,128)S(1)} %copy-done.13, bf16[512,2048]{1,0:T(8,128)(2,1)S(1)} %copy-done.10, f32[512]{0:T(512)S(1)} %multiply_multiply_fusion, f32[2048]{0:T(1024)S(1)} %copy-done.56, f32[512]{0:T(512)S(1)} %copy-done.59, bf16[256,2048]{1,0:T(8,128)(2,1)S(1)} %get-tuple-element.74, ...), kind=kLoop, calls=%fused_computation.34 | loop fusion | flops 23068672 | bytes 20985856 | tf_op jit(solution)/shard_map/add | solution.py:428
  (300 shorter events, 101.4 us)
Async XLA Ops:
  7.2 25.5 %copy-start = (bf16[2048,512]{1,0:T(8,128)(2,1)S(1)}, bf16[2048,512]{1,0:T(8,128)(2,1)}, u32[]{:S(2)}) copy-start(bf16[2048,512]{1,0:T(8,128)(2,1)} %param.17) | copy-start | bytes 6291460
  7.2 8.4 %copy-start.45 = (bf16[2048,256]{1,0:T(8,128)(2,1)S(1)}, bf16[2048,256]{1,0:T(8,128)(2,1)}, u32[]{:S(2)}) copy-start(bf16[2048,256]{1,0:T(8,128)(2,1)} %param.18) | copy-start | bytes 3145732
  7.2 54.1 %all-gather.3.cloned.1.call-start = ((), (), s32[]{:S(2)}) async-start(), calls=%async_computation.1 | async-start | bytes 4718592 | tf_op jit(solution)/shard_map/all_gather | solution.py:286
  7.3 8.4 %copy-start.5 = (bf16[512,2048]{1,0:T(8,128)(2,1)S(1)}, bf16[512,2048]{1,0:T(8,128)(2,1)}, u32[]{:S(2)}) copy-start(bf16[512,2048]{1,0:T(8,128)(2,1)} %param.13) | copy-start | bytes 6291460
  10.9 21.7 %copy-start.58 = (f32[512]{0:T(512)}, f32[512]{0:T(512)S(1)}, u32[]{:S(2)}) copy-start(f32[512]{0:T(512)S(1)} %fusion.60) | copy-start | bytes 6148
  11.6 21.0 %copy-start.55 = (f32[2048]{0:T(1024)}, f32[2048]{0:T(1024)S(1)}, u32[]{:S(2)}) copy-start(f32[2048]{0:T(1024)S(1)} %convert_element_type.202) | copy-start | bytes 24580
  16.6 5.3 copy-start.63
  19.0 21.7 %copy-start.23 = (f32[512,64]{1,0:T(8,128)}, f32[512,64]{1,0:T(8,128)S(1)}, u32[]{:S(2)}) copy-start(f32[512,64]{1,0:T(8,128)S(1)} %get-tuple-element.101) | copy-start | bytes 393220
  21.9 184.9 %all-reduce.6.cloned.1.call-start = ((), (), s32[]{:S(2)}) async-start(), calls=%async_computation.2 | async-start | bytes 2621440 | tf_op jit(solution)/shard_map/psum | solution.py:330
  43.3 36.1 %copy-start.1 = (bf16[64,8,4,128]{3,1,2,0:T(8,128)(2,1)}, bf16[64,8,4,128]{3,1,2,0:T(8,128)(2,1)S(1)}, u32[]{:S(2)}) copy-start(bf16[64,8,4,128]{3,1,2,0:T(8,128)(2,1)S(1)} %copy.92) | copy-start | bytes 1572868
  94.1 10.3 %copy-start.46 = (bf16[512,128]{0,1:T(8,128)(2,1)}, bf16[512,128]{0,1:T(8,128)(2,1)S(1)}, u32[]{:S(2)}) copy-start(bf16[512,128]{0,1:T(8,128)(2,1)S(1)} %fusion.22) | copy-start | bytes 393220
  94.1 6.8 slice-start
  97.5 6.9 copy-start.48
  110.5 11.3 %collective-permute-start = (bf16[96,2048]{1,0:T(8,128)(2,1)S(1)}, bf16[96,2048]{1,0:T(8,128)(2,1)S(1)}, u32[]{:S(2)}, u32[]{:S(2)}) collective-permute-start(bf16[96,2048]{1,0:T(8,128)(2,1)S(1)} %dynamic-slice_convert_fusion.6), channel_id=1, source_target_pairs={{0,1},{1,0},{2,3},{3,2},{4,5},{5,4},{6,7},{7,6},{8,9},{9,8},{10,11... | collective-permute-start | bytes 1179656 | tf_op jit(solution)/shard_map/ppermute | solution.py:209
  123.0 11.4 %collective-permute-start.1 = (bf16[48,2048]{1,0:T(8,128)(2,1)S(1)}, bf16[48,2048]{1,0:T(8,128)(2,1)S(1)}, u32[]{:S(2)}, u32[]{:S(2)}) collective-permute-start(bf16[48,2048]{1,0:T(8,128)(2,1)S(1)} %dynamic-slice_convert_fusion.7), channel_id=1, source_target_pairs={{0,2},{1,3},{2,0},{3,1},{4,6},{5,7},{6,4},{7,5},{8,10},{9,11},{10,... | collective-permute-start | bytes 589832 | tf_op jit(solution)/shard_map/ppermute | solution.py:209
  134.5 11.1 %collective-permute-start.2 = (bf16[48,2048]{1,0:T(8,128)(2,1)S(1)}, bf16[48,2048]{1,0:T(8,128)(2,1)S(1)}, u32[]{:S(2)}, u32[]{:S(2)}) collective-permute-start(bf16[48,2048]{1,0:T(8,128)(2,1)S(1)} %add_convert_fusion.8), channel_id=1, source_target_pairs={{0,2},{1,3},{2,0},{3,1},{4,6},{5,7},{6,4},{7,5},{8,10},{9,11},{10,... | collective-permute-start | bytes 589832 | tf_op jit(solution)/shard_map/ppermute | solution.py:214
  137.6 420.8 %all-reduce.10.cloned.1.call-start = ((), (), s32[]{:S(2)}) async-start(), calls=%async_computation.5 | async-start | bytes 34603008 | tf_op jit(solution)/shard_map/psum | solution.py:344
  145.6 28.9 %collective-permute-start.3 = (bf16[96,2048]{1,0:T(8,128)(2,1)S(1)}, bf16[96,2048]{1,0:T(8,128)(2,1)}, u32[]{:S(2)}, u32[]{:S(2)}) collective-permute-start(bf16[96,2048]{1,0:T(8,128)(2,1)S(1)} %pad_maximum_fusion.10), channel_id=1, source_target_pairs={{0,1},{1,0},{2,3},{3,2},{4,5},{5,4},{6,7},{7,6},{8,9},{9,8},{10,11... | collective-permute-start | bytes 1179656 | tf_op jit(solution)/shard_map/ppermute | solution.py:214
  145.7 8.3 %copy-start.62 = (bf16[2048]{0:T(1024)(128)(2,1)S(1)}, bf16[2048]{0:T(1024)(128)(2,1)}, u32[]{:S(2)}) copy-start(bf16[2048]{0:T(1024)(128)(2,1)} %param.21) | copy-start | bytes 12292
  175.7 193.0 %copy-start.18 = (bf16[96,2048]{1,0:T(8,128)(2,1)}, bf16[96,2048]{1,0:T(8,128)(2,1)S(1)}, u32[]{:S(2)}) copy-start(bf16[96,2048]{1,0:T(8,128)(2,1)S(1)} %get-tuple-element.93) | copy-start | bytes 1179652
  175.7 193.0 %copy-start.20 = (bf16[96,2048]{1,0:T(8,128)(2,1)}, bf16[96,2048]{1,0:T(8,128)(2,1)S(1)}, u32[]{:S(2)}) copy-start(bf16[96,2048]{1,0:T(8,128)(2,1)S(1)} %get-tuple-element.94) | copy-start | bytes 1179652
  209.9 9.3 %slice-start.6 = ((s8[5767168]{0:T(1024)(128)(4,1)}), s8[4194304]{0:T(1024)(128)(4,1)S(1)}, s32[]{:S(2)}) async-start(s8[5767168]{0:T(1024)(128)(4,1)} %bitcast.101), calls=%async_computation.12 | async-start | bytes 8388608
  213.2 6.0 slice-start.7
  213.2 6.0 copy-start.64
  223.9 19.3 %copy-start.65 = (bf16[512,1408]{1,0:T(8,128)(2,1)}, bf16[512,1408]{1,0:T(8,128)(2,1)S(1)}, u32[]{:S(2)}) copy-start(bf16[512,1408]{1,0:T(8,128)(2,1)S(1)} %get-tuple-element.68) | copy-start | bytes 4325380
  227.3 10.9 %slice-start.8 = ((s8[5767168]{0:T(1024)(128)(4,1)}), s8[4194304]{0:T(1024)(128)(4,1)S(1)}, s32[]{:S(2)}) async-start(s8[5767168]{0:T(1024)(128)(4,1)} %bitcast.103), calls=%async_computation.14 | async-start | bytes 8388608
  232.7 5.5 slice-start.9
  251.1 25.4 %collective-permute-start.4 = (bf16[256,2048]{1,0:T(8,128)(2,1)}, bf16[256,2048]{1,0:T(8,128)(2,1)}, u32[]{:S(2)}, u32[]{:S(2)}) collective-permute-start(bf16[256,2048]{1,0:T(8,128)(2,1)} %dynamic-slice_convert_fusion.2), channel_id=1, source_target_pairs={{0,1},{1,0},{2,3},{3,2},{4,5},{5,4},{6,7},{7,6},{8,9},{9,8},{10,11... | collective-permute-start | bytes 3145736 | tf_op jit(solution)/shard_map/ppermute | solution.py:209
  252.5 29.9 %copy-start.4 = (s32[16]{0:T(128)S(1)}, s32[16]{0:T(128)}, u32[]{:S(2)}) copy-start(s32[16]{0:T(128)} %chunk_ref.1) | copy-start | bytes 196
  252.6 30.0 %copy-start.57 = (s32[1,1,16,256]{3,2,1,0:T(8,128)S(1)}, s32[1,1,16,256]{3,2,1,0:T(8,128)}, u32[]{:S(2)}) copy-start(s32[1,1,16,256]{3,2,1,0:T(8,128)} %get-tuple-element.104) | copy-start | bytes 49156
  252.6 305.8 %reduce-scatter.2.cloned.1.call-start = ((), (), s32[]{:S(2)}) async-start(), calls=%async_computation.3 | async-start | bytes 4718592 | tf_op jit(solution)/shard_map/reduce_scatter | solution.py:376
  280.8 25.0 %collective-permute-start.5 = (bf16[128,2048]{1,0:T(8,128)(2,1)}, bf16[128,2048]{1,0:T(8,128)(2,1)}, u32[]{:S(2)}, u32[]{:S(2)}) collective-permute-start(bf16[128,2048]{1,0:T(8,128)(2,1)} %dynamic-slice_convert_fusion.5), channel_id=1, source_target_pairs={{0,2},{1,3},{2,0},{3,1},{4,6},{5,7},{6,4},{7,5},{8,10},{9,11},{10,... | collective-permute-start | bytes 1572872 | tf_op jit(solution)/shard_map/ppermute | solution.py:209
  308.2 24.9 %collective-permute-start.6 = (bf16[128,2048]{1,0:T(8,128)(2,1)}, bf16[128,2048]{1,0:T(8,128)(2,1)}, u32[]{:S(2)}, u32[]{:S(2)}) collective-permute-start(bf16[128,2048]{1,0:T(8,128)(2,1)} %add_convert_fusion.4), channel_id=1, source_target_pairs={{0,2},{1,3},{2,0},{3,1},{4,6},{5,7},{6,4},{7,5},{8,10},{9,11},{10,... | collective-permute-start | bytes 1572872 | tf_op jit(solution)/shard_map/ppermute | solution.py:214
  336.3 25.4 %collective-permute-start.7 = (bf16[256,2048]{1,0:T(8,128)(2,1)}, bf16[256,2048]{1,0:T(8,128)(2,1)}, u32[]{:S(2)}, u32[]{:S(2)}) collective-permute-start(bf16[256,2048]{1,0:T(8,128)(2,1)} %pad_maximum_fusion.2), channel_id=1, source_target_pairs={{0,1},{1,0},{2,3},{3,2},{4,5},{5,4},{6,7},{7,6},{8,9},{9,8},{10,11... | collective-permute-start | bytes 3145736 | tf_op jit(solution)/shard_map/ppermute | solution.py:214
  338.3 23.4 %copy-start.29 = (bf16[128,2048]{1,0:T(8,128)(2,1)S(1)}, bf16[128,2048]{1,0:T(8,128)(2,1)}, u32[]{:S(2)}) copy-start(bf16[128,2048]{1,0:T(8,128)(2,1)} %copy-done.28) | copy-start | bytes 1572868
  338.3 23.3 %copy-start.31 = (bf16[128,2048]{1,0:T(8,128)(2,1)S(1)}, bf16[128,2048]{1,0:T(8,128)(2,1)}, u32[]{:S(2)}) copy-start(bf16[128,2048]{1,0:T(8,128)(2,1)} %copy-done.30) | copy-start | bytes 1572868
  372.6 70.2 %copy-start.11 = (f32[512,2048]{1,0:T(8,128)}, f32[512,2048]{1,0:T(8,128)S(1)}, u32[]{:S(2)}) copy-start(f32[512,2048]{1,0:T(8,128)S(1)} %convert_add_fusion.1) | copy-start | bytes 12582916
  449.0 261.8 %all-reduce.8.cloned.1.call-start = ((), (), s32[]{:S(2)}) async-start(), calls=%async_computation.4 | async-start | bytes 12582912 | tf_op jit(solution)/shard_map/psum | solution.py:344
  451.1 24.3 %collective-permute-start.8 = (bf16[256,2048]{1,0:T(8,128)(2,1)S(1)}, bf16[256,2048]{1,0:T(8,128)(2,1)S(1)}, u32[]{:S(2)}, u32[]{:S(2)}) collective-permute-start(bf16[256,2048]{1,0:T(8,128)(2,1)S(1)} %dynamic-slice_convert_fusion.1), channel_id=1, source_target_pairs={{0,1},{1,0},{2,3},{3,2},{4,5},{5,4},{6,7},{7,6},{8,9},{9,8},{10,11... | collective-permute-start | bytes 3145736 | tf_op jit(solution)/shard_map/ppermute | solution.py:209
  477.4 52.9 %copy-start.24 = (f32[512,64]{1,0:T(8,128)S(1)}, f32[512,64]{1,0:T(8,128)}, u32[]{:S(2)}) copy-start(f32[512,64]{1,0:T(8,128)} %copy-done.23) | copy-start | bytes 393220
  477.4 24.5 %collective-permute-start.9 = (bf16[128,2048]{1,0:T(8,128)(2,1)S(1)}, bf16[128,2048]{1,0:T(8,128)(2,1)S(1)}, u32[]{:S(2)}, u32[]{:S(2)}) collective-permute-start(bf16[128,2048]{1,0:T(8,128)(2,1)S(1)} %dynamic-slice_convert_fusion.4), channel_id=1, source_target_pairs={{0,2},{1,3},{2,0},{3,1},{4,6},{5,7},{6,4},{7,5},{8,10},{9,11},{10,... | collective-permute-start | bytes 1572872 | tf_op jit(solution)/shard_map/ppermute | solution.py:209
  502.8 26.0 %collective-permute-start.10 = (bf16[128,2048]{1,0:T(8,128)(2,1)}, bf16[128,2048]{1,0:T(8,128)(2,1)}, u32[]{:S(2)}, u32[]{:S(2)}) collective-permute-start(bf16[128,2048]{1,0:T(8,128)(2,1)} %add_convert_fusion.3), channel_id=1, source_target_pairs={{0,2},{1,3},{2,0},{3,1},{4,6},{5,7},{6,4},{7,5},{8,10},{9,11},{10,... | collective-permute-start | bytes 1572872 | tf_op jit(solution)/shard_map/ppermute | solution.py:214
  504.1 26.2 %copy-start.22 = (f32[512,4,128]{2,1,0:T(4,128)S(1)}, f32[512,4,128]{2,1,0:T(4,128)}, u32[]{:S(2)}) copy-start(f32[512,4,128]{2,1,0:T(4,128)} %reshape.285) | copy-start | bytes 3145732
  504.1 26.2 %copy-start.33 = (f32[512,64]{1,0:T(8,128)S(1)}, f32[512,64]{1,0:T(8,128)}, u32[]{:S(2)}) copy-start(f32[512,64]{1,0:T(8,128)} %get-tuple-element.99) | copy-start | bytes 393220
  530.3 25.0 %collective-permute-start.11 = (bf16[256,2048]{1,0:T(8,128)(2,1)S(1)}, bf16[256,2048]{1,0:T(8,128)(2,1)S(1)}, u32[]{:S(2)}, u32[]{:S(2)}) collective-permute-start(bf16[256,2048]{1,0:T(8,128)(2,1)S(1)} %pad_maximum_fusion.3), channel_id=1, source_target_pairs={{0,1},{1,0},{2,3},{3,2},{4,5},{5,4},{6,7},{7,6},{8,9},{9,8},{10,11... | collective-permute-start | bytes 3145736 | tf_op jit(solution)/shard_map/ppermute | solution.py:214
  532.4 5.5 copy-start.36
  558.4 5.7 copy-start.44
  579.5 24.1 %collective-permute-start.12 = (bf16[256,2048]{1,0:T(8,128)(2,1)S(1)}, bf16[256,2048]{1,0:T(8,128)(2,1)S(1)}, u32[]{:S(2)}, u32[]{:S(2)}) collective-permute-start(bf16[256,2048]{1,0:T(8,128)(2,1)S(1)} %dynamic-slice_convert_fusion), channel_id=1, source_target_pairs={{0,1},{1,0},{2,3},{3,2},{4,5},{5,4},{6,7},{7,6},{8,9},{9,8},{10,11... | collective-permute-start | bytes 3145736 | tf_op jit(solution)/shard_map/ppermute | solution.py:209
  605.2 24.1 %collective-permute-start.13 = (bf16[128,2048]{1,0:T(8,128)(2,1)S(1)}, bf16[128,2048]{1,0:T(8,128)(2,1)S(1)}, u32[]{:S(2)}, u32[]{:S(2)}) collective-permute-start(bf16[128,2048]{1,0:T(8,128)(2,1)S(1)} %dynamic-slice_convert_fusion.3), channel_id=1, source_target_pairs={{0,2},{1,3},{2,0},{3,1},{4,6},{5,7},{6,4},{7,5},{8,10},{9,11},{10,... | collective-permute-start | bytes 1572872 | tf_op jit(solution)/shard_map/ppermute | solution.py:209
  630.7 24.9 %collective-permute-start.14 = (bf16[128,2048]{1,0:T(8,128)(2,1)S(1)}, bf16[128,2048]{1,0:T(8,128)(2,1)S(1)}, u32[]{:S(2)}, u32[]{:S(2)}) collective-permute-start(bf16[128,2048]{1,0:T(8,128)(2,1)S(1)} %add_convert_fusion.1), channel_id=1, source_target_pairs={{0,2},{1,3},{2,0},{3,1},{4,6},{5,7},{6,4},{7,5},{8,10},{9,11},{10,... | collective-permute-start | bytes 1572872 | tf_op jit(solution)/shard_map/ppermute | solution.py:214
  655.7 36.5 %slice-start.4 = ((s8[5767168]{0:T(1024)(128)(4,1)}), s8[4194304]{0:T(1024)(128)(4,1)S(1)}, s32[]{:S(2)}) async-start(s8[5767168]{0:T(1024)(128)(4,1)} %bitcast.74), calls=%async_computation.10 | async-start | bytes 8388608
  656.7 64.0 %collective-permute-start.15 = (bf16[256,2048]{1,0:T(8,128)(2,1)}, bf16[256,2048]{1,0:T(8,128)(2,1)}, u32[]{:S(2)}, u32[]{:S(2)}) collective-permute-start(bf16[256,2048]{1,0:T(8,128)(2,1)} %pad_maximum_fusion.5), channel_id=1, source_target_pairs={{0,1},{1,0},{2,3},{3,2},{4,5},{5,4},{6,7},{7,6},{8,9},{9,8},{10,11... | collective-permute-start | bytes 3145736 | tf_op jit(solution)/shard_map/ppermute | solution.py:214
  656.7 1.2 collective-permute-start.16
  657.9 4.0 collective-permute-start.17
  660.3 3.6 collective-permute-start.21
  661.9 3.7 collective-permute-start.18
  663.9 3.7 collective-permute-start.22
  665.6 16.7 %collective-permute-start.19 = (f32[2048]{0:T(1024)S(1)}, f32[2048]{0:T(1024)S(1)}, u32[]{:S(2)}, u32[]{:S(2)}) collective-permute-start(f32[2048]{0:T(1024)S(1)} %add.319), channel_id=1, source_target_pairs={{0,1},{1,0},{2,3},{3,2},{4,5},{5,4},{6,7},{7,6},{8,9},{9,8},{10,11... | collective-permute-start | bytes 24584 | tf_op jit(solution)/shard_map/ppermute | solution.py:228
  667.6 15.5 %collective-permute-start.23 = (f32[2048]{0:T(1024)S(1)}, f32[2048]{0:T(1024)S(1)}, u32[]{:S(2)}, u32[]{:S(2)}) collective-permute-start(f32[2048]{0:T(1024)S(1)} %add.323), channel_id=1, source_target_pairs={{0,16},{4,20},{8,24},{12,28},{16,0},{20,4},{24,8},{28,12},{1,17},{... | collective-permute-start | bytes 24584 | tf_op jit(solution)/shard_map/ppermute | solution.py:228
  682.2 21.1 %collective-permute-start.20 = (f32[2048]{0:T(1024)S(1)}, f32[2048]{0:T(1024)S(1)}, u32[]{:S(2)}, u32[]{:S(2)}) collective-permute-start(f32[2048]{0:T(1024)S(1)} %add.320), channel_id=1, source_target_pairs={{0,2},{1,3},{2,0},{3,1},{4,6},{5,7},{6,4},{7,5},{8,10},{9,11},{10,... | collective-permute-start | bytes 24584 | tf_op jit(solution)/shard_map/ppermute | solution.py:228
  683.7 8.4 %slice-start.5 = ((s8[5767168]{0:T(1024)(128)(4,1)}), s8[1572864]{0:T(1024)(128)(4,1)S(1)}, s32[]{:S(2)}) async-start(s8[5767168]{0:T(1024)(128)(4,1)} %bitcast.74), calls=%async_computation.11 | async-start | bytes 3145728
  683.7 13.6 %slice-start.2 = ((s8[5767168]{0:T(1024)(128)(4,1)}), s8[4194304]{0:T(1024)(128)(4,1)S(1)}, s32[]{:S(2)}) async-start(s8[5767168]{0:T(1024)(128)(4,1)} %bitcast.72), calls=%async_computation.8 | async-start | bytes 8388608
  710.7 5.8 copy-start.42
  718.1 6.0 copy-start.17
  (41 other events, 117.4 us)
Sparse Core Ops, SparseCore 0:
  22.0 39.3 all-gather.2
  137.7 68.9 all-reduce.5
  252.7 221.6 all-reduce.9
  478.2 51.2 reduce-scatter.1
  606.1 104.6 all-reduce.7

commit v10 on v6

--- a/solution.py
+++ b/solution.py
@@ -387,16 +387,12 @@
     grad_middle = grad_out + d_middle_norm
     d_branch = (keep_rows * grad_middle).astype(jnp.bfloat16)
     grad_w_out = left_trans(attended, d_branch)
-    grad_w_gate, grad_w_up, grad_w_down, grad_w_out = lax.optimization_barrier(
-        (grad_w_gate, grad_w_up, grad_w_down, grad_w_out)
-    )
     d_attended = right_trans(d_branch, w_out).astype(jnp.bfloat16)
     d_queries, d_key_all, d_value_all = attention_backward(
         query_low, all_kv, d_attended, lse, local_groups=local_groups, chunk=half_rows,
         **mask_args,
     )
     d_kv_own = permute_scatter(jnp.concatenate([d_key_all, d_value_all], axis=1), "dp")
-    d_kv_own, grad_w_out = lax.optimization_barrier((d_kv_own, grad_w_out))
     d_key_own = d_kv_own[:, :kv_width]
     d_value_own = d_kv_own[:, kv_width:]
     d_queries = d_queries.reshape(row_count, local_heads, HEAD_DIM)
@@ -419,15 +415,29 @@
         + right_trans(d_key_low, w_key)
         + right_trans(d_value_low, w_value)
     )
+    unit_normed = source * lax.rsqrt(jnp.mean(source * source, axis=-1, keepdims=True) + EPS)
+    grad_gain_one = jnp.sum(d_normed_part * unit_normed, axis=0)
     (
         down_sum,
         d_normed_part,
+        grad_gain_one,
         grad_w_out,
         grad_w_query,
         grad_w_key,
         grad_w_value,
     ) = lax.optimization_barrier(
-        (down_sum, d_normed_part, grad_w_out, grad_w_query, grad_w_key, grad_w_value)
+        (down_sum, d_normed_part, grad_gain_one, grad_w_out, grad_w_query, grad_w_key, grad_w_value)
+    )
+    (
+        grad_w_gate,
+        grad_w_up,
+        grad_w_down,
+        grad_w_out,
+        grad_w_query,
+        grad_w_key,
+        grad_w_value,
+    ) = lax.optimization_barrier(
+        (grad_w_gate, grad_w_up, grad_w_down, grad_w_out, grad_w_query, grad_w_key, grad_w_value)
     )
     grad_w_out, grad_w_query, grad_w_key, grad_w_value = dp_sum(
         [grad_w_out, grad_w_query, grad_w_key, grad_w_value]
@@ -436,10 +446,10 @@
         grad.astype(jnp.float32) for grad in (grad_w_gate, grad_w_up, grad_w_down)
     ]
     output = (middle + keep_rows * down_sum).astype(jnp.bfloat16)
+    grad_gain_one = permute_allsum(permute_allsum(grad_gain_one, "dp"), "tensor")
     (d_normed,) = permute_sum([d_normed_part], [0], "tensor")
-    d_source_norm, grad_gain_one = norm_one_back(d_normed)
+    d_source_norm, _ = norm_one_back(d_normed)
     grad_input = grad_middle + d_source_norm
-    grad_gain_one = permute_allsum(grad_gain_one, "dp")
     grad_gain_two = permute_allsum(grad_gain_two, "dp")
     grad_w_out, grad_w_query, grad_w_key, grad_w_value = [
         grad.astype(jnp.float32) for grad in (grad_w_out, grad_w_query, grad_w_key, grad_w_value)

time: 793 us -> 838 us (1.057)
  waiting for transfers between devices: 416 us -> 453 us
    psum x2, waiting for transfers between devices: 68.9 us -> 128 us  [dp_sum(): return [lax.psum(grad.astype(jnp.bfloat16), 'dp') for grad in grads]]
    ppermute x8, waiting for transfers between devices: 133 us -> 89.3 us  [permute_sum(): got = lax.ppermute(pieces, axis, partner_perm(size, 1 << step))]
    ppermute x6 -> x8, waiting for transfers between devices: 6.12 us -> 20 us  [permute_allsum(): value = value + lax.ppermute(value, axis, partner_perm(size, 1 << step))]
    unnamed x182 -> x180, local copies, waits for them, and re-layouts: 20.2 us -> 26 us
  transfers between devices with their start and end apart: 29 -> 31, of which waited for: 24 -> 24; matrix products, arithmetic and copies ran while one was open for 14% -> 14% of each run, Pallas kernels for 9% -> 8%
where the time goes in v10:
time: 838 us; the launch traced here: 831 us
  waiting for transfers between devices  453 us (54%)
  matrix products  116 us (14%)
  other arithmetic  96.9 us (12%)
  Pallas kernels  68.9 us (8%)
  local copies, waits for them, and re-layouts  43 us (5%)
  starting transfers between devices  27.2 us (3%)
  between operations  15.5 us (2%)
  blocking collectives  10.7 us (1%)
    psum x2, waiting for transfers between devices, dp_sum(): return [lax.psum(grad.astype(jnp.bfloat16), 'dp') for grad in grads]  128 us
    ppermute x8, waiting for transfers between devices, permute_sum(): got = lax.ppermute(send, axis, partner_perm(size, 1 << step))  128 us
    ppermute x8, waiting for transfers between devices, permute_sum(): got = lax.ppermute(pieces, axis, partner_perm(size, 1 << step))  89.3 us
    pallas_call x1, Pallas kernels, attention_backward(): pl.pallas_call(kernel, grid_spec=grid_spec, out_shape=[jax.ShapeDtypeStru...  68.9 us
    dot_general x11, matrix products, right_trans(): lax.dot_general(left, right, (((1,), (1,)), ((), ())), preferred_element_...  52.7 us
    ppermute x3, waiting for transfers between devices, permute_scatter(): got = lax.ppermute(send, axis, partner_perm(size, 1 << step))  39.2 us
    psum x1, waiting for transfers between devices, on_device(): branch_top = lax.psum(branch_part[:sc_rows].astype(jnp.bfloat16), 'tensor')  31 us
    convert_element_type x7, other arithmetic, on_device(): grad.astype(jnp.float32)  29 us
  transfers between devices with their start and end apart: 31, of which 24 were waited for; matrix products, arithmetic and copies ran while one was open for 14% of the time, Pallas kernels for 8%

profile of v10, /device:TPU:0, one launch (start us, length us, event | category | flops | bytes accessed | tf_op | source)
XLA Modules:
  0.0 831.3 jit_solution(1329546431622381644)
XLA Ops:
  11.0 3.3 convolution_convert_fusion.1
  20.7 3.6 fusion.70
  26.9 2.4 copy.61
  32.0 10.7 %all-gather = bf16[8,1,512]{2,1,0:T(2,128)(2,1)S(1)} all-gather(bf16[1,1,512]{2,1,0:T(2,128)(2,1)S(1)} %reshape.288), channel_id=1, replica_groups=mesh['dp'=8,'tensor'=4] {'dp'}, dimensions={0}, use_global_device_ids=true | all-gather | bytes 9216 | tf_op jit(solution)/shard_map/all_gather | solution.py:312
  42.8 17.3 %all-gather.3.cloned.1.call-done.k_ref.v_ref = bf16[4096,512]{1,0:T(8,128)(2,1)} async-done(((bf16[512,512]{1,0:T(8,128)(2,1)}), bf16[4096,512]{1,0:T(8,128)(2,1)}) %all-gather.3.cloned.1.call-update) | async-done | bytes 4194320 | tf_op jit(solution)/shard_map/all_gather | solution.py:309
  60.1 4.6 fusion.76
  66.0 4.6 fusion.77
  71.9 5.0 fusion.78
  78.2 6.9 fusion.79
  85.1 4.6 fusion.2
  89.7 3.3 fusion.22
  93.0 3.4 fusion.23
  106.9 9.8 %collective-permute-done = bf16[96,2048]{1,0:T(8,128)(2,1)S(1)} collective-permute-done((bf16[96,2048]{1,0:T(8,128)(2,1)S(1)}, bf16[96,2048]{1,0:T(8,128)(2,1)S(1)}, u32[]{:S(2)}, u32[]{:S(2)}) %collective-permute-start) | collective-permute-done | bytes 393248 | tf_op jit(solution)/shard_map/ppermute | solution.py:209
  117.9 2.5 collective-permute-start.1
  120.4 8.9 %collective-permute-done.1 = bf16[48,2048]{1,0:T(8,128)(2,1)S(1)} collective-permute-done((bf16[48,2048]{1,0:T(8,128)(2,1)S(1)}, bf16[48,2048]{1,0:T(8,128)(2,1)S(1)}, u32[]{:S(2)}, u32[]{:S(2)}) %collective-permute-start.1) | collective-permute-done | bytes 196640 | tf_op jit(solution)/shard_map/ppermute | solution.py:209
  129.5 3.0 slice.196
  132.7 7.8 collective-permute-done.2
  140.6 8.3 %fusion.36 = f32[512,1408]{1,0:T(8,128)} fusion(bf16[1408,2048]{1,0:T(8,128)(2,1)} %param.24, bf16[512,2048]{1,0:T(8,128)(2,1)} %param.25, f32[512]{0:T(512)S(1)} %get-tuple-element.104), kind=kOutput, calls=%fused_computation.116 | convolution fusion | flops 2955935744 | bytes 10749952 | tf_op jit(solution)/shard_map/dot_general | solution.py:49
  148.9 20.5 %collective-permute-done.3 = bf16[96,2048]{1,0:T(8,128)(2,1)} collective-permute-done((bf16[96,2048]{1,0:T(8,128)(2,1)S(1)}, bf16[96,2048]{1,0:T(8,128)(2,1)}, u32[]{:S(2)}, u32[]{:S(2)}) %collective-permute-start.3) | collective-permute-done | bytes 393248 | tf_op jit(solution)/shard_map/ppermute | solution.py:214
  170.7 31.0 %all-reduce.6.cloned.1.call-done = bf16[320,2048]{1,0:T(8,128)(2,1)} async-done(((bf16[320,2048]{1,0:T(8,128)(2,1)}), bf16[320,2048]{1,0:T(8,128)(2,1)}) %all-reduce.6.cloned.1.call-update) | async-done | bytes 1310736 | tf_op jit(solution)/shard_map/psum | solution.py:353
  201.6 3.1 multiply_reduce_fusion.2
  204.7 3.2 multiply_convert_fusion.1
  208.0 5.9 fusion.80
  213.9 4.5 multiply_convert_fusion.2
  218.4 5.3 fusion.82
  223.7 5.0 fusion.84
  228.7 5.3 fusion.83
  234.0 5.6 fusion.34
  239.6 7.8 convolution_add_fusion
  251.9 23.9 %collective-permute-done.4 = bf16[256,2048]{1,0:T(8,128)(2,1)} collective-permute-done((bf16[256,2048]{1,0:T(8,128)(2,1)}, bf16[256,2048]{1,0:T(8,128)(2,1)}, u32[]{:S(2)}, u32[]{:S(2)}) %collective-permute-start.4) | collective-permute-done | bytes 1048608 | tf_op jit(solution)/shard_map/ppermute | solution.py:209
  282.9 22.4 %collective-permute-done.5 = bf16[128,2048]{1,0:T(8,128)(2,1)} collective-permute-done((bf16[128,2048]{1,0:T(8,128)(2,1)}, bf16[128,2048]{1,0:T(8,128)(2,1)}, u32[]{:S(2)}, u32[]{:S(2)}) %collective-permute-start.5) | collective-permute-done | bytes 524320 | tf_op jit(solution)/shard_map/ppermute | solution.py:209
  305.2 2.3 add_convert_fusion.4
  309.5 22.9 %collective-permute-done.6 = bf16[128,2048]{1,0:T(8,128)(2,1)} collective-permute-done((bf16[128,2048]{1,0:T(8,128)(2,1)}, bf16[128,2048]{1,0:T(8,128)(2,1)}, u32[]{:S(2)}, u32[]{:S(2)}) %collective-permute-start.6) | collective-permute-done | bytes 524320 | tf_op jit(solution)/shard_map/ppermute | solution.py:214
  337.6 5.9 fusion.81
  343.6 17.3 %collective-permute-done.7 = bf16[256,2048]{1,0:T(8,128)(2,1)} collective-permute-done((bf16[256,2048]{1,0:T(8,128)(2,1)}, bf16[256,2048]{1,0:T(8,128)(2,1)}, u32[]{:S(2)}, u32[]{:S(2)}) %collective-permute-start.7) | collective-permute-done | bytes 1048608 | tf_op jit(solution)/shard_map/ppermute | solution.py:214
  364.7 2.9 multiply_reduce_fusion
  369.0 4.1 convert_add_fusion.1
  374.8 68.9 %shard_map.212 = (f32[512,512]{1,0:T(8,128)S(1)}, f32[4096,256]{1,0:T(8,128)}, f32[4096,256]{1,0:T(8,128)}) custom-call(s32[16]{0:T(128)S(1)} %copy-done.4, s32[2]{0:T(128)S(1)} %dynamic_slice.85.qblock_ref, bf16[512,512]{1,0:T(8,128)(2,1)S(1)} %bitcast.65, bf16[4096,512]{1,0:T(8,128)(2,1)} %all-gather.3.cloned.1.call-done.k_ref.v_ref, ...), custom_call_target="tpu_custom_call" | custom-call | flops 10737418240 | bytes 25165824 | tf_op jit(solution)/shard_map/pallas_call | solution.py:173
  443.8 3.0 constant_dynamic-update-slice_fusion.1
  448.8 3.4 copy-done.27
  457.7 3.0 collective-permute-start.9
  462.3 2.8 fusion.38
  465.1 19.4 %collective-permute-done.9 = bf16[128,2048]{1,0:T(8,128)(2,1)S(1)} collective-permute-done((bf16[128,2048]{1,0:T(8,128)(2,1)S(1)}, bf16[128,2048]{1,0:T(8,128)(2,1)S(1)}, u32[]{:S(2)}, u32[]{:S(2)}) %collective-permute-start.9) | collective-permute-done | bytes 524320 | tf_op jit(solution)/shard_map/ppermute | solution.py:209
  484.7 2.4 convert_add_fusion.2
  489.2 20.8 %collective-permute-done.10 = bf16[128,2048]{1,0:T(8,128)(2,1)S(1)} collective-permute-done((bf16[128,2048]{1,0:T(8,128)(2,1)S(1)}, bf16[128,2048]{1,0:T(8,128)(2,1)S(1)}, u32[]{:S(2)}, u32[]{:S(2)}) %collective-permute-start.10) | collective-permute-done | bytes 524320 | tf_op jit(solution)/shard_map/ppermute | solution.py:214
  510.3 2.7 fusion.55
  513.0 3.3 fusion.40
  516.3 19.2 %collective-permute-done.13 = bf16[1024,512]{1,0:T(8,128)(2,1)S(1)} collective-permute-done((bf16[1024,512]{1,0:T(8,128)(2,1)S(1)}, bf16[1024,512]{1,0:T(8,128)(2,1)S(1)}, u32[]{:S(2)}, u32[]{:S(2)}) %collective-permute-start.13) | collective-permute-done | bytes 1048608 | tf_op jit(solution)/shard_map/ppermute | solution.py:242
  538.4 2.6 maximum_convert_fusion.1
  541.0 19.9 %collective-permute-done.14 = bf16[512,512]{1,0:T(8,128)(2,1)S(1)} collective-permute-done((bf16[512,512]{1,0:T(8,128)(2,1)S(1)}, bf16[512,512]{1,0:T(8,128)(2,1)S(1)}, u32[]{:S(2)}, u32[]{:S(2)}) %collective-permute-start.14) | collective-permute-done | bytes 524320 | tf_op jit(solution)/shard_map/ppermute | solution.py:242
  565.8 3.7 fusion.44
  574.2 3.8 fusion.9
  580.2 21.5 %collective-permute-done.15 = bf16[256,2048]{1,0:T(8,128)(2,1)S(1)} collective-permute-done((bf16[256,2048]{1,0:T(8,128)(2,1)S(1)}, bf16[256,2048]{1,0:T(8,128)(2,1)S(1)}, u32[]{:S(2)}, u32[]{:S(2)}) %collective-permute-start.15) | collective-permute-done | bytes 1048608 | tf_op jit(solution)/shard_map/ppermute | solution.py:209
  603.5 21.9 %collective-permute-done.16 = bf16[128,2048]{1,0:T(8,128)(2,1)S(1)} collective-permute-done((bf16[128,2048]{1,0:T(8,128)(2,1)S(1)}, bf16[128,2048]{1,0:T(8,128)(2,1)S(1)}, u32[]{:S(2)}, u32[]{:S(2)}) %collective-permute-start.16) | collective-permute-done | bytes 524320 | tf_op jit(solution)/shard_map/ppermute | solution.py:209
  625.6 80.8 %all-reduce.10.cloned.1.call-done = (bf16[2048,1408]{1,0:T(8,128)(2,1)}, bf16[2048,1408]{1,0:T(8,128)(2,1)}, bf16[1408,2048]{1,0:T(8,128)(2,1)}) async-done(((bf16[2048,1408]{1,0:T(8,128)(2,1)}, bf16[2048,1408]{1,0:T(8,128)(2,1)}, bf16[1408,2048]{1,0:T(8,128)(2,1)}), (bf16[2048,1408]{1,0:T(8,128)(2,1)}, bf16[2048,1408]{1,0:T(8,128)(2,1)}, bf16[1408,2048]{1,0:T(8,128)(2,1)})) %all-reduce.10.cloned.1.call-update) | async-done | bytes 17301520 | tf_op jit(solution)/shard_map/psum | solution.py:367
  718.7 12.8 %collective-permute-done.22 = f32[2048]{0:T(1024)S(1)} collective-permute-done((f32[2048]{0:T(1024)S(1)}, f32[2048]{0:T(1024)S(1)}, u32[]{:S(2)}, u32[]{:S(2)}) %collective-permute-start.22) | collective-permute-done | bytes 8224 | tf_op jit(solution)/shard_map/ppermute | solution.py:251
  731.5 2.4 collective-permute-start.23
  736.7 8.0 convert_element_type.278
  744.7 5.2 convert_element_type.279
  749.9 6.0 convert_element_type.280
  759.4 7.8 fusion.11
  767.2 47.5 %all-reduce.8.cloned.1.call-done = (bf16[2048,512]{1,0:T(8,128)(2,1)}, bf16[2048,256]{1,0:T(8,128)(2,1)}, bf16[2048,256]{1,0:T(8,128)(2,1)}, bf16[512,2048]{1,0:T(8,128)(2,1)}) async-done(((bf16[2048,512]{1,0:T(8,128)(2,1)}, bf16[2048,256]{1,0:T(8,128)(2,1)}, bf16[2048,256]{1,0:T(8,128)(2,1)}, bf16[512,2048]{1,0:T(8,128)(2,1)}), (bf16[2048,512]{1,0:T(8,128)(2,1)}, bf16[2048,256]{1,0:T(8,128)(2,1)}, ...) | async-done | bytes 6291472 | tf_op jit(solution)/shard_map/psum | solution.py:367
  814.7 4.3 convert_element_type.271
  822.0 2.5 convert_element_type.277
  (325 shorter events, 107.5 us)
Async XLA Ops:
  7.2 93.5 %copy-start = (bf16[512,2048]{1,0:T(8,128)(2,1)S(1)}, bf16[512,2048]{1,0:T(8,128)(2,1)}, u32[]{:S(2)}) copy-start(bf16[512,2048]{1,0:T(8,128)(2,1)} %param.20) | copy-start | bytes 6291460
  7.2 7.1 copy-start.48
  7.2 52.9 %all-gather.3.cloned.1.call-start = ((), (), s32[]{:S(2)}) async-start(), calls=%async_computation | async-start | bytes 4718592 | tf_op jit(solution)/shard_map/all_gather | solution.py:309
  7.3 7.0 copy-start.5
  8.1 12.6 %copy-start.59 = (f32[2048]{0:T(1024)}, f32[2048]{0:T(1024)S(1)}, u32[]{:S(2)}) copy-start(f32[2048]{0:T(1024)S(1)} %convert_element_type.216) | copy-start | bytes 24580
  11.0 9.7 %copy-start.63 = (f32[512]{0:T(512)}, f32[512]{0:T(512)S(1)}, u32[]{:S(2)}) copy-start(f32[512]{0:T(512)S(1)} %fusion.60) | copy-start | bytes 6148
  17.8 11.5 %copy-start.25 = (f32[512,64]{1,0:T(8,128)}, f32[512,64]{1,0:T(8,128)S(1)}, u32[]{:S(2)}) copy-start(f32[512,64]{1,0:T(8,128)S(1)} %get-tuple-element.103) | copy-start | bytes 393220
  20.7 181.0 %all-reduce.6.cloned.1.call-start = ((), (), s32[]{:S(2)}) async-start(), calls=%async_computation.1 | async-start | bytes 2621440 | tf_op jit(solution)/shard_map/psum | solution.py:353
  32.0 46.2 %copy-start.1 = (bf16[64,8,4,128]{3,1,2,0:T(8,128)(2,1)}, bf16[64,8,4,128]{3,1,2,0:T(8,128)(2,1)S(1)}, u32[]{:S(2)}) copy-start(bf16[64,8,4,128]{3,1,2,0:T(8,128)(2,1)S(1)} %copy.90) | copy-start | bytes 1572868
  93.0 7.7 copy-start.50
  105.3 11.3 %collective-permute-start = (bf16[96,2048]{1,0:T(8,128)(2,1)S(1)}, bf16[96,2048]{1,0:T(8,128)(2,1)S(1)}, u32[]{:S(2)}, u32[]{:S(2)}) collective-permute-start(bf16[96,2048]{1,0:T(8,128)(2,1)S(1)} %dynamic-slice_convert_fusion.9), channel_id=1, source_target_pairs={{0,1},{1,0},{2,3},{3,2},{4,5},{5,4},{6,7},{7,6},{8,9},{9,8},{10,11... | collective-permute-start | bytes 1179656 | tf_op jit(solution)/shard_map/ppermute | solution.py:209
  117.9 11.4 %collective-permute-start.1 = (bf16[48,2048]{1,0:T(8,128)(2,1)S(1)}, bf16[48,2048]{1,0:T(8,128)(2,1)S(1)}, u32[]{:S(2)}, u32[]{:S(2)}) collective-permute-start(bf16[48,2048]{1,0:T(8,128)(2,1)S(1)} %dynamic-slice_convert_fusion.10), channel_id=1, source_target_pairs={{0,2},{1,3},{2,0},{3,1},{4,6},{5,7},{6,4},{7,5},{8,10},{9,11},{10,... | collective-permute-start | bytes 589832 | tf_op jit(solution)/shard_map/ppermute | solution.py:209
  129.4 11.1 %collective-permute-start.2 = (bf16[48,2048]{1,0:T(8,128)(2,1)S(1)}, bf16[48,2048]{1,0:T(8,128)(2,1)S(1)}, u32[]{:S(2)}, u32[]{:S(2)}) collective-permute-start(bf16[48,2048]{1,0:T(8,128)(2,1)S(1)} %add_convert_fusion.8), channel_id=1, source_target_pairs={{0,2},{1,3},{2,0},{3,1},{4,6},{5,7},{6,4},{7,5},{8,10},{9,11},{10,... | collective-permute-start | bytes 589832 | tf_op jit(solution)/shard_map/ppermute | solution.py:214
  132.5 573.9 %all-reduce.10.cloned.1.call-start = ((), (), s32[]{:S(2)}) async-start(), calls=%async_computation.3 | async-start | bytes 34603008 | tf_op jit(solution)/shard_map/psum | solution.py:367
  140.5 28.9 %collective-permute-start.3 = (bf16[96,2048]{1,0:T(8,128)(2,1)S(1)}, bf16[96,2048]{1,0:T(8,128)(2,1)}, u32[]{:S(2)}, u32[]{:S(2)}) collective-permute-start(bf16[96,2048]{1,0:T(8,128)(2,1)S(1)} %pad_maximum_fusion.9), channel_id=1, source_target_pairs={{0,1},{1,0},{2,3},{3,2},{4,5},{5,4},{6,7},{7,6},{8,9},{9,8},{10,11... | collective-permute-start | bytes 1179656 | tf_op jit(solution)/shard_map/ppermute | solution.py:214
  140.6 8.3 %copy-start.65 = (bf16[2048]{0:T(1024)(128)(2,1)S(1)}, bf16[2048]{0:T(1024)(128)(2,1)}, u32[]{:S(2)}) copy-start(bf16[2048]{0:T(1024)(128)(2,1)} %param.21) | copy-start | bytes 12292
  170.6 198.4 %copy-start.19 = (bf16[96,2048]{1,0:T(8,128)(2,1)}, bf16[96,2048]{1,0:T(8,128)(2,1)S(1)}, u32[]{:S(2)}) copy-start(bf16[96,2048]{1,0:T(8,128)(2,1)S(1)} %get-tuple-element.95) | copy-start | bytes 1179652
  170.6 198.4 %copy-start.21 = (bf16[96,2048]{1,0:T(8,128)(2,1)}, bf16[96,2048]{1,0:T(8,128)(2,1)S(1)}, u32[]{:S(2)}) copy-start(bf16[96,2048]{1,0:T(8,128)(2,1)S(1)} %get-tuple-element.96) | copy-start | bytes 1179652
  204.7 9.2 %slice-start.8 = ((s8[5767168]{0:T(1024)(128)(4,1)}), s8[4194304]{0:T(1024)(128)(4,1)S(1)}, s32[]{:S(2)}) async-start(s8[5767168]{0:T(1024)(128)(4,1)} %bitcast.101), calls=%async_computation.12 | async-start | bytes 8388608
  208.0 5.9 slice-start.9
  208.0 5.9 copy-start.69
  218.4 10.3 %copy-start.68 = (bf16[512,1408]{1,0:T(8,128)(2,1)}, bf16[512,1408]{1,0:T(8,128)(2,1)S(1)}, u32[]{:S(2)}) copy-start(bf16[512,1408]{1,0:T(8,128)(2,1)S(1)} %get-tuple-element.68) | copy-start | bytes 4325380
  218.4 15.5 %copy-start.70 = (bf16[512,1408]{1,0:T(8,128)(2,1)}, bf16[512,1408]{1,0:T(8,128)(2,1)S(1)}, u32[]{:S(2)}) copy-start(bf16[512,1408]{1,0:T(8,128)(2,1)S(1)} %get-tuple-element.70) | copy-start | bytes 4325380
  250.5 25.4 %collective-permute-start.4 = (bf16[256,2048]{1,0:T(8,128)(2,1)}, bf16[256,2048]{1,0:T(8,128)(2,1)}, u32[]{:S(2)}, u32[]{:S(2)}) collective-permute-start(bf16[256,2048]{1,0:T(8,128)(2,1)} %dynamic-slice_convert_fusion.4), channel_id=1, source_target_pairs={{0,1},{1,0},{2,3},{3,2},{4,5},{5,4},{6,7},{7,6},{8,9},{9,8},{10,11... | collective-permute-start | bytes 3145736 | tf_op jit(solution)/shard_map/ppermute | solution.py:209
  280.2 25.0 %collective-permute-start.5 = (bf16[128,2048]{1,0:T(8,128)(2,1)}, bf16[128,2048]{1,0:T(8,128)(2,1)}, u32[]{:S(2)}, u32[]{:S(2)}) collective-permute-start(bf16[128,2048]{1,0:T(8,128)(2,1)} %dynamic-slice_convert_fusion.8), channel_id=1, source_target_pairs={{0,2},{1,3},{2,0},{3,1},{4,6},{5,7},{6,4},{7,5},{8,10},{9,11},{10,... | collective-permute-start | bytes 1572872 | tf_op jit(solution)/shard_map/ppermute | solution.py:209
  307.5 24.8 %collective-permute-start.6 = (bf16[128,2048]{1,0:T(8,128)(2,1)}, bf16[128,2048]{1,0:T(8,128)(2,1)}, u32[]{:S(2)}, u32[]{:S(2)}) collective-permute-start(bf16[128,2048]{1,0:T(8,128)(2,1)} %add_convert_fusion.4), channel_id=1, source_target_pairs={{0,2},{1,3},{2,0},{3,1},{4,6},{5,7},{6,4},{7,5},{8,10},{9,11},{10,... | collective-permute-start | bytes 1572872 | tf_op jit(solution)/shard_map/ppermute | solution.py:214
  335.5 25.4 %collective-permute-start.7 = (bf16[256,2048]{1,0:T(8,128)(2,1)}, bf16[256,2048]{1,0:T(8,128)(2,1)}, u32[]{:S(2)}, u32[]{:S(2)}) collective-permute-start(bf16[256,2048]{1,0:T(8,128)(2,1)} %pad_maximum_fusion.1), channel_id=1, source_target_pairs={{0,1},{1,0},{2,3},{3,2},{4,5},{5,4},{6,7},{7,6},{8,9},{9,8},{10,11... | collective-permute-start | bytes 3145736 | tf_op jit(solution)/shard_map/ppermute | solution.py:214
  337.6 23.3 %copy-start.31 = (bf16[128,2048]{1,0:T(8,128)(2,1)S(1)}, bf16[128,2048]{1,0:T(8,128)(2,1)}, u32[]{:S(2)}) copy-start(bf16[128,2048]{1,0:T(8,128)(2,1)} %copy-done.30) | copy-start | bytes 1572868
  337.6 23.3 %copy-start.33 = (bf16[128,2048]{1,0:T(8,128)(2,1)S(1)}, bf16[128,2048]{1,0:T(8,128)(2,1)}, u32[]{:S(2)}) copy-start(bf16[128,2048]{1,0:T(8,128)(2,1)} %copy-done.32) | copy-start | bytes 1572868
  343.6 24.1 %copy-start.38 = (f32[512,2048]{1,0:T(8,128)}, f32[512,2048]{1,0:T(8,128)S(1)}, u32[]{:S(2)}) copy-start(f32[512,2048]{1,0:T(8,128)S(1)} %fusion.81) | copy-start | bytes 12582916
  368.8 86.6 %collective-permute-start.8 = (bf16[256,2048]{1,0:T(8,128)(2,1)}, bf16[256,2048]{1,0:T(8,128)(2,1)}, u32[]{:S(2)}, u32[]{:S(2)}) collective-permute-start(bf16[256,2048]{1,0:T(8,128)(2,1)} %dynamic-slice_convert_fusion.3), channel_id=1, source_target_pairs={{0,1},{1,0},{2,3},{3,2},{4,5},{5,4},{6,7},{7,6},{8,9},{9,8},{10,11... | collective-permute-start | bytes 3145736 | tf_op jit(solution)/shard_map/ppermute | solution.py:209
  373.1 70.6 %copy-start.12 = (f32[512,2048]{1,0:T(8,128)}, f32[512,2048]{1,0:T(8,128)S(1)}, u32[]{:S(2)}) copy-start(f32[512,2048]{1,0:T(8,128)S(1)} %convert_add_fusion.1) | copy-start | bytes 12582916
  453.7 30.9 %collective-permute-start.12 = (bf16[2048,512]{1,0:T(8,128)(2,1)}, bf16[2048,512]{1,0:T(8,128)(2,1)}, u32[]{:S(2)}, u32[]{:S(2)}) collective-permute-start(bf16[2048,512]{1,0:T(8,128)(2,1)} %dynamic-slice_convert_fusion), channel_id=1, source_target_pairs={{0,4},{4,0},{8,12},{12,8},{16,20},{20,16},{24,28},{28,24},{1,5},{5... | collective-permute-start | bytes 6291464 | tf_op jit(solution)/shard_map/ppermute | solution.py:242
  453.8 360.9 %all-reduce.8.cloned.1.call-start = ((), (), s32[]{:S(2)}) async-start(), calls=%async_computation.2 | async-start | bytes 12582912 | tf_op jit(solution)/shard_map/psum | solution.py:367
  454.0 6.7 copy-start.26
  457.7 26.8 %collective-permute-start.9 = (bf16[128,2048]{1,0:T(8,128)(2,1)S(1)}, bf16[128,2048]{1,0:T(8,128)(2,1)S(1)}, u32[]{:S(2)}, u32[]{:S(2)}) collective-permute-start(bf16[128,2048]{1,0:T(8,128)(2,1)S(1)} %dynamic-slice_convert_fusion.7), channel_id=1, source_target_pairs={{0,2},{1,3},{2,0},{3,1},{4,6},{5,7},{6,4},{7,5},{8,10},{9,11},{10,... | collective-permute-start | bytes 1572872 | tf_op jit(solution)/shard_map/ppermute | solution.py:209
  461.5 23.2 %slice-start.2 = ((s8[8388608]{0:T(1024)(128)(4,1)}), s8[4194304]{0:T(1024)(128)(4,1)S(1)}, s32[]{:S(2)}) async-start(s8[8388608]{0:T(1024)(128)(4,1)} %bitcast.70), calls=%async_computation.6 | async-start | bytes 8388608
  462.3 22.4 %slice-start.3 = ((s8[8388608]{0:T(1024)(128)(4,1)}), s8[4194304]{0:T(1024)(128)(4,1)S(1)}, s32[]{:S(2)}) async-start(s8[8388608]{0:T(1024)(128)(4,1)} %bitcast.70), calls=%async_computation.7 | async-start | bytes 8388608
  484.6 25.4 %collective-permute-start.10 = (bf16[128,2048]{1,0:T(8,128)(2,1)S(1)}, bf16[128,2048]{1,0:T(8,128)(2,1)S(1)}, u32[]{:S(2)}, u32[]{:S(2)}) collective-permute-start(bf16[128,2048]{1,0:T(8,128)(2,1)S(1)} %add_convert_fusion.3), channel_id=1, source_target_pairs={{0,2},{1,3},{2,0},{3,1},{4,6},{5,7},{6,4},{7,5},{8,10},{9,11},{10,... | collective-permute-start | bytes 1572872 | tf_op jit(solution)/shard_map/ppermute | solution.py:214
  487.1 23.1 %copy-start.13 = (f32[512,2048]{1,0:T(8,128)S(1)}, f32[512,2048]{1,0:T(8,128)}, u32[]{:S(2)}) copy-start(f32[512,2048]{1,0:T(8,128)} %copy-done.12) | copy-start | bytes 12582916
  487.1 23.1 %copy-start.51 = (bf16[512,128]{0,1:T(8,128)(2,1)S(1)}, bf16[512,128]{0,1:T(8,128)(2,1)}, u32[]{:S(2)}) copy-start(bf16[512,128]{0,1:T(8,128)(2,1)} %copy-done.50) | copy-start | bytes 393220
  487.1 23.1 %copy-start.53 = (bf16[512,128]{0,1:T(8,128)(2,1)S(1)}, bf16[512,128]{0,1:T(8,128)(2,1)}, u32[]{:S(2)}) copy-start(bf16[512,128]{0,1:T(8,128)(2,1)} %copy-done.52) | copy-start | bytes 393220
  487.1 23.1 %copy-start.55 = (bf16[512,128]{0,1:T(8,128)(2,1)S(1)}, bf16[512,128]{0,1:T(8,128)(2,1)}, u32[]{:S(2)}) copy-start(bf16[512,128]{0,1:T(8,128)(2,1)} %copy-done.54) | copy-start | bytes 393220
  487.1 23.1 %copy-start.57 = (bf16[512,128]{0,1:T(8,128)(2,1)S(1)}, bf16[512,128]{0,1:T(8,128)(2,1)}, u32[]{:S(2)}) copy-start(bf16[512,128]{0,1:T(8,128)(2,1)} %copy-done.56) | copy-start | bytes 393220
  487.3 48.2 %collective-permute-start.13 = (bf16[1024,512]{1,0:T(8,128)(2,1)S(1)}, bf16[1024,512]{1,0:T(8,128)(2,1)S(1)}, u32[]{:S(2)}, u32[]{:S(2)}) collective-permute-start(bf16[1024,512]{1,0:T(8,128)(2,1)S(1)} %dynamic-slice_convert_fusion.2), channel_id=1, source_target_pairs={{0,8},{4,12},{8,0},{12,4},{16,24},{20,28},{24,16},{28,20},{1,9},{5... | collective-permute-start | bytes 3145736 | tf_op jit(solution)/shard_map/ppermute | solution.py:242
  510.2 27.7 %collective-permute-start.11 = (bf16[256,2048]{1,0:T(8,128)(2,1)S(1)}, bf16[256,2048]{1,0:T(8,128)(2,1)S(1)}, u32[]{:S(2)}, u32[]{:S(2)}) collective-permute-start(bf16[256,2048]{1,0:T(8,128)(2,1)S(1)} %pad_maximum_fusion.2), channel_id=1, source_target_pairs={{0,1},{1,0},{2,3},{3,2},{4,5},{5,4},{6,7},{7,6},{8,9},{9,8},{10,11... | collective-permute-start | bytes 3145736 | tf_op jit(solution)/shard_map/ppermute | solution.py:214
  535.9 25.0 %collective-permute-start.14 = (bf16[512,512]{1,0:T(8,128)(2,1)S(1)}, bf16[512,512]{1,0:T(8,128)(2,1)S(1)}, u32[]{:S(2)}, u32[]{:S(2)}) collective-permute-start(bf16[512,512]{1,0:T(8,128)(2,1)S(1)} %dynamic-slice_convert_fusion.6), channel_id=1, source_target_pairs={{0,16},{4,20},{8,24},{12,28},{16,0},{20,4},{24,8},{28,12},{1,17},{... | collective-permute-start | bytes 1572872 | tf_op jit(solution)/shard_map/ppermute | solution.py:242
  578.2 23.5 %collective-permute-start.15 = (bf16[256,2048]{1,0:T(8,128)(2,1)S(1)}, bf16[256,2048]{1,0:T(8,128)(2,1)S(1)}, u32[]{:S(2)}, u32[]{:S(2)}) collective-permute-start(bf16[256,2048]{1,0:T(8,128)(2,1)S(1)} %dynamic-slice_convert_fusion.1), channel_id=1, source_target_pairs={{0,1},{1,0},{2,3},{3,2},{4,5},{5,4},{6,7},{7,6},{8,9},{9,8},{10,11... | collective-permute-start | bytes 3145736 | tf_op jit(solution)/shard_map/ppermute | solution.py:209
  602.1 23.3 %collective-permute-start.16 = (bf16[128,2048]{1,0:T(8,128)(2,1)S(1)}, bf16[128,2048]{1,0:T(8,128)(2,1)S(1)}, u32[]{:S(2)}, u32[]{:S(2)}) collective-permute-start(bf16[128,2048]{1,0:T(8,128)(2,1)S(1)} %dynamic-slice_convert_fusion.5), channel_id=1, source_target_pairs={{0,2},{1,3},{2,0},{3,1},{4,6},{5,7},{6,4},{7,5},{8,10},{9,11},{10,... | collective-permute-start | bytes 1572872 | tf_op jit(solution)/shard_map/ppermute | solution.py:209
  625.5 80.9 %collective-permute-start.17 = (bf16[128,2048]{1,0:T(8,128)(2,1)S(1)}, bf16[128,2048]{1,0:T(8,128)(2,1)S(1)}, u32[]{:S(2)}, u32[]{:S(2)}) collective-permute-start(bf16[128,2048]{1,0:T(8,128)(2,1)S(1)} %add_convert_fusion.1), channel_id=1, source_target_pairs={{0,2},{1,3},{2,0},{3,1},{4,6},{5,7},{6,4},{7,5},{8,10},{9,11},{10,... | collective-permute-start | bytes 1572872 | tf_op jit(solution)/shard_map/ppermute | solution.py:214
  706.5 38.2 %slice-start.6 = ((s8[5767168]{0:T(1024)(128)(4,1)}), s8[4194304]{0:T(1024)(128)(4,1)S(1)}, s32[]{:S(2)}) async-start(s8[5767168]{0:T(1024)(128)(4,1)} %bitcast.74), calls=%async_computation.10 | async-start | bytes 8388608
  706.6 49.3 %collective-permute-start.18 = (bf16[256,2048]{1,0:T(8,128)(2,1)S(1)}, bf16[256,2048]{1,0:T(8,128)(2,1)S(1)}, u32[]{:S(2)}, u32[]{:S(2)}) collective-permute-start(bf16[256,2048]{1,0:T(8,128)(2,1)S(1)} %pad_maximum_fusion.4), channel_id=1, source_target_pairs={{0,1},{1,0},{2,3},{3,2},{4,5},{5,4},{6,7},{7,6},{8,9},{9,8},{10,11... | collective-permute-start | bytes 3145736 | tf_op jit(solution)/shard_map/ppermute | solution.py:214
  708.2 1.2 collective-permute-start.19
  709.3 3.7 collective-permute-start.20
  710.8 3.5 collective-permute-start.24
  713.0 3.7 collective-permute-start.21
  714.3 3.7 collective-permute-start.25
  716.7 14.8 %collective-permute-start.22 = (f32[2048]{0:T(1024)S(1)}, f32[2048]{0:T(1024)S(1)}, u32[]{:S(2)}, u32[]{:S(2)}) collective-permute-start(f32[2048]{0:T(1024)S(1)} %add.353), channel_id=1, source_target_pairs={{0,1},{1,0},{2,3},{3,2},{4,5},{5,4},{6,7},{7,6},{8,9},{9,8},{10,11... | collective-permute-start | bytes 24584 | tf_op jit(solution)/shard_map/ppermute | solution.py:251
  718.0 15.9 %collective-permute-start.26 = (f32[2048]{0:T(1024)S(1)}, f32[2048]{0:T(1024)S(1)}, u32[]{:S(2)}, u32[]{:S(2)}) collective-permute-start(f32[2048]{0:T(1024)S(1)} %add.357), channel_id=1, source_target_pairs={{0,16},{4,20},{8,24},{12,28},{16,0},{20,4},{24,8},{28,12},{1,17},{... | collective-permute-start | bytes 24584 | tf_op jit(solution)/shard_map/ppermute | solution.py:251
  731.5 4.5 collective-permute-start.23
  736.7 8.1 slice-start.7
  736.7 13.2 %slice-start.4 = ((s8[5767168]{0:T(1024)(128)(4,1)}), s8[4194304]{0:T(1024)(128)(4,1)S(1)}, s32[]{:S(2)}) async-start(s8[5767168]{0:T(1024)(128)(4,1)} %bitcast.72), calls=%async_computation.8 | async-start | bytes 8388608
  749.9 8.4 %copy-start.18 = (f32[512,2048]{1,0:T(8,128)S(1)}, f32[512,2048]{1,0:T(8,128)}, u32[]{:S(2)}) copy-start(f32[512,2048]{1,0:T(8,128)} %maximum_convert_fusion.1) | copy-start | bytes 12582916
  814.7 5.8 copy-start.46
  (48 other events, 146.7 us)
Sparse Core Ops, SparseCore 0:
  20.8 39.3 all-gather.2
  132.6 68.9 all-reduce.5
  453.9 252.4 all-reduce.9
  710.4 104.2 all-reduce.7

commit v11 on v6

--- a/solution.py
+++ b/solution.py
@@ -419,15 +419,18 @@
         + right_trans(d_key_low, w_key)
         + right_trans(d_value_low, w_value)
     )
+    unit_normed = source * lax.rsqrt(jnp.mean(source * source, axis=-1, keepdims=True) + EPS)
+    grad_gain_one = jnp.sum(d_normed_part * unit_normed, axis=0)
     (
         down_sum,
         d_normed_part,
+        grad_gain_one,
         grad_w_out,
         grad_w_query,
         grad_w_key,
         grad_w_value,
     ) = lax.optimization_barrier(
-        (down_sum, d_normed_part, grad_w_out, grad_w_query, grad_w_key, grad_w_value)
+        (down_sum, d_normed_part, grad_gain_one, grad_w_out, grad_w_query, grad_w_key, grad_w_value)
     )
     grad_w_out, grad_w_query, grad_w_key, grad_w_value = dp_sum(
         [grad_w_out, grad_w_query, grad_w_key, grad_w_value]
@@ -436,10 +439,10 @@
         grad.astype(jnp.float32) for grad in (grad_w_gate, grad_w_up, grad_w_down)
     ]
     output = (middle + keep_rows * down_sum).astype(jnp.bfloat16)
+    grad_gain_one = permute_allsum(permute_allsum(grad_gain_one, "dp"), "tensor")
     (d_normed,) = permute_sum([d_normed_part], [0], "tensor")
-    d_source_norm, grad_gain_one = norm_one_back(d_normed)
+    d_source_norm, _ = norm_one_back(d_normed)
     grad_input = grad_middle + d_source_norm
-    grad_gain_one = permute_allsum(grad_gain_one, "dp")
     grad_gain_two = permute_allsum(grad_gain_two, "dp")
     grad_w_out, grad_w_query, grad_w_key, grad_w_value = [
         grad.astype(jnp.float32) for grad in (grad_w_out, grad_w_query, grad_w_key, grad_w_value)

time: 793 us -> 771 us (0.972)
  waiting for transfers between devices: 416 us -> 381 us
    psum x2, waiting for transfers between devices: 68.9 us -> 43.1 us  [dp_sum(): return [lax.psum(grad.astype(jnp.bfloat16), 'dp') for grad in grads]]
    ppermute x8, waiting for transfers between devices: 133 us -> 115 us  [permute_sum(): got = lax.ppermute(pieces, axis, partner_perm(size, 1 << step))]
    ppermute x6 -> x8, waiting for transfers between devices: 6.12 us -> 17.4 us  [permute_allsum(): value = value + lax.ppermute(value, axis, partner_perm(size, 1 << step))]
    unnamed x182 -> x172, local copies, waits for them, and re-layouts: 20.2 us -> 20.1 us
  transfers between devices with their start and end apart: 29 -> 31, of which waited for: 24 -> 24; matrix products, arithmetic and copies ran while one was open for 14% -> 14% of each run, Pallas kernels for 9% -> 9%
where the time goes in v11:
time: 771 us; the launch traced here: 765 us
  waiting for transfers between devices  381 us (49%)
  matrix products  120 us (16%)
  other arithmetic  102 us (13%)
  Pallas kernels  68.6 us (9%)
  local copies, waits for them, and re-layouts  40.3 us (5%)
  starting transfers between devices  27.2 us (4%)
  between operations  15.5 us (2%)
  blocking collectives  10.6 us (1%)
    ppermute x8, waiting for transfers between devices, permute_sum(): got = lax.ppermute(send, axis, partner_perm(size, 1 << step))  127 us
    ppermute x8, waiting for transfers between devices, permute_sum(): got = lax.ppermute(pieces, axis, partner_perm(size, 1 << step))  115 us
    pallas_call x1, Pallas kernels, attention_backward(): pl.pallas_call(kernel, grid_spec=grid_spec, out_shape=[jax.ShapeDtypeStru...  68.6 us
    dot_general x11, matrix products, right_trans(): lax.dot_general(left, right, (((1,), (1,)), ((), ())), preferred_element_...  47.4 us
    psum x2, waiting for transfers between devices, dp_sum(): return [lax.psum(grad.astype(jnp.bfloat16), 'dp') for grad in grads]  43.1 us
    dot_general x7, matrix products, left_trans(): lax.dot_general(left, right, (((0,), (0,)), ((), ())), preferred_element_...  31.9 us
    psum x1, waiting for transfers between devices, on_device(): branch_top = lax.psum(branch_part[:sc_rows].astype(jnp.bfloat16), 'tensor')  31 us
    ppermute x3, waiting for transfers between devices, permute_scatter(): got = lax.ppermute(send, axis, partner_perm(size, 1 << step))  29.7 us
  transfers between devices with their start and end apart: 31, of which 24 were waited for; matrix products, arithmetic and copies ran while one was open for 14% of the time, Pallas kernels for 9%

profile of v11, /device:TPU:0, one launch (start us, length us, event | category | flops | bytes accessed | tf_op | source)
XLA Modules:
  0.0 765.5 jit_solution(6170827578975543198)
XLA Ops:
  12.4 3.3 convolution_convert_fusion.1
  22.0 10.6 %all-gather = bf16[8,1,512]{2,1,0:T(2,128)(2,1)S(1)} all-gather(bf16[1,1,512]{2,1,0:T(2,128)(2,1)S(1)} %reshape.288), channel_id=1, replica_groups=mesh['dp'=8,'tensor'=4] {'dp'}, dimensions={0}, use_global_device_ids=true | all-gather | bytes 9216 | tf_op jit(solution)/shard_map/all_gather | solution.py:312
  32.7 3.1 fusion.70
  43.3 18.1 %all-gather.3.cloned.1.call-done.k_ref.v_ref = bf16[4096,512]{1,0:T(8,128)(2,1)} async-done(((bf16[512,512]{1,0:T(8,128)(2,1)}), bf16[4096,512]{1,0:T(8,128)(2,1)}) %all-gather.3.cloned.1.call-update) | async-done | bytes 4194320 | tf_op jit(solution)/shard_map/all_gather | solution.py:309
  61.4 4.6 fusion.76
  67.2 4.6 fusion.77
  73.5 4.6 fusion.78
  79.4 6.9 fusion.79
  86.3 4.6 fusion.2
  90.9 3.2 fusion.22
  94.2 3.4 fusion.23
  97.6 3.4 fusion.24
  101.1 3.4 fusion.25
  104.5 3.3 fusion.56
  112.1 9.8 %collective-permute-done = bf16[96,2048]{1,0:T(8,128)(2,1)S(1)} collective-permute-done((bf16[96,2048]{1,0:T(8,128)(2,1)S(1)}, bf16[96,2048]{1,0:T(8,128)(2,1)S(1)}, u32[]{:S(2)}, u32[]{:S(2)}) %collective-permute-start) | collective-permute-done | bytes 393248 | tf_op jit(solution)/shard_map/ppermute | solution.py:209
  125.6 8.9 %collective-permute-done.1 = bf16[48,2048]{1,0:T(8,128)(2,1)S(1)} collective-permute-done((bf16[48,2048]{1,0:T(8,128)(2,1)S(1)}, bf16[48,2048]{1,0:T(8,128)(2,1)S(1)}, u32[]{:S(2)}, u32[]{:S(2)}) %collective-permute-start.1) | collective-permute-done | bytes 196640 | tf_op jit(solution)/shard_map/ppermute | solution.py:209
  134.6 3.0 slice.195
  137.8 7.8 %collective-permute-done.2 = bf16[48,2048]{1,0:T(8,128)(2,1)S(1)} collective-permute-done((bf16[48,2048]{1,0:T(8,128)(2,1)S(1)}, bf16[48,2048]{1,0:T(8,128)(2,1)S(1)}, u32[]{:S(2)}, u32[]{:S(2)}) %collective-permute-start.2) | collective-permute-done | bytes 196640 | tf_op jit(solution)/shard_map/ppermute | solution.py:214
  145.8 8.3 %fusion.36 = f32[512,1408]{1,0:T(8,128)} fusion(bf16[1408,2048]{1,0:T(8,128)(2,1)} %param.24, bf16[512,2048]{1,0:T(8,128)(2,1)} %param.25, f32[512]{0:T(512)S(1)} %get-tuple-element.102), kind=kOutput, calls=%fused_computation.116 | convolution fusion | flops 2955935744 | bytes 10749952 | tf_op jit(solution)/shard_map/dot_general | solution.py:49
  154.1 20.5 %collective-permute-done.3 = bf16[96,2048]{1,0:T(8,128)(2,1)} collective-permute-done((bf16[96,2048]{1,0:T(8,128)(2,1)S(1)}, bf16[96,2048]{1,0:T(8,128)(2,1)}, u32[]{:S(2)}, u32[]{:S(2)}) %collective-permute-start.3) | collective-permute-done | bytes 393248 | tf_op jit(solution)/shard_map/ppermute | solution.py:214
  175.8 31.0 %all-reduce.6.cloned.1.call-done = bf16[320,2048]{1,0:T(8,128)(2,1)} async-done(((bf16[320,2048]{1,0:T(8,128)(2,1)}), bf16[320,2048]{1,0:T(8,128)(2,1)}) %all-reduce.6.cloned.1.call-update) | async-done | bytes 1310736 | tf_op jit(solution)/shard_map/psum | solution.py:353
  206.8 3.1 multiply_reduce_fusion.2
  209.9 3.3 multiply_convert_fusion.1
  213.3 5.9 fusion.80
  219.2 4.7 multiply_convert_fusion.2
  224.0 3.4 fusion.84
  227.4 5.3 fusion.82
  232.8 5.5 fusion.83
  238.3 5.0 convolution_add_fusion
  243.3 5.2 fusion.34
  248.5 2.7 dynamic-slice_convert_fusion.4
  252.7 23.9 %collective-permute-done.4 = bf16[256,2048]{1,0:T(8,128)(2,1)} collective-permute-done((bf16[256,2048]{1,0:T(8,128)(2,1)}, bf16[256,2048]{1,0:T(8,128)(2,1)}, u32[]{:S(2)}, u32[]{:S(2)}) %collective-permute-start.4) | collective-permute-done | bytes 1048608 | tf_op jit(solution)/shard_map/ppermute | solution.py:209
  283.6 22.4 %collective-permute-done.5 = bf16[128,2048]{1,0:T(8,128)(2,1)} collective-permute-done((bf16[128,2048]{1,0:T(8,128)(2,1)}, bf16[128,2048]{1,0:T(8,128)(2,1)}, u32[]{:S(2)}, u32[]{:S(2)}) %collective-permute-start.5) | collective-permute-done | bytes 524320 | tf_op jit(solution)/shard_map/ppermute | solution.py:209
  307.6 24.4 %collective-permute-done.6 = bf16[128,2048]{1,0:T(8,128)(2,1)S(1)} collective-permute-done((bf16[128,2048]{1,0:T(8,128)(2,1)S(1)}, bf16[128,2048]{1,0:T(8,128)(2,1)S(1)}, u32[]{:S(2)}, u32[]{:S(2)}) %collective-permute-start.6) | collective-permute-done | bytes 524320 | tf_op jit(solution)/shard_map/ppermute | solution.py:214
  339.0 6.3 fusion.81
  345.3 14.1 %collective-permute-done.7 = bf16[256,2048]{1,0:T(8,128)(2,1)} collective-permute-done((bf16[256,2048]{1,0:T(8,128)(2,1)}, bf16[256,2048]{1,0:T(8,128)(2,1)}, u32[]{:S(2)}, u32[]{:S(2)}) %collective-permute-start.7) | collective-permute-done | bytes 1048608 | tf_op jit(solution)/shard_map/ppermute | solution.py:214
  363.2 2.8 multiply_reduce_fusion
  366.1 3.8 convert_add_fusion.1
  372.9 68.6 %shard_map.212 = (f32[512,512]{1,0:T(8,128)S(1)}, f32[4096,256]{1,0:T(8,128)}, f32[4096,256]{1,0:T(8,128)}) custom-call(s32[16]{0:T(128)S(1)} %copy-done.5, s32[2]{0:T(128)S(1)} %dynamic_slice.85.qblock_ref, bf16[512,512]{1,0:T(8,128)(2,1)S(1)} %bitcast.67, bf16[4096,512]{1,0:T(8,128)(2,1)} %all-gather.3.cloned.1.call-done.k_ref.v_ref, ...), custom_call_target="tpu_custom_call" | custom-call | flops 10737418240 | bytes 25165824 | tf_op jit(solution)/shard_map/pallas_call | solution.py:173
  441.5 3.0 constant_dynamic-update-slice_fusion.1
  455.9 5.7 fusion.55
  461.6 15.9 %collective-permute-done.9 = bf16[128,2048]{1,0:T(8,128)(2,1)} collective-permute-done((bf16[128,2048]{1,0:T(8,128)(2,1)}, bf16[128,2048]{1,0:T(8,128)(2,1)}, u32[]{:S(2)}, u32[]{:S(2)}) %collective-permute-start.9) | collective-permute-done | bytes 524320 | tf_op jit(solution)/shard_map/ppermute | solution.py:209
  484.3 20.2 %collective-permute-done.10 = bf16[128,2048]{1,0:T(8,128)(2,1)S(1)} collective-permute-done((bf16[128,2048]{1,0:T(8,128)(2,1)S(1)}, bf16[128,2048]{1,0:T(8,128)(2,1)S(1)}, u32[]{:S(2)}, u32[]{:S(2)}) %collective-permute-start.10) | collective-permute-done | bytes 524320 | tf_op jit(solution)/shard_map/ppermute | solution.py:214
  506.5 2.8 fusion.38
  509.3 15.3 %collective-permute-done.13 = bf16[1024,512]{1,0:T(8,128)(2,1)S(1)} collective-permute-done((bf16[1024,512]{1,0:T(8,128)(2,1)S(1)}, bf16[1024,512]{1,0:T(8,128)(2,1)S(1)}, u32[]{:S(2)}, u32[]{:S(2)}) %collective-permute-start.13) | collective-permute-done | bytes 1048608 | tf_op jit(solution)/shard_map/ppermute | solution.py:242
  526.4 3.3 collective-permute-done.11
  530.3 2.6 maximum_convert_fusion.1
  532.8 14.3 %collective-permute-done.14 = bf16[512,512]{1,0:T(8,128)(2,1)S(1)} collective-permute-done((bf16[512,512]{1,0:T(8,128)(2,1)S(1)}, bf16[512,512]{1,0:T(8,128)(2,1)S(1)}, u32[]{:S(2)}, u32[]{:S(2)}) %collective-permute-start.14) | collective-permute-done | bytes 524320 | tf_op jit(solution)/shard_map/ppermute | solution.py:242
  547.3 36.3 %all-reduce.10.cloned.1.call-done = (bf16[2048,1408]{1,0:T(8,128)(2,1)}, bf16[2048,1408]{1,0:T(8,128)(2,1)}, bf16[1408,2048]{1,0:T(8,128)(2,1)}) async-done(((bf16[2048,1408]{1,0:T(8,128)(2,1)}, bf16[2048,1408]{1,0:T(8,128)(2,1)}, bf16[1408,2048]{1,0:T(8,128)(2,1)}), (bf16[2048,1408]{1,0:T(8,128)(2,1)}, bf16[2048,1408]{1,0:T(8,128)(2,1)}, bf16[1408,2048]{1,0:T(8,128)(2,1)})) %all-reduce.10.cloned.1.call-update) | async-done | bytes 17301520 | tf_op jit(solution)/shard_map/psum | solution.py:367
  584.5 3.6 fusion.54
  588.0 2.8 fusion.53
  594.6 3.8 fusion.43
  600.5 3.8 fusion.9
  606.4 23.0 %collective-permute-done.15 = bf16[256,2048]{1,0:T(8,128)(2,1)S(1)} collective-permute-done((bf16[256,2048]{1,0:T(8,128)(2,1)S(1)}, bf16[256,2048]{1,0:T(8,128)(2,1)S(1)}, u32[]{:S(2)}, u32[]{:S(2)}) %collective-permute-start.15) | collective-permute-done | bytes 1048608 | tf_op jit(solution)/shard_map/ppermute | solution.py:209
  633.2 22.8 %collective-permute-done.16 = bf16[128,2048]{1,0:T(8,128)(2,1)S(1)} collective-permute-done((bf16[128,2048]{1,0:T(8,128)(2,1)S(1)}, bf16[128,2048]{1,0:T(8,128)(2,1)S(1)}, u32[]{:S(2)}, u32[]{:S(2)}) %collective-permute-start.16) | collective-permute-done | bytes 524320 | tf_op jit(solution)/shard_map/ppermute | solution.py:209
  657.5 24.3 %collective-permute-done.17 = bf16[128,2048]{1,0:T(8,128)(2,1)S(1)} collective-permute-done((bf16[128,2048]{1,0:T(8,128)(2,1)S(1)}, bf16[128,2048]{1,0:T(8,128)(2,1)S(1)}, u32[]{:S(2)}, u32[]{:S(2)}) %collective-permute-start.17) | collective-permute-done | bytes 524320 | tf_op jit(solution)/shard_map/ppermute | solution.py:214
  694.7 13.9 %collective-permute-done.22 = f32[2048]{0:T(1024)S(1)} collective-permute-done((f32[2048]{0:T(1024)S(1)}, f32[2048]{0:T(1024)S(1)}, u32[]{:S(2)}, u32[]{:S(2)}) %collective-permute-start.22) | collective-permute-done | bytes 8224 | tf_op jit(solution)/shard_map/ppermute | solution.py:251
  709.7 8.5 %convert_element_type.278 = f32[2048,1408]{1,0:T(8,128)} convert(bf16[2048,1408]{1,0:T(8,128)(2,1)} %get-tuple-element.52) | non-fusion elementwise | flops 2883584 | bytes 17301504 | tf_op jit(solution)/shard_map/convert_element_type | solution.py:439
  718.1 5.2 convert_element_type.279
  723.3 6.0 convert_element_type.280
  729.9 6.8 all-reduce.8.cloned.1.call-done
  736.8 4.3 convert_element_type.271
  744.1 2.7 convert_element_type.277
  750.6 8.1 %fusion.11 = (f32[512,2048]{1,0:T(8,128)}, bf16[512,2048]{1,0:T(8,128)(2,1)}) fusion(f32[512,2048]{1,0:T(8,128)S(1)} %copy-done.13, bf16[512,2048]{1,0:T(8,128)(2,1)S(1)} %copy-done.11, f32[512]{0:T(512)S(1)} %multiply_multiply_fusion, f32[2048]{0:T(1024)S(1)} %copy-done.57, f32[512]{0:T(512)S(1)} %copy-done.60, bf16[256,2048]{1,0:T(8,128)(2,1)S(1)} %get-tuple-element.74, ...), kind=kLoop, calls=%fused_computation.34 | loop fusion | flops 23068672 | bytes 20985856 | tf_op jit(solution)/shard_map/add | solution.py:445
  (317 shorter events, 114.0 us)
Async XLA Ops:
  7.2 25.5 %copy-start = (bf16[2048,512]{1,0:T(8,128)(2,1)S(1)}, bf16[2048,512]{1,0:T(8,128)(2,1)}, u32[]{:S(2)}) copy-start(bf16[2048,512]{1,0:T(8,128)(2,1)} %param.17) | copy-start | bytes 6291460
  7.2 8.5 %copy-start.48 = (bf16[2048,256]{1,0:T(8,128)(2,1)S(1)}, bf16[2048,256]{1,0:T(8,128)(2,1)}, u32[]{:S(2)}) copy-start(bf16[2048,256]{1,0:T(8,128)(2,1)} %param.18) | copy-start | bytes 3145732
  7.2 54.2 %all-gather.3.cloned.1.call-start = ((), (), s32[]{:S(2)}) async-start(), calls=%async_computation | async-start | bytes 4718592 | tf_op jit(solution)/shard_map/all_gather | solution.py:309
  7.3 8.4 %copy-start.6 = (bf16[512,2048]{1,0:T(8,128)(2,1)S(1)}, bf16[512,2048]{1,0:T(8,128)(2,1)}, u32[]{:S(2)}) copy-start(bf16[512,2048]{1,0:T(8,128)(2,1)} %param.13) | copy-start | bytes 6291460
  11.0 21.7 %copy-start.59 = (f32[512]{0:T(512)}, f32[512]{0:T(512)S(1)}, u32[]{:S(2)}) copy-start(f32[512]{0:T(512)S(1)} %fusion.60) | copy-start | bytes 6148
  11.7 21.0 %copy-start.56 = (f32[2048]{0:T(1024)}, f32[2048]{0:T(1024)S(1)}, u32[]{:S(2)}) copy-start(f32[2048]{0:T(1024)S(1)} %convert_element_type.216) | copy-start | bytes 24580
  19.0 21.7 %copy-start.23 = (f32[512,64]{1,0:T(8,128)}, f32[512,64]{1,0:T(8,128)S(1)}, u32[]{:S(2)}) copy-start(f32[512,64]{1,0:T(8,128)S(1)} %get-tuple-element.101) | copy-start | bytes 393220
  21.9 184.9 %all-reduce.6.cloned.1.call-start = ((), (), s32[]{:S(2)}) async-start(), calls=%async_computation.1 | async-start | bytes 2621440 | tf_op jit(solution)/shard_map/psum | solution.py:353
  43.3 36.1 %copy-start.2 = (bf16[64,8,4,128]{3,1,2,0:T(8,128)(2,1)}, bf16[64,8,4,128]{3,1,2,0:T(8,128)(2,1)S(1)}, u32[]{:S(2)}) copy-start(bf16[64,8,4,128]{3,1,2,0:T(8,128)(2,1)S(1)} %copy.92) | copy-start | bytes 1572868
  94.2 10.3 %copy-start.49 = (bf16[512,128]{0,1:T(8,128)(2,1)}, bf16[512,128]{0,1:T(8,128)(2,1)S(1)}, u32[]{:S(2)}) copy-start(bf16[512,128]{0,1:T(8,128)(2,1)S(1)} %fusion.22) | copy-start | bytes 393220
  94.2 6.8 slice-start
  97.6 6.9 copy-start.51
  110.5 11.3 %collective-permute-start = (bf16[96,2048]{1,0:T(8,128)(2,1)S(1)}, bf16[96,2048]{1,0:T(8,128)(2,1)S(1)}, u32[]{:S(2)}, u32[]{:S(2)}) collective-permute-start(bf16[96,2048]{1,0:T(8,128)(2,1)S(1)} %dynamic-slice_convert_fusion.9), channel_id=1, source_target_pairs={{0,1},{1,0},{2,3},{3,2},{4,5},{5,4},{6,7},{7,6},{8,9},{9,8},{10,11... | collective-permute-start | bytes 1179656 | tf_op jit(solution)/shard_map/ppermute | solution.py:209
  123.1 11.4 %collective-permute-start.1 = (bf16[48,2048]{1,0:T(8,128)(2,1)S(1)}, bf16[48,2048]{1,0:T(8,128)(2,1)S(1)}, u32[]{:S(2)}, u32[]{:S(2)}) collective-permute-start(bf16[48,2048]{1,0:T(8,128)(2,1)S(1)} %dynamic-slice_convert_fusion.10), channel_id=1, source_target_pairs={{0,2},{1,3},{2,0},{3,1},{4,6},{5,7},{6,4},{7,5},{8,10},{9,11},{10,... | collective-permute-start | bytes 589832 | tf_op jit(solution)/shard_map/ppermute | solution.py:209
  134.5 11.1 %collective-permute-start.2 = (bf16[48,2048]{1,0:T(8,128)(2,1)S(1)}, bf16[48,2048]{1,0:T(8,128)(2,1)S(1)}, u32[]{:S(2)}, u32[]{:S(2)}) collective-permute-start(bf16[48,2048]{1,0:T(8,128)(2,1)S(1)} %add_convert_fusion.8), channel_id=1, source_target_pairs={{0,2},{1,3},{2,0},{3,1},{4,6},{5,7},{6,4},{7,5},{8,10},{9,11},{10,... | collective-permute-start | bytes 589832 | tf_op jit(solution)/shard_map/ppermute | solution.py:214
  137.6 446.0 %all-reduce.10.cloned.1.call-start = ((), (), s32[]{:S(2)}) async-start(), calls=%async_computation.3 | async-start | bytes 34603008 | tf_op jit(solution)/shard_map/psum | solution.py:367
  145.7 28.9 %collective-permute-start.3 = (bf16[96,2048]{1,0:T(8,128)(2,1)S(1)}, bf16[96,2048]{1,0:T(8,128)(2,1)}, u32[]{:S(2)}, u32[]{:S(2)}) collective-permute-start(bf16[96,2048]{1,0:T(8,128)(2,1)S(1)} %pad_maximum_fusion.9), channel_id=1, source_target_pairs={{0,1},{1,0},{2,3},{3,2},{4,5},{5,4},{6,7},{7,6},{8,9},{9,8},{10,11... | collective-permute-start | bytes 1179656 | tf_op jit(solution)/shard_map/ppermute | solution.py:214
  145.8 8.3 %copy-start.63 = (bf16[2048]{0:T(1024)(128)(2,1)S(1)}, bf16[2048]{0:T(1024)(128)(2,1)}, u32[]{:S(2)}) copy-start(bf16[2048]{0:T(1024)(128)(2,1)} %param.21) | copy-start | bytes 12292
  175.8 190.3 %copy-start.18 = (bf16[96,2048]{1,0:T(8,128)(2,1)}, bf16[96,2048]{1,0:T(8,128)(2,1)S(1)}, u32[]{:S(2)}) copy-start(bf16[96,2048]{1,0:T(8,128)(2,1)S(1)} %get-tuple-element.93) | copy-start | bytes 1179652
  175.8 190.3 %copy-start.20 = (bf16[96,2048]{1,0:T(8,128)(2,1)}, bf16[96,2048]{1,0:T(8,128)(2,1)S(1)}, u32[]{:S(2)}) copy-start(bf16[96,2048]{1,0:T(8,128)(2,1)S(1)} %get-tuple-element.94) | copy-start | bytes 1179652
  209.9 9.3 %slice-start.6 = ((s8[5767168]{0:T(1024)(128)(4,1)}), s8[4194304]{0:T(1024)(128)(4,1)S(1)}, s32[]{:S(2)}) async-start(s8[5767168]{0:T(1024)(128)(4,1)} %bitcast.101), calls=%async_computation.10 | async-start | bytes 8388608
  213.3 6.0 slice-start.7
  213.3 6.0 copy-start.65
  223.9 19.3 %copy-start.66 = (bf16[512,1408]{1,0:T(8,128)(2,1)}, bf16[512,1408]{1,0:T(8,128)(2,1)S(1)}, u32[]{:S(2)}) copy-start(bf16[512,1408]{1,0:T(8,128)(2,1)S(1)} %get-tuple-element.68) | copy-start | bytes 4325380
  227.4 10.9 %slice-start.8 = ((s8[5767168]{0:T(1024)(128)(4,1)}), s8[4194304]{0:T(1024)(128)(4,1)S(1)}, s32[]{:S(2)}) async-start(s8[5767168]{0:T(1024)(128)(4,1)} %bitcast.103), calls=%async_computation.12 | async-start | bytes 8388608
  248.5 34.1 %copy-start.5 = (s32[16]{0:T(128)S(1)}, s32[16]{0:T(128)}, u32[]{:S(2)}) copy-start(s32[16]{0:T(128)} %chunk_ref.1) | copy-start | bytes 196
  248.5 34.2 %copy-start.58 = (s32[1,1,16,256]{3,2,1,0:T(8,128)S(1)}, s32[1,1,16,256]{3,2,1,0:T(8,128)}, u32[]{:S(2)}) copy-start(s32[1,1,16,256]{3,2,1,0:T(8,128)} %get-tuple-element.104) | copy-start | bytes 49156
  251.2 25.4 %collective-permute-start.4 = (bf16[256,2048]{1,0:T(8,128)(2,1)}, bf16[256,2048]{1,0:T(8,128)(2,1)}, u32[]{:S(2)}, u32[]{:S(2)}) collective-permute-start(bf16[256,2048]{1,0:T(8,128)(2,1)} %dynamic-slice_convert_fusion.4), channel_id=1, source_target_pairs={{0,1},{1,0},{2,3},{3,2},{4,5},{5,4},{6,7},{7,6},{8,9},{9,8},{10,11... | collective-permute-start | bytes 3145736 | tf_op jit(solution)/shard_map/ppermute | solution.py:209
  281.0 25.0 %collective-permute-start.5 = (bf16[128,2048]{1,0:T(8,128)(2,1)}, bf16[128,2048]{1,0:T(8,128)(2,1)}, u32[]{:S(2)}, u32[]{:S(2)}) collective-permute-start(bf16[128,2048]{1,0:T(8,128)(2,1)} %dynamic-slice_convert_fusion.8), channel_id=1, source_target_pairs={{0,2},{1,3},{2,0},{3,1},{4,6},{5,7},{6,4},{7,5},{8,10},{9,11},{10,... | collective-permute-start | bytes 1572872 | tf_op jit(solution)/shard_map/ppermute | solution.py:209
  307.5 24.6 %collective-permute-start.6 = (bf16[128,2048]{1,0:T(8,128)(2,1)S(1)}, bf16[128,2048]{1,0:T(8,128)(2,1)S(1)}, u32[]{:S(2)}, u32[]{:S(2)}) collective-permute-start(bf16[128,2048]{1,0:T(8,128)(2,1)S(1)} %add_convert_fusion.4), channel_id=1, source_target_pairs={{0,2},{1,3},{2,0},{3,1},{4,6},{5,7},{6,4},{7,5},{8,10},{9,11},{10,... | collective-permute-start | bytes 1572872 | tf_op jit(solution)/shard_map/ppermute | solution.py:214
  334.0 25.4 %collective-permute-start.7 = (bf16[256,2048]{1,0:T(8,128)(2,1)}, bf16[256,2048]{1,0:T(8,128)(2,1)}, u32[]{:S(2)}, u32[]{:S(2)}) collective-permute-start(bf16[256,2048]{1,0:T(8,128)(2,1)} %pad_maximum_fusion.1), channel_id=1, source_target_pairs={{0,1},{1,0},{2,3},{3,2},{4,5},{5,4},{6,7},{7,6},{8,9},{9,8},{10,11... | collective-permute-start | bytes 3145736 | tf_op jit(solution)/shard_map/ppermute | solution.py:214
  338.9 397.9 %all-reduce.8.cloned.1.call-start = ((), (), s32[]{:S(2)}) async-start(), calls=%async_computation.2 | async-start | bytes 12582912 | tf_op jit(solution)/shard_map/psum | solution.py:367
  339.0 20.4 %copy-start.32 = (bf16[128,2048]{1,0:T(8,128)(2,1)S(1)}, bf16[128,2048]{1,0:T(8,128)(2,1)}, u32[]{:S(2)}) copy-start(bf16[128,2048]{1,0:T(8,128)(2,1)} %copy-done.31) | copy-start | bytes 1572868
  339.0 20.4 %copy-start.34 = (bf16[128,2048]{1,0:T(8,128)(2,1)S(1)}, bf16[128,2048]{1,0:T(8,128)(2,1)}, u32[]{:S(2)}) copy-start(bf16[128,2048]{1,0:T(8,128)(2,1)} %copy-done.33) | copy-start | bytes 1572868
  372.2 76.4 %collective-permute-start.8 = (bf16[256,2048]{1,0:T(8,128)(2,1)S(1)}, bf16[256,2048]{1,0:T(8,128)(2,1)S(1)}, u32[]{:S(2)}, u32[]{:S(2)}) collective-permute-start(bf16[256,2048]{1,0:T(8,128)(2,1)S(1)} %dynamic-slice_convert_fusion.3), channel_id=1, source_target_pairs={{0,1},{1,0},{2,3},{3,2},{4,5},{5,4},{6,7},{7,6},{8,9},{9,8},{10,11... | collective-permute-start | bytes 3145736 | tf_op jit(solution)/shard_map/ppermute | solution.py:209
  448.6 7.3 copy-start.50
  448.6 7.3 copy-start.52
  448.6 30.6 %collective-permute-start.12 = (bf16[2048,512]{1,0:T(8,128)(2,1)}, bf16[2048,512]{1,0:T(8,128)(2,1)}, u32[]{:S(2)}, u32[]{:S(2)}) collective-permute-start(bf16[2048,512]{1,0:T(8,128)(2,1)} %dynamic-slice_convert_fusion), channel_id=1, source_target_pairs={{0,4},{4,0},{8,12},{12,8},{16,20},{20,16},{24,28},{28,24},{1,5},{5... | collective-permute-start | bytes 6291464 | tf_op jit(solution)/shard_map/ppermute | solution.py:242
  452.2 25.3 %collective-permute-start.9 = (bf16[128,2048]{1,0:T(8,128)(2,1)}, bf16[128,2048]{1,0:T(8,128)(2,1)}, u32[]{:S(2)}, u32[]{:S(2)}) collective-permute-start(bf16[128,2048]{1,0:T(8,128)(2,1)} %dynamic-slice_convert_fusion.7), channel_id=1, source_target_pairs={{0,2},{1,3},{2,0},{3,1},{4,6},{5,7},{6,4},{7,5},{8,10},{9,11},{10,... | collective-permute-start | bytes 1572872 | tf_op jit(solution)/shard_map/ppermute | solution.py:209
  455.9 23.2 %copy-start.26 = (f32[4096,512]{1,0:T(8,128)S(1)}, f32[4096,512]{1,0:T(8,128)}, u32[]{:S(2)}) copy-start(f32[4096,512]{1,0:T(8,128)} %copy-done.25) | copy-start | bytes 25165828
  479.1 25.5 %collective-permute-start.10 = (bf16[128,2048]{1,0:T(8,128)(2,1)S(1)}, bf16[128,2048]{1,0:T(8,128)(2,1)S(1)}, u32[]{:S(2)}, u32[]{:S(2)}) collective-permute-start(bf16[128,2048]{1,0:T(8,128)(2,1)S(1)} %add_convert_fusion.3), channel_id=1, source_target_pairs={{0,2},{1,3},{2,0},{3,1},{4,6},{5,7},{6,4},{7,5},{8,10},{9,11},{10,... | collective-permute-start | bytes 1572872 | tf_op jit(solution)/shard_map/ppermute | solution.py:214
  481.6 23.3 %copy-start.22 = (f32[512,4,128]{2,1,0:T(4,128)S(1)}, f32[512,4,128]{2,1,0:T(4,128)}, u32[]{:S(2)}) copy-start(f32[512,4,128]{2,1,0:T(4,128)} %reshape.285) | copy-start | bytes 3145732
  481.6 23.3 %copy-start.24 = (f32[512,64]{1,0:T(8,128)S(1)}, f32[512,64]{1,0:T(8,128)}, u32[]{:S(2)}) copy-start(f32[512,64]{1,0:T(8,128)} %copy-done.23) | copy-start | bytes 393220
  481.6 23.3 %copy-start.36 = (f32[512,64]{1,0:T(8,128)S(1)}, f32[512,64]{1,0:T(8,128)}, u32[]{:S(2)}) copy-start(f32[512,64]{1,0:T(8,128)} %get-tuple-element.99) | copy-start | bytes 393220
  481.8 42.8 %collective-permute-start.13 = (bf16[1024,512]{1,0:T(8,128)(2,1)S(1)}, bf16[1024,512]{1,0:T(8,128)(2,1)S(1)}, u32[]{:S(2)}, u32[]{:S(2)}) collective-permute-start(bf16[1024,512]{1,0:T(8,128)(2,1)S(1)} %dynamic-slice_convert_fusion.2), channel_id=1, source_target_pairs={{0,8},{4,12},{8,0},{12,4},{16,24},{20,28},{24,16},{28,20},{1,9},{5... | collective-permute-start | bytes 3145736 | tf_op jit(solution)/shard_map/ppermute | solution.py:242
  504.8 24.9 %collective-permute-start.11 = (bf16[256,2048]{1,0:T(8,128)(2,1)S(1)}, bf16[256,2048]{1,0:T(8,128)(2,1)S(1)}, u32[]{:S(2)}, u32[]{:S(2)}) collective-permute-start(bf16[256,2048]{1,0:T(8,128)(2,1)S(1)} %pad_maximum_fusion.2), channel_id=1, source_target_pairs={{0,1},{1,0},{2,3},{3,2},{4,5},{5,4},{6,7},{7,6},{8,9},{9,8},{10,11... | collective-permute-start | bytes 3145736 | tf_op jit(solution)/shard_map/ppermute | solution.py:214
  525.0 22.2 %collective-permute-start.14 = (bf16[512,512]{1,0:T(8,128)(2,1)S(1)}, bf16[512,512]{1,0:T(8,128)(2,1)S(1)}, u32[]{:S(2)}, u32[]{:S(2)}) collective-permute-start(bf16[512,512]{1,0:T(8,128)(2,1)S(1)} %dynamic-slice_convert_fusion.6), channel_id=1, source_target_pairs={{0,16},{4,20},{8,24},{12,28},{16,0},{20,4},{24,8},{28,12},{1,17},{... | collective-permute-start | bytes 1572872 | tf_op jit(solution)/shard_map/ppermute | solution.py:242
  604.4 25.0 %collective-permute-start.15 = (bf16[256,2048]{1,0:T(8,128)(2,1)S(1)}, bf16[256,2048]{1,0:T(8,128)(2,1)S(1)}, u32[]{:S(2)}, u32[]{:S(2)}) collective-permute-start(bf16[256,2048]{1,0:T(8,128)(2,1)S(1)} %dynamic-slice_convert_fusion.1), channel_id=1, source_target_pairs={{0,1},{1,0},{2,3},{3,2},{4,5},{5,4},{6,7},{7,6},{8,9},{9,8},{10,11... | collective-permute-start | bytes 3145736 | tf_op jit(solution)/shard_map/ppermute | solution.py:209
  631.0 25.0 %collective-permute-start.16 = (bf16[128,2048]{1,0:T(8,128)(2,1)S(1)}, bf16[128,2048]{1,0:T(8,128)(2,1)S(1)}, u32[]{:S(2)}, u32[]{:S(2)}) collective-permute-start(bf16[128,2048]{1,0:T(8,128)(2,1)S(1)} %dynamic-slice_convert_fusion.5), channel_id=1, source_target_pairs={{0,2},{1,3},{2,0},{3,1},{4,6},{5,7},{6,4},{7,5},{8,10},{9,11},{10,... | collective-permute-start | bytes 1572872 | tf_op jit(solution)/shard_map/ppermute | solution.py:209
  657.5 24.4 %collective-permute-start.17 = (bf16[128,2048]{1,0:T(8,128)(2,1)S(1)}, bf16[128,2048]{1,0:T(8,128)(2,1)S(1)}, u32[]{:S(2)}, u32[]{:S(2)}) collective-permute-start(bf16[128,2048]{1,0:T(8,128)(2,1)S(1)} %add_convert_fusion.1), channel_id=1, source_target_pairs={{0,2},{1,3},{2,0},{3,1},{4,6},{5,7},{6,4},{7,5},{8,10},{9,11},{10,... | collective-permute-start | bytes 1572872 | tf_op jit(solution)/shard_map/ppermute | solution.py:214
  682.0 36.2 %slice-start.4 = ((s8[5767168]{0:T(1024)(128)(4,1)}), s8[4194304]{0:T(1024)(128)(4,1)S(1)}, s32[]{:S(2)}) async-start(s8[5767168]{0:T(1024)(128)(4,1)} %bitcast.74), calls=%async_computation.8 | async-start | bytes 8388608
  683.0 63.8 %collective-permute-start.18 = (bf16[256,2048]{1,0:T(8,128)(2,1)}, bf16[256,2048]{1,0:T(8,128)(2,1)}, u32[]{:S(2)}, u32[]{:S(2)}) collective-permute-start(bf16[256,2048]{1,0:T(8,128)(2,1)} %pad_maximum_fusion.4), channel_id=1, source_target_pairs={{0,1},{1,0},{2,3},{3,2},{4,5},{5,4},{6,7},{7,6},{8,9},{9,8},{10,11... | collective-permute-start | bytes 3145736 | tf_op jit(solution)/shard_map/ppermute | solution.py:214
  683.0 1.2 collective-permute-start.19
  684.2 3.9 collective-permute-start.20
  686.5 2.5 collective-permute-start.24
  688.1 3.7 collective-permute-start.21
  689.0 4.8 collective-permute-start.25
  691.8 16.8 %collective-permute-start.22 = (f32[2048]{0:T(1024)S(1)}, f32[2048]{0:T(1024)S(1)}, u32[]{:S(2)}, u32[]{:S(2)}) collective-permute-start(f32[2048]{0:T(1024)S(1)} %add.353), channel_id=1, source_target_pairs={{0,1},{1,0},{2,3},{3,2},{4,5},{5,4},{6,7},{7,6},{8,9},{9,8},{10,11... | collective-permute-start | bytes 24584 | tf_op jit(solution)/shard_map/ppermute | solution.py:251
  693.8 15.3 %collective-permute-start.26 = (f32[2048]{0:T(1024)S(1)}, f32[2048]{0:T(1024)S(1)}, u32[]{:S(2)}, u32[]{:S(2)}) collective-permute-start(f32[2048]{0:T(1024)S(1)} %add.357), channel_id=1, source_target_pairs={{0,16},{4,20},{8,24},{12,28},{16,0},{20,4},{24,8},{28,12},{1,17},{... | collective-permute-start | bytes 24584 | tf_op jit(solution)/shard_map/ppermute | solution.py:251
  708.5 20.8 %collective-permute-start.23 = (f32[2048]{0:T(1024)S(1)}, f32[2048]{0:T(1024)S(1)}, u32[]{:S(2)}, u32[]{:S(2)}) collective-permute-start(f32[2048]{0:T(1024)S(1)} %add.354), channel_id=1, source_target_pairs={{0,2},{1,3},{2,0},{3,1},{4,6},{5,7},{6,4},{7,5},{8,10},{9,11},{10,... | collective-permute-start | bytes 24584 | tf_op jit(solution)/shard_map/ppermute | solution.py:251
  709.7 8.5 %slice-start.5 = ((s8[5767168]{0:T(1024)(128)(4,1)}), s8[1572864]{0:T(1024)(128)(4,1)S(1)}, s32[]{:S(2)}) async-start(s8[5767168]{0:T(1024)(128)(4,1)} %bitcast.74), calls=%async_computation.9 | async-start | bytes 3145728
  709.7 13.6 %slice-start.2 = ((s8[5767168]{0:T(1024)(128)(4,1)}), s8[4194304]{0:T(1024)(128)(4,1)S(1)}, s32[]{:S(2)}) async-start(s8[5767168]{0:T(1024)(128)(4,1)} %bitcast.72), calls=%async_computation.6 | async-start | bytes 8388608
  736.8 5.8 copy-start.45
  744.1 6.0 copy-start.17
  (44 other events, 130.9 us)
Sparse Core Ops, SparseCore 0:
  22.0 39.2 all-gather.2
  137.7 68.9 all-reduce.5
  339.0 244.5 all-reduce.9
  633.4 103.3 all-reduce.7
